TPU v7x, 256 devices: a whole 4x4x8 slice. The times are simulated.
256 devices in a mesh: gx: 32 (over y, z_hi, core), gz: 8 (over z_lo, x).
Axes of the slice: x: 4, y: 4, z: 8 (z_hi: 4, z_lo: 2; z = z_hi * 2 + z_lo), core: 2. Of those that a mesh axis runs over, the one named last changes fastest.
Arguments:
- scalars: float32 [2, 4096, 128, 256], P(None, 'gx', 'gz'), may hold values from -6 to 6
- diffusivity: float32 [4096, 128, 256], P('gx', 'gz'), may hold values from 0.01 to 0.1
- reaction_rate: float32 [4096, 128, 256], P('gx', 'gz'), may hold values from 0.05 to 1
- block_inverse: float32 [2, 32, 128, 128], P(None, 'gx'), may hold values from 0 to 1
- block_response: float32 [2, 32, 128], P(None, 'gx'), may hold values from 0 to 1, as said below
- mean_profile: float32 [2, 256], replicated, may hold values from -4 to 4
- recycle_gain: float32 [2, 256], replicated, may hold values from 0.5 to 1.5
- station_index: int32 [1], replicated, may hold values from 0 to 4095
- span_shift: int32 [1], replicated, may hold values from 0 to 127
Outputs:
- transported: float32 [2, 4096, 128, 256], P(None, 'gx', 'gz')
Inputs may be any that keep to these rules, and one draw needn't show every extreme that they name: `block_response`: every entry is positive.
All inputs are finite; a program needn't handle non-finite values.
Results may differ from a plain program's by a relative error of at most 0.0003.
Values sent between devices are 32-bit elements; how exact they have to be, the bound alone decides.
No kernel may reach another device: no remote copies, remote signals or barrier semaphores. Data moves between devices by JAX's collectives and lax.ppermute only.
A program may use at most 64 MiB of HBM per device.

v0:
```python
import jax
import jax.numpy as jnp
from jax import lax
from jax.sharding import PartitionSpec as P

reaction_yields = (-1.0, 1.0)


def from_root(x, axis, root):
    mine = lax.axis_index(axis) == root
    return lax.psum(jnp.where(mine, x, jnp.zeros_like(x)), axis)


def with_halo(x, sides, width, wrap):
    for axis, dim in sides:
        devices, length = (lax.axis_size(axis), x.shape[dim])
        up = [(i, (i + 1) % devices) for i in range(devices if wrap else devices - 1)]
        down = [(j, i) for i, j in up]
        last = lax.slice_in_dim(x, length - width, length, axis=dim)
        first = lax.slice_in_dim(x, 0, width, axis=dim)
        before = lax.ppermute(last, axis, up)
        after = lax.ppermute(first, axis, down)
        x = jnp.concatenate([before, x, after], axis=dim)
    return x


def prefix(part, axis, combine, identity):
    place = lax.axis_index(axis)
    gathered = jax.tree.map(lambda a: lax.all_gather(a, axis), part)
    state = jax.tree.map(lambda a, e: jnp.zeros_like(a) + jnp.asarray(e, a.dtype), part, identity)

    def one(hop, state):
        return combine(
            state, jax.tree.map(lambda a: lax.dynamic_index_in_dim(a, hop, 0, False), gathered)
        )

    return lax.fori_loop(0, place, one, state)


def fourth_order(padded, dimension, length):

    def shifted(offset):
        return lax.slice_in_dim(padded, offset, offset + length, axis=dimension)

    return (
        -shifted(0) + 16.0 * shifted(1) - 30.0 * shifted(2) + 16.0 * shifted(3) - shifted(4)
    ) / 12.0


def make_inflow(station_plane, mean_profile, recycle_gain, span_shift):
    span_mean = jnp.mean(station_plane, axis=1, keepdims=True)
    rolled = jnp.roll(station_plane, span_shift[0], axis=1)
    return mean_profile[:, None, :] + recycle_gain[:, None, :] * (rolled - span_mean)


def explicit_part(stream_padded, span_padded, center, diffusivity, reaction_rate):
    wall_padded = jnp.pad(center, ((0, 0), (0, 0), (0, 0), (2, 2)))
    laplacian = fourth_order(stream_padded, 1, center.shape[1])
    laplacian = laplacian + fourth_order(span_padded, 2, center.shape[2])
    laplacian = laplacian + fourth_order(wall_padded, 3, center.shape[3])
    reaction = reaction_rate * jax.nn.softplus(center[0]) * jax.nn.softplus(center[1])
    source = jnp.stack([reaction_yields[0] * reaction, reaction_yields[1] * reaction])
    return center + diffusivity[None] * laplacian + source


def on_device(
    scalars,
    diffusivity,
    reaction_rate,
    block_inverse,
    block_response,
    mean_profile,
    recycle_gain,
    station_index,
    span_shift,
):
    plane_count = scalars.shape[1]
    span_cells = scalars.shape[2]
    stream_devices = lax.axis_size("gx")
    stream_rank = lax.axis_index("gx")
    span_rank = lax.axis_index("gz")
    owner_row = station_index[0] // plane_count
    local_plane = station_index[0] - owner_row * plane_count
    own_slice = lax.dynamic_index_in_dim(scalars, local_plane, 1, keepdims=False)
    arrived = from_root(own_slice, "gx", owner_row)
    station_plane = lax.all_gather(arrived, "gz", axis=1, tiled=True)
    inflow_full = make_inflow(station_plane, mean_profile, recycle_gain, span_shift)
    inflow = lax.dynamic_slice_in_dim(inflow_full, span_rank * span_cells, span_cells, 1)
    stream_padded = with_halo(scalars, (("gx", 1),), 2, False)
    edge_shape = (scalars.shape[0], 2, scalars.shape[2], scalars.shape[3])
    inlet_planes = jnp.broadcast_to(inflow[:, None], edge_shape)
    outlet_planes = jnp.broadcast_to(scalars[:, -1:], edge_shape)
    head_planes = jnp.where(stream_rank == 0, inlet_planes, stream_padded[:, :2])
    tail_planes = jnp.where(stream_rank == stream_devices - 1, outlet_planes, stream_padded[:, -2:])
    window = jnp.concatenate([head_planes, stream_padded[:, 2:-2], tail_planes], axis=1)
    span_padded = with_halo(scalars, (("gz", 2),), 2, True)
    explicit = explicit_part(window, span_padded, scalars, diffusivity, reaction_rate)
    local_part = jnp.einsum(
        "sij,sjzy->sizy", block_inverse[:, 0], explicit, precision=lax.Precision.HIGHEST
    )
    response = block_response[:, 0]
    exit_plane = local_part[:, -1]
    exit_ratio = response[:, -1]

    def compose(earlier_part, later_part):
        return (
            earlier_part[0] * later_part[0],
            later_part[0][:, None, None] * earlier_part[1] + later_part[1],
        )

    identity = (jnp.ones_like(exit_ratio), jnp.zeros_like(exit_plane))
    through, upstream_sum = prefix((exit_ratio, exit_plane), "gx", compose, identity)
    incoming = through[:, None, None] * inflow + upstream_sum
    return local_part + response[:, :, None, None] * incoming[:, None]


def solution(mesh):
    return jax.shard_map(
        on_device,
        mesh=mesh,
        in_specs=(
            P(None, "gx", "gz", None),
            P("gx", "gz", None),
            P("gx", "gz", None),
            P(None, "gx", None, None),
            P(None, "gx", None),
            P(),
            P(),
            P(),
            P(),
        ),
        out_specs=P(None, "gx", "gz", None),
        check_vma=False,
    )
```

profile of v0, /device:TPU:217, one launch (start us, length us, event | category | flops | bytes accessed | tf_op | source)
XLA Modules:
  0.0 334.0 jit_solution(15417572126514026074)
XLA Ops:
  6.5 1.6 fusion.48
  8.1 1.3 collective-permute-start
  9.4 3.8 %collective-permute-start.1 = (f32[2,2,16,256]{3,2,1,0:T(8,128)}, f32[2,2,16,256]{3,2,1,0:T(8,128)}, u32[]{:S(2)}, u32[]{:S(2)}) collective-permute-start(f32[2,2,16,256]{3,2,1,0:T(8,128)} %get-tuple-element.62), channel_id=1, source_target_pairs={{8,0},{16,8},{24,16},{32,24},{40,32},{48,40},{56,48},{64,56},{72,6... | collective-permute-start | bytes 196616 | tf_op jit(solution)/shard_map/ppermute | solution.py:22
  13.3 3.6 %fusion.47 = (f32[2,128,2,256]{3,2,1,0:T(2,128)}, f32[2,128,2,256]{3,2,1,0:T(2,128)}) fusion(f32[2,128,16,256]{3,2,1,0:T(8,128)} %param.11), kind=kLoop, calls=%fused_computation.82 | loop fusion | bytes 2097152 | tf_op jit(solution)/shard_map/slice | solution.py:20
  16.9 2.9 collective-permute-start.3
  21.1 1.4 slice_bitcast_fusion
  22.5 0.9 slice_reduce_fusion
  24.2 1.3 dynamic-slice
  26.3 137.6 %all-reduce.2 = (f32[2,16,256]{2,1,0:T(8,128)S(1)}, f32[64]{0:T(128)S(1)}) all-reduce(f32[2,16,256]{2,1,0:T(8,128)S(1)} %fusion.44, f32[64]{0:T(128)S(1)} %dynamic-update-slice), channel_id=1, replica_groups=mesh['gx'=32,'gz'=8] {'gx'}, use_global_device_ids=true, to_apply=%region_0.1 | all-reduce | flops 8256 | bytes 66048 | tf_op jit(solution)/shard_map/psum | solution.py:11
  163.9 22.5 %all_gather.9 = f32[2,128,256]{2,1,0:T(8,128)S(1)} all-gather(f32[2,16,256]{2,1,0:T(8,128)S(1)} %get-tuple-element.53), channel_id=1, replica_groups=mesh['gx'=32,'gz'=8] {'gz'}, dimensions={1}, use_global_device_ids=true | all-gather | bytes 294912 | tf_op jit(solution)/shard_map/all_gather | solution.py:86
  186.5 6.7 %multiply_bitcast_fusion = (f32[1,128,16,256]{3,2,1,0:T(8,128)S(1)}, f32[128,16,256]{2,1,0:T(8,128)}) fusion(f32[2,128,16,256]{3,2,1,0:T(8,128)} %param.11, f32[128,16,256]{2,1,0:T(8,128)} %param.13), kind=kLoop, calls=%fused_computation.64 | loop fusion | flops 7864320 | bytes 10485760 | tf_op jit(solution)/shard_map/stack | solution.py:62
  193.1 1.6 broadcast_multiply_fusion
  195.4 4.7 %constant_dynamic-update-slice_fusion.1 = f32[2,128,18,256]{3,2,1,0:T(8,128)} fusion(f32[2,128,16,256]{3,2,1,0:T(8,128)} %param.11), kind=kLoop, calls=%fused_computation.78 | loop fusion | bytes 8388608
  200.0 0.9 broadcast_select_fusion.1
  201.7 1.1 constant_dynamic-update-slice_fusion
  202.7 25.1 %fusion.8 = f32[2,128,16,256]{3,2,1,0:T(8,128)S(1)} fusion(f32[2,128,16,256]{3,2,1,0:T(8,128)} %param.11, f32[2,2,16,256]{3,2,1,0:T(8,128)S(1)} %broadcast_select_fusion, f32[2,2,16,256]{3,2,1,0:T(8,128)S(1)} %broadcast_select_fusion.1, f32[2,128,2,256]{3,2,1,0:T(2,128)S(1)} %collective-permute-done.2, ...), kind=kLoop, calls=%fused_computation.22 | loop fusion | flops 35651584 | bytes 23724032 | tf_op jit(solution)/shard_map/add | solution.py:63
  227.8 6.3 %fusion.29 = f32[2,128,16,256]{3,1,2,0:T(8,128)S(1)} fusion(f32[2,128,16,256]{3,2,1,0:T(8,128)S(1)} %fusion.8, f32[2,1,128,128]{3,2,1,0:T(8,128)S(1)} %copy-done), kind=kOutput, calls=%fused_computation.49 | convolution fusion | flops 1610612736 | bytes 8519680 | tf_op jit(solution)/shard_map/sij,sjzy->sizy/dot_general | solution.py:98
  234.2 2.0 copy-done.1
  237.0 56.6 %all-gather.4.cloned.1.call-done = f32[64,1,16,256]{3,2,1,0:T(8,128)} async-done(((f32[2,1,16,256]{3,2,1,0:T(8,128)}), f32[64,1,16,256]{3,2,1,0:T(8,128)}) %all-gather.4.cloned.1.call-update) | async-done | bytes 1048592 | tf_op jit(solution)/shard_map/all_gather | solution.py:29
  293.6 26.3 %while.12 = (s32[]{:T(128)}, f32[2]{0:T(128)S(1)}, f32[2,16,256]{2,1,0:T(8,128)S(1)}, s32[]{:T(128)}, f32[32,2]{1,0:T(8,128)S(1)}, /*index=5*/f32[32,2,16,256]{3,2,1,0:T(8,128)}, s32[]{:T(128)}, s32[]{:T(128)}, s32[]{:T(128)}) while((s32[]{:T(128)}, f32[2]{0:T(128)S(1)}, f32[2,16,256]{2,1,0:T(8,128)S(1)}, s32[]{:T(128)}, ...), condition=%wide.region_3.4_spmd, body=%wide.region_2.3_spmd.sunk | while | flops 16391 | bytes 98479 | solution.py:37
  294.5 0.8 bitcast_add_fusion.2
  297.0 0.8 bitcast_add_fusion.2
  297.9 0.8 bitcast_add_fusion.2
  299.6 0.8 bitcast_add_fusion.2
  300.4 0.8 bitcast_add_fusion.2
  302.9 0.8 bitcast_add_fusion.2
  303.8 0.8 bitcast_add_fusion.2
  306.3 0.8 bitcast_add_fusion.2
  307.2 0.8 bitcast_add_fusion.2
  309.7 0.8 bitcast_add_fusion.2
  320.0 2.7 multiply_add_fusion
  322.7 4.4 %copy.19 = f32[2,128,16,256]{3,2,1,0:T(8,128)} copy(f32[2,128,16,256]{3,1,2,0:T(8,128)S(1)} %multiply_add_fusion) | data formatting | bytes 8388608 | tf_op jit(solution)/shard_map/add | solution.py:114
  (83 shorter events, 21.3 us)
Async XLA Ops:
  6.5 221.3 %copy-start = (f32[2,1,128,128]{3,2,1,0:T(8,128)S(1)}, f32[2,1,128,128]{3,2,1,0:T(8,128)}, u32[]{:S(2)}) copy-start(f32[2,1,128,128]{3,2,1,0:T(8,128)} %param.14) | copy-start | bytes 393220
  6.5 287.1 %all-gather.4.cloned.1.call-start = ((), (), s32[]{:S(2)}) async-start(), calls=%async_computation | async-start | bytes 1081344 | tf_op jit(solution)/shard_map/all_gather | solution.py:29
  8.1 191.9 %collective-permute-start = (f32[2,2,16,256]{3,2,1,0:T(8,128)}, f32[2,2,16,256]{3,2,1,0:T(8,128)}, u32[]{:S(2)}, u32[]{:S(2)}) collective-permute-start(f32[2,2,16,256]{3,2,1,0:T(8,128)} %get-tuple-element.61), channel_id=1, source_target_pairs={{0,8},{8,16},{16,24},{24,32},{32,40},{40,48},{48,56},{56,64},{64,7... | collective-permute-start | bytes 196616 | tf_op jit(solution)/shard_map/ppermute | solution.py:21
  9.4 191.5 %collective-permute-start.1 = (f32[2,2,16,256]{3,2,1,0:T(8,128)}, f32[2,2,16,256]{3,2,1,0:T(8,128)}, u32[]{:S(2)}, u32[]{:S(2)}) collective-permute-start(f32[2,2,16,256]{3,2,1,0:T(8,128)} %get-tuple-element.62), channel_id=1, source_target_pairs={{8,0},{16,8},{24,16},{32,24},{40,32},{48,40},{56,48},{64,56},{72,6... | collective-permute-start | bytes 196616 | tf_op jit(solution)/shard_map/ppermute | solution.py:22
  16.9 184.8 %collective-permute-start.3 = (f32[2,128,2,256]{3,2,1,0:T(2,128)}, f32[2,128,2,256]{3,2,1,0:T(2,128)S(1)}, u32[]{:S(2)}, u32[]{:S(2)}) collective-permute-start(f32[2,128,2,256]{3,2,1,0:T(2,128)} %get-tuple-element.59), channel_id=1, source_target_pairs={{1,0},{2,1},{3,2},{4,3},{5,4},{6,5},{7,6},{0,7},{9,8},{10,9},{11,1... | collective-permute-start | bytes 1572872 | tf_op jit(solution)/shard_map/ppermute | solution.py:22
  19.8 182.9 %collective-permute-start.2 = (f32[2,128,2,256]{3,2,1,0:T(2,128)}, f32[2,128,2,256]{3,2,1,0:T(2,128)S(1)}, u32[]{:S(2)}, u32[]{:S(2)}) collective-permute-start(f32[2,128,2,256]{3,2,1,0:T(2,128)} %get-tuple-element.60), channel_id=1, source_target_pairs={{0,1},{1,2},{2,3},{3,4},{4,5},{5,6},{6,7},{7,0},{8,9},{9,10},{10,1... | collective-permute-start | bytes 1572872 | tf_op jit(solution)/shard_map/ppermute | solution.py:21
  186.4 6.7 %copy-start.2 = (f32[128,16,256]{2,1,0:T(8,128)S(1)}, f32[128,16,256]{2,1,0:T(8,128)}, u32[]{:S(2)}) copy-start(f32[128,16,256]{2,1,0:T(8,128)} %param.12) | copy-start | bytes 6291460
  193.1 1.6 copy-start.3
  193.1 1.6 copy-start.4
  227.8 92.1 %copy-start.5 = (f32[2,1,128]{2,1,0:T(1,128)S(1)}, f32[2,1,128]{2,1,0:T(1,128)}, u32[]{:S(2)}) copy-start(f32[2,1,128]{2,1,0:T(1,128)} %param.15) | copy-start | bytes 3076
  234.2 2.0 copy-start.1
Sparse Core Ops, SparseCore 0:
  237.0 56.5 all-gather.3
where the time goes:
time: 337 us; the launch traced here: 334 us
  blocking collectives  160 us (47%)
  other arithmetic  65.5 us (19%)
  waiting for transfers between devices  56.6 us (17%)
  local copies, waits for them, and re-layouts  21.9 us (6%)
  between operations  15.5 us (5%)
  starting transfers between devices  8.06 us (2%)
  matrix products  6.35 us (2%)
    psum x1, blocking collectives, from_root(): return lax.psum(jnp.where(mine, x, jnp.zeros_like(x)), axis)  138 us
    all_gather x1, waiting for transfers between devices, prefix(): gathered = jax.tree.map(lambda a: lax.all_gather(a, axis), part)  56.6 us
    add x31, other arithmetic, compose(): later_part[0][:, None, None] * earlier_part[1] + later_part[1]  25.9 us
    add x1, other arithmetic, explicit_part(): return center + diffusivity[None] * laplacian + source  25.1 us
    all_gather x1, blocking collectives, on_device(): station_plane = lax.all_gather(arrived, 'gz', axis=1, tiled=True)  22.5 us
    unnamed x16, local copies, waits for them, and re-layouts  8.19 us
    ppermute x2, starting transfers between devices, with_halo(): after = lax.ppermute(first, axis, down)  6.77 us
  transfers between devices with their start and end apart: 5, of which 1 were waited for; matrix products, arithmetic and copies ran while one was open for 7% of the time, Pallas kernels for 0%

commit v1 on v0

--- a/solution.py
+++ b/solution.py
@@ -6,9 +6,52 @@
 reaction_yields = (-1.0, 1.0)
 
 
-def from_root(x, axis, root):
-    mine = lax.axis_index(axis) == root
-    return lax.psum(jnp.where(mine, x, jnp.zeros_like(x)), axis)
+def xor_sum(x, axis):
+    devices = lax.axis_size(axis)
+    step = 1
+    while step < devices:
+        pairs = [(i, i ^ step) for i in range(devices)]
+        x = x + lax.ppermute(x, axis, pairs)
+        step *= 2
+    return x
+
+
+def xor_gather(x, axis, dim):
+    devices = lax.axis_size(axis)
+    place = lax.axis_index(axis)
+    step = 1
+    while step < devices:
+        pairs = [(i, i ^ step) for i in range(devices)]
+        other = lax.ppermute(x, axis, pairs)
+        low = (place & step) == 0
+        x = jnp.where(
+            low, jnp.concatenate([x, other], dim), jnp.concatenate([other, x], dim)
+        )
+        step *= 2
+    return x
+
+
+def compose(earlier, later):
+    return (earlier[0] * later[0], later[0][:, None, None] * earlier[1] + later[1])
+
+
+def exclusive_scan(part, axis):
+    devices = lax.axis_size(axis)
+    place = lax.axis_index(axis)
+    total = part
+    before = (jnp.ones_like(part[0]), jnp.zeros_like(part[1]))
+    step = 1
+    while step < devices:
+        pairs = [(i, i ^ step) for i in range(devices)]
+        other = lax.ppermute(total, axis, pairs)
+        later = (place & step) != 0
+        new_before = compose(other, before)
+        before = jax.tree.map(lambda a, b: jnp.where(later, a, b), new_before, before)
+        total = jax.tree.map(
+            lambda a, b: jnp.where(later, a, b), compose(other, total), compose(total, other)
+        )
+        step *= 2
+    return before
 
 
 def with_halo(x, sides, width, wrap):
@@ -22,19 +65,6 @@
         after = lax.ppermute(first, axis, down)
         x = jnp.concatenate([before, x, after], axis=dim)
     return x
-
-
-def prefix(part, axis, combine, identity):
-    place = lax.axis_index(axis)
-    gathered = jax.tree.map(lambda a: lax.all_gather(a, axis), part)
-    state = jax.tree.map(lambda a, e: jnp.zeros_like(a) + jnp.asarray(e, a.dtype), part, identity)
-
-    def one(hop, state):
-        return combine(
-            state, jax.tree.map(lambda a: lax.dynamic_index_in_dim(a, hop, 0, False), gathered)
-        )
-
-    return lax.fori_loop(0, place, one, state)
 
 
 def fourth_order(padded, dimension, length):
@@ -82,8 +112,9 @@
     owner_row = station_index[0] // plane_count
     local_plane = station_index[0] - owner_row * plane_count
     own_slice = lax.dynamic_index_in_dim(scalars, local_plane, 1, keepdims=False)
-    arrived = from_root(own_slice, "gx", owner_row)
-    station_plane = lax.all_gather(arrived, "gz", axis=1, tiled=True)
+    mine = stream_rank == owner_row
+    arrived = xor_sum(jnp.where(mine, own_slice, jnp.zeros_like(own_slice)), "gx")
+    station_plane = xor_gather(arrived, "gz", 1)
     inflow_full = make_inflow(station_plane, mean_profile, recycle_gain, span_shift)
     inflow = lax.dynamic_slice_in_dim(inflow_full, span_rank * span_cells, span_cells, 1)
     stream_padded = with_halo(scalars, (("gx", 1),), 2, False)
@@ -95,22 +126,17 @@
     window = jnp.concatenate([head_planes, stream_padded[:, 2:-2], tail_planes], axis=1)
     span_padded = with_halo(scalars, (("gz", 2),), 2, True)
     explicit = explicit_part(window, span_padded, scalars, diffusivity, reaction_rate)
+    inverse = block_inverse[:, 0]
+    response = block_response[:, 0]
+    exit_plane = jnp.einsum(
+        "sj,sjzy->szy", inverse[:, -1], explicit, precision=lax.Precision.HIGHEST
+    )
+    exit_ratio = response[:, -1]
+    through, upstream_sum = exclusive_scan((exit_ratio, exit_plane), "gx")
+    incoming = through[:, None, None] * inflow + upstream_sum
     local_part = jnp.einsum(
-        "sij,sjzy->sizy", block_inverse[:, 0], explicit, precision=lax.Precision.HIGHEST
+        "sij,sjzy->sizy", inverse, explicit, precision=lax.Precision.HIGHEST
     )
-    response = block_response[:, 0]
-    exit_plane = local_part[:, -1]
-    exit_ratio = response[:, -1]
-
-    def compose(earlier_part, later_part):
-        return (
-            earlier_part[0] * later_part[0],
-            later_part[0][:, None, None] * earlier_part[1] + later_part[1],
-        )
-
-    identity = (jnp.ones_like(exit_ratio), jnp.zeros_like(exit_plane))
-    through, upstream_sum = prefix((exit_ratio, exit_plane), "gx", compose, identity)
-    incoming = through[:, None, None] * inflow + upstream_sum
     return local_part + response[:, :, None, None] * incoming[:, None]
 
 

time: 337 us -> 139 us (0.41)
  the two profiles are of different devices: /device:TPU:217 before, /device:TPU:32 now
where the time goes in v1:
time: 139 us; the launch traced here: 138 us
  starting transfers between devices  45.7 us (33%)
  other arithmetic  36.7 us (26%)
  local copies, waits for them, and re-layouts  21.1 us (15%)
  waiting for transfers between devices  20.2 us (15%)
  matrix products  12.4 us (9%)
  between operations  1.6 us (1%)
    add x1, other arithmetic, explicit_part(): return center + diffusivity[None] * laplacian + source  25.8 us
    ppermute x5, starting transfers between devices, xor_sum(): x = x + lax.ppermute(x, axis, pairs)  19.9 us
    ppermute x10, starting transfers between devices, exclusive_scan(): other = lax.ppermute(total, axis, pairs)  15.2 us
    ppermute x10, waiting for transfers between devices, exclusive_scan(): other = lax.ppermute(total, axis, pairs)  11 us
    dot_general x1, matrix products, on_device(): jnp.einsum('sij,sjzy->sizy', inverse, explicit, precision=lax.Precision.H...  6.63 us
    ppermute x3, waiting for transfers between devices, xor_gather(): other = lax.ppermute(x, axis, pairs)  6.02 us
    another operation x1, other arithmetic, explicit_part(): jnp.stack([reaction_yields[0] * reaction, reaction_yields[1] * reaction])  5.99 us
    dot_general x1, matrix products, on_device(): jnp.einsum('sj,sjzy->szy', inverse[:, -1], explicit, precision=lax.Precis...  5.75 us
  transfers between devices with their start and end apart: 22, of which 10 were waited for; matrix products, arithmetic and copies ran while one was open for 14% of the time, Pallas kernels for 0%

profile of v1, /device:TPU:32, one launch (start us, length us, event | category | flops | bytes accessed | tf_op | source)
XLA Modules:
  0.0 137.7 jit_solution(7280597928285954221)
XLA Ops:
  1.6 1.2 collective-permute-done
  2.8 3.3 %collective-permute-start.1 = (f32[2,16,256]{2,1,0:T(8,128)S(1)}, f32[2,16,256]{2,1,0:T(8,128)S(1)}, u32[]{:S(2)}, u32[]{:S(2)}) collective-permute-start(f32[2,16,256]{2,1,0:T(8,128)S(1)} %add.124), channel_id=1, source_target_pairs={{0,16},{8,24},{16,0},{24,8},{32,48},{40,56},{48,32},{56,40},{64,80... | collective-permute-start | bytes 98312 | tf_op jit(solution)/shard_map/ppermute | solution.py:14
  6.1 1.9 %collective-permute-done.1 = f32[2,16,256]{2,1,0:T(8,128)S(1)} collective-permute-done((f32[2,16,256]{2,1,0:T(8,128)S(1)}, f32[2,16,256]{2,1,0:T(8,128)S(1)}, u32[]{:S(2)}, u32[]{:S(2)}) %collective-permute-start.1) | collective-permute-done | bytes 32800 | tf_op jit(solution)/shard_map/ppermute | solution.py:14
  8.0 5.9 %collective-permute-start.2 = (f32[2,16,256]{2,1,0:T(8,128)S(1)}, f32[2,16,256]{2,1,0:T(8,128)S(1)}, u32[]{:S(2)}, u32[]{:S(2)}) collective-permute-start(f32[2,16,256]{2,1,0:T(8,128)S(1)} %add.125), channel_id=1, source_target_pairs={{0,32},{8,40},{16,48},{24,56},{32,0},{40,8},{48,16},{56,24},{64,96... | collective-permute-start | bytes 98312 | tf_op jit(solution)/shard_map/ppermute | solution.py:14
  14.8 1.3 collective-permute-start.8
  16.1 1.3 collective-permute-start.9
  17.5 7.6 %collective-permute-start.3 = (f32[2,16,256]{2,1,0:T(8,128)S(1)}, f32[2,16,256]{2,1,0:T(8,128)S(1)}, u32[]{:S(2)}, u32[]{:S(2)}) collective-permute-start(f32[2,16,256]{2,1,0:T(8,128)S(1)} %add.126), channel_id=1, source_target_pairs={{0,64},{8,72},{16,80},{24,88},{32,96},{40,104},{48,112},{56,120},{... | collective-permute-start | bytes 98312 | tf_op jit(solution)/shard_map/ppermute | solution.py:14
  25.1 3.6 %fusion.43 = (f32[2,128,2,256]{3,2,1,0:T(2,128)}, f32[2,128,2,256]{3,2,1,0:T(2,128)}) fusion(f32[2,128,16,256]{3,2,1,0:T(8,128)} %param.9), kind=kLoop, calls=%fused_computation.95 | loop fusion | bytes 2097152 | tf_op jit(solution)/shard_map/slice | solution.py:63
  28.7 3.2 %collective-permute-start.11 = (f32[2,128,2,256]{3,2,1,0:T(2,128)}, f32[2,128,2,256]{3,2,1,0:T(2,128)S(1)}, u32[]{:S(2)}, u32[]{:S(2)}) collective-permute-start(f32[2,128,2,256]{3,2,1,0:T(2,128)} %get-tuple-element.14), channel_id=1, source_target_pairs={{1,0},{2,1},{3,2},{4,3},{5,4},{6,5},{7,6},{0,7},{9,8},{10,9},{11,1... | collective-permute-start | bytes 1572872 | tf_op jit(solution)/shard_map/ppermute | solution.py:65
  31.9 3.0 %collective-permute-start.4 = (f32[2,16,256]{2,1,0:T(8,128)S(1)}, f32[2,16,256]{2,1,0:T(8,128)S(1)}, u32[]{:S(2)}, u32[]{:S(2)}) collective-permute-start(f32[2,16,256]{2,1,0:T(8,128)S(1)} %add.127), channel_id=1, source_target_pairs={{0,128},{8,136},{16,144},{24,152},{32,160},{40,168},{48,176},{56,1... | collective-permute-start | bytes 98312 | tf_op jit(solution)/shard_map/ppermute | solution.py:14
  34.9 6.0 %multiply_bitcast_fusion = (f32[1,128,16,256]{3,2,1,0:T(8,128)S(1)}, f32[128,16,256]{2,1,0:T(8,128)}) fusion(f32[2,128,16,256]{3,2,1,0:T(8,128)} %param.9, f32[128,16,256]{2,1,0:T(8,128)S(1)} %copy-done), kind=kLoop, calls=%fused_computation.59 | loop fusion | flops 7864320 | bytes 10485760 | tf_op jit(solution)/shard_map/stack | solution.py:92
  41.3 1.6 %broadcast_multiply_fusion = f32[128,16,256]{2,1,0:T(8,128)} fusion(f32[128,16,256]{2,1,0:T(8,128)S(1)} %copy-done.1), kind=kLoop, calls=%fused_computation.60 | loop fusion | flops 524288 | bytes 4194304 | tf_op jit(solution)/shard_map/mul | solution.py:93
  42.9 2.1 %collective-permute-done.5 = f32[2,16,256]{2,1,0:T(8,128)} collective-permute-done((f32[2,16,256]{2,1,0:T(8,128)S(1)}, f32[2,16,256]{2,1,0:T(8,128)}, u32[]{:S(2)}, u32[]{:S(2)}) %collective-permute-start.5) | collective-permute-done | bytes 32800 | tf_op jit(solution)/shard_map/ppermute | solution.py:25
  45.9 3.2 %collective-permute-start.6 = (f32[2,32,256]{2,1,0:T(8,128)S(1)}, f32[2,32,256]{2,1,0:T(8,128)}, u32[]{:S(2)}, u32[]{:S(2)}) collective-permute-start(f32[2,32,256]{2,1,0:T(8,128)S(1)} %maximum_select_fusion.2), channel_id=1, source_target_pairs={{0,2},{1,3},{2,0},{3,1},{4,6},{5,7},{6,4},{7,5},{8,10},{9,11},{10,... | collective-permute-start | bytes 196616 | tf_op jit(solution)/shard_map/ppermute | solution.py:25
  49.1 4.7 %constant_dynamic-update-slice_fusion.1 = f32[2,128,18,256]{3,2,1,0:T(8,128)} fusion(f32[2,128,16,256]{3,2,1,0:T(8,128)} %param.9), kind=kLoop, calls=%fused_computation.84 | loop fusion | bytes 8388608
  55.4 1.3 collective-permute-start.7
  56.7 3.9 %collective-permute-done.7 = f32[2,64,256]{2,1,0:T(8,128)S(1)} collective-permute-done((f32[2,64,256]{2,1,0:T(8,128)S(1)}, f32[2,64,256]{2,1,0:T(8,128)S(1)}, u32[]{:S(2)}, u32[]{:S(2)}) %collective-permute-start.7) | collective-permute-done | bytes 131104 | tf_op jit(solution)/shard_map/ppermute | solution.py:25
  61.8 25.8 %fusion.8 = f32[2,128,16,256]{3,2,1,0:T(8,128)} fusion(f32[2,128,16,256]{3,2,1,0:T(8,128)} %param.9, f32[2,2,16,256]{3,2,1,0:T(8,128)S(1)} %broadcast_select_fusion, f32[2,2,16,256]{3,2,1,0:T(8,128)S(1)} %broadcast_select_fusion.1, f32[2,128,2,256]{3,2,1,0:T(2,128)S(1)} %collective-permute-done.10, f32[2,128,18,256]{3,2,1,0:T(8,128)} %constant_dynamic-update-slice_fusion, ...), kind=kLoop, calls=%fused_computation.20 | loop fusion | flops 35651584 | bytes 23724032 | tf_op jit(solution)/shard_map/add | solution.py:93
  87.6 5.3 %copy.12 = f32[2,128,16,256]{1,3,2,0:T(8,128)} copy(f32[2,128,16,256]{3,2,1,0:T(8,128)} %fusion.8) | data formatting | bytes 8388608 | tf_op jit(solution)/shard_map/add | solution.py:93
  93.0 5.8 %fusion.40 = f32[2,1,16,256]{3,1,2,0:T(1,128)S(1)} fusion(f32[2,128,16,256]{1,3,2,0:T(8,128)} %copy.12, f32[2,128,128]{2,1,0:T(8,128)S(1)} %bitcast.75), kind=kOutput, calls=%fused_computation.86 | convolution fusion | flops 12582912 | bytes 4228096 | tf_op jit(solution)/shard_map/sj,sjzy->szy/dot_general | solution.py:131
  100.5 2.9 %collective-permute-start.13 = (f32[2]{0:T(128)S(1)}, f32[2]{0:T(128)S(1)}, u32[]{:S(2)}, u32[]{:S(2)}) collective-permute-start(f32[2]{0:T(128)S(1)} %mul.223), channel_id=1, source_target_pairs={{0,16},{8,24},{16,0},{24,8},{32,48},{40,56},{48,32},{56,40},{64,80... | collective-permute-start | bytes 32 | tf_op jit(solution)/shard_map/ppermute | solution.py:46
  103.4 1.9 %collective-permute-done.13 = f32[2]{0:T(128)S(1)} collective-permute-done((f32[2]{0:T(128)S(1)}, f32[2]{0:T(128)S(1)}, u32[]{:S(2)}, u32[]{:S(2)}) %collective-permute-start.13) | collective-permute-done | bytes 40 | tf_op jit(solution)/shard_map/ppermute | solution.py:46
  105.9 5.6 %collective-permute-start.14 = (f32[2]{0:T(128)S(1)}, f32[2]{0:T(128)S(1)}, u32[]{:S(2)}, u32[]{:S(2)}) collective-permute-start(f32[2]{0:T(128)S(1)} %mul.224), channel_id=1, source_target_pairs={{0,32},{8,40},{16,48},{24,56},{32,0},{40,8},{48,16},{56,24},{64,96... | collective-permute-start | bytes 32 | tf_op jit(solution)/shard_map/ppermute | solution.py:46
  111.4 2.1 %collective-permute-done.14 = f32[2]{0:T(128)S(1)} collective-permute-done((f32[2]{0:T(128)S(1)}, f32[2]{0:T(128)S(1)}, u32[]{:S(2)}, u32[]{:S(2)}) %collective-permute-start.14) | collective-permute-done | bytes 40 | tf_op jit(solution)/shard_map/ppermute | solution.py:46
  114.1 1.6 %collective-permute-start.15 = (f32[2]{0:T(128)S(1)}, f32[2]{0:T(128)S(1)}, u32[]{:S(2)}, u32[]{:S(2)}) collective-permute-start(f32[2]{0:T(128)S(1)} %mul.225), channel_id=1, source_target_pairs={{0,64},{8,72},{16,80},{24,88},{32,96},{40,104},{48,112},{56,120},{... | collective-permute-start | bytes 32 | tf_op jit(solution)/shard_map/ppermute | solution.py:46
  115.7 2.0 %collective-permute-done.15 = f32[2]{0:T(128)S(1)} collective-permute-done((f32[2]{0:T(128)S(1)}, f32[2]{0:T(128)S(1)}, u32[]{:S(2)}, u32[]{:S(2)}) %collective-permute-start.15) | collective-permute-done | bytes 40 | tf_op jit(solution)/shard_map/ppermute | solution.py:46
  117.8 2.2 %collective-permute-start.16 = (f32[2]{0:T(128)S(1)}, f32[2]{0:T(128)S(1)}, u32[]{:S(2)}, u32[]{:S(2)}) collective-permute-start(f32[2]{0:T(128)S(1)} %mul.226), channel_id=1, source_target_pairs={{0,128},{8,136},{16,144},{24,152},{32,160},{40,168},{48,176},{56,1... | collective-permute-start | bytes 32 | tf_op jit(solution)/shard_map/ppermute | solution.py:46
  120.1 1.4 collective-permute-start.21
  121.4 1.4 %collective-permute-done.16 = f32[2]{0:T(128)S(1)} collective-permute-done((f32[2]{0:T(128)S(1)}, f32[2]{0:T(128)S(1)}, u32[]{:S(2)}, u32[]{:S(2)}) %collective-permute-start.16) | collective-permute-done | bytes 40 | tf_op jit(solution)/shard_map/ppermute | solution.py:46
  122.8 2.7 %collective-permute-done.21 = f32[2,16,256]{2,1,0:T(8,128)S(1)} collective-permute-done((f32[2,16,256]{2,1,0:T(8,128)S(1)}, f32[2,16,256]{2,1,0:T(8,128)S(1)}, u32[]{:S(2)}, u32[]{:S(2)}) %collective-permute-start.21) | collective-permute-done | bytes 32800 | tf_op jit(solution)/shard_map/ppermute | solution.py:46
  125.6 6.6 %bitcast_add_fusion = f32[2,128,16,256]{1,3,2,0:T(8,128)} fusion(f32[2,128,16,256]{1,3,2,0:T(8,128)} %copy.12, f32[2,16,256]{2,1,0:T(8,128)S(1)} %fusion.38, f32[2,128]{1,0:T(2,128)S(1)} %bitcast.78, f32[2,1,128,128]{3,2,1,0:T(8,128)S(1)} %copy-done.2), kind=kOutput, calls=%fused_computation.44 | convolution fusion | flops 1612709888 | bytes 8553472 | tf_op jit(solution)/shard_map/sij,sjzy->sizy/dot_general | solution.py:137
  132.2 5.4 %copy.13 = f32[2,128,16,256]{3,2,1,0:T(8,128)} copy(f32[2,128,16,256]{1,3,2,0:T(8,128)} %bitcast_add_fusion) | data formatting | bytes 8388608 | tf_op jit(solution)/shard_map/add | solution.py:140
  (60 shorter events, 8.2 us)
Async XLA Ops:
  0.7 34.2 %copy-start = (f32[128,16,256]{2,1,0:T(8,128)S(1)}, f32[128,16,256]{2,1,0:T(8,128)}, u32[]{:S(2)}) copy-start(f32[128,16,256]{2,1,0:T(8,128)} %param.11) | copy-start | bytes 6291460
  1.6 1.2 collective-permute-start
  2.8 5.2 %collective-permute-start.1 = (f32[2,16,256]{2,1,0:T(8,128)S(1)}, f32[2,16,256]{2,1,0:T(8,128)S(1)}, u32[]{:S(2)}, u32[]{:S(2)}) collective-permute-start(f32[2,16,256]{2,1,0:T(8,128)S(1)} %add.124), channel_id=1, source_target_pairs={{0,16},{8,24},{16,0},{24,8},{32,48},{40,56},{48,32},{56,40},{64,80... | collective-permute-start | bytes 98312 | tf_op jit(solution)/shard_map/ppermute | solution.py:14
  8.0 9.4 %collective-permute-start.2 = (f32[2,16,256]{2,1,0:T(8,128)S(1)}, f32[2,16,256]{2,1,0:T(8,128)S(1)}, u32[]{:S(2)}, u32[]{:S(2)}) collective-permute-start(f32[2,16,256]{2,1,0:T(8,128)S(1)} %add.125), channel_id=1, source_target_pairs={{0,32},{8,40},{16,48},{24,56},{32,0},{40,8},{48,16},{56,24},{64,96... | collective-permute-start | bytes 98312 | tf_op jit(solution)/shard_map/ppermute | solution.py:14
  14.8 45.9 %collective-permute-start.8 = (f32[2,2,16,256]{3,2,1,0:T(8,128)S(1)}, f32[2,2,16,256]{3,2,1,0:T(8,128)S(1)}, u32[]{:S(2)}, u32[]{:S(2)}) collective-permute-start(f32[2,2,16,256]{3,2,1,0:T(8,128)S(1)} %get-tuple-element.18), channel_id=1, source_target_pairs={{0,8},{8,16},{16,24},{24,32},{32,40},{40,48},{48,56},{56,64},{64,7... | collective-permute-start | bytes 196616 | tf_op jit(solution)/shard_map/ppermute | solution.py:64
  16.1 40.5 %collective-permute-start.9 = (f32[2,2,16,256]{3,2,1,0:T(8,128)S(1)}, f32[2,2,16,256]{3,2,1,0:T(8,128)S(1)}, u32[]{:S(2)}, u32[]{:S(2)}) collective-permute-start(f32[2,2,16,256]{3,2,1,0:T(8,128)S(1)} %get-tuple-element.19), channel_id=1, source_target_pairs={{8,0},{16,8},{24,16},{32,24},{40,32},{48,40},{56,48},{64,56},{72,6... | collective-permute-start | bytes 196616 | tf_op jit(solution)/shard_map/ppermute | solution.py:65
  17.5 14.4 %collective-permute-start.3 = (f32[2,16,256]{2,1,0:T(8,128)S(1)}, f32[2,16,256]{2,1,0:T(8,128)S(1)}, u32[]{:S(2)}, u32[]{:S(2)}) collective-permute-start(f32[2,16,256]{2,1,0:T(8,128)S(1)} %add.126), channel_id=1, source_target_pairs={{0,64},{8,72},{16,80},{24,88},{32,96},{40,104},{48,112},{56,120},{... | collective-permute-start | bytes 98312 | tf_op jit(solution)/shard_map/ppermute | solution.py:14
  28.7 32.1 %collective-permute-start.11 = (f32[2,128,2,256]{3,2,1,0:T(2,128)}, f32[2,128,2,256]{3,2,1,0:T(2,128)S(1)}, u32[]{:S(2)}, u32[]{:S(2)}) collective-permute-start(f32[2,128,2,256]{3,2,1,0:T(2,128)} %get-tuple-element.14), channel_id=1, source_target_pairs={{1,0},{2,1},{3,2},{4,3},{5,4},{6,5},{7,6},{0,7},{9,8},{10,9},{11,1... | collective-permute-start | bytes 1572872 | tf_op jit(solution)/shard_map/ppermute | solution.py:65
  31.9 30.0 %collective-permute-start.10 = (f32[2,128,2,256]{3,2,1,0:T(2,128)}, f32[2,128,2,256]{3,2,1,0:T(2,128)S(1)}, u32[]{:S(2)}, u32[]{:S(2)}) collective-permute-start(f32[2,128,2,256]{3,2,1,0:T(2,128)} %get-tuple-element.15), channel_id=1, source_target_pairs={{0,1},{1,2},{2,3},{3,4},{4,5},{5,6},{6,7},{7,0},{8,9},{9,10},{10,1... | collective-permute-start | bytes 1572872 | tf_op jit(solution)/shard_map/ppermute | solution.py:64
  31.9 9.4 %copy-start.1 = (f32[128,16,256]{2,1,0:T(8,128)S(1)}, f32[128,16,256]{2,1,0:T(8,128)}, u32[]{:S(2)}) copy-start(f32[128,16,256]{2,1,0:T(8,128)} %param.10) | copy-start | bytes 6291460
  31.9 9.0 %collective-permute-start.4 = (f32[2,16,256]{2,1,0:T(8,128)S(1)}, f32[2,16,256]{2,1,0:T(8,128)S(1)}, u32[]{:S(2)}, u32[]{:S(2)}) collective-permute-start(f32[2,16,256]{2,1,0:T(8,128)S(1)} %add.127), channel_id=1, source_target_pairs={{0,128},{8,136},{16,144},{24,152},{32,160},{40,168},{48,176},{56,1... | collective-permute-start | bytes 98312 | tf_op jit(solution)/shard_map/ppermute | solution.py:14
  40.9 4.1 %collective-permute-start.5 = (f32[2,16,256]{2,1,0:T(8,128)S(1)}, f32[2,16,256]{2,1,0:T(8,128)}, u32[]{:S(2)}, u32[]{:S(2)}) collective-permute-start(f32[2,16,256]{2,1,0:T(8,128)S(1)} %add.128), channel_id=1, source_target_pairs={{0,1},{1,0},{2,3},{3,2},{4,5},{5,4},{6,7},{7,6},{8,9},{9,8},{10,11... | collective-permute-start | bytes 98312 | tf_op jit(solution)/shard_map/ppermute | solution.py:25
  45.9 14.8 %copy-start.3 = (f32[2,256]{1,0:T(2,128)S(1)}, f32[2,256]{1,0:T(2,128)}, u32[]{:S(2)}) copy-start(f32[2,256]{1,0:T(2,128)} %param.14) | copy-start | bytes 6148
  45.9 14.8 %copy-start.4 = (f32[2,256]{1,0:T(2,128)S(1)}, f32[2,256]{1,0:T(2,128)}, u32[]{:S(2)}) copy-start(f32[2,256]{1,0:T(2,128)} %param.15) | copy-start | bytes 6148
  45.9 8.6 %collective-permute-start.6 = (f32[2,32,256]{2,1,0:T(8,128)S(1)}, f32[2,32,256]{2,1,0:T(8,128)}, u32[]{:S(2)}, u32[]{:S(2)}) collective-permute-start(f32[2,32,256]{2,1,0:T(8,128)S(1)} %maximum_select_fusion.2), channel_id=1, source_target_pairs={{0,2},{1,3},{2,0},{3,1},{4,6},{5,7},{6,4},{7,5},{8,10},{9,11},{10,... | collective-permute-start | bytes 196616 | tf_op jit(solution)/shard_map/ppermute | solution.py:25
  55.4 5.2 %collective-permute-start.7 = (f32[2,64,256]{2,1,0:T(8,128)S(1)}, f32[2,64,256]{2,1,0:T(8,128)S(1)}, u32[]{:S(2)}, u32[]{:S(2)}) collective-permute-start(f32[2,64,256]{2,1,0:T(8,128)S(1)} %maximum_select_fusion.1), channel_id=1, source_target_pairs={{0,4},{1,5},{2,6},{3,7},{4,0},{5,1},{6,2},{7,3},{8,12},{9,13},{10,... | collective-permute-start | bytes 393224 | tf_op jit(solution)/shard_map/ppermute | solution.py:25
  87.6 5.3 %copy-start.2 = (f32[2,1,128,128]{3,2,1,0:T(8,128)S(1)}, f32[2,1,128,128]{3,2,1,0:T(8,128)}, u32[]{:S(2)}) copy-start(f32[2,1,128,128]{3,2,1,0:T(8,128)} %param.12) | copy-start | bytes 393220
  93.0 5.9 %copy-start.5 = (f32[2,1,128]{2,1,0:T(1,128)S(1)}, f32[2,1,128]{2,1,0:T(1,128)}, u32[]{:S(2)}) copy-start(f32[2,1,128]{2,1,0:T(1,128)} %param.13) | copy-start | bytes 3076
  98.7 1.7 %collective-permute-start.17 = (f32[2,16,256]{2,1,0:T(8,128)S(1)}, f32[2,16,256]{2,1,0:T(8,128)S(1)}, u32[]{:S(2)}, u32[]{:S(2)}) collective-permute-start(f32[2,16,256]{2,1,0:T(8,128)S(1)} %bitcast.76), channel_id=1, source_target_pairs={{0,8},{8,0},{16,24},{24,16},{32,40},{40,32},{48,56},{56,48},{64,72... | collective-permute-start | bytes 98312 | tf_op jit(solution)/shard_map/ppermute | solution.py:46
  99.0 1.4 %collective-permute-start.12 = (f32[2]{0:T(128)S(1)}, f32[2]{0:T(128)S(1)}, u32[]{:S(2)}, u32[]{:S(2)}) collective-permute-start(f32[2]{0:T(128)S(1)} %slice_reduce_fusion), channel_id=1, source_target_pairs={{0,8},{8,0},{16,24},{24,16},{32,40},{40,32},{48,56},{56,48},{64,72... | collective-permute-start | bytes 32 | tf_op jit(solution)/shard_map/ppermute | solution.py:46
  100.5 4.9 %collective-permute-start.18 = (f32[2,16,256]{2,1,0:T(8,128)S(1)}, f32[2,16,256]{2,1,0:T(8,128)S(1)}, u32[]{:S(2)}, u32[]{:S(2)}) collective-permute-start(f32[2,16,256]{2,1,0:T(8,128)S(1)} %add_select_fusion.7), channel_id=1, source_target_pairs={{0,16},{8,24},{16,0},{24,8},{32,48},{40,56},{48,32},{56,40},{64,80... | collective-permute-start | bytes 98312 | tf_op jit(solution)/shard_map/ppermute | solution.py:46
  100.5 4.8 %collective-permute-start.13 = (f32[2]{0:T(128)S(1)}, f32[2]{0:T(128)S(1)}, u32[]{:S(2)}, u32[]{:S(2)}) collective-permute-start(f32[2]{0:T(128)S(1)} %mul.223), channel_id=1, source_target_pairs={{0,16},{8,24},{16,0},{24,8},{32,48},{40,56},{48,32},{56,40},{64,80... | collective-permute-start | bytes 32 | tf_op jit(solution)/shard_map/ppermute | solution.py:46
  105.5 8.1 %collective-permute-start.19 = (f32[2,16,256]{2,1,0:T(8,128)S(1)}, f32[2,16,256]{2,1,0:T(8,128)S(1)}, u32[]{:S(2)}, u32[]{:S(2)}) collective-permute-start(f32[2,16,256]{2,1,0:T(8,128)S(1)} %add_select_fusion.6), channel_id=1, source_target_pairs={{0,32},{8,40},{16,48},{24,56},{32,0},{40,8},{48,16},{56,24},{64,96... | collective-permute-start | bytes 98312 | tf_op jit(solution)/shard_map/ppermute | solution.py:46
  105.9 7.7 %collective-permute-start.14 = (f32[2]{0:T(128)S(1)}, f32[2]{0:T(128)S(1)}, u32[]{:S(2)}, u32[]{:S(2)}) collective-permute-start(f32[2]{0:T(128)S(1)} %mul.224), channel_id=1, source_target_pairs={{0,32},{8,40},{16,48},{24,56},{32,0},{40,8},{48,16},{56,24},{64,96... | collective-permute-start | bytes 32 | tf_op jit(solution)/shard_map/ppermute | solution.py:46
  113.7 6.3 %collective-permute-start.20 = (f32[2,16,256]{2,1,0:T(8,128)S(1)}, f32[2,16,256]{2,1,0:T(8,128)S(1)}, u32[]{:S(2)}, u32[]{:S(2)}) collective-permute-start(f32[2,16,256]{2,1,0:T(8,128)S(1)} %add_select_fusion.5), channel_id=1, source_target_pairs={{0,64},{8,72},{16,80},{24,88},{32,96},{40,104},{48,112},{56,120},{... | collective-permute-start | bytes 98312 | tf_op jit(solution)/shard_map/ppermute | solution.py:46
  114.1 3.6 %collective-permute-start.15 = (f32[2]{0:T(128)S(1)}, f32[2]{0:T(128)S(1)}, u32[]{:S(2)}, u32[]{:S(2)}) collective-permute-start(f32[2]{0:T(128)S(1)} %mul.225), channel_id=1, source_target_pairs={{0,64},{8,72},{16,80},{24,88},{32,96},{40,104},{48,112},{56,120},{... | collective-permute-start | bytes 32 | tf_op jit(solution)/shard_map/ppermute | solution.py:46
  117.8 5.0 %collective-permute-start.16 = (f32[2]{0:T(128)S(1)}, f32[2]{0:T(128)S(1)}, u32[]{:S(2)}, u32[]{:S(2)}) collective-permute-start(f32[2]{0:T(128)S(1)} %mul.226), channel_id=1, source_target_pairs={{0,128},{8,136},{16,144},{24,152},{32,160},{40,168},{48,176},{56,1... | collective-permute-start | bytes 32 | tf_op jit(solution)/shard_map/ppermute | solution.py:46
  120.1 5.4 %collective-permute-start.21 = (f32[2,16,256]{2,1,0:T(8,128)S(1)}, f32[2,16,256]{2,1,0:T(8,128)S(1)}, u32[]{:S(2)}, u32[]{:S(2)}) collective-permute-start(f32[2,16,256]{2,1,0:T(8,128)S(1)} %add_select_fusion.4), channel_id=1, source_target_pairs={{0,128},{8,136},{16,144},{24,152},{32,160},{40,168},{48,176},{56,1... | collective-permute-start | bytes 98312 | tf_op jit(solution)/shard_map/ppermute | solution.py:46

commit v2 on v1

--- a/solution.py
+++ b/solution.py
@@ -32,7 +32,7 @@
 
 
 def compose(earlier, later):
-    return (earlier[0] * later[0], later[0][:, None, None] * earlier[1] + later[1])
+    return (later[0] * earlier[0], later[0] * earlier[1] + later[1])
 
 
 def exclusive_scan(part, axis):
@@ -43,7 +43,8 @@
     step = 1
     while step < devices:
         pairs = [(i, i ^ step) for i in range(devices)]
-        other = lax.ppermute(total, axis, pairs)
+        other = lax.ppermute(jnp.stack(total), axis, pairs)
+        other = (other[0], other[1])
         later = (place & step) != 0
         new_before = compose(other, before)
         before = jax.tree.map(lambda a, b: jnp.where(later, a, b), new_before, before)
@@ -109,6 +110,7 @@
     stream_devices = lax.axis_size("gx")
     stream_rank = lax.axis_index("gx")
     span_rank = lax.axis_index("gz")
+    at_inlet = stream_rank == 0
     owner_row = station_index[0] // plane_count
     local_plane = station_index[0] - owner_row * plane_count
     own_slice = lax.dynamic_index_in_dim(scalars, local_plane, 1, keepdims=False)
@@ -119,25 +121,37 @@
     inflow = lax.dynamic_slice_in_dim(inflow_full, span_rank * span_cells, span_cells, 1)
     stream_padded = with_halo(scalars, (("gx", 1),), 2, False)
     edge_shape = (scalars.shape[0], 2, scalars.shape[2], scalars.shape[3])
-    inlet_planes = jnp.broadcast_to(inflow[:, None], edge_shape)
     outlet_planes = jnp.broadcast_to(scalars[:, -1:], edge_shape)
-    head_planes = jnp.where(stream_rank == 0, inlet_planes, stream_padded[:, :2])
+    head_planes = jnp.where(at_inlet, jnp.zeros(edge_shape, scalars.dtype), stream_padded[:, :2])
     tail_planes = jnp.where(stream_rank == stream_devices - 1, outlet_planes, stream_padded[:, -2:])
     window = jnp.concatenate([head_planes, stream_padded[:, 2:-2], tail_planes], axis=1)
     span_padded = with_halo(scalars, (("gz", 2),), 2, True)
     explicit = explicit_part(window, span_padded, scalars, diffusivity, reaction_rate)
     inverse = block_inverse[:, 0]
     response = block_response[:, 0]
+    first_gain = jnp.where(at_inlet, diffusivity[0] * (15.0 / 12.0), 0.0)
+    second_gain = jnp.where(at_inlet, diffusivity[1] * (-1.0 / 12.0), 0.0)
     exit_plane = jnp.einsum(
         "sj,sjzy->szy", inverse[:, -1], explicit, precision=lax.Precision.HIGHEST
     )
-    exit_ratio = response[:, -1]
-    through, upstream_sum = exclusive_scan((exit_ratio, exit_plane), "gx")
-    incoming = through[:, None, None] * inflow + upstream_sum
+    exit_gain = (
+        response[:, -1][:, None, None]
+        + inverse[:, -1, 0][:, None, None] * first_gain
+        + inverse[:, -1, 1][:, None, None] * second_gain
+    )
+    through, upstream_sum = exclusive_scan((exit_gain, exit_plane), "gx")
+    incoming = through * inflow + upstream_sum
     local_part = jnp.einsum(
         "sij,sjzy->sizy", inverse, explicit, precision=lax.Precision.HIGHEST
     )
-    return local_part + response[:, :, None, None] * incoming[:, None]
+    first_in = first_gain * inflow
+    second_in = second_gain * inflow
+    return (
+        local_part
+        + response[:, :, None, None] * incoming[:, None]
+        + inverse[:, :, 0][:, :, None, None] * first_in[:, None]
+        + inverse[:, :, 1][:, :, None, None] * second_in[:, None]
+    )
 
 
 def solution(mesh):

time: 139 us -> 130 us (0.935)
  the two profiles are of different devices: /device:TPU:32 before, /device:TPU:2 now
where the time goes in v2:
time: 130 us; the launch traced here: 129 us
  starting transfers between devices  36.5 us (28%)
  other arithmetic  36.5 us (28%)
  waiting for transfers between devices  21.4 us (16%)
  local copies, waits for them, and re-layouts  19.9 us (15%)
  matrix products  13.1 us (10%)
  between operations  1.59 us (1%)
    add x1, other arithmetic, explicit_part(): return center + diffusivity[None] * laplacian + source  25.9 us
    ppermute x5, starting transfers between devices, xor_sum(): x = x + lax.ppermute(x, axis, pairs)  18.6 us
    ppermute x5, waiting for transfers between devices, exclusive_scan(): other = lax.ppermute(jnp.stack(total), axis, pairs)  16.7 us
    dot_general x1, matrix products, on_device(): jnp.einsum('sij,sjzy->sizy', inverse, explicit, precision=lax.Precision.H...  7.34 us
    ppermute x5, starting transfers between devices, exclusive_scan(): other = lax.ppermute(jnp.stack(total), axis, pairs)  7.03 us
    another operation x1, other arithmetic, explicit_part(): jnp.stack([reaction_yields[0] * reaction, reaction_yields[1] * reaction])  6.72 us
    dot_general x1, matrix products, on_device(): jnp.einsum('sj,sjzy->szy', inverse[:, -1], explicit, precision=lax.Precis...  5.77 us
    add x1, local copies, waits for them, and re-layouts, on_device(): local_part + response[:, :, None, None] * incoming[:, None]  5.43 us
  transfers between devices with their start and end apart: 17, of which 8 were waited for; matrix products, arithmetic and copies ran while one was open for 43% of the time, Pallas kernels for 0%

profile of v2, /device:TPU:2, one launch (start us, length us, event | category | flops | bytes accessed | tf_op | source)
XLA Modules:
  0.0 129.1 jit_solution(5675786878636248918)
XLA Ops:
  0.0 1.5 %fusion.59 = (f32[2,2,16,256]{3,2,1,0:T(8,128)}, f32[2,2,16,256]{3,2,1,0:T(8,128)}) fusion(f32[2,128,16,256]{3,2,1,0:T(8,128)} %param.9), kind=kLoop, calls=%fused_computation.140 | loop fusion | bytes 262144 | tf_op jit(solution)/shard_map/slice | solution.py:63
  1.5 1.3 collective-permute-start.1
  2.8 3.0 %collective-permute-start = (f32[2,2,16,256]{3,2,1,0:T(8,128)}, f32[2,2,16,256]{3,2,1,0:T(8,128)S(1)}, u32[]{:S(2)}, u32[]{:S(2)}) collective-permute-start(f32[2,2,16,256]{3,2,1,0:T(8,128)} %get-tuple-element.21), channel_id=1, source_target_pairs={{0,8},{8,16},{16,24},{24,32},{32,40},{40,48},{48,56},{56,64},{64,7... | collective-permute-start | bytes 196616 | tf_op jit(solution)/shard_map/ppermute | solution.py:65
  5.9 3.6 %fusion.58 = (f32[2,128,2,256]{3,2,1,0:T(2,128)}, f32[2,128,2,256]{3,2,1,0:T(2,128)}) fusion(f32[2,128,16,256]{3,2,1,0:T(8,128)} %param.9), kind=kLoop, calls=%fused_computation.139 | loop fusion | bytes 2097152 | tf_op jit(solution)/shard_map/slice | solution.py:64
  9.4 1.5 %collective-permute-start.2 = (f32[2,128,2,256]{3,2,1,0:T(2,128)}, f32[2,128,2,256]{3,2,1,0:T(2,128)S(1)}, u32[]{:S(2)}, u32[]{:S(2)}) collective-permute-start(f32[2,128,2,256]{3,2,1,0:T(2,128)} %get-tuple-element.20), channel_id=1, source_target_pairs={{0,1},{1,2},{2,3},{3,4},{4,5},{5,6},{6,7},{7,0},{8,9},{9,10},{10,1... | collective-permute-start | bytes 1572872 | tf_op jit(solution)/shard_map/ppermute | solution.py:65
  13.2 2.1 %collective-permute-start.9 = (f32[2,16,256]{2,1,0:T(8,128)S(1)}, f32[2,16,256]{2,1,0:T(8,128)S(1)}, u32[]{:S(2)}, u32[]{:S(2)}) collective-permute-start(f32[2,16,256]{2,1,0:T(8,128)S(1)} %get-tuple-element.17), channel_id=1, source_target_pairs={{0,8},{8,0},{16,24},{24,16},{32,40},{40,32},{48,56},{56,48},{64,72... | collective-permute-start | bytes 98312 | tf_op jit(solution)/shard_map/ppermute | solution.py:14
  15.2 6.7 %multiply_bitcast_fusion = (f32[1,128,16,256]{3,2,1,0:T(8,128)S(1)}, f32[128,16,256]{2,1,0:T(8,128)}) fusion(f32[2,128,16,256]{3,2,1,0:T(8,128)} %param.9, f32[128,16,256]{2,1,0:T(8,128)} %param.11), kind=kLoop, calls=%fused_computation.61 | loop fusion | flops 7864320 | bytes 10485760 | tf_op jit(solution)/shard_map/stack | solution.py:93
  22.0 1.6 %broadcast_multiply_fusion = f32[128,16,256]{2,1,0:T(8,128)} fusion(f32[128,16,256]{2,1,0:T(8,128)S(1)} %copy-done.1), kind=kLoop, calls=%fused_computation.62 | loop fusion | flops 524288 | bytes 4194304 | tf_op jit(solution)/shard_map/mul | solution.py:94
  24.1 4.6 %collective-permute-start.10 = (f32[2,16,256]{2,1,0:T(8,128)S(1)}, f32[2,16,256]{2,1,0:T(8,128)S(1)}, u32[]{:S(2)}, u32[]{:S(2)}) collective-permute-start(f32[2,16,256]{2,1,0:T(8,128)S(1)} %add.198), channel_id=1, source_target_pairs={{0,16},{8,24},{16,0},{24,8},{32,48},{40,56},{48,32},{56,40},{64,80... | collective-permute-start | bytes 98312 | tf_op jit(solution)/shard_map/ppermute | solution.py:14
  28.6 2.5 %constant_dynamic-update-slice_fusion.1 = f32[2,128,18,256]{3,2,1,0:T(8,128)} fusion(f32[2,128,16,256]{3,2,1,0:T(8,128)S(1)} %copy-done), kind=kLoop, calls=%fused_computation.131 | loop fusion | bytes 8388608
  31.1 5.5 %collective-permute-start.11 = (f32[2,16,256]{2,1,0:T(8,128)S(1)}, f32[2,16,256]{2,1,0:T(8,128)S(1)}, u32[]{:S(2)}, u32[]{:S(2)}) collective-permute-start(f32[2,16,256]{2,1,0:T(8,128)S(1)} %add.199), channel_id=1, source_target_pairs={{0,32},{8,40},{16,48},{24,56},{32,0},{40,8},{48,16},{56,24},{64,96... | collective-permute-start | bytes 98312 | tf_op jit(solution)/shard_map/ppermute | solution.py:14
  36.6 0.8 broadcast_select_fusion
  37.4 1.7 %collective-permute-done.11 = f32[2,16,256]{2,1,0:T(8,128)S(1)} collective-permute-done((f32[2,16,256]{2,1,0:T(8,128)S(1)}, f32[2,16,256]{2,1,0:T(8,128)S(1)}, u32[]{:S(2)}, u32[]{:S(2)}) %collective-permute-start.11) | collective-permute-done | bytes 32800 | tf_op jit(solution)/shard_map/ppermute | solution.py:14
  39.1 2.7 %collective-permute-start.12 = (f32[2,16,256]{2,1,0:T(8,128)S(1)}, f32[2,16,256]{2,1,0:T(8,128)S(1)}, u32[]{:S(2)}, u32[]{:S(2)}) collective-permute-start(f32[2,16,256]{2,1,0:T(8,128)S(1)} %add.200), channel_id=1, source_target_pairs={{0,64},{8,72},{16,80},{24,88},{32,96},{40,104},{48,112},{56,120},{... | collective-permute-start | bytes 98312 | tf_op jit(solution)/shard_map/ppermute | solution.py:14
  41.9 1.9 %collective-permute-done.12 = f32[2,16,256]{2,1,0:T(8,128)S(1)} collective-permute-done((f32[2,16,256]{2,1,0:T(8,128)S(1)}, f32[2,16,256]{2,1,0:T(8,128)S(1)}, u32[]{:S(2)}, u32[]{:S(2)}) %collective-permute-start.12) | collective-permute-done | bytes 32800 | tf_op jit(solution)/shard_map/ppermute | solution.py:14
  43.8 3.8 %collective-permute-start.13 = (f32[2,16,256]{2,1,0:T(8,128)S(1)}, f32[2,16,256]{2,1,0:T(8,128)S(1)}, u32[]{:S(2)}, u32[]{:S(2)}) collective-permute-start(f32[2,16,256]{2,1,0:T(8,128)S(1)} %add.201), channel_id=1, source_target_pairs={{0,128},{8,136},{16,144},{24,152},{32,160},{40,168},{48,176},{56,1... | collective-permute-start | bytes 98312 | tf_op jit(solution)/shard_map/ppermute | solution.py:14
  47.6 1.1 constant_dynamic-update-slice_fusion
  48.6 25.9 %fusion.8 = f32[2,128,16,256]{3,2,1,0:T(8,128)} fusion(f32[2,128,16,256]{3,2,1,0:T(8,128)} %param.9, f32[2,2,16,256]{3,2,1,0:T(8,128)S(1)} %broadcast_select_fusion, f32[2,2,16,256]{3,2,1,0:T(8,128)S(1)} %broadcast_select_fusion.1, f32[2,128,2,256]{3,2,1,0:T(2,128)S(1)} %collective-permute-done.2, f32[2,128,18,256]{3,2,1,0:T(8,128)} %constant_dynamic-update-slice_fusion, ...), kind=kLoop, calls=%fused_computation.20 | loop fusion | flops 35651584 | bytes 23724032 | tf_op jit(solution)/shard_map/add | solution.py:94
  74.5 5.3 %copy.12 = f32[2,128,16,256]{1,3,2,0:T(8,128)} copy(f32[2,128,16,256]{3,2,1,0:T(8,128)} %fusion.8) | data formatting | bytes 8388608 | tf_op jit(solution)/shard_map/add | solution.py:94
  79.9 5.8 %fusion.55 = f32[2,1,16,256]{3,1,2,0:T(1,128)S(1)} fusion(f32[2,128,16,256]{1,3,2,0:T(8,128)} %copy.12, f32[2,128,128]{2,1,0:T(8,128)S(1)} %bitcast.177), kind=kOutput, calls=%fused_computation.133 | convolution fusion | flops 12582912 | bytes 4228096 | tf_op jit(solution)/shard_map/sj,sjzy->szy/dot_general | solution.py:134
  86.7 2.7 %collective-permute-start.14 = (f32[2,16,256]{2,1,0:T(8,128)S(1)}, f32[2,16,256]{2,1,0:T(8,128)S(1)}, u32[]{:S(2)}, u32[]{:S(2)}) collective-permute-start(f32[2,16,256]{2,1,0:T(8,128)S(1)} %add.202), channel_id=1, source_target_pairs={{0,1},{1,0},{2,3},{3,2},{4,5},{5,4},{6,7},{7,6},{8,9},{9,8},{10,11... | collective-permute-start | bytes 98312 | tf_op jit(solution)/shard_map/ppermute | solution.py:25
  89.6 0.9 collective-permute-start.5
  90.5 0.9 collective-permute-done.14
  91.5 1.4 %collective-permute-start.15 = (f32[2,32,256]{2,1,0:T(8,128)S(1)}, f32[2,32,256]{2,1,0:T(8,128)S(1)}, u32[]{:S(2)}, u32[]{:S(2)}) collective-permute-start(f32[2,32,256]{2,1,0:T(8,128)S(1)} %maximum_select_fusion.2), channel_id=1, source_target_pairs={{0,2},{1,3},{2,0},{3,1},{4,6},{5,7},{6,4},{7,5},{8,10},{9,11},{10,... | collective-permute-start | bytes 196616 | tf_op jit(solution)/shard_map/ppermute | solution.py:25
  92.9 2.9 %collective-permute-done.5 = f32[2,2,16,256]{3,2,1,0:T(8,128)S(1)} collective-permute-done((f32[2,2,16,256]{3,2,1,0:T(8,128)S(1)}, f32[2,2,16,256]{3,2,1,0:T(8,128)S(1)}, u32[]{:S(2)}, u32[]{:S(2)}) %collective-permute-start.5) | collective-permute-done | bytes 65568 | tf_op jit(solution)/shard_map/ppermute | solution.py:46
  95.9 4.6 %collective-permute-start.6 = (f32[2,2,16,256]{3,2,1,0:T(8,128)S(1)}, f32[2,2,16,256]{3,2,1,0:T(8,128)S(1)}, u32[]{:S(2)}, u32[]{:S(2)}) collective-permute-start(f32[2,2,16,256]{3,2,1,0:T(8,128)S(1)} %pad_maximum_fusion.5), channel_id=1, source_target_pairs={{0,32},{8,40},{16,48},{24,56},{32,0},{40,8},{48,16},{56,24},{64,96... | collective-permute-start | bytes 196616 | tf_op jit(solution)/shard_map/ppermute | solution.py:46
  100.7 4.9 %collective-permute-done.6 = f32[2,2,16,256]{3,2,1,0:T(8,128)S(1)} collective-permute-done((f32[2,2,16,256]{3,2,1,0:T(8,128)S(1)}, f32[2,2,16,256]{3,2,1,0:T(8,128)S(1)}, u32[]{:S(2)}, u32[]{:S(2)}) %collective-permute-start.6) | collective-permute-done | bytes 65568 | tf_op jit(solution)/shard_map/ppermute | solution.py:46
  105.7 1.1 collective-permute-start.7
  107.0 3.3 %collective-permute-done.7 = f32[2,2,16,256]{3,2,1,0:T(8,128)S(1)} collective-permute-done((f32[2,2,16,256]{3,2,1,0:T(8,128)S(1)}, f32[2,2,16,256]{3,2,1,0:T(8,128)S(1)}, u32[]{:S(2)}, u32[]{:S(2)}) %collective-permute-start.7) | collective-permute-done | bytes 65568 | tf_op jit(solution)/shard_map/ppermute | solution.py:46
  110.7 5.6 %collective-permute-done.8 = f32[2,2,16,256]{3,2,1,0:T(8,128)S(1)} collective-permute-done((f32[2,2,16,256]{3,2,1,0:T(8,128)S(1)}, f32[2,2,16,256]{3,2,1,0:T(8,128)S(1)}, u32[]{:S(2)}, u32[]{:S(2)}) %collective-permute-start.8) | collective-permute-done | bytes 65568 | tf_op jit(solution)/shard_map/ppermute | solution.py:46
  116.3 7.3 %fusion.28 = f32[2,128,16,256]{1,3,2,0:T(8,128)} fusion(f32[2,128,16,256]{1,3,2,0:T(8,128)} %copy.12, f32[2,16,256]{2,1,0:T(8,128)S(1)} %get-tuple-element.26, f32[2,128]{1,0:T(2,128)S(1)} %get-tuple-element.8, f32[2,16,256]{2,1,0:T(8,128)S(1)} %get-tuple-element.25, f32[2,128]{1,0:T(2,128)S(1)} %get-tuple-element.7, ...), kind=kOutput, calls=%fused_computation.46 | convolution fusion | flops 1616904192 | bytes 8621056 | tf_op jit(solution)/shard_map/sij,sjzy->sizy/dot_general | solution.py:144
  123.7 5.4 %copy.13 = f32[2,128,16,256]{3,2,1,0:T(8,128)} copy(f32[2,128,16,256]{1,3,2,0:T(8,128)} %fusion.28) | data formatting | bytes 8388608 | tf_op jit(solution)/shard_map/add | solution.py:150
  (58 shorter events, 3.5 us)
Async XLA Ops:
  1.5 35.1 %collective-permute-start.1 = (f32[2,2,16,256]{3,2,1,0:T(8,128)}, f32[2,2,16,256]{3,2,1,0:T(8,128)}, u32[]{:S(2)}, u32[]{:S(2)}) collective-permute-start(f32[2,2,16,256]{3,2,1,0:T(8,128)} %get-tuple-element.22), channel_id=1, source_target_pairs={{8,0},{16,8},{24,16},{32,24},{40,32},{48,40},{56,48},{64,56},{72,6... | collective-permute-start | bytes 196616 | tf_op jit(solution)/shard_map/ppermute | solution.py:66
  2.8 39.1 %collective-permute-start = (f32[2,2,16,256]{3,2,1,0:T(8,128)}, f32[2,2,16,256]{3,2,1,0:T(8,128)S(1)}, u32[]{:S(2)}, u32[]{:S(2)}) collective-permute-start(f32[2,2,16,256]{3,2,1,0:T(8,128)} %get-tuple-element.21), channel_id=1, source_target_pairs={{0,8},{8,16},{16,24},{24,32},{32,40},{40,48},{48,56},{56,64},{64,7... | collective-permute-start | bytes 196616 | tf_op jit(solution)/shard_map/ppermute | solution.py:65
  9.4 39.2 %collective-permute-start.2 = (f32[2,128,2,256]{3,2,1,0:T(2,128)}, f32[2,128,2,256]{3,2,1,0:T(2,128)S(1)}, u32[]{:S(2)}, u32[]{:S(2)}) collective-permute-start(f32[2,128,2,256]{3,2,1,0:T(2,128)} %get-tuple-element.20), channel_id=1, source_target_pairs={{0,1},{1,2},{2,3},{3,4},{4,5},{5,6},{6,7},{7,0},{8,9},{9,10},{10,1... | collective-permute-start | bytes 1572872 | tf_op jit(solution)/shard_map/ppermute | solution.py:65
  10.9 36.7 %collective-permute-start.3 = (f32[2,128,2,256]{3,2,1,0:T(2,128)}, f32[2,128,2,256]{3,2,1,0:T(2,128)S(1)}, u32[]{:S(2)}, u32[]{:S(2)}) collective-permute-start(f32[2,128,2,256]{3,2,1,0:T(2,128)} %get-tuple-element.19), channel_id=1, source_target_pairs={{1,0},{2,1},{3,2},{4,3},{5,4},{6,5},{7,6},{0,7},{9,8},{10,9},{11,1... | collective-permute-start | bytes 1572872 | tf_op jit(solution)/shard_map/ppermute | solution.py:66
  13.2 10.9 %collective-permute-start.9 = (f32[2,16,256]{2,1,0:T(8,128)S(1)}, f32[2,16,256]{2,1,0:T(8,128)S(1)}, u32[]{:S(2)}, u32[]{:S(2)}) collective-permute-start(f32[2,16,256]{2,1,0:T(8,128)S(1)} %get-tuple-element.17), channel_id=1, source_target_pairs={{0,8},{8,0},{16,24},{24,16},{32,40},{40,32},{48,56},{56,48},{64,72... | collective-permute-start | bytes 98312 | tf_op jit(solution)/shard_map/ppermute | solution.py:14
  15.2 6.7 %copy-start.1 = (f32[128,16,256]{2,1,0:T(8,128)S(1)}, f32[128,16,256]{2,1,0:T(8,128)}, u32[]{:S(2)}) copy-start(f32[128,16,256]{2,1,0:T(8,128)} %param.10) | copy-start | bytes 6291460
  15.2 8.4 %copy-start.2 = (f32[2,1,128,128]{3,2,1,0:T(8,128)S(1)}, f32[2,1,128,128]{3,2,1,0:T(8,128)}, u32[]{:S(2)}) copy-start(f32[2,1,128,128]{3,2,1,0:T(8,128)} %param.12) | copy-start | bytes 393220
  22.0 1.8 %copy-start.3 = (f32[2,1,128]{2,1,0:T(1,128)S(1)}, f32[2,1,128]{2,1,0:T(1,128)}, u32[]{:S(2)}) copy-start(f32[2,1,128]{2,1,0:T(1,128)} %param.13) | copy-start | bytes 3076
  22.0 6.7 %copy-start = (f32[2,128,16,256]{3,2,1,0:T(8,128)S(1)}, f32[2,128,16,256]{3,2,1,0:T(8,128)}, u32[]{:S(2)}) copy-start(f32[2,128,16,256]{3,2,1,0:T(8,128)} %param.9) | copy-start | bytes 12582916
  24.1 7.0 %collective-permute-start.10 = (f32[2,16,256]{2,1,0:T(8,128)S(1)}, f32[2,16,256]{2,1,0:T(8,128)S(1)}, u32[]{:S(2)}, u32[]{:S(2)}) collective-permute-start(f32[2,16,256]{2,1,0:T(8,128)S(1)} %add.198), channel_id=1, source_target_pairs={{0,16},{8,24},{16,0},{24,8},{32,48},{40,56},{48,32},{56,40},{64,80... | collective-permute-start | bytes 98312 | tf_op jit(solution)/shard_map/ppermute | solution.py:14
  31.1 8.0 %collective-permute-start.11 = (f32[2,16,256]{2,1,0:T(8,128)S(1)}, f32[2,16,256]{2,1,0:T(8,128)S(1)}, u32[]{:S(2)}, u32[]{:S(2)}) collective-permute-start(f32[2,16,256]{2,1,0:T(8,128)S(1)} %add.199), channel_id=1, source_target_pairs={{0,32},{8,40},{16,48},{24,56},{32,0},{40,8},{48,16},{56,24},{64,96... | collective-permute-start | bytes 98312 | tf_op jit(solution)/shard_map/ppermute | solution.py:14
  39.1 4.6 %collective-permute-start.12 = (f32[2,16,256]{2,1,0:T(8,128)S(1)}, f32[2,16,256]{2,1,0:T(8,128)S(1)}, u32[]{:S(2)}, u32[]{:S(2)}) collective-permute-start(f32[2,16,256]{2,1,0:T(8,128)S(1)} %add.200), channel_id=1, source_target_pairs={{0,64},{8,72},{16,80},{24,88},{32,96},{40,104},{48,112},{56,120},{... | collective-permute-start | bytes 98312 | tf_op jit(solution)/shard_map/ppermute | solution.py:14
  43.8 42.9 %collective-permute-start.13 = (f32[2,16,256]{2,1,0:T(8,128)S(1)}, f32[2,16,256]{2,1,0:T(8,128)S(1)}, u32[]{:S(2)}, u32[]{:S(2)}) collective-permute-start(f32[2,16,256]{2,1,0:T(8,128)S(1)} %add.201), channel_id=1, source_target_pairs={{0,128},{8,136},{16,144},{24,152},{32,160},{40,168},{48,176},{56,1... | collective-permute-start | bytes 98312 | tf_op jit(solution)/shard_map/ppermute | solution.py:14
  79.8 36.4 %copy-start.4 = (f32[2,256]{1,0:T(2,128)S(1)}, f32[2,256]{1,0:T(2,128)}, u32[]{:S(2)}) copy-start(f32[2,256]{1,0:T(2,128)} %param.15) | copy-start | bytes 6148
  79.8 36.4 %copy-start.5 = (f32[2,256]{1,0:T(2,128)S(1)}, f32[2,256]{1,0:T(2,128)}, u32[]{:S(2)}) copy-start(f32[2,256]{1,0:T(2,128)} %param.14) | copy-start | bytes 6148
  85.7 3.8 %collective-permute-start.4 = (f32[2,2,16,256]{3,2,1,0:T(8,128)S(1)}, f32[2,2,16,256]{3,2,1,0:T(8,128)S(1)}, u32[]{:S(2)}, u32[]{:S(2)}) collective-permute-start(f32[2,2,16,256]{3,2,1,0:T(8,128)S(1)} %pad_maximum_fusion.3), channel_id=1, source_target_pairs={{0,8},{8,0},{16,24},{24,16},{32,40},{40,32},{48,56},{56,48},{64,72... | collective-permute-start | bytes 196616 | tf_op jit(solution)/shard_map/ppermute | solution.py:46
  86.7 4.8 %collective-permute-start.14 = (f32[2,16,256]{2,1,0:T(8,128)S(1)}, f32[2,16,256]{2,1,0:T(8,128)S(1)}, u32[]{:S(2)}, u32[]{:S(2)}) collective-permute-start(f32[2,16,256]{2,1,0:T(8,128)S(1)} %add.202), channel_id=1, source_target_pairs={{0,1},{1,0},{2,3},{3,2},{4,5},{5,4},{6,7},{7,6},{8,9},{9,8},{10,11... | collective-permute-start | bytes 98312 | tf_op jit(solution)/shard_map/ppermute | solution.py:25
  89.6 6.2 %collective-permute-start.5 = (f32[2,2,16,256]{3,2,1,0:T(8,128)S(1)}, f32[2,2,16,256]{3,2,1,0:T(8,128)S(1)}, u32[]{:S(2)}, u32[]{:S(2)}) collective-permute-start(f32[2,2,16,256]{3,2,1,0:T(8,128)S(1)} %pad_maximum_fusion.4), channel_id=1, source_target_pairs={{0,16},{8,24},{16,0},{24,8},{32,48},{40,56},{48,32},{56,40},{64,80... | collective-permute-start | bytes 196616 | tf_op jit(solution)/shard_map/ppermute | solution.py:46
  91.5 9.1 %collective-permute-start.15 = (f32[2,32,256]{2,1,0:T(8,128)S(1)}, f32[2,32,256]{2,1,0:T(8,128)S(1)}, u32[]{:S(2)}, u32[]{:S(2)}) collective-permute-start(f32[2,32,256]{2,1,0:T(8,128)S(1)} %maximum_select_fusion.2), channel_id=1, source_target_pairs={{0,2},{1,3},{2,0},{3,1},{4,6},{5,7},{6,4},{7,5},{8,10},{9,11},{10,... | collective-permute-start | bytes 196616 | tf_op jit(solution)/shard_map/ppermute | solution.py:25
  95.9 9.7 %collective-permute-start.6 = (f32[2,2,16,256]{3,2,1,0:T(8,128)S(1)}, f32[2,2,16,256]{3,2,1,0:T(8,128)S(1)}, u32[]{:S(2)}, u32[]{:S(2)}) collective-permute-start(f32[2,2,16,256]{3,2,1,0:T(8,128)S(1)} %pad_maximum_fusion.5), channel_id=1, source_target_pairs={{0,32},{8,40},{16,48},{24,56},{32,0},{40,8},{48,16},{56,24},{64,96... | collective-permute-start | bytes 196616 | tf_op jit(solution)/shard_map/ppermute | solution.py:46
  100.6 6.4 %collective-permute-start.16 = (f32[2,64,256]{2,1,0:T(8,128)S(1)}, f32[2,64,256]{2,1,0:T(8,128)S(1)}, u32[]{:S(2)}, u32[]{:S(2)}) collective-permute-start(f32[2,64,256]{2,1,0:T(8,128)S(1)} %maximum_select_fusion.1), channel_id=1, source_target_pairs={{0,4},{1,5},{2,6},{3,7},{4,0},{5,1},{6,2},{7,3},{8,12},{9,13},{10,... | collective-permute-start | bytes 393224 | tf_op jit(solution)/shard_map/ppermute | solution.py:25
  105.7 4.6 %collective-permute-start.7 = (f32[2,2,16,256]{3,2,1,0:T(8,128)S(1)}, f32[2,2,16,256]{3,2,1,0:T(8,128)S(1)}, u32[]{:S(2)}, u32[]{:S(2)}) collective-permute-start(f32[2,2,16,256]{3,2,1,0:T(8,128)S(1)} %pad_maximum_fusion.6), channel_id=1, source_target_pairs={{0,64},{8,72},{16,80},{24,88},{32,96},{40,104},{48,112},{56,120},{... | collective-permute-start | bytes 196616 | tf_op jit(solution)/shard_map/ppermute | solution.py:46
  110.4 5.9 %collective-permute-start.8 = (f32[2,2,16,256]{3,2,1,0:T(8,128)S(1)}, f32[2,2,16,256]{3,2,1,0:T(8,128)S(1)}, u32[]{:S(2)}, u32[]{:S(2)}) collective-permute-start(f32[2,2,16,256]{3,2,1,0:T(8,128)S(1)} %pad_maximum_fusion.7), channel_id=1, source_target_pairs={{0,128},{8,136},{16,144},{24,152},{32,160},{40,168},{48,176},{56,1... | collective-permute-start | bytes 196616 | tf_op jit(solution)/shard_map/ppermute | solution.py:46

commit v3 on v2

--- a/solution.py
+++ b/solution.py
@@ -115,10 +115,7 @@
     local_plane = station_index[0] - owner_row * plane_count
     own_slice = lax.dynamic_index_in_dim(scalars, local_plane, 1, keepdims=False)
     mine = stream_rank == owner_row
-    arrived = xor_sum(jnp.where(mine, own_slice, jnp.zeros_like(own_slice)), "gx")
-    station_plane = xor_gather(arrived, "gz", 1)
-    inflow_full = make_inflow(station_plane, mean_profile, recycle_gain, span_shift)
-    inflow = lax.dynamic_slice_in_dim(inflow_full, span_rank * span_cells, span_cells, 1)
+    candidate = jnp.where(mine, own_slice, jnp.zeros_like(own_slice))
     stream_padded = with_halo(scalars, (("gx", 1),), 2, False)
     edge_shape = (scalars.shape[0], 2, scalars.shape[2], scalars.shape[3])
     outlet_planes = jnp.broadcast_to(scalars[:, -1:], edge_shape)
@@ -127,6 +124,11 @@
     window = jnp.concatenate([head_planes, stream_padded[:, 2:-2], tail_planes], axis=1)
     span_padded = with_halo(scalars, (("gz", 2),), 2, True)
     explicit = explicit_part(window, span_padded, scalars, diffusivity, reaction_rate)
+    candidate, explicit = lax.optimization_barrier((candidate, explicit))
+    arrived = xor_sum(candidate, "gx")
+    station_plane = xor_gather(arrived, "gz", 1)
+    inflow_full = make_inflow(station_plane, mean_profile, recycle_gain, span_shift)
+    inflow = lax.dynamic_slice_in_dim(inflow_full, span_rank * span_cells, span_cells, 1)
     inverse = block_inverse[:, 0]
     response = block_response[:, 0]
     first_gain = jnp.where(at_inlet, diffusivity[0] * (15.0 / 12.0), 0.0)

time: 130 us -> 130 us (level)
  the two profiles are of different devices: /device:TPU:2 before, /device:TPU:32 now
where the time goes in v3:
time: 130 us; the launch traced here: 127 us
  other arithmetic  35.9 us (28%)
  starting transfers between devices  33.9 us (26%)
  local copies, waits for them, and re-layouts  22.1 us (17%)
  waiting for transfers between devices  20.5 us (16%)
  matrix products  13.1 us (10%)
  between operations  1.61 us (1%)
    add x1, other arithmetic, explicit_part(): return center + diffusivity[None] * laplacian + source  25.8 us
    ppermute x5, starting transfers between devices, xor_sum(): x = x + lax.ppermute(x, axis, pairs)  12.9 us
    ppermute x5, starting transfers between devices, exclusive_scan(): other = lax.ppermute(jnp.stack(total), axis, pairs)  11.8 us
    ppermute x3, waiting for transfers between devices, xor_gather(): other = lax.ppermute(x, axis, pairs)  9.84 us
    ppermute x5, waiting for transfers between devices, xor_sum(): x = x + lax.ppermute(x, axis, pairs)  9.78 us
    another operation x1, other arithmetic, explicit_part(): jnp.stack([reaction_yields[0] * reaction, reaction_yields[1] * reaction])  7.9 us
    dot_general x1, matrix products, on_device(): jnp.einsum('sij,sjzy->sizy', inverse, explicit, precision=lax.Precision.H...  7.32 us
    dot_general x1, matrix products, on_device(): jnp.einsum('sj,sjzy->szy', inverse[:, -1], explicit, precision=lax.Precis...  5.77 us
  transfers between devices with their start and end apart: 17, of which 8 were waited for; matrix products, arithmetic and copies ran while one was open for 16% of the time, Pallas kernels for 0%

profile of v3, /device:TPU:32, one launch (start us, length us, event | category | flops | bytes accessed | tf_op | source)
XLA Modules:
  0.0 127.1 jit_solution(6661552037015150152)
XLA Ops:
  0.0 1.5 %fusion.59 = (f32[2,2,16,256]{3,2,1,0:T(8,128)}, f32[2,2,16,256]{3,2,1,0:T(8,128)}) fusion(f32[2,128,16,256]{3,2,1,0:T(8,128)} %param.9), kind=kLoop, calls=%fused_computation.140 | loop fusion | bytes 262144 | tf_op jit(solution)/shard_map/slice | solution.py:63
  1.5 1.3 %collective-permute-start.1 = (f32[2,2,16,256]{3,2,1,0:T(8,128)}, f32[2,2,16,256]{3,2,1,0:T(8,128)S(1)}, u32[]{:S(2)}, u32[]{:S(2)}) collective-permute-start(f32[2,2,16,256]{3,2,1,0:T(8,128)} %get-tuple-element.24), channel_id=1, source_target_pairs={{8,0},{16,8},{24,16},{32,24},{40,32},{48,40},{56,48},{64,56},{72,6... | collective-permute-start | bytes 196616 | tf_op jit(solution)/shard_map/ppermute | solution.py:66
  2.8 3.0 %collective-permute-start = (f32[2,2,16,256]{3,2,1,0:T(8,128)}, f32[2,2,16,256]{3,2,1,0:T(8,128)S(1)}, u32[]{:S(2)}, u32[]{:S(2)}) collective-permute-start(f32[2,2,16,256]{3,2,1,0:T(8,128)} %get-tuple-element.23), channel_id=1, source_target_pairs={{0,8},{8,16},{16,24},{24,32},{32,40},{40,48},{48,56},{56,64},{64,7... | collective-permute-start | bytes 196616 | tf_op jit(solution)/shard_map/ppermute | solution.py:65
  5.9 3.6 %fusion.58 = (f32[2,128,2,256]{3,2,1,0:T(2,128)}, f32[2,128,2,256]{3,2,1,0:T(2,128)}) fusion(f32[2,128,16,256]{3,2,1,0:T(8,128)} %param.9), kind=kLoop, calls=%fused_computation.139 | loop fusion | bytes 2097152 | tf_op jit(solution)/shard_map/slice | solution.py:64
  9.4 1.5 %collective-permute-start.2 = (f32[2,128,2,256]{3,2,1,0:T(2,128)}, f32[2,128,2,256]{3,2,1,0:T(2,128)S(1)}, u32[]{:S(2)}, u32[]{:S(2)}) collective-permute-start(f32[2,128,2,256]{3,2,1,0:T(2,128)} %get-tuple-element.22), channel_id=1, source_target_pairs={{0,1},{1,2},{2,3},{3,4},{4,5},{5,6},{6,7},{7,0},{8,9},{9,10},{10,1... | collective-permute-start | bytes 1572872 | tf_op jit(solution)/shard_map/ppermute | solution.py:65
  10.9 2.6 %collective-permute-start.3 = (f32[2,128,2,256]{3,2,1,0:T(2,128)}, f32[2,128,2,256]{3,2,1,0:T(2,128)S(1)}, u32[]{:S(2)}, u32[]{:S(2)}) collective-permute-start(f32[2,128,2,256]{3,2,1,0:T(2,128)} %get-tuple-element.21), channel_id=1, source_target_pairs={{1,0},{2,1},{3,2},{4,3},{5,4},{6,5},{7,6},{0,7},{9,8},{10,9},{11,1... | collective-permute-start | bytes 1572872 | tf_op jit(solution)/shard_map/ppermute | solution.py:66
  14.3 7.9 %multiply_bitcast_fusion = (f32[1,128,16,256]{3,2,1,0:T(8,128)S(1)}, f32[128,16,256]{2,1,0:T(8,128)}, f32[128,16,256]{2,1,0:T(8,128)}) fusion(f32[2,128,16,256]{3,2,1,0:T(8,128)} %param.9, f32[128,16,256]{2,1,0:T(8,128)} %param.11, f32[128,16,256]{2,1,0:T(8,128)} %param.10), kind=kLoop, calls=%fused_computation.61 | loop fusion | flops 8388608 | bytes 14680064 | tf_op jit(solution)/shard_map/stack | solution.py:93
  22.2 0.7 select_bitcast_fusion.2
  23.3 0.8 slice_bitcast_fusion.6
  24.1 4.7 %constant_dynamic-update-slice_fusion.1 = f32[2,128,18,256]{3,2,1,0:T(8,128)} fusion(f32[2,128,16,256]{3,2,1,0:T(8,128)} %param.9), kind=kLoop, calls=%fused_computation.131 | loop fusion | bytes 8388608
  28.8 1.0 constant_dynamic-update-slice_fusion
  29.9 25.8 %fusion.8 = f32[2,128,16,256]{3,2,1,0:T(8,128)} fusion(f32[2,128,16,256]{3,2,1,0:T(8,128)} %param.9, f32[2,2,16,256]{3,2,1,0:T(8,128)S(1)} %broadcast_select_fusion, f32[2,2,16,256]{3,2,1,0:T(8,128)S(1)} %broadcast_select_fusion.1, f32[2,128,2,256]{3,2,1,0:T(2,128)S(1)} %collective-permute-done.2, f32[2,128,18,256]{3,2,1,0:T(8,128)} %constant_dynamic-update-slice_fusion, ...), kind=kLoop, calls=%fused_computation.20 | loop fusion | flops 35651584 | bytes 23724032 | tf_op jit(solution)/shard_map/add | solution.py:94
  55.7 5.3 %copy.12 = f32[2,128,16,256]{1,3,2,0:T(8,128)} copy(f32[2,128,16,256]{3,2,1,0:T(8,128)} %fusion.8) | data formatting | bytes 8388608 | tf_op jit(solution)/shard_map/optimization_barrier | solution.py:127
  61.0 5.8 %fusion.55 = f32[2,1,16,256]{3,1,2,0:T(1,128)S(1)} fusion(f32[2,128,16,256]{1,3,2,0:T(8,128)} %copy.12, f32[2,128,128]{2,1,0:T(8,128)S(1)} %bitcast.177), kind=kOutput, calls=%fused_computation.133 | convolution fusion | flops 12582912 | bytes 4228096 | tf_op jit(solution)/shard_map/sj,sjzy->szy/dot_general | solution.py:136
  66.8 2.4 %collective-permute-start.4 = (f32[2,2,16,256]{3,2,1,0:T(8,128)S(1)}, f32[2,2,16,256]{3,2,1,0:T(8,128)S(1)}, u32[]{:S(2)}, u32[]{:S(2)}) collective-permute-start(f32[2,2,16,256]{3,2,1,0:T(8,128)S(1)} %pad_maximum_fusion.3), channel_id=1, source_target_pairs={{0,8},{8,0},{16,24},{24,16},{32,40},{40,32},{48,56},{56,48},{64,72... | collective-permute-start | bytes 196616 | tf_op jit(solution)/shard_map/ppermute | solution.py:46
  69.5 0.9 collective-permute-done.9
  70.5 3.6 %collective-permute-start.10 = (f32[2,16,256]{2,1,0:T(8,128)S(1)}, f32[2,16,256]{2,1,0:T(8,128)S(1)}, u32[]{:S(2)}, u32[]{:S(2)}) collective-permute-start(f32[2,16,256]{2,1,0:T(8,128)S(1)} %add.198), channel_id=1, source_target_pairs={{0,16},{8,24},{16,0},{24,8},{32,48},{40,56},{48,32},{56,40},{64,80... | collective-permute-start | bytes 98312 | tf_op jit(solution)/shard_map/ppermute | solution.py:14
  74.3 3.3 %collective-permute-done.10 = f32[2,16,256]{2,1,0:T(8,128)S(1)} collective-permute-done((f32[2,16,256]{2,1,0:T(8,128)S(1)}, f32[2,16,256]{2,1,0:T(8,128)S(1)}, u32[]{:S(2)}, u32[]{:S(2)}) %collective-permute-start.10) | collective-permute-done | bytes 32800 | tf_op jit(solution)/shard_map/ppermute | solution.py:14
  77.6 5.7 %collective-permute-start.11 = (f32[2,16,256]{2,1,0:T(8,128)S(1)}, f32[2,16,256]{2,1,0:T(8,128)S(1)}, u32[]{:S(2)}, u32[]{:S(2)}) collective-permute-start(f32[2,16,256]{2,1,0:T(8,128)S(1)} %add.199), channel_id=1, source_target_pairs={{0,32},{8,40},{16,48},{24,56},{32,0},{40,8},{48,16},{56,24},{64,96... | collective-permute-start | bytes 98312 | tf_op jit(solution)/shard_map/ppermute | solution.py:14
  83.3 2.3 %collective-permute-done.11 = f32[2,16,256]{2,1,0:T(8,128)S(1)} collective-permute-done((f32[2,16,256]{2,1,0:T(8,128)S(1)}, f32[2,16,256]{2,1,0:T(8,128)S(1)}, u32[]{:S(2)}, u32[]{:S(2)}) %collective-permute-start.11) | collective-permute-done | bytes 32800 | tf_op jit(solution)/shard_map/ppermute | solution.py:14
  85.7 1.6 %collective-permute-start.12 = (f32[2,16,256]{2,1,0:T(8,128)S(1)}, f32[2,16,256]{2,1,0:T(8,128)S(1)}, u32[]{:S(2)}, u32[]{:S(2)}) collective-permute-start(f32[2,16,256]{2,1,0:T(8,128)S(1)} %add.200), channel_id=1, source_target_pairs={{0,64},{8,72},{16,80},{24,88},{32,96},{40,104},{48,112},{56,120},{... | collective-permute-start | bytes 98312 | tf_op jit(solution)/shard_map/ppermute | solution.py:14
  87.4 5.2 %collective-permute-start.6 = (f32[2,2,16,256]{3,2,1,0:T(8,128)S(1)}, f32[2,2,16,256]{3,2,1,0:T(8,128)S(1)}, u32[]{:S(2)}, u32[]{:S(2)}) collective-permute-start(f32[2,2,16,256]{3,2,1,0:T(8,128)S(1)} %pad_maximum_fusion.5), channel_id=1, source_target_pairs={{0,32},{8,40},{16,48},{24,56},{32,0},{40,8},{48,16},{56,24},{64,96... | collective-permute-start | bytes 196616 | tf_op jit(solution)/shard_map/ppermute | solution.py:46
  92.6 1.7 %collective-permute-start.13 = (f32[2,16,256]{2,1,0:T(8,128)S(1)}, f32[2,16,256]{2,1,0:T(8,128)S(1)}, u32[]{:S(2)}, u32[]{:S(2)}) collective-permute-start(f32[2,16,256]{2,1,0:T(8,128)S(1)} %add.201), channel_id=1, source_target_pairs={{0,128},{8,136},{16,144},{24,152},{32,160},{40,168},{48,176},{56,1... | collective-permute-start | bytes 98312 | tf_op jit(solution)/shard_map/ppermute | solution.py:14
  95.2 3.2 %collective-permute-done.13 = f32[2,16,256]{2,1,0:T(8,128)S(1)} collective-permute-done((f32[2,16,256]{2,1,0:T(8,128)S(1)}, f32[2,16,256]{2,1,0:T(8,128)S(1)}, u32[]{:S(2)}, u32[]{:S(2)}) %collective-permute-start.13) | collective-permute-done | bytes 32800 | tf_op jit(solution)/shard_map/ppermute | solution.py:14
  99.1 3.2 %collective-permute-done.14 = f32[2,16,256]{2,1,0:T(8,128)S(1)} collective-permute-done((f32[2,16,256]{2,1,0:T(8,128)S(1)}, f32[2,16,256]{2,1,0:T(8,128)S(1)}, u32[]{:S(2)}, u32[]{:S(2)}) %collective-permute-start.14) | collective-permute-done | bytes 32800 | tf_op jit(solution)/shard_map/ppermute | solution.py:25
  102.4 0.7 collective-permute-start.15
  103.1 5.2 %collective-permute-done.15 = f32[2,32,256]{2,1,0:T(8,128)S(1)} collective-permute-done((f32[2,32,256]{2,1,0:T(8,128)S(1)}, f32[2,32,256]{2,1,0:T(8,128)S(1)}, u32[]{:S(2)}, u32[]{:S(2)}) %collective-permute-start.15) | collective-permute-done | bytes 65568 | tf_op jit(solution)/shard_map/ppermute | solution.py:25
  108.4 3.5 %collective-permute-start.8 = (f32[2,2,16,256]{3,2,1,0:T(8,128)S(1)}, f32[2,2,16,256]{3,2,1,0:T(8,128)S(1)}, u32[]{:S(2)}, u32[]{:S(2)}) collective-permute-start(f32[2,2,16,256]{3,2,1,0:T(8,128)S(1)} %pad_maximum_fusion.7), channel_id=1, source_target_pairs={{0,128},{8,136},{16,144},{24,152},{32,160},{40,168},{48,176},{56,1... | collective-permute-start | bytes 196616 | tf_op jit(solution)/shard_map/ppermute | solution.py:46
  111.9 1.4 %collective-permute-done.16 = f32[2,64,256]{2,1,0:T(8,128)S(1)} collective-permute-done((f32[2,64,256]{2,1,0:T(8,128)S(1)}, f32[2,64,256]{2,1,0:T(8,128)S(1)}, u32[]{:S(2)}, u32[]{:S(2)}) %collective-permute-start.16) | collective-permute-done | bytes 131104 | tf_op jit(solution)/shard_map/ppermute | solution.py:25
  113.4 0.9 collective-permute-done.8
  114.3 7.3 %fusion.28 = f32[2,128,16,256]{1,3,2,0:T(8,128)} fusion(f32[2,128,16,256]{1,3,2,0:T(8,128)} %copy.12, f32[2,16,256]{2,1,0:T(8,128)S(1)} %get-tuple-element.30, f32[2,128]{1,0:T(2,128)S(1)} %get-tuple-element.12, f32[2,16,256]{2,1,0:T(8,128)S(1)} %get-tuple-element.29, f32[2,128]{1,0:T(2,128)S(1)} %get-tuple-element.11, ...), kind=kOutput, calls=%fused_computation.46 | convolution fusion | flops 1616904192 | bytes 8621056 | tf_op jit(solution)/shard_map/sij,sjzy->sizy/dot_general | solution.py:146
  121.6 5.4 %copy.13 = f32[2,128,16,256]{3,2,1,0:T(8,128)} copy(f32[2,128,16,256]{1,3,2,0:T(8,128)} %fusion.28) | data formatting | bytes 8388608 | tf_op jit(solution)/shard_map/add | solution.py:152
  (53 shorter events, 2.3 us)
Async XLA Ops:
  1.5 27.3 %collective-permute-start.1 = (f32[2,2,16,256]{3,2,1,0:T(8,128)}, f32[2,2,16,256]{3,2,1,0:T(8,128)S(1)}, u32[]{:S(2)}, u32[]{:S(2)}) collective-permute-start(f32[2,2,16,256]{3,2,1,0:T(8,128)} %get-tuple-element.24), channel_id=1, source_target_pairs={{8,0},{16,8},{24,16},{32,24},{40,32},{48,40},{56,48},{64,56},{72,6... | collective-permute-start | bytes 196616 | tf_op jit(solution)/shard_map/ppermute | solution.py:66
  2.8 26.0 %collective-permute-start = (f32[2,2,16,256]{3,2,1,0:T(8,128)}, f32[2,2,16,256]{3,2,1,0:T(8,128)S(1)}, u32[]{:S(2)}, u32[]{:S(2)}) collective-permute-start(f32[2,2,16,256]{3,2,1,0:T(8,128)} %get-tuple-element.23), channel_id=1, source_target_pairs={{0,8},{8,16},{16,24},{24,32},{32,40},{40,48},{48,56},{56,64},{64,7... | collective-permute-start | bytes 196616 | tf_op jit(solution)/shard_map/ppermute | solution.py:65
  9.4 20.5 %collective-permute-start.2 = (f32[2,128,2,256]{3,2,1,0:T(2,128)}, f32[2,128,2,256]{3,2,1,0:T(2,128)S(1)}, u32[]{:S(2)}, u32[]{:S(2)}) collective-permute-start(f32[2,128,2,256]{3,2,1,0:T(2,128)} %get-tuple-element.22), channel_id=1, source_target_pairs={{0,1},{1,2},{2,3},{3,4},{4,5},{5,6},{6,7},{7,0},{8,9},{9,10},{10,1... | collective-permute-start | bytes 1572872 | tf_op jit(solution)/shard_map/ppermute | solution.py:65
  10.9 17.9 %collective-permute-start.3 = (f32[2,128,2,256]{3,2,1,0:T(2,128)}, f32[2,128,2,256]{3,2,1,0:T(2,128)S(1)}, u32[]{:S(2)}, u32[]{:S(2)}) collective-permute-start(f32[2,128,2,256]{3,2,1,0:T(2,128)} %get-tuple-element.21), channel_id=1, source_target_pairs={{1,0},{2,1},{3,2},{4,3},{5,4},{6,5},{7,6},{0,7},{9,8},{10,9},{11,1... | collective-permute-start | bytes 1572872 | tf_op jit(solution)/shard_map/ppermute | solution.py:66
  14.2 8.7 %copy-start = (f32[2,1,128,128]{3,2,1,0:T(8,128)S(1)}, f32[2,1,128,128]{3,2,1,0:T(8,128)}, u32[]{:S(2)}) copy-start(f32[2,1,128,128]{3,2,1,0:T(8,128)} %param.12) | copy-start | bytes 393220
  14.3 8.8 %copy-start.1 = (f32[2,1,128]{2,1,0:T(1,128)S(1)}, f32[2,1,128]{2,1,0:T(1,128)}, u32[]{:S(2)}) copy-start(f32[2,1,128]{2,1,0:T(1,128)} %param.13) | copy-start | bytes 3076
  61.0 53.2 %copy-start.2 = (f32[2,256]{1,0:T(2,128)S(1)}, f32[2,256]{1,0:T(2,128)}, u32[]{:S(2)}) copy-start(f32[2,256]{1,0:T(2,128)} %param.15) | copy-start | bytes 6148
  61.0 53.2 %copy-start.3 = (f32[2,256]{1,0:T(2,128)S(1)}, f32[2,256]{1,0:T(2,128)}, u32[]{:S(2)}) copy-start(f32[2,256]{1,0:T(2,128)} %param.14) | copy-start | bytes 6148
  66.8 7.2 %collective-permute-start.4 = (f32[2,2,16,256]{3,2,1,0:T(8,128)S(1)}, f32[2,2,16,256]{3,2,1,0:T(8,128)S(1)}, u32[]{:S(2)}, u32[]{:S(2)}) collective-permute-start(f32[2,2,16,256]{3,2,1,0:T(8,128)S(1)} %pad_maximum_fusion.3), channel_id=1, source_target_pairs={{0,8},{8,0},{16,24},{24,16},{32,40},{40,32},{48,56},{56,48},{64,72... | collective-permute-start | bytes 196616 | tf_op jit(solution)/shard_map/ppermute | solution.py:46
  69.2 1.2 collective-permute-start.9
  70.5 7.1 %collective-permute-start.10 = (f32[2,16,256]{2,1,0:T(8,128)S(1)}, f32[2,16,256]{2,1,0:T(8,128)S(1)}, u32[]{:S(2)}, u32[]{:S(2)}) collective-permute-start(f32[2,16,256]{2,1,0:T(8,128)S(1)} %add.198), channel_id=1, source_target_pairs={{0,16},{8,24},{16,0},{24,8},{32,48},{40,56},{48,32},{56,40},{64,80... | collective-permute-start | bytes 98312 | tf_op jit(solution)/shard_map/ppermute | solution.py:14
  74.2 13.0 %collective-permute-start.5 = (f32[2,2,16,256]{3,2,1,0:T(8,128)S(1)}, f32[2,2,16,256]{3,2,1,0:T(8,128)S(1)}, u32[]{:S(2)}, u32[]{:S(2)}) collective-permute-start(f32[2,2,16,256]{3,2,1,0:T(8,128)S(1)} %pad_maximum_fusion.4), channel_id=1, source_target_pairs={{0,16},{8,24},{16,0},{24,8},{32,48},{40,56},{48,32},{56,40},{64,80... | collective-permute-start | bytes 196616 | tf_op jit(solution)/shard_map/ppermute | solution.py:46
  77.6 8.1 %collective-permute-start.11 = (f32[2,16,256]{2,1,0:T(8,128)S(1)}, f32[2,16,256]{2,1,0:T(8,128)S(1)}, u32[]{:S(2)}, u32[]{:S(2)}) collective-permute-start(f32[2,16,256]{2,1,0:T(8,128)S(1)} %add.199), channel_id=1, source_target_pairs={{0,32},{8,40},{16,48},{24,56},{32,0},{40,8},{48,16},{56,24},{64,96... | collective-permute-start | bytes 98312 | tf_op jit(solution)/shard_map/ppermute | solution.py:14
  85.7 6.9 %collective-permute-start.12 = (f32[2,16,256]{2,1,0:T(8,128)S(1)}, f32[2,16,256]{2,1,0:T(8,128)S(1)}, u32[]{:S(2)}, u32[]{:S(2)}) collective-permute-start(f32[2,16,256]{2,1,0:T(8,128)S(1)} %add.200), channel_id=1, source_target_pairs={{0,64},{8,72},{16,80},{24,88},{32,96},{40,104},{48,112},{56,120},{... | collective-permute-start | bytes 98312 | tf_op jit(solution)/shard_map/ppermute | solution.py:14
  87.4 11.1 %collective-permute-start.6 = (f32[2,2,16,256]{3,2,1,0:T(8,128)S(1)}, f32[2,2,16,256]{3,2,1,0:T(8,128)S(1)}, u32[]{:S(2)}, u32[]{:S(2)}) collective-permute-start(f32[2,2,16,256]{3,2,1,0:T(8,128)S(1)} %pad_maximum_fusion.5), channel_id=1, source_target_pairs={{0,32},{8,40},{16,48},{24,56},{32,0},{40,8},{48,16},{56,24},{64,96... | collective-permute-start | bytes 196616 | tf_op jit(solution)/shard_map/ppermute | solution.py:46
  92.6 5.9 %collective-permute-start.13 = (f32[2,16,256]{2,1,0:T(8,128)S(1)}, f32[2,16,256]{2,1,0:T(8,128)S(1)}, u32[]{:S(2)}, u32[]{:S(2)}) collective-permute-start(f32[2,16,256]{2,1,0:T(8,128)S(1)} %add.201), channel_id=1, source_target_pairs={{0,128},{8,136},{16,144},{24,152},{32,160},{40,168},{48,176},{56,1... | collective-permute-start | bytes 98312 | tf_op jit(solution)/shard_map/ppermute | solution.py:14
  98.5 3.9 %collective-permute-start.14 = (f32[2,16,256]{2,1,0:T(8,128)S(1)}, f32[2,16,256]{2,1,0:T(8,128)S(1)}, u32[]{:S(2)}, u32[]{:S(2)}) collective-permute-start(f32[2,16,256]{2,1,0:T(8,128)S(1)} %add.202), channel_id=1, source_target_pairs={{0,1},{1,0},{2,3},{3,2},{4,5},{5,4},{6,7},{7,6},{8,9},{9,8},{10,11... | collective-permute-start | bytes 98312 | tf_op jit(solution)/shard_map/ppermute | solution.py:25
  98.6 4.4 %collective-permute-start.7 = (f32[2,2,16,256]{3,2,1,0:T(8,128)S(1)}, f32[2,2,16,256]{3,2,1,0:T(8,128)S(1)}, u32[]{:S(2)}, u32[]{:S(2)}) collective-permute-start(f32[2,2,16,256]{3,2,1,0:T(8,128)S(1)} %pad_maximum_fusion.6), channel_id=1, source_target_pairs={{0,64},{8,72},{16,80},{24,88},{32,96},{40,104},{48,112},{56,120},{... | collective-permute-start | bytes 196616 | tf_op jit(solution)/shard_map/ppermute | solution.py:46
  102.4 5.9 %collective-permute-start.15 = (f32[2,32,256]{2,1,0:T(8,128)S(1)}, f32[2,32,256]{2,1,0:T(8,128)S(1)}, u32[]{:S(2)}, u32[]{:S(2)}) collective-permute-start(f32[2,32,256]{2,1,0:T(8,128)S(1)} %maximum_select_fusion.2), channel_id=1, source_target_pairs={{0,2},{1,3},{2,0},{3,1},{4,6},{5,7},{6,4},{7,5},{8,10},{9,11},{10,... | collective-permute-start | bytes 196616 | tf_op jit(solution)/shard_map/ppermute | solution.py:25
  108.3 5.1 %collective-permute-start.16 = (f32[2,64,256]{2,1,0:T(8,128)S(1)}, f32[2,64,256]{2,1,0:T(8,128)S(1)}, u32[]{:S(2)}, u32[]{:S(2)}) collective-permute-start(f32[2,64,256]{2,1,0:T(8,128)S(1)} %maximum_select_fusion.1), channel_id=1, source_target_pairs={{0,4},{1,5},{2,6},{3,7},{4,0},{5,1},{6,2},{7,3},{8,12},{9,13},{10,... | collective-permute-start | bytes 393224 | tf_op jit(solution)/shard_map/ppermute | solution.py:25
  108.4 5.9 %collective-permute-start.8 = (f32[2,2,16,256]{3,2,1,0:T(8,128)S(1)}, f32[2,2,16,256]{3,2,1,0:T(8,128)S(1)}, u32[]{:S(2)}, u32[]{:S(2)}) collective-permute-start(f32[2,2,16,256]{3,2,1,0:T(8,128)S(1)} %pad_maximum_fusion.7), channel_id=1, source_target_pairs={{0,128},{8,136},{16,144},{24,152},{32,160},{40,168},{48,176},{56,1... | collective-permute-start | bytes 196616 | tf_op jit(solution)/shard_map/ppermute | solution.py:46

commit v4 on v2

--- a/solution.py
+++ b/solution.py
@@ -35,7 +35,7 @@
     return (later[0] * earlier[0], later[0] * earlier[1] + later[1])
 
 
-def exclusive_scan(part, axis):
+def exclusive_scan(part, carried, axis):
     devices = lax.axis_size(axis)
     place = lax.axis_index(axis)
     total = part
@@ -43,7 +43,8 @@
     step = 1
     while step < devices:
         pairs = [(i, i ^ step) for i in range(devices)]
-        other = lax.ppermute(jnp.stack(total), axis, pairs)
+        other = lax.ppermute(jnp.stack(total + (carried,)), axis, pairs)
+        carried = carried + other[2]
         other = (other[0], other[1])
         later = (place & step) != 0
         new_before = compose(other, before)
@@ -52,7 +53,7 @@
             lambda a, b: jnp.where(later, a, b), compose(other, total), compose(total, other)
         )
         step *= 2
-    return before
+    return before, carried
 
 
 def with_halo(x, sides, width, wrap):
@@ -115,10 +116,10 @@
     local_plane = station_index[0] - owner_row * plane_count
     own_slice = lax.dynamic_index_in_dim(scalars, local_plane, 1, keepdims=False)
     mine = stream_rank == owner_row
-    arrived = xor_sum(jnp.where(mine, own_slice, jnp.zeros_like(own_slice)), "gx")
-    station_plane = xor_gather(arrived, "gz", 1)
+    station_plane = xor_gather(own_slice, "gz", 1)
     inflow_full = make_inflow(station_plane, mean_profile, recycle_gain, span_shift)
-    inflow = lax.dynamic_slice_in_dim(inflow_full, span_rank * span_cells, span_cells, 1)
+    own_inflow = lax.dynamic_slice_in_dim(inflow_full, span_rank * span_cells, span_cells, 1)
+    candidate = jnp.where(mine, own_inflow, jnp.zeros_like(own_inflow))
     stream_padded = with_halo(scalars, (("gx", 1),), 2, False)
     edge_shape = (scalars.shape[0], 2, scalars.shape[2], scalars.shape[3])
     outlet_planes = jnp.broadcast_to(scalars[:, -1:], edge_shape)
@@ -139,7 +140,7 @@
         + inverse[:, -1, 0][:, None, None] * first_gain
         + inverse[:, -1, 1][:, None, None] * second_gain
     )
-    through, upstream_sum = exclusive_scan((exit_gain, exit_plane), "gx")
+    (through, upstream_sum), inflow = exclusive_scan((exit_gain, exit_plane), candidate, "gx")
     incoming = through * inflow + upstream_sum
     local_part = jnp.einsum(
         "sij,sjzy->sizy", inverse, explicit, precision=lax.Precision.HIGHEST

time: 130 us -> 128 us (0.985)
  the two profiles are of different devices: /device:TPU:2 before, /device:TPU:12 now
where the time goes in v4:
time: 128 us
  other arithmetic  34.8 us (27%)
  waiting for transfers between devices  34.3 us (27%)
  local copies, waits for them, and re-layouts  22 us (17%)
  starting transfers between devices  21.9 us (17%)
  matrix products  13.1 us (10%)
  between operations  1.62 us (1%)
    add x1, other arithmetic, explicit_part(): return center + diffusivity[None] * laplacian + source  25.8 us
    ppermute x5, waiting for transfers between devices, exclusive_scan(): other = lax.ppermute(jnp.stack(total + (carried,)), axis, pairs)  24.7 us
    ppermute x3, waiting for transfers between devices, xor_gather(): other = lax.ppermute(x, axis, pairs)  9.67 us
    ppermute x2, starting transfers between devices, with_halo(): after = lax.ppermute(first, axis, down)  8.07 us
    dot_general x1, matrix products, on_device(): jnp.einsum('sij,sjzy->sizy', inverse, explicit, precision=lax.Precision.H...  7.31 us
    another operation x1, other arithmetic, explicit_part(): jnp.stack([reaction_yields[0] * reaction, reaction_yields[1] * reaction])  6.71 us
    dot_general x1, matrix products, on_device(): jnp.einsum('sj,sjzy->szy', inverse[:, -1], explicit, precision=lax.Precis...  5.74 us
    ppermute x5, starting transfers between devices, exclusive_scan(): other = lax.ppermute(jnp.stack(total + (carried,)), axis, pairs)  5.7 us
  transfers between devices with their start and end apart: 12, of which 7 were waited for; matrix products, arithmetic and copies ran while one was open for 14% of the time, Pallas kernels for 0%

profile of v4, /device:TPU:12, one launch (start us, length us, event | category | flops | bytes accessed | tf_op | source)
XLA Modules:
  0.0 127.7 jit_solution(9389765086506248766)
XLA Ops:
  0.0 0.9 fusion.68
  0.9 7.5 %collective-permute-start.1 = (f32[2,2,16,256]{3,2,1,0:T(8,128)S(1)}, f32[2,2,16,256]{3,2,1,0:T(8,128)S(1)}, u32[]{:S(2)}, u32[]{:S(2)}) collective-permute-start(f32[2,2,16,256]{3,2,1,0:T(8,128)S(1)} %get-tuple-element.22), channel_id=1, source_target_pairs={{8,0},{16,8},{24,16},{32,24},{40,32},{48,40},{56,48},{64,56},{72,6... | collective-permute-start | bytes 196616 | tf_op jit(solution)/shard_map/ppermute | solution.py:67
  8.4 1.9 %collective-permute-start = (f32[2,2,16,256]{3,2,1,0:T(8,128)S(1)}, f32[2,2,16,256]{3,2,1,0:T(8,128)S(1)}, u32[]{:S(2)}, u32[]{:S(2)}) collective-permute-start(f32[2,2,16,256]{3,2,1,0:T(8,128)S(1)} %get-tuple-element.21), channel_id=1, source_target_pairs={{0,8},{8,16},{16,24},{24,32},{32,40},{40,48},{48,56},{56,64},{64,7... | collective-permute-start | bytes 196616 | tf_op jit(solution)/shard_map/ppermute | solution.py:66
  10.4 3.6 %fusion.67 = (f32[2,128,2,256]{3,2,1,0:T(2,128)}, f32[2,128,2,256]{3,2,1,0:T(2,128)}) fusion(f32[2,128,16,256]{3,2,1,0:T(8,128)} %param.9), kind=kLoop, calls=%fused_computation.152 | loop fusion | bytes 2097152 | tf_op jit(solution)/shard_map/slice | solution.py:65
  13.9 0.5 collective-permute-start.3
  14.4 1.5 %collective-permute-start.2 = (f32[2,128,2,256]{3,2,1,0:T(2,128)}, f32[2,128,2,256]{3,2,1,0:T(2,128)S(1)}, u32[]{:S(2)}, u32[]{:S(2)}) collective-permute-start(f32[2,128,2,256]{3,2,1,0:T(2,128)} %get-tuple-element.20), channel_id=1, source_target_pairs={{0,1},{1,2},{2,3},{3,4},{4,5},{5,6},{6,7},{7,0},{8,9},{9,10},{10,1... | collective-permute-start | bytes 1572872 | tf_op jit(solution)/shard_map/ppermute | solution.py:66
  16.6 0.8 dynamic-slice_bitcast_fusion
  17.4 3.3 %collective-permute-start.4 = (f32[2,16,256]{2,1,0:T(8,128)S(1)}, f32[2,16,256]{2,1,0:T(8,128)S(1)}, u32[]{:S(2)}, u32[]{:S(2)}) collective-permute-start(f32[2,16,256]{2,1,0:T(8,128)S(1)} %get-tuple-element.17), channel_id=1, source_target_pairs={{0,1},{1,0},{2,3},{3,2},{4,5},{5,4},{6,7},{7,6},{8,9},{9,8},{10,11... | collective-permute-start | bytes 98312 | tf_op jit(solution)/shard_map/ppermute | solution.py:25
  20.7 6.7 %multiply_bitcast_fusion = (f32[1,128,16,256]{3,2,1,0:T(8,128)S(1)}, f32[128,16,256]{2,1,0:T(8,128)}) fusion(f32[2,128,16,256]{3,2,1,0:T(8,128)} %param.9, f32[128,16,256]{2,1,0:T(8,128)} %param.11), kind=kLoop, calls=%fused_computation.61 | loop fusion | flops 7864320 | bytes 10485760 | tf_op jit(solution)/shard_map/stack | solution.py:94
  27.4 1.6 %broadcast_multiply_fusion = f32[128,16,256]{2,1,0:T(8,128)} fusion(f32[128,16,256]{2,1,0:T(8,128)S(1)} %copy-done.1), kind=kLoop, calls=%fused_computation.62 | loop fusion | flops 524288 | bytes 4194304 | tf_op jit(solution)/shard_map/mul | solution.py:95
  29.1 0.2 slice_reduce_fusion.3
  29.2 0.2 slice_reduce_fusion.4
  29.5 0.9 copy-done
  30.4 2.5 %constant_dynamic-update-slice_fusion.1 = f32[2,128,18,256]{3,2,1,0:T(8,128)} fusion(f32[2,128,16,256]{3,2,1,0:T(8,128)S(1)} %copy-done), kind=kLoop, calls=%fused_computation.143 | loop fusion | bytes 8388608
  33.7 5.7 %collective-permute-done.5 = f32[2,32,256]{2,1,0:T(8,128)S(1)} collective-permute-done((f32[2,32,256]{2,1,0:T(8,128)S(1)}, f32[2,32,256]{2,1,0:T(8,128)S(1)}, u32[]{:S(2)}, u32[]{:S(2)}) %collective-permute-start.5) | collective-permute-done | bytes 65568 | tf_op jit(solution)/shard_map/ppermute | solution.py:25
  39.5 1.3 %collective-permute-start.6 = (f32[2,64,256]{2,1,0:T(8,128)S(1)}, f32[2,64,256]{2,1,0:T(8,128)S(1)}, u32[]{:S(2)}, u32[]{:S(2)}) collective-permute-start(f32[2,64,256]{2,1,0:T(8,128)S(1)} %maximum_select_fusion.1), channel_id=1, source_target_pairs={{0,4},{1,5},{2,6},{3,7},{4,0},{5,1},{6,2},{7,3},{8,12},{9,13},{10,... | collective-permute-start | bytes 393224 | tf_op jit(solution)/shard_map/ppermute | solution.py:25
  40.8 3.9 %collective-permute-done.6 = f32[2,64,256]{2,1,0:T(8,128)S(1)} collective-permute-done((f32[2,64,256]{2,1,0:T(8,128)S(1)}, f32[2,64,256]{2,1,0:T(8,128)S(1)}, u32[]{:S(2)}, u32[]{:S(2)}) %collective-permute-start.6) | collective-permute-done | bytes 131104 | tf_op jit(solution)/shard_map/ppermute | solution.py:25
  44.8 2.1 %constant_dynamic-update-slice_fusion = f32[2,128,18,256]{3,2,1,0:T(8,128)} fusion(f32[2,128,18,256]{3,2,1,0:T(8,128)} %constant_dynamic-update-slice_fusion.1, f32[2,128,2,256]{3,2,1,0:T(2,128)} %collective-permute-done.3), kind=kLoop, calls=%fused_computation.142 | loop fusion | bytes 1048576 | tf_op jit(solution)/shard_map/concatenate | solution.py:68
  46.9 25.8 %fusion.8 = f32[2,128,16,256]{3,2,1,0:T(8,128)} fusion(f32[2,128,16,256]{3,2,1,0:T(8,128)} %param.9, f32[2,2,16,256]{3,2,1,0:T(8,128)S(1)} %broadcast_select_fusion, f32[2,2,16,256]{3,2,1,0:T(8,128)S(1)} %broadcast_select_fusion.1, f32[2,128,2,256]{3,2,1,0:T(2,128)S(1)} %collective-permute-done.2, f32[2,128,18,256]{3,2,1,0:T(8,128)} %constant_dynamic-update-slice_fusion, ...), kind=kLoop, calls=%fused_computation.20 | loop fusion | flops 35651584 | bytes 23724032 | tf_op jit(solution)/shard_map/add | solution.py:95
  72.7 5.3 %copy.12 = f32[2,128,16,256]{1,3,2,0:T(8,128)} copy(f32[2,128,16,256]{3,2,1,0:T(8,128)} %fusion.8) | data formatting | bytes 8388608 | tf_op jit(solution)/shard_map/add | solution.py:95
  78.0 5.7 %fusion.62 = f32[2,1,16,256]{3,1,2,0:T(1,128)S(1)} fusion(f32[2,128,16,256]{1,3,2,0:T(8,128)} %copy.12, f32[2,128,128]{2,1,0:T(8,128)S(1)} %bitcast.225), kind=kOutput, calls=%fused_computation.145 | convolution fusion | flops 12582912 | bytes 4228096 | tf_op jit(solution)/shard_map/sj,sjzy->szy/dot_general | solution.py:135
  83.9 1.3 %collective-permute-done.7 = f32[3,2,16,256]{3,2,1,0:T(8,128)S(1)} collective-permute-done((f32[3,2,16,256]{3,2,1,0:T(8,128)S(1)}, f32[3,2,16,256]{3,2,1,0:T(8,128)S(1)}, u32[]{:S(2)}, u32[]{:S(2)}) %collective-permute-start.7) | collective-permute-done | bytes 98336 | tf_op jit(solution)/shard_map/ppermute | solution.py:46
  85.4 0.1 collective-permute-start.8
  85.5 7.8 %collective-permute-done.8 = f32[3,2,16,256]{3,2,1,0:T(8,128)S(1)} collective-permute-done((f32[3,2,16,256]{3,2,1,0:T(8,128)S(1)}, f32[3,2,16,256]{3,2,1,0:T(8,128)S(1)}, u32[]{:S(2)}, u32[]{:S(2)}) %collective-permute-start.8) | collective-permute-done | bytes 98336 | tf_op jit(solution)/shard_map/ppermute | solution.py:46
  93.4 3.2 %collective-permute-start.9 = (f32[3,2,16,256]{3,2,1,0:T(8,128)S(1)}, f32[3,2,16,256]{3,2,1,0:T(8,128)S(1)}, u32[]{:S(2)}, u32[]{:S(2)}) collective-permute-start(f32[3,2,16,256]{3,2,1,0:T(8,128)S(1)} %pad_maximum_fusion.5), channel_id=1, source_target_pairs={{0,32},{8,40},{16,48},{24,56},{32,0},{40,8},{48,16},{56,24},{64,96... | collective-permute-start | bytes 294920 | tf_op jit(solution)/shard_map/ppermute | solution.py:46
  96.7 7.1 %collective-permute-done.9 = f32[3,2,16,256]{3,2,1,0:T(8,128)S(1)} collective-permute-done((f32[3,2,16,256]{3,2,1,0:T(8,128)S(1)}, f32[3,2,16,256]{3,2,1,0:T(8,128)S(1)}, u32[]{:S(2)}, u32[]{:S(2)}) %collective-permute-start.9) | collective-permute-done | bytes 98336 | tf_op jit(solution)/shard_map/ppermute | solution.py:46
  104.0 4.6 %collective-permute-done.10 = f32[3,2,16,256]{3,2,1,0:T(8,128)S(1)} collective-permute-done((f32[3,2,16,256]{3,2,1,0:T(8,128)S(1)}, f32[3,2,16,256]{3,2,1,0:T(8,128)S(1)}, u32[]{:S(2)}, u32[]{:S(2)}) %collective-permute-start.10) | collective-permute-done | bytes 98336 | tf_op jit(solution)/shard_map/ppermute | solution.py:46
  108.6 2.2 %collective-permute-start.11 = (f32[3,2,16,256]{3,2,1,0:T(8,128)S(1)}, f32[3,2,16,256]{3,2,1,0:T(8,128)S(1)}, u32[]{:S(2)}, u32[]{:S(2)}) collective-permute-start(f32[3,2,16,256]{3,2,1,0:T(8,128)S(1)} %pad_maximum_fusion.7), channel_id=1, source_target_pairs={{0,128},{8,136},{16,144},{24,152},{32,160},{40,168},{48,176},{56,1... | collective-permute-start | bytes 294920 | tf_op jit(solution)/shard_map/ppermute | solution.py:46
  110.8 0.2 slice_reduce_fusion.1
  111.0 3.8 %collective-permute-done.11 = f32[3,2,16,256]{3,2,1,0:T(8,128)S(1)} collective-permute-done((f32[3,2,16,256]{3,2,1,0:T(8,128)S(1)}, f32[3,2,16,256]{3,2,1,0:T(8,128)S(1)}, u32[]{:S(2)}, u32[]{:S(2)}) %collective-permute-start.11) | collective-permute-done | bytes 98336 | tf_op jit(solution)/shard_map/ppermute | solution.py:46
  114.9 7.3 %fusion.28 = f32[2,128,16,256]{1,3,2,0:T(8,128)} fusion(f32[2,128,16,256]{1,3,2,0:T(8,128)} %copy.12, f32[2,16,256]{2,1,0:T(8,128)S(1)} %get-tuple-element.33, f32[2,128]{1,0:T(2,128)S(1)} %get-tuple-element.6, f32[2,16,256]{2,1,0:T(8,128)S(1)} %get-tuple-element.32, f32[2,128]{1,0:T(2,128)S(1)} %get-tuple-element.5, ...), kind=kOutput, calls=%fused_computation.46 | convolution fusion | flops 1616904192 | bytes 8621056 | tf_op jit(solution)/shard_map/sij,sjzy->sizy/dot_general | solution.py:145
  122.2 5.4 %copy.13 = f32[2,128,16,256]{3,2,1,0:T(8,128)} copy(f32[2,128,16,256]{1,3,2,0:T(8,128)} %fusion.28) | data formatting | bytes 8388608 | tf_op jit(solution)/shard_map/add | solution.py:151
  (44 shorter events, 1.0 us)
Async XLA Ops:
  0.9 32.8 %collective-permute-start.1 = (f32[2,2,16,256]{3,2,1,0:T(8,128)S(1)}, f32[2,2,16,256]{3,2,1,0:T(8,128)S(1)}, u32[]{:S(2)}, u32[]{:S(2)}) collective-permute-start(f32[2,2,16,256]{3,2,1,0:T(8,128)S(1)} %get-tuple-element.22), channel_id=1, source_target_pairs={{8,0},{16,8},{24,16},{32,24},{40,32},{48,40},{56,48},{64,56},{72,6... | collective-permute-start | bytes 196616 | tf_op jit(solution)/shard_map/ppermute | solution.py:67
  8.4 32.3 %collective-permute-start = (f32[2,2,16,256]{3,2,1,0:T(8,128)S(1)}, f32[2,2,16,256]{3,2,1,0:T(8,128)S(1)}, u32[]{:S(2)}, u32[]{:S(2)}) collective-permute-start(f32[2,2,16,256]{3,2,1,0:T(8,128)S(1)} %get-tuple-element.21), channel_id=1, source_target_pairs={{0,8},{8,16},{16,24},{24,32},{32,40},{40,48},{48,56},{56,64},{64,7... | collective-permute-start | bytes 196616 | tf_op jit(solution)/shard_map/ppermute | solution.py:66
  13.9 30.9 %collective-permute-start.3 = (f32[2,128,2,256]{3,2,1,0:T(2,128)}, f32[2,128,2,256]{3,2,1,0:T(2,128)}, u32[]{:S(2)}, u32[]{:S(2)}) collective-permute-start(f32[2,128,2,256]{3,2,1,0:T(2,128)} %get-tuple-element.19), channel_id=1, source_target_pairs={{1,0},{2,1},{3,2},{4,3},{5,4},{6,5},{7,6},{0,7},{9,8},{10,9},{11,1... | collective-permute-start | bytes 1572872 | tf_op jit(solution)/shard_map/ppermute | solution.py:67
  14.4 32.4 %collective-permute-start.2 = (f32[2,128,2,256]{3,2,1,0:T(2,128)}, f32[2,128,2,256]{3,2,1,0:T(2,128)S(1)}, u32[]{:S(2)}, u32[]{:S(2)}) collective-permute-start(f32[2,128,2,256]{3,2,1,0:T(2,128)} %get-tuple-element.20), channel_id=1, source_target_pairs={{0,1},{1,2},{2,3},{3,4},{4,5},{5,6},{6,7},{7,0},{8,9},{9,10},{10,1... | collective-permute-start | bytes 1572872 | tf_op jit(solution)/shard_map/ppermute | solution.py:66
  17.4 16.2 %collective-permute-start.4 = (f32[2,16,256]{2,1,0:T(8,128)S(1)}, f32[2,16,256]{2,1,0:T(8,128)S(1)}, u32[]{:S(2)}, u32[]{:S(2)}) collective-permute-start(f32[2,16,256]{2,1,0:T(8,128)S(1)} %get-tuple-element.17), channel_id=1, source_target_pairs={{0,1},{1,0},{2,3},{3,2},{4,5},{5,4},{6,7},{7,6},{8,9},{9,8},{10,11... | collective-permute-start | bytes 98312 | tf_op jit(solution)/shard_map/ppermute | solution.py:25
  20.7 6.7 %copy-start.1 = (f32[128,16,256]{2,1,0:T(8,128)S(1)}, f32[128,16,256]{2,1,0:T(8,128)}, u32[]{:S(2)}) copy-start(f32[128,16,256]{2,1,0:T(8,128)} %param.10) | copy-start | bytes 6291460
  20.7 8.3 %copy-start.2 = (f32[2,1,128,128]{3,2,1,0:T(8,128)S(1)}, f32[2,1,128,128]{3,2,1,0:T(8,128)}, u32[]{:S(2)}) copy-start(f32[2,1,128,128]{3,2,1,0:T(8,128)} %param.12) | copy-start | bytes 393220
  27.4 1.8 %copy-start.5 = (f32[2,1,128]{2,1,0:T(1,128)S(1)}, f32[2,1,128]{2,1,0:T(1,128)}, u32[]{:S(2)}) copy-start(f32[2,1,128]{2,1,0:T(1,128)} %param.13) | copy-start | bytes 3076
  27.4 3.0 %copy-start = (f32[2,128,16,256]{3,2,1,0:T(8,128)S(1)}, f32[2,128,16,256]{3,2,1,0:T(8,128)}, u32[]{:S(2)}) copy-start(f32[2,128,16,256]{3,2,1,0:T(8,128)} %param.9) | copy-start | bytes 12582916
  30.4 14.4 %copy-start.3 = (f32[2,256]{1,0:T(2,128)S(1)}, f32[2,256]{1,0:T(2,128)}, u32[]{:S(2)}) copy-start(f32[2,256]{1,0:T(2,128)} %param.15) | copy-start | bytes 6148
  30.4 14.4 %copy-start.4 = (f32[2,256]{1,0:T(2,128)S(1)}, f32[2,256]{1,0:T(2,128)}, u32[]{:S(2)}) copy-start(f32[2,256]{1,0:T(2,128)} %param.14) | copy-start | bytes 6148
  33.6 5.9 %collective-permute-start.5 = (f32[2,32,256]{2,1,0:T(8,128)S(1)}, f32[2,32,256]{2,1,0:T(8,128)S(1)}, u32[]{:S(2)}, u32[]{:S(2)}) collective-permute-start(f32[2,32,256]{2,1,0:T(8,128)S(1)} %maximum_select_fusion.2), channel_id=1, source_target_pairs={{0,2},{1,3},{2,0},{3,1},{4,6},{5,7},{6,4},{7,5},{8,10},{9,11},{10,... | collective-permute-start | bytes 196616 | tf_op jit(solution)/shard_map/ppermute | solution.py:25
  39.5 5.2 %collective-permute-start.6 = (f32[2,64,256]{2,1,0:T(8,128)S(1)}, f32[2,64,256]{2,1,0:T(8,128)S(1)}, u32[]{:S(2)}, u32[]{:S(2)}) collective-permute-start(f32[2,64,256]{2,1,0:T(8,128)S(1)} %maximum_select_fusion.1), channel_id=1, source_target_pairs={{0,4},{1,5},{2,6},{3,7},{4,0},{5,1},{6,2},{7,3},{8,12},{9,13},{10,... | collective-permute-start | bytes 393224 | tf_op jit(solution)/shard_map/ppermute | solution.py:25
  83.8 1.4 %collective-permute-start.7 = (f32[3,2,16,256]{3,2,1,0:T(8,128)S(1)}, f32[3,2,16,256]{3,2,1,0:T(8,128)S(1)}, u32[]{:S(2)}, u32[]{:S(2)}) collective-permute-start(f32[3,2,16,256]{3,2,1,0:T(8,128)S(1)} %pad_maximum_fusion.3), channel_id=1, source_target_pairs={{0,8},{8,0},{16,24},{24,16},{32,40},{40,32},{48,56},{56,48},{64,72... | collective-permute-start | bytes 294920 | tf_op jit(solution)/shard_map/ppermute | solution.py:46
  85.4 7.9 %collective-permute-start.8 = (f32[3,2,16,256]{3,2,1,0:T(8,128)S(1)}, f32[3,2,16,256]{3,2,1,0:T(8,128)S(1)}, u32[]{:S(2)}, u32[]{:S(2)}) collective-permute-start(f32[3,2,16,256]{3,2,1,0:T(8,128)S(1)} %pad_maximum_fusion.4), channel_id=1, source_target_pairs={{0,16},{8,24},{16,0},{24,8},{32,48},{40,56},{48,32},{56,40},{64,80... | collective-permute-start | bytes 294920 | tf_op jit(solution)/shard_map/ppermute | solution.py:46
  93.4 10.4 %collective-permute-start.9 = (f32[3,2,16,256]{3,2,1,0:T(8,128)S(1)}, f32[3,2,16,256]{3,2,1,0:T(8,128)S(1)}, u32[]{:S(2)}, u32[]{:S(2)}) collective-permute-start(f32[3,2,16,256]{3,2,1,0:T(8,128)S(1)} %pad_maximum_fusion.5), channel_id=1, source_target_pairs={{0,32},{8,40},{16,48},{24,56},{32,0},{40,8},{48,16},{56,24},{64,96... | collective-permute-start | bytes 294920 | tf_op jit(solution)/shard_map/ppermute | solution.py:46
  103.9 4.7 %collective-permute-start.10 = (f32[3,2,16,256]{3,2,1,0:T(8,128)S(1)}, f32[3,2,16,256]{3,2,1,0:T(8,128)S(1)}, u32[]{:S(2)}, u32[]{:S(2)}) collective-permute-start(f32[3,2,16,256]{3,2,1,0:T(8,128)S(1)} %pad_maximum_fusion.6), channel_id=1, source_target_pairs={{0,64},{8,72},{16,80},{24,88},{32,96},{40,104},{48,112},{56,120},{... | collective-permute-start | bytes 294920 | tf_op jit(solution)/shard_map/ppermute | solution.py:46
  108.6 6.2 %collective-permute-start.11 = (f32[3,2,16,256]{3,2,1,0:T(8,128)S(1)}, f32[3,2,16,256]{3,2,1,0:T(8,128)S(1)}, u32[]{:S(2)}, u32[]{:S(2)}) collective-permute-start(f32[3,2,16,256]{3,2,1,0:T(8,128)S(1)} %pad_maximum_fusion.7), channel_id=1, source_target_pairs={{0,128},{8,136},{16,144},{24,152},{32,160},{40,168},{48,176},{56,1... | collective-permute-start | bytes 294920 | tf_op jit(solution)/shard_map/ppermute | solution.py:46

commit v5 on v4

--- a/solution.py
+++ b/solution.py
@@ -1,9 +1,124 @@
+import functools
+
 import jax
 import jax.numpy as jnp
 from jax import lax
+from jax.experimental import pallas as pl
+from jax.experimental.pallas import tpu as pltpu
 from jax.sharding import PartitionSpec as P
 
 reaction_yields = (-1.0, 1.0)
+
+
+def softplus(v):
+    return jnp.maximum(v, 0.0) + jnp.log1p(jnp.exp(-jnp.abs(v)))
+
+
+def explicit_kernel(planes, rows, width,
+                    s_ref, head_ref, tail_ref, before_ref, after_ref, diff_ref, rate_ref, inv_ref,
+                    out_ref, exit_ref, ex_ref):
+    row = lax.broadcasted_iota(jnp.int32, (rows, width), 0)
+    lane = lax.broadcasted_iota(jnp.int32, (rows, width), 1)
+
+    def plane(s, k):
+        if isinstance(k, int) and k < 0:
+            return head_ref[s, pl.ds((k + 2) * rows, rows), :]
+        if isinstance(k, int) and k >= planes:
+            return tail_ref[s, pl.ds((k - planes) * rows, rows), :]
+        start = k * rows if isinstance(k, int) else pl.multiple_of(k * rows, rows)
+        return s_ref[s, pl.ds(start, rows), :]
+
+    def halo_row(ref, s, j, r):
+        return jnp.broadcast_to(ref[s, j, pl.ds(r, 1), :], (rows, width))
+
+    def one_plane(j, jm2, jm1, jp1, jp2):
+        centers = []
+        laps = []
+        for s in range(2):
+            c = plane(s, j)
+            sm2, sm1, sp1, sp2 = plane(s, jm2), plane(s, jm1), plane(s, jp1), plane(s, jp2)
+            b0, b1 = halo_row(before_ref, s, j, 0), halo_row(before_ref, s, j, 1)
+            a0, a1 = halo_row(after_ref, s, j, 0), halo_row(after_ref, s, j, 1)
+            zm1 = jnp.where(row == 0, b1, pltpu.roll(c, 1, 0))
+            zm2 = jnp.where(row == 0, b0, jnp.where(row == 1, b1, pltpu.roll(c, 2, 0)))
+            zp1 = jnp.where(row == rows - 1, a0, pltpu.roll(c, rows - 1, 0))
+            zp2 = jnp.where(row == rows - 1, a1, jnp.where(row == rows - 2, a0, pltpu.roll(c, rows - 2, 0)))
+            ym1 = jnp.where(lane < 1, 0.0, pltpu.roll(c, 1, 1))
+            ym2 = jnp.where(lane < 2, 0.0, pltpu.roll(c, 2, 1))
+            yp1 = jnp.where(lane >= width - 1, 0.0, pltpu.roll(c, width - 1, 1))
+            yp2 = jnp.where(lane >= width - 2, 0.0, pltpu.roll(c, width - 2, 1))
+            lap = (-sm2 + 16.0 * sm1 - 30.0 * c + 16.0 * sp1 - sp2) / 12.0
+            lap = lap + (-zm2 + 16.0 * zm1 - 30.0 * c + 16.0 * zp1 - zp2) / 12.0
+            lap = lap + (-ym2 + 16.0 * ym1 - 30.0 * c + 16.0 * yp1 - yp2) / 12.0
+            centers.append(c)
+            laps.append(lap)
+        start = j * rows if isinstance(j, int) else pl.multiple_of(j * rows, rows)
+        d = diff_ref[pl.ds(start, rows), :]
+        reaction = rate_ref[pl.ds(start, rows), :] * softplus(centers[0]) * softplus(centers[1])
+        for s in range(2):
+            value = centers[s] + d * laps[s] + reaction_yields[s] * reaction
+            for h in range(width // 128):
+                ex_ref[s, h, pl.ds(start, rows), :] = value[:, h * 128:(h + 1) * 128]
+
+    for j in (0, 1):
+        one_plane(j, j - 2, j - 1, j + 1, j + 2)
+
+    def body(j, carry):
+        one_plane(j, j - 2, j - 1, j + 1, j + 2)
+        return carry
+
+    lax.fori_loop(2, planes - 2, body, 0)
+    for j in (planes - 2, planes - 1):
+        one_plane(j, j - 2, j - 1, j + 1, j + 2)
+
+    for s in range(2):
+        inv = inv_ref[s]
+        for h in range(width // 128):
+
+            def mm(z, carry):
+                b = ex_ref[s, h, pl.ds(z, planes, stride=rows), :]
+                r = jnp.dot(
+                    inv, b, precision=lax.Precision.HIGHEST, preferred_element_type=jnp.float32
+                )
+                ex_ref[s, h, pl.ds(z, planes, stride=rows), :] = r
+                return carry
+
+            lax.fori_loop(0, rows, mm, 0)
+            exit_ref[s, :, pl.ds(h * 128, 128)] = ex_ref[s, h, pl.ds((planes - 1) * rows, rows), :]
+
+    chunk = 8 * rows
+
+    def put(c, carry):
+        start = pl.multiple_of(c * chunk, chunk)
+        for s in range(2):
+            for h in range(width // 128):
+                out_ref[s, pl.ds(start, chunk), pl.ds(h * 128, 128)] = ex_ref[s, h, pl.ds(start, chunk), :]
+        return carry
+
+    lax.fori_loop(0, planes // 8, put, 0)
+
+
+def explicit_local(scalars, head, tail, before, after, diffusivity, reaction_rate, inverse):
+    species, planes, rows, width = scalars.shape
+    flat = lambda a: a.reshape(a.shape[:-3] + (a.shape[-3] * rows, width))
+    vmem = pl.BlockSpec(memory_space=pltpu.VMEM)
+    out, exit_plane = pl.pallas_call(
+        functools.partial(explicit_kernel, planes, rows, width),
+        out_shape=(
+            jax.ShapeDtypeStruct((species, planes * rows, width), jnp.float32),
+            jax.ShapeDtypeStruct((species, rows, width), jnp.float32),
+        ),
+        in_specs=[vmem] * 8,
+        out_specs=(vmem, vmem),
+        scratch_shapes=[pltpu.VMEM((species, width // 128, planes * rows, 128), jnp.float32)],
+        compiler_params=pltpu.CompilerParams(vmem_limit_bytes=60 * 1024 * 1024),
+        cost_estimate=pl.CostEstimate(
+            flops=species * planes * rows * width * (2 * planes + 60),
+            transcendentals=2 * planes * rows * width * 2,
+            bytes_accessed=4 * (3 * species + 2) * planes * rows * width,
+        ),
+    )(flat(scalars), flat(head), flat(tail), before, after, flat(diffusivity), flat(reaction_rate), inverse)
+    return out.reshape(scalars.shape), exit_plane
 
 
 def xor_sum(x, axis):
@@ -56,43 +171,19 @@
     return before, carried
 
 
-def with_halo(x, sides, width, wrap):
-    for axis, dim in sides:
-        devices, length = (lax.axis_size(axis), x.shape[dim])
-        up = [(i, (i + 1) % devices) for i in range(devices if wrap else devices - 1)]
-        down = [(j, i) for i, j in up]
-        last = lax.slice_in_dim(x, length - width, length, axis=dim)
-        first = lax.slice_in_dim(x, 0, width, axis=dim)
-        before = lax.ppermute(last, axis, up)
-        after = lax.ppermute(first, axis, down)
-        x = jnp.concatenate([before, x, after], axis=dim)
-    return x
-
-
-def fourth_order(padded, dimension, length):
-
-    def shifted(offset):
-        return lax.slice_in_dim(padded, offset, offset + length, axis=dimension)
-
-    return (
-        -shifted(0) + 16.0 * shifted(1) - 30.0 * shifted(2) + 16.0 * shifted(3) - shifted(4)
-    ) / 12.0
+def halos(x, axis, dim, width, wrap):
+    devices, length = (lax.axis_size(axis), x.shape[dim])
+    up = [(i, (i + 1) % devices) for i in range(devices if wrap else devices - 1)]
+    down = [(j, i) for i, j in up]
+    last = lax.slice_in_dim(x, length - width, length, axis=dim)
+    first = lax.slice_in_dim(x, 0, width, axis=dim)
+    return lax.ppermute(last, axis, up), lax.ppermute(first, axis, down)
 
 
 def make_inflow(station_plane, mean_profile, recycle_gain, span_shift):
     span_mean = jnp.mean(station_plane, axis=1, keepdims=True)
     rolled = jnp.roll(station_plane, span_shift[0], axis=1)
     return mean_profile[:, None, :] + recycle_gain[:, None, :] * (rolled - span_mean)
-
-
-def explicit_part(stream_padded, span_padded, center, diffusivity, reaction_rate):
-    wall_padded = jnp.pad(center, ((0, 0), (0, 0), (0, 0), (2, 2)))
-    laplacian = fourth_order(stream_padded, 1, center.shape[1])
-    laplacian = laplacian + fourth_order(span_padded, 2, center.shape[2])
-    laplacian = laplacian + fourth_order(wall_padded, 3, center.shape[3])
-    reaction = reaction_rate * jax.nn.softplus(center[0]) * jax.nn.softplus(center[1])
-    source = jnp.stack([reaction_yields[0] * reaction, reaction_yields[1] * reaction])
-    return center + diffusivity[None] * laplacian + source
 
 
 def on_device(
@@ -120,20 +211,18 @@
     inflow_full = make_inflow(station_plane, mean_profile, recycle_gain, span_shift)
     own_inflow = lax.dynamic_slice_in_dim(inflow_full, span_rank * span_cells, span_cells, 1)
     candidate = jnp.where(mine, own_inflow, jnp.zeros_like(own_inflow))
-    stream_padded = with_halo(scalars, (("gx", 1),), 2, False)
+    head_planes, tail_planes = halos(scalars, "gx", 1, 2, False)
     edge_shape = (scalars.shape[0], 2, scalars.shape[2], scalars.shape[3])
     outlet_planes = jnp.broadcast_to(scalars[:, -1:], edge_shape)
-    head_planes = jnp.where(at_inlet, jnp.zeros(edge_shape, scalars.dtype), stream_padded[:, :2])
-    tail_planes = jnp.where(stream_rank == stream_devices - 1, outlet_planes, stream_padded[:, -2:])
-    window = jnp.concatenate([head_planes, stream_padded[:, 2:-2], tail_planes], axis=1)
-    span_padded = with_halo(scalars, (("gz", 2),), 2, True)
-    explicit = explicit_part(window, span_padded, scalars, diffusivity, reaction_rate)
+    head_planes = jnp.where(at_inlet, jnp.zeros(edge_shape, scalars.dtype), head_planes)
+    tail_planes = jnp.where(stream_rank == stream_devices - 1, outlet_planes, tail_planes)
+    before_rows, after_rows = halos(scalars, "gz", 2, 2, True)
     inverse = block_inverse[:, 0]
     response = block_response[:, 0]
     first_gain = jnp.where(at_inlet, diffusivity[0] * (15.0 / 12.0), 0.0)
     second_gain = jnp.where(at_inlet, diffusivity[1] * (-1.0 / 12.0), 0.0)
-    exit_plane = jnp.einsum(
-        "sj,sjzy->szy", inverse[:, -1], explicit, precision=lax.Precision.HIGHEST
+    local_part, exit_plane = explicit_local(
+        scalars, head_planes, tail_planes, before_rows, after_rows, diffusivity, reaction_rate, inverse
     )
     exit_gain = (
         response[:, -1][:, None, None]
@@ -142,9 +231,6 @@
     )
     (through, upstream_sum), inflow = exclusive_scan((exit_gain, exit_plane), candidate, "gx")
     incoming = through * inflow + upstream_sum
-    local_part = jnp.einsum(
-        "sij,sjzy->sizy", inverse, explicit, precision=lax.Precision.HIGHEST
-    )
     first_in = first_gain * inflow
     second_in = second_gain * inflow
     return (

time: 128 us -> 112 us (0.88)
  the two profiles are of different devices: /device:TPU:12 before, /device:TPU:32 now
where the time goes in v5:
time: 112 us; the launch traced here: 110 us
  Pallas kernels  35.7 us (32%)
  waiting for transfers between devices  29.5 us (26%)
  starting transfers between devices  27.3 us (24%)
  other arithmetic  8.98 us (8%)
  local copies, waits for them, and re-layouts  7.27 us (6%)
  between operations  1.55 us (1%)
    pallas_call x1, Pallas kernels, explicit_local(): pl.pallas_call(functools.partial(explicit_kernel, planes, rows, width), o...  35.7 us
    ppermute x5, starting transfers between devices, exclusive_scan(): other = lax.ppermute(jnp.stack(total + (carried,)), axis, pairs)  16.4 us
    ppermute x5, waiting for transfers between devices, exclusive_scan(): other = lax.ppermute(jnp.stack(total + (carried,)), axis, pairs)  15.5 us
    ppermute x3, waiting for transfers between devices, xor_gather(): other = lax.ppermute(x, axis, pairs)  13.9 us
    ppermute x4, starting transfers between devices, halos(): return (lax.ppermute(last, axis, up), lax.ppermute(first, axis, down))  6.43 us
    ppermute x3, starting transfers between devices, xor_gather(): other = lax.ppermute(x, axis, pairs)  4.51 us
    add x1, other arithmetic, on_device(): local_part + response[:, :, None, None] * incoming[:, None]  4.12 us
    slice x2, local copies, waits for them, and re-layouts, halos(): first = lax.slice_in_dim(x, 0, width, axis=dim)  3.47 us
  transfers between devices with their start and end apart: 12, of which 7 were waited for; matrix products, arithmetic and copies ran while one was open for 8% of the time, Pallas kernels for 0%

profile of v5, /device:TPU:32, one launch (start us, length us, event | category | flops | bytes accessed | tf_op | source)
XLA Modules:
  0.0 110.3 jit_solution(10658922562165080067)
XLA Ops:
  0.7 0.8 dynamic-slice_bitcast_fusion
  1.5 1.5 %collective-permute-start.4 = (f32[2,16,256]{2,1,0:T(8,128)S(1)}, f32[2,16,256]{2,1,0:T(8,128)S(1)}, u32[]{:S(2)}, u32[]{:S(2)}) collective-permute-start(f32[2,16,256]{2,1,0:T(8,128)S(1)} %get-tuple-element.19), channel_id=1, source_target_pairs={{0,1},{1,0},{2,3},{3,2},{4,5},{5,4},{6,7},{7,6},{8,9},{9,8},{10,11... | collective-permute-start | bytes 98312 | tf_op jit(solution)/shard_map/ppermute | solution.py:140
  3.0 0.9 fusion.26
  3.9 1.3 %collective-permute-start.1 = (f32[2,2,16,256]{3,2,1,0:T(8,128)S(1)}, f32[2,2,16,256]{3,2,1,0:T(8,128)S(1)}, u32[]{:S(2)}, u32[]{:S(2)}) collective-permute-start(f32[2,2,16,256]{3,2,1,0:T(8,128)S(1)} %get-tuple-element.23), channel_id=1, source_target_pairs={{8,0},{16,8},{24,16},{32,24},{40,32},{48,40},{56,48},{64,56},{72,6... | collective-permute-start | bytes 196616 | tf_op jit(solution)/shard_map/ppermute | solution.py:180
  5.2 3.0 %collective-permute-start = (f32[2,2,16,256]{3,2,1,0:T(8,128)S(1)}, f32[2,2,16,256]{3,2,1,0:T(8,128)S(1)}, u32[]{:S(2)}, u32[]{:S(2)}) collective-permute-start(f32[2,2,16,256]{3,2,1,0:T(8,128)S(1)} %get-tuple-element.24), channel_id=1, source_target_pairs={{0,8},{8,16},{16,24},{24,32},{32,40},{40,48},{48,56},{56,64},{64,7... | collective-permute-start | bytes 196616 | tf_op jit(solution)/shard_map/ppermute | solution.py:180
  8.2 2.6 %fusion.25 = (f32[2,128,2,256]{3,2,1,0:T(2,128)S(1)}, f32[2,128,2,256]{3,2,1,0:T(2,128)S(1)}) fusion(f32[2,128,16,256]{3,2,1,0:T(8,128)} %param.9), kind=kLoop, calls=%fused_computation.83 | loop fusion | bytes 2097152 | tf_op jit(solution)/shard_map/slice | solution.py:179
  10.8 1.7 %collective-permute-start.3 = (f32[2,128,2,256]{3,2,1,0:T(2,128)S(1)}, f32[2,128,2,256]{3,2,1,0:T(2,128)S(1)}, u32[]{:S(2)}, u32[]{:S(2)}) collective-permute-start(f32[2,128,2,256]{3,2,1,0:T(2,128)S(1)} %get-tuple-element.21), channel_id=1, source_target_pairs={{1,0},{2,1},{3,2},{4,3},{5,4},{6,5},{7,6},{0,7},{9,8},{10,9},{11,1... | collective-permute-start | bytes 1572872 | tf_op jit(solution)/shard_map/ppermute | solution.py:180
  12.6 0.4 collective-permute-start.2
  12.9 0.9 slice_reduce_fusion.4
  13.8 0.9 slice_reduce_fusion.3
  14.7 0.8 select_bitcast_fusion.1
  16.3 2.8 %collective-permute-start.5 = (f32[2,32,256]{2,1,0:T(8,128)S(1)}, f32[2,32,256]{2,1,0:T(8,128)S(1)}, u32[]{:S(2)}, u32[]{:S(2)}) collective-permute-start(f32[2,32,256]{2,1,0:T(8,128)S(1)} %maximum_select_fusion.2), channel_id=1, source_target_pairs={{0,2},{1,3},{2,0},{3,1},{4,6},{5,7},{6,4},{7,5},{8,10},{9,11},{10,... | collective-permute-start | bytes 196616 | tf_op jit(solution)/shard_map/ppermute | solution.py:140
  19.1 0.6 broadcast_select_fusion
  19.7 9.0 %collective-permute-done.5 = f32[2,32,256]{2,1,0:T(8,128)S(1)} collective-permute-done((f32[2,32,256]{2,1,0:T(8,128)S(1)}, f32[2,32,256]{2,1,0:T(8,128)S(1)}, u32[]{:S(2)}, u32[]{:S(2)}) %collective-permute-start.5) | collective-permute-done | bytes 65568 | tf_op jit(solution)/shard_map/ppermute | solution.py:140
  28.9 0.6 broadcast_select_fusion.1
  29.6 4.9 %collective-permute-done.6 = f32[2,64,256]{2,1,0:T(8,128)S(1)} collective-permute-done((f32[2,64,256]{2,1,0:T(8,128)S(1)}, f32[2,64,256]{2,1,0:T(8,128)S(1)}, u32[]{:S(2)}, u32[]{:S(2)}) %collective-permute-start.6) | collective-permute-done | bytes 131104 | tf_op jit(solution)/shard_map/ppermute | solution.py:140
  34.6 0.7 fusion.27
  35.3 0.8 copy-done.1
  36.3 35.7 %shard_map.91 = (f32[2,2048,256]{2,1,0:T(8,128)}, f32[2,16,256]{2,1,0:T(8,128)}) custom-call(f32[2,2048,256]{2,1,0:T(8,128)} %bitcast.165, f32[2,32,256]{2,1,0:T(8,128)} %bitcast.177, f32[2,32,256]{2,1,0:T(8,128)} %bitcast.176, f32[2,128,2,256]{3,2,1,0:T(2,128)} %copy-done.2, f32[2,128,2,256]{3,2,1,0:T(2,128)} %copy-done.1, f32[2048,256]{1,0:T(8,128)} %bitcast.167, ...), custom_call_target="tpu_custom_call" | custom-call | flops 331350016 | bytes 16777216 | tf_op jit(solution)/shard_map/pallas_call | solution.py:105
  72.0 0.8 pad_maximum_fusion
  72.8 0.5 collective-permute-start.7
  73.3 0.9 collective-permute-done.7
  74.3 0.8 fusion.19
  75.2 3.1 %collective-permute-start.8 = (f32[3,2,16,256]{3,2,1,0:T(8,128)S(1)}, f32[3,2,16,256]{3,2,1,0:T(8,128)S(1)}, u32[]{:S(2)}, u32[]{:S(2)}) collective-permute-start(f32[3,2,16,256]{3,2,1,0:T(8,128)S(1)} %pad_maximum_fusion.1), channel_id=1, source_target_pairs={{0,16},{8,24},{16,0},{24,8},{32,48},{40,56},{48,32},{56,40},{64,80... | collective-permute-start | bytes 294920 | tf_op jit(solution)/shard_map/ppermute | solution.py:161
  78.3 4.1 %collective-permute-done.8 = f32[3,2,16,256]{3,2,1,0:T(8,128)S(1)} collective-permute-done((f32[3,2,16,256]{3,2,1,0:T(8,128)S(1)}, f32[3,2,16,256]{3,2,1,0:T(8,128)S(1)}, u32[]{:S(2)}, u32[]{:S(2)}) %collective-permute-start.8) | collective-permute-done | bytes 98336 | tf_op jit(solution)/shard_map/ppermute | solution.py:161
  82.5 7.0 %collective-permute-start.9 = (f32[3,2,16,256]{3,2,1,0:T(8,128)S(1)}, f32[3,2,16,256]{3,2,1,0:T(8,128)S(1)}, u32[]{:S(2)}, u32[]{:S(2)}) collective-permute-start(f32[3,2,16,256]{3,2,1,0:T(8,128)S(1)} %pad_maximum_fusion.2), channel_id=1, source_target_pairs={{0,32},{8,40},{16,48},{24,56},{32,0},{40,8},{48,16},{56,24},{64,96... | collective-permute-start | bytes 294920 | tf_op jit(solution)/shard_map/ppermute | solution.py:161
  89.5 5.1 %collective-permute-done.9 = f32[3,2,16,256]{3,2,1,0:T(8,128)S(1)} collective-permute-done((f32[3,2,16,256]{3,2,1,0:T(8,128)S(1)}, f32[3,2,16,256]{3,2,1,0:T(8,128)S(1)}, u32[]{:S(2)}, u32[]{:S(2)}) %collective-permute-start.9) | collective-permute-done | bytes 98336 | tf_op jit(solution)/shard_map/ppermute | solution.py:161
  94.7 1.7 %collective-permute-start.10 = (f32[3,2,16,256]{3,2,1,0:T(8,128)S(1)}, f32[3,2,16,256]{3,2,1,0:T(8,128)S(1)}, u32[]{:S(2)}, u32[]{:S(2)}) collective-permute-start(f32[3,2,16,256]{3,2,1,0:T(8,128)S(1)} %pad_maximum_fusion.3), channel_id=1, source_target_pairs={{0,64},{8,72},{16,80},{24,88},{32,96},{40,104},{48,112},{56,120},{... | collective-permute-start | bytes 294920 | tf_op jit(solution)/shard_map/ppermute | solution.py:161
  96.5 3.0 %collective-permute-done.10 = f32[3,2,16,256]{3,2,1,0:T(8,128)S(1)} collective-permute-done((f32[3,2,16,256]{3,2,1,0:T(8,128)S(1)}, f32[3,2,16,256]{3,2,1,0:T(8,128)S(1)}, u32[]{:S(2)}, u32[]{:S(2)}) %collective-permute-start.10) | collective-permute-done | bytes 98336 | tf_op jit(solution)/shard_map/ppermute | solution.py:161
  99.5 4.0 %collective-permute-start.11 = (f32[3,2,16,256]{3,2,1,0:T(8,128)S(1)}, f32[3,2,16,256]{3,2,1,0:T(8,128)S(1)}, u32[]{:S(2)}, u32[]{:S(2)}) collective-permute-start(f32[3,2,16,256]{3,2,1,0:T(8,128)S(1)} %pad_maximum_fusion.4), channel_id=1, source_target_pairs={{0,128},{8,136},{16,144},{24,152},{32,160},{40,168},{48,176},{56,1... | collective-permute-start | bytes 294920 | tf_op jit(solution)/shard_map/ppermute | solution.py:161
  103.7 2.4 %collective-permute-done.11 = f32[3,2,16,256]{3,2,1,0:T(8,128)S(1)} collective-permute-done((f32[3,2,16,256]{3,2,1,0:T(8,128)S(1)}, f32[3,2,16,256]{3,2,1,0:T(8,128)S(1)}, u32[]{:S(2)}, u32[]{:S(2)}) %collective-permute-start.11) | collective-permute-done | bytes 98336 | tf_op jit(solution)/shard_map/ppermute | solution.py:161
  106.2 4.1 %multiply_add_fusion = f32[2,128,16,256]{3,2,1,0:T(8,128)} fusion(f32[2,128,16,256]{3,2,1,0:T(8,128)} %bitcast.166, f32[2,16,256]{2,1,0:T(8,128)S(1)} %get-tuple-element.35, f32[2,128]{1,0:T(2,128)S(1)} %get-tuple-element.10, f32[2,16,256]{2,1,0:T(8,128)S(1)} %get-tuple-element.34, f32[2,128]{1,0:T(2,128)S(1)} %get-tuple-element.9, ...), kind=kLoop, calls=%fused_computation | loop fusion | flops 6291456 | bytes 8489984 | tf_op jit(solution)/shard_map/add | solution.py:237
  (36 shorter events, 1.1 us)
Async XLA Ops:
  1.5 14.7 %collective-permute-start.4 = (f32[2,16,256]{2,1,0:T(8,128)S(1)}, f32[2,16,256]{2,1,0:T(8,128)S(1)}, u32[]{:S(2)}, u32[]{:S(2)}) collective-permute-start(f32[2,16,256]{2,1,0:T(8,128)S(1)} %get-tuple-element.19), channel_id=1, source_target_pairs={{0,1},{1,0},{2,3},{3,2},{4,5},{5,4},{6,7},{7,6},{8,9},{9,8},{10,11... | collective-permute-start | bytes 98312 | tf_op jit(solution)/shard_map/ppermute | solution.py:140
  3.9 15.2 %collective-permute-start.1 = (f32[2,2,16,256]{3,2,1,0:T(8,128)S(1)}, f32[2,2,16,256]{3,2,1,0:T(8,128)S(1)}, u32[]{:S(2)}, u32[]{:S(2)}) collective-permute-start(f32[2,2,16,256]{3,2,1,0:T(8,128)S(1)} %get-tuple-element.23), channel_id=1, source_target_pairs={{8,0},{16,8},{24,16},{32,24},{40,32},{48,40},{56,48},{64,56},{72,6... | collective-permute-start | bytes 196616 | tf_op jit(solution)/shard_map/ppermute | solution.py:180
  5.2 23.7 %collective-permute-start = (f32[2,2,16,256]{3,2,1,0:T(8,128)S(1)}, f32[2,2,16,256]{3,2,1,0:T(8,128)S(1)}, u32[]{:S(2)}, u32[]{:S(2)}) collective-permute-start(f32[2,2,16,256]{3,2,1,0:T(8,128)S(1)} %get-tuple-element.24), channel_id=1, source_target_pairs={{0,8},{8,16},{16,24},{24,32},{32,40},{40,48},{48,56},{56,64},{64,7... | collective-permute-start | bytes 196616 | tf_op jit(solution)/shard_map/ppermute | solution.py:180
  10.8 24.5 %collective-permute-start.3 = (f32[2,128,2,256]{3,2,1,0:T(2,128)S(1)}, f32[2,128,2,256]{3,2,1,0:T(2,128)S(1)}, u32[]{:S(2)}, u32[]{:S(2)}) collective-permute-start(f32[2,128,2,256]{3,2,1,0:T(2,128)S(1)} %get-tuple-element.21), channel_id=1, source_target_pairs={{1,0},{2,1},{3,2},{4,3},{5,4},{6,5},{7,6},{0,7},{9,8},{10,9},{11,1... | collective-permute-start | bytes 1572872 | tf_op jit(solution)/shard_map/ppermute | solution.py:180
  12.6 22.8 %collective-permute-start.2 = (f32[2,128,2,256]{3,2,1,0:T(2,128)S(1)}, f32[2,128,2,256]{3,2,1,0:T(2,128)S(1)}, u32[]{:S(2)}, u32[]{:S(2)}) collective-permute-start(f32[2,128,2,256]{3,2,1,0:T(2,128)S(1)} %get-tuple-element.22), channel_id=1, source_target_pairs={{0,1},{1,2},{2,3},{3,4},{4,5},{5,6},{6,7},{7,0},{8,9},{9,10},{10,1... | collective-permute-start | bytes 1572872 | tf_op jit(solution)/shard_map/ppermute | solution.py:180
  16.3 12.5 %collective-permute-start.5 = (f32[2,32,256]{2,1,0:T(8,128)S(1)}, f32[2,32,256]{2,1,0:T(8,128)S(1)}, u32[]{:S(2)}, u32[]{:S(2)}) collective-permute-start(f32[2,32,256]{2,1,0:T(8,128)S(1)} %maximum_select_fusion.2), channel_id=1, source_target_pairs={{0,2},{1,3},{2,0},{3,1},{4,6},{5,7},{6,4},{7,5},{8,10},{9,11},{10,... | collective-permute-start | bytes 196616 | tf_op jit(solution)/shard_map/ppermute | solution.py:140
  28.7 5.8 %collective-permute-start.6 = (f32[2,64,256]{2,1,0:T(8,128)S(1)}, f32[2,64,256]{2,1,0:T(8,128)S(1)}, u32[]{:S(2)}, u32[]{:S(2)}) collective-permute-start(f32[2,64,256]{2,1,0:T(8,128)S(1)} %maximum_select_fusion.1), channel_id=1, source_target_pairs={{0,4},{1,5},{2,6},{3,7},{4,0},{5,1},{6,2},{7,3},{8,12},{9,13},{10,... | collective-permute-start | bytes 393224 | tf_op jit(solution)/shard_map/ppermute | solution.py:140
  35.3 0.8 copy-start.1
  35.3 1.0 copy-start.2
  36.3 38.0 %copy-start.3 = (f32[2,256]{1,0:T(2,128)S(1)}, f32[2,256]{1,0:T(2,128)}, u32[]{:S(2)}) copy-start(f32[2,256]{1,0:T(2,128)} %param.15) | copy-start | bytes 6148
  36.3 38.0 %copy-start.4 = (f32[2,256]{1,0:T(2,128)S(1)}, f32[2,256]{1,0:T(2,128)}, u32[]{:S(2)}) copy-start(f32[2,256]{1,0:T(2,128)} %param.14) | copy-start | bytes 6148
  36.3 67.2 %copy-start = (f32[2,1,128,128]{3,2,1,0:T(8,128)S(1)}, f32[2,1,128,128]{3,2,1,0:T(8,128)}, u32[]{:S(2)}) copy-start(f32[2,1,128,128]{3,2,1,0:T(8,128)} %param.12) | copy-start | bytes 393220
  36.3 69.9 %copy-start.5 = (f32[2,1,128]{2,1,0:T(1,128)S(1)}, f32[2,1,128]{2,1,0:T(1,128)}, u32[]{:S(2)}) copy-start(f32[2,1,128]{2,1,0:T(1,128)} %param.13) | copy-start | bytes 3076
  72.8 1.5 %collective-permute-start.7 = (f32[3,2,16,256]{3,2,1,0:T(8,128)S(1)}, f32[3,2,16,256]{3,2,1,0:T(8,128)S(1)}, u32[]{:S(2)}, u32[]{:S(2)}) collective-permute-start(f32[3,2,16,256]{3,2,1,0:T(8,128)S(1)} %pad_maximum_fusion), channel_id=1, source_target_pairs={{0,8},{8,0},{16,24},{24,16},{32,40},{40,32},{48,56},{56,48},{64,72... | collective-permute-start | bytes 294920 | tf_op jit(solution)/shard_map/ppermute | solution.py:161
  75.2 7.2 %collective-permute-start.8 = (f32[3,2,16,256]{3,2,1,0:T(8,128)S(1)}, f32[3,2,16,256]{3,2,1,0:T(8,128)S(1)}, u32[]{:S(2)}, u32[]{:S(2)}) collective-permute-start(f32[3,2,16,256]{3,2,1,0:T(8,128)S(1)} %pad_maximum_fusion.1), channel_id=1, source_target_pairs={{0,16},{8,24},{16,0},{24,8},{32,48},{40,56},{48,32},{56,40},{64,80... | collective-permute-start | bytes 294920 | tf_op jit(solution)/shard_map/ppermute | solution.py:161
  82.5 12.1 %collective-permute-start.9 = (f32[3,2,16,256]{3,2,1,0:T(8,128)S(1)}, f32[3,2,16,256]{3,2,1,0:T(8,128)S(1)}, u32[]{:S(2)}, u32[]{:S(2)}) collective-permute-start(f32[3,2,16,256]{3,2,1,0:T(8,128)S(1)} %pad_maximum_fusion.2), channel_id=1, source_target_pairs={{0,32},{8,40},{16,48},{24,56},{32,0},{40,8},{48,16},{56,24},{64,96... | collective-permute-start | bytes 294920 | tf_op jit(solution)/shard_map/ppermute | solution.py:161
  94.7 4.7 %collective-permute-start.10 = (f32[3,2,16,256]{3,2,1,0:T(8,128)S(1)}, f32[3,2,16,256]{3,2,1,0:T(8,128)S(1)}, u32[]{:S(2)}, u32[]{:S(2)}) collective-permute-start(f32[3,2,16,256]{3,2,1,0:T(8,128)S(1)} %pad_maximum_fusion.3), channel_id=1, source_target_pairs={{0,64},{8,72},{16,80},{24,88},{32,96},{40,104},{48,112},{56,120},{... | collective-permute-start | bytes 294920 | tf_op jit(solution)/shard_map/ppermute | solution.py:161
  99.5 6.6 %collective-permute-start.11 = (f32[3,2,16,256]{3,2,1,0:T(8,128)S(1)}, f32[3,2,16,256]{3,2,1,0:T(8,128)S(1)}, u32[]{:S(2)}, u32[]{:S(2)}) collective-permute-start(f32[3,2,16,256]{3,2,1,0:T(8,128)S(1)} %pad_maximum_fusion.4), channel_id=1, source_target_pairs={{0,128},{8,136},{16,144},{24,152},{32,160},{40,168},{48,176},{56,1... | collective-permute-start | bytes 294920 | tf_op jit(solution)/shard_map/ppermute | solution.py:161

commit v6 on v5

--- a/solution.py
+++ b/solution.py
@@ -32,6 +32,10 @@
         return jnp.broadcast_to(ref[s, j, pl.ds(r, 1), :], (rows, width))
 
     def one_plane(j, jm2, jm1, jp1, jp2):
+        first_row, second_row = row == 0, row == 1
+        last_row, next_to_last_row = row == rows - 1, row == rows - 2
+        first_lane, second_lane = lane < 1, lane < 2
+        last_lane, next_to_last_lane = lane >= width - 1, lane >= width - 2
         centers = []
         laps = []
         for s in range(2):
@@ -39,17 +43,17 @@
             sm2, sm1, sp1, sp2 = plane(s, jm2), plane(s, jm1), plane(s, jp1), plane(s, jp2)
             b0, b1 = halo_row(before_ref, s, j, 0), halo_row(before_ref, s, j, 1)
             a0, a1 = halo_row(after_ref, s, j, 0), halo_row(after_ref, s, j, 1)
-            zm1 = jnp.where(row == 0, b1, pltpu.roll(c, 1, 0))
-            zm2 = jnp.where(row == 0, b0, jnp.where(row == 1, b1, pltpu.roll(c, 2, 0)))
-            zp1 = jnp.where(row == rows - 1, a0, pltpu.roll(c, rows - 1, 0))
-            zp2 = jnp.where(row == rows - 1, a1, jnp.where(row == rows - 2, a0, pltpu.roll(c, rows - 2, 0)))
-            ym1 = jnp.where(lane < 1, 0.0, pltpu.roll(c, 1, 1))
-            ym2 = jnp.where(lane < 2, 0.0, pltpu.roll(c, 2, 1))
-            yp1 = jnp.where(lane >= width - 1, 0.0, pltpu.roll(c, width - 1, 1))
-            yp2 = jnp.where(lane >= width - 2, 0.0, pltpu.roll(c, width - 2, 1))
-            lap = (-sm2 + 16.0 * sm1 - 30.0 * c + 16.0 * sp1 - sp2) / 12.0
-            lap = lap + (-zm2 + 16.0 * zm1 - 30.0 * c + 16.0 * zp1 - zp2) / 12.0
-            lap = lap + (-ym2 + 16.0 * ym1 - 30.0 * c + 16.0 * yp1 - yp2) / 12.0
+            zm1 = jnp.where(first_row, b1, pltpu.roll(c, 1, 0))
+            zm2 = jnp.where(first_row, b0, jnp.where(second_row, b1, pltpu.roll(c, 2, 0)))
+            zp1 = jnp.where(last_row, a0, pltpu.roll(c, rows - 1, 0))
+            zp2 = jnp.where(last_row, a1, jnp.where(next_to_last_row, a0, pltpu.roll(c, rows - 2, 0)))
+            ym1 = jnp.where(first_lane, 0.0, pltpu.roll(c, 1, 1))
+            ym2 = jnp.where(second_lane, 0.0, pltpu.roll(c, 2, 1))
+            yp1 = jnp.where(last_lane, 0.0, pltpu.roll(c, width - 1, 1))
+            yp2 = jnp.where(next_to_last_lane, 0.0, pltpu.roll(c, width - 2, 1))
+            near = (sm1 + sp1) + (zm1 + zp1) + (ym1 + yp1)
+            far = (sm2 + sp2) + (zm2 + zp2) + (ym2 + yp2)
+            lap = (16.0 * near - far - 90.0 * c) * (1.0 / 12.0)
             centers.append(c)
             laps.append(lap)
         start = j * rows if isinstance(j, int) else pl.multiple_of(j * rows, rows)

time: 112 us -> 112 us (level)
  no operation moved by 1% of the time
where the time goes in v6:
time: 112 us; the launch traced here: 111 us
  Pallas kernels  36.3 us (32%)
  waiting for transfers between devices  29.5 us (26%)
  starting transfers between devices  27.3 us (24%)
  other arithmetic  8.98 us (8%)
  local copies, waits for them, and re-layouts  7.21 us (6%)
  between operations  1.55 us (1%)
    pallas_call x1, Pallas kernels, explicit_local(): pl.pallas_call(functools.partial(explicit_kernel, planes, rows, width), o...  36.3 us
    ppermute x5, starting transfers between devices, exclusive_scan(): other = lax.ppermute(jnp.stack(total + (carried,)), axis, pairs)  16.4 us
    ppermute x5, waiting for transfers between devices, exclusive_scan(): other = lax.ppermute(jnp.stack(total + (carried,)), axis, pairs)  15.5 us
    ppermute x3, waiting for transfers between devices, xor_gather(): other = lax.ppermute(x, axis, pairs)  13.9 us
    ppermute x4, starting transfers between devices, halos(): return (lax.ppermute(last, axis, up), lax.ppermute(first, axis, down))  6.43 us
    ppermute x3, starting transfers between devices, xor_gather(): other = lax.ppermute(x, axis, pairs)  4.51 us
    add x1, other arithmetic, on_device(): local_part + response[:, :, None, None] * incoming[:, None]  4.12 us
    slice x2, local copies, waits for them, and re-layouts, halos(): first = lax.slice_in_dim(x, 0, width, axis=dim)  3.47 us
  transfers between devices with their start and end apart: 12, of which 7 were waited for; matrix products, arithmetic and copies ran while one was open for 8% of the time, Pallas kernels for 0%

profile of v6, /device:TPU:32, one launch (start us, length us, event | category | flops | bytes accessed | tf_op | source)
XLA Modules:
  0.0 110.8 jit_solution(17146460603809988686)
XLA Ops:
  0.7 0.8 dynamic-slice_bitcast_fusion
  1.5 1.5 %collective-permute-start.4 = (f32[2,16,256]{2,1,0:T(8,128)S(1)}, f32[2,16,256]{2,1,0:T(8,128)S(1)}, u32[]{:S(2)}, u32[]{:S(2)}) collective-permute-start(f32[2,16,256]{2,1,0:T(8,128)S(1)} %get-tuple-element.19), channel_id=1, source_target_pairs={{0,1},{1,0},{2,3},{3,2},{4,5},{5,4},{6,7},{7,6},{8,9},{9,8},{10,11... | collective-permute-start | bytes 98312 | tf_op jit(solution)/shard_map/ppermute | solution.py:144
  3.0 0.9 fusion.26
  3.8 1.3 %collective-permute-start.1 = (f32[2,2,16,256]{3,2,1,0:T(8,128)S(1)}, f32[2,2,16,256]{3,2,1,0:T(8,128)S(1)}, u32[]{:S(2)}, u32[]{:S(2)}) collective-permute-start(f32[2,2,16,256]{3,2,1,0:T(8,128)S(1)} %get-tuple-element.23), channel_id=1, source_target_pairs={{8,0},{16,8},{24,16},{32,24},{40,32},{48,40},{56,48},{64,56},{72,6... | collective-permute-start | bytes 196616 | tf_op jit(solution)/shard_map/ppermute | solution.py:184
  5.1 3.0 %collective-permute-start = (f32[2,2,16,256]{3,2,1,0:T(8,128)S(1)}, f32[2,2,16,256]{3,2,1,0:T(8,128)S(1)}, u32[]{:S(2)}, u32[]{:S(2)}) collective-permute-start(f32[2,2,16,256]{3,2,1,0:T(8,128)S(1)} %get-tuple-element.24), channel_id=1, source_target_pairs={{0,8},{8,16},{16,24},{24,32},{32,40},{40,48},{48,56},{56,64},{64,7... | collective-permute-start | bytes 196616 | tf_op jit(solution)/shard_map/ppermute | solution.py:184
  8.2 2.6 %fusion.25 = (f32[2,128,2,256]{3,2,1,0:T(2,128)S(1)}, f32[2,128,2,256]{3,2,1,0:T(2,128)S(1)}) fusion(f32[2,128,16,256]{3,2,1,0:T(8,128)} %param.9), kind=kLoop, calls=%fused_computation.83 | loop fusion | bytes 2097152 | tf_op jit(solution)/shard_map/slice | solution.py:183
  10.8 1.7 %collective-permute-start.3 = (f32[2,128,2,256]{3,2,1,0:T(2,128)S(1)}, f32[2,128,2,256]{3,2,1,0:T(2,128)S(1)}, u32[]{:S(2)}, u32[]{:S(2)}) collective-permute-start(f32[2,128,2,256]{3,2,1,0:T(2,128)S(1)} %get-tuple-element.21), channel_id=1, source_target_pairs={{1,0},{2,1},{3,2},{4,3},{5,4},{6,5},{7,6},{0,7},{9,8},{10,9},{11,1... | collective-permute-start | bytes 1572872 | tf_op jit(solution)/shard_map/ppermute | solution.py:184
  12.5 0.4 collective-permute-start.2
  12.9 0.9 slice_reduce_fusion.4
  13.7 0.9 slice_reduce_fusion.3
  14.7 0.8 select_bitcast_fusion.1
  16.2 2.8 %collective-permute-start.5 = (f32[2,32,256]{2,1,0:T(8,128)S(1)}, f32[2,32,256]{2,1,0:T(8,128)S(1)}, u32[]{:S(2)}, u32[]{:S(2)}) collective-permute-start(f32[2,32,256]{2,1,0:T(8,128)S(1)} %maximum_select_fusion.2), channel_id=1, source_target_pairs={{0,2},{1,3},{2,0},{3,1},{4,6},{5,7},{6,4},{7,5},{8,10},{9,11},{10,... | collective-permute-start | bytes 196616 | tf_op jit(solution)/shard_map/ppermute | solution.py:144
  19.0 0.6 broadcast_select_fusion
  19.7 9.0 %collective-permute-done.5 = f32[2,32,256]{2,1,0:T(8,128)S(1)} collective-permute-done((f32[2,32,256]{2,1,0:T(8,128)S(1)}, f32[2,32,256]{2,1,0:T(8,128)S(1)}, u32[]{:S(2)}, u32[]{:S(2)}) %collective-permute-start.5) | collective-permute-done | bytes 65568 | tf_op jit(solution)/shard_map/ppermute | solution.py:144
  28.9 0.6 broadcast_select_fusion.1
  29.5 4.9 %collective-permute-done.6 = f32[2,64,256]{2,1,0:T(8,128)S(1)} collective-permute-done((f32[2,64,256]{2,1,0:T(8,128)S(1)}, f32[2,64,256]{2,1,0:T(8,128)S(1)}, u32[]{:S(2)}, u32[]{:S(2)}) %collective-permute-start.6) | collective-permute-done | bytes 131104 | tf_op jit(solution)/shard_map/ppermute | solution.py:144
  34.5 0.7 fusion.27
  35.3 0.8 copy-done.1
  36.2 36.3 %shard_map.91 = (f32[2,2048,256]{2,1,0:T(8,128)}, f32[2,16,256]{2,1,0:T(8,128)}) custom-call(f32[2,2048,256]{2,1,0:T(8,128)} %bitcast.165, f32[2,32,256]{2,1,0:T(8,128)} %bitcast.177, f32[2,32,256]{2,1,0:T(8,128)} %bitcast.176, f32[2,128,2,256]{3,2,1,0:T(2,128)} %copy-done.2, f32[2,128,2,256]{3,2,1,0:T(2,128)} %copy-done.1, f32[2048,256]{1,0:T(8,128)} %bitcast.167, ...), custom_call_target="tpu_custom_call" | custom-call | flops 331350016 | bytes 16777216 | tf_op jit(solution)/shard_map/pallas_call | solution.py:109
  72.5 0.8 pad_maximum_fusion
  73.3 0.5 collective-permute-start.7
  73.8 0.9 collective-permute-done.7
  74.8 0.8 fusion.19
  75.7 3.1 %collective-permute-start.8 = (f32[3,2,16,256]{3,2,1,0:T(8,128)S(1)}, f32[3,2,16,256]{3,2,1,0:T(8,128)S(1)}, u32[]{:S(2)}, u32[]{:S(2)}) collective-permute-start(f32[3,2,16,256]{3,2,1,0:T(8,128)S(1)} %pad_maximum_fusion.1), channel_id=1, source_target_pairs={{0,16},{8,24},{16,0},{24,8},{32,48},{40,56},{48,32},{56,40},{64,80... | collective-permute-start | bytes 294920 | tf_op jit(solution)/shard_map/ppermute | solution.py:165
  78.8 4.1 %collective-permute-done.8 = f32[3,2,16,256]{3,2,1,0:T(8,128)S(1)} collective-permute-done((f32[3,2,16,256]{3,2,1,0:T(8,128)S(1)}, f32[3,2,16,256]{3,2,1,0:T(8,128)S(1)}, u32[]{:S(2)}, u32[]{:S(2)}) %collective-permute-start.8) | collective-permute-done | bytes 98336 | tf_op jit(solution)/shard_map/ppermute | solution.py:165
  83.0 7.0 %collective-permute-start.9 = (f32[3,2,16,256]{3,2,1,0:T(8,128)S(1)}, f32[3,2,16,256]{3,2,1,0:T(8,128)S(1)}, u32[]{:S(2)}, u32[]{:S(2)}) collective-permute-start(f32[3,2,16,256]{3,2,1,0:T(8,128)S(1)} %pad_maximum_fusion.2), channel_id=1, source_target_pairs={{0,32},{8,40},{16,48},{24,56},{32,0},{40,8},{48,16},{56,24},{64,96... | collective-permute-start | bytes 294920 | tf_op jit(solution)/shard_map/ppermute | solution.py:165
  90.0 5.1 %collective-permute-done.9 = f32[3,2,16,256]{3,2,1,0:T(8,128)S(1)} collective-permute-done((f32[3,2,16,256]{3,2,1,0:T(8,128)S(1)}, f32[3,2,16,256]{3,2,1,0:T(8,128)S(1)}, u32[]{:S(2)}, u32[]{:S(2)}) %collective-permute-start.9) | collective-permute-done | bytes 98336 | tf_op jit(solution)/shard_map/ppermute | solution.py:165
  95.3 1.7 %collective-permute-start.10 = (f32[3,2,16,256]{3,2,1,0:T(8,128)S(1)}, f32[3,2,16,256]{3,2,1,0:T(8,128)S(1)}, u32[]{:S(2)}, u32[]{:S(2)}) collective-permute-start(f32[3,2,16,256]{3,2,1,0:T(8,128)S(1)} %pad_maximum_fusion.3), channel_id=1, source_target_pairs={{0,64},{8,72},{16,80},{24,88},{32,96},{40,104},{48,112},{56,120},{... | collective-permute-start | bytes 294920 | tf_op jit(solution)/shard_map/ppermute | solution.py:165
  97.0 3.0 %collective-permute-done.10 = f32[3,2,16,256]{3,2,1,0:T(8,128)S(1)} collective-permute-done((f32[3,2,16,256]{3,2,1,0:T(8,128)S(1)}, f32[3,2,16,256]{3,2,1,0:T(8,128)S(1)}, u32[]{:S(2)}, u32[]{:S(2)}) %collective-permute-start.10) | collective-permute-done | bytes 98336 | tf_op jit(solution)/shard_map/ppermute | solution.py:165
  100.0 4.0 %collective-permute-start.11 = (f32[3,2,16,256]{3,2,1,0:T(8,128)S(1)}, f32[3,2,16,256]{3,2,1,0:T(8,128)S(1)}, u32[]{:S(2)}, u32[]{:S(2)}) collective-permute-start(f32[3,2,16,256]{3,2,1,0:T(8,128)S(1)} %pad_maximum_fusion.4), channel_id=1, source_target_pairs={{0,128},{8,136},{16,144},{24,152},{32,160},{40,168},{48,176},{56,1... | collective-permute-start | bytes 294920 | tf_op jit(solution)/shard_map/ppermute | solution.py:165
  104.2 2.4 %collective-permute-done.11 = f32[3,2,16,256]{3,2,1,0:T(8,128)S(1)} collective-permute-done((f32[3,2,16,256]{3,2,1,0:T(8,128)S(1)}, f32[3,2,16,256]{3,2,1,0:T(8,128)S(1)}, u32[]{:S(2)}, u32[]{:S(2)}) %collective-permute-start.11) | collective-permute-done | bytes 98336 | tf_op jit(solution)/shard_map/ppermute | solution.py:165
  106.7 4.1 %multiply_add_fusion = f32[2,128,16,256]{3,2,1,0:T(8,128)} fusion(f32[2,128,16,256]{3,2,1,0:T(8,128)} %bitcast.166, f32[2,16,256]{2,1,0:T(8,128)S(1)} %get-tuple-element.35, f32[2,128]{1,0:T(2,128)S(1)} %get-tuple-element.10, f32[2,16,256]{2,1,0:T(8,128)S(1)} %get-tuple-element.34, f32[2,128]{1,0:T(2,128)S(1)} %get-tuple-element.9, ...), kind=kLoop, calls=%fused_computation | loop fusion | flops 6291456 | bytes 8489984 | tf_op jit(solution)/shard_map/add | solution.py:241
  (36 shorter events, 1.1 us)
Async XLA Ops:
  1.5 14.7 %collective-permute-start.4 = (f32[2,16,256]{2,1,0:T(8,128)S(1)}, f32[2,16,256]{2,1,0:T(8,128)S(1)}, u32[]{:S(2)}, u32[]{:S(2)}) collective-permute-start(f32[2,16,256]{2,1,0:T(8,128)S(1)} %get-tuple-element.19), channel_id=1, source_target_pairs={{0,1},{1,0},{2,3},{3,2},{4,5},{5,4},{6,7},{7,6},{8,9},{9,8},{10,11... | collective-permute-start | bytes 98312 | tf_op jit(solution)/shard_map/ppermute | solution.py:144
  3.8 15.2 %collective-permute-start.1 = (f32[2,2,16,256]{3,2,1,0:T(8,128)S(1)}, f32[2,2,16,256]{3,2,1,0:T(8,128)S(1)}, u32[]{:S(2)}, u32[]{:S(2)}) collective-permute-start(f32[2,2,16,256]{3,2,1,0:T(8,128)S(1)} %get-tuple-element.23), channel_id=1, source_target_pairs={{8,0},{16,8},{24,16},{32,24},{40,32},{48,40},{56,48},{64,56},{72,6... | collective-permute-start | bytes 196616 | tf_op jit(solution)/shard_map/ppermute | solution.py:184
  5.1 23.7 %collective-permute-start = (f32[2,2,16,256]{3,2,1,0:T(8,128)S(1)}, f32[2,2,16,256]{3,2,1,0:T(8,128)S(1)}, u32[]{:S(2)}, u32[]{:S(2)}) collective-permute-start(f32[2,2,16,256]{3,2,1,0:T(8,128)S(1)} %get-tuple-element.24), channel_id=1, source_target_pairs={{0,8},{8,16},{16,24},{24,32},{32,40},{40,48},{48,56},{56,64},{64,7... | collective-permute-start | bytes 196616 | tf_op jit(solution)/shard_map/ppermute | solution.py:184
  10.8 24.5 %collective-permute-start.3 = (f32[2,128,2,256]{3,2,1,0:T(2,128)S(1)}, f32[2,128,2,256]{3,2,1,0:T(2,128)S(1)}, u32[]{:S(2)}, u32[]{:S(2)}) collective-permute-start(f32[2,128,2,256]{3,2,1,0:T(2,128)S(1)} %get-tuple-element.21), channel_id=1, source_target_pairs={{1,0},{2,1},{3,2},{4,3},{5,4},{6,5},{7,6},{0,7},{9,8},{10,9},{11,1... | collective-permute-start | bytes 1572872 | tf_op jit(solution)/shard_map/ppermute | solution.py:184
  12.5 22.8 %collective-permute-start.2 = (f32[2,128,2,256]{3,2,1,0:T(2,128)S(1)}, f32[2,128,2,256]{3,2,1,0:T(2,128)S(1)}, u32[]{:S(2)}, u32[]{:S(2)}) collective-permute-start(f32[2,128,2,256]{3,2,1,0:T(2,128)S(1)} %get-tuple-element.22), channel_id=1, source_target_pairs={{0,1},{1,2},{2,3},{3,4},{4,5},{5,6},{6,7},{7,0},{8,9},{9,10},{10,1... | collective-permute-start | bytes 1572872 | tf_op jit(solution)/shard_map/ppermute | solution.py:184
  16.2 12.5 %collective-permute-start.5 = (f32[2,32,256]{2,1,0:T(8,128)S(1)}, f32[2,32,256]{2,1,0:T(8,128)S(1)}, u32[]{:S(2)}, u32[]{:S(2)}) collective-permute-start(f32[2,32,256]{2,1,0:T(8,128)S(1)} %maximum_select_fusion.2), channel_id=1, source_target_pairs={{0,2},{1,3},{2,0},{3,1},{4,6},{5,7},{6,4},{7,5},{8,10},{9,11},{10,... | collective-permute-start | bytes 196616 | tf_op jit(solution)/shard_map/ppermute | solution.py:144
  28.7 5.8 %collective-permute-start.6 = (f32[2,64,256]{2,1,0:T(8,128)S(1)}, f32[2,64,256]{2,1,0:T(8,128)S(1)}, u32[]{:S(2)}, u32[]{:S(2)}) collective-permute-start(f32[2,64,256]{2,1,0:T(8,128)S(1)} %maximum_select_fusion.1), channel_id=1, source_target_pairs={{0,4},{1,5},{2,6},{3,7},{4,0},{5,1},{6,2},{7,3},{8,12},{9,13},{10,... | collective-permute-start | bytes 393224 | tf_op jit(solution)/shard_map/ppermute | solution.py:144
  35.2 0.8 copy-start.1
  35.3 1.0 copy-start.2
  36.2 38.6 %copy-start.3 = (f32[2,256]{1,0:T(2,128)S(1)}, f32[2,256]{1,0:T(2,128)}, u32[]{:S(2)}) copy-start(f32[2,256]{1,0:T(2,128)} %param.15) | copy-start | bytes 6148
  36.2 38.6 %copy-start.4 = (f32[2,256]{1,0:T(2,128)S(1)}, f32[2,256]{1,0:T(2,128)}, u32[]{:S(2)}) copy-start(f32[2,256]{1,0:T(2,128)} %param.14) | copy-start | bytes 6148
  36.2 67.8 %copy-start = (f32[2,1,128,128]{3,2,1,0:T(8,128)S(1)}, f32[2,1,128,128]{3,2,1,0:T(8,128)}, u32[]{:S(2)}) copy-start(f32[2,1,128,128]{3,2,1,0:T(8,128)} %param.12) | copy-start | bytes 393220
  36.2 70.5 %copy-start.5 = (f32[2,1,128]{2,1,0:T(1,128)S(1)}, f32[2,1,128]{2,1,0:T(1,128)}, u32[]{:S(2)}) copy-start(f32[2,1,128]{2,1,0:T(1,128)} %param.13) | copy-start | bytes 3076
  73.3 1.5 %collective-permute-start.7 = (f32[3,2,16,256]{3,2,1,0:T(8,128)S(1)}, f32[3,2,16,256]{3,2,1,0:T(8,128)S(1)}, u32[]{:S(2)}, u32[]{:S(2)}) collective-permute-start(f32[3,2,16,256]{3,2,1,0:T(8,128)S(1)} %pad_maximum_fusion), channel_id=1, source_target_pairs={{0,8},{8,0},{16,24},{24,16},{32,40},{40,32},{48,56},{56,48},{64,72... | collective-permute-start | bytes 294920 | tf_op jit(solution)/shard_map/ppermute | solution.py:165
  75.7 7.2 %collective-permute-start.8 = (f32[3,2,16,256]{3,2,1,0:T(8,128)S(1)}, f32[3,2,16,256]{3,2,1,0:T(8,128)S(1)}, u32[]{:S(2)}, u32[]{:S(2)}) collective-permute-start(f32[3,2,16,256]{3,2,1,0:T(8,128)S(1)} %pad_maximum_fusion.1), channel_id=1, source_target_pairs={{0,16},{8,24},{16,0},{24,8},{32,48},{40,56},{48,32},{56,40},{64,80... | collective-permute-start | bytes 294920 | tf_op jit(solution)/shard_map/ppermute | solution.py:165
  83.0 12.1 %collective-permute-start.9 = (f32[3,2,16,256]{3,2,1,0:T(8,128)S(1)}, f32[3,2,16,256]{3,2,1,0:T(8,128)S(1)}, u32[]{:S(2)}, u32[]{:S(2)}) collective-permute-start(f32[3,2,16,256]{3,2,1,0:T(8,128)S(1)} %pad_maximum_fusion.2), channel_id=1, source_target_pairs={{0,32},{8,40},{16,48},{24,56},{32,0},{40,8},{48,16},{56,24},{64,96... | collective-permute-start | bytes 294920 | tf_op jit(solution)/shard_map/ppermute | solution.py:165
  95.3 4.7 %collective-permute-start.10 = (f32[3,2,16,256]{3,2,1,0:T(8,128)S(1)}, f32[3,2,16,256]{3,2,1,0:T(8,128)S(1)}, u32[]{:S(2)}, u32[]{:S(2)}) collective-permute-start(f32[3,2,16,256]{3,2,1,0:T(8,128)S(1)} %pad_maximum_fusion.3), channel_id=1, source_target_pairs={{0,64},{8,72},{16,80},{24,88},{32,96},{40,104},{48,112},{56,120},{... | collective-permute-start | bytes 294920 | tf_op jit(solution)/shard_map/ppermute | solution.py:165
  100.0 6.6 %collective-permute-start.11 = (f32[3,2,16,256]{3,2,1,0:T(8,128)S(1)}, f32[3,2,16,256]{3,2,1,0:T(8,128)S(1)}, u32[]{:S(2)}, u32[]{:S(2)}) collective-permute-start(f32[3,2,16,256]{3,2,1,0:T(8,128)S(1)} %pad_maximum_fusion.4), channel_id=1, source_target_pairs={{0,128},{8,136},{16,144},{24,152},{32,160},{40,168},{48,176},{56,1... | collective-permute-start | bytes 294920 | tf_op jit(solution)/shard_map/ppermute | solution.py:165

commit v7 on v6

--- a/solution.py
+++ b/solution.py
@@ -71,7 +71,7 @@
         one_plane(j, j - 2, j - 1, j + 1, j + 2)
         return carry
 
-    lax.fori_loop(2, planes - 2, body, 0)
+    lax.fori_loop(2, planes - 2, body, 0, unroll=4)
     for j in (planes - 2, planes - 1):
         one_plane(j, j - 2, j - 1, j + 1, j + 2)
 
@@ -87,7 +87,7 @@
                 ex_ref[s, h, pl.ds(z, planes, stride=rows), :] = r
                 return carry
 
-            lax.fori_loop(0, rows, mm, 0)
+            lax.fori_loop(0, rows, mm, 0, unroll=True)
             exit_ref[s, :, pl.ds(h * 128, 128)] = ex_ref[s, h, pl.ds((planes - 1) * rows, rows), :]
 
     chunk = 8 * rows

time: 112 us -> 95 us (0.85)
  Pallas kernels: 36.3 us -> 19.1 us
    pallas_call x1, Pallas kernels: 36.3 us -> 19.1 us  [explicit_local(): pl.pallas_call(functools.partial(explicit_kernel, planes, rows, width), o...]
  transfers between devices with their start and end apart: 12 -> 12, of which waited for: 7 -> 7; matrix products, arithmetic and copies ran while one was open for 8% -> 9% of each run, Pallas kernels for 0% -> 0%
where the time goes in v7:
time: 95 us; the launch traced here: 93.6 us
  waiting for transfers between devices  29.5 us (31%)
  starting transfers between devices  27.3 us (29%)
  Pallas kernels  19.1 us (20%)
  other arithmetic  8.98 us (9%)
  local copies, waits for them, and re-layouts  7.21 us (8%)
  between operations  1.55 us (2%)
    pallas_call x1, Pallas kernels, explicit_local(): pl.pallas_call(functools.partial(explicit_kernel, planes, rows, width), o...  19.1 us
    ppermute x5, starting transfers between devices, exclusive_scan(): other = lax.ppermute(jnp.stack(total + (carried,)), axis, pairs)  16.4 us
    ppermute x5, waiting for transfers between devices, exclusive_scan(): other = lax.ppermute(jnp.stack(total + (carried,)), axis, pairs)  15.5 us
    ppermute x3, waiting for transfers between devices, xor_gather(): other = lax.ppermute(x, axis, pairs)  13.9 us
    ppermute x4, starting transfers between devices, halos(): return (lax.ppermute(last, axis, up), lax.ppermute(first, axis, down))  6.43 us
    ppermute x3, starting transfers between devices, xor_gather(): other = lax.ppermute(x, axis, pairs)  4.51 us
    add x1, other arithmetic, on_device(): local_part + response[:, :, None, None] * incoming[:, None]  4.12 us
    slice x2, local copies, waits for them, and re-layouts, halos(): first = lax.slice_in_dim(x, 0, width, axis=dim)  3.47 us
  transfers between devices with their start and end apart: 12, of which 7 were waited for; matrix products, arithmetic and copies ran while one was open for 9% of the time, Pallas kernels for 0%

profile of v7, /device:TPU:32, one launch (start us, length us, event | category | flops | bytes accessed | tf_op | source)
XLA Modules:
  0.0 93.6 jit_solution(187003027627051345)
XLA Ops:
  0.7 0.8 dynamic-slice_bitcast_fusion
  1.5 1.5 %collective-permute-start.4 = (f32[2,16,256]{2,1,0:T(8,128)S(1)}, f32[2,16,256]{2,1,0:T(8,128)S(1)}, u32[]{:S(2)}, u32[]{:S(2)}) collective-permute-start(f32[2,16,256]{2,1,0:T(8,128)S(1)} %get-tuple-element.19), channel_id=1, source_target_pairs={{0,1},{1,0},{2,3},{3,2},{4,5},{5,4},{6,7},{7,6},{8,9},{9,8},{10,11... | collective-permute-start | bytes 98312 | tf_op jit(solution)/shard_map/ppermute | solution.py:144
  3.0 0.9 fusion.26
  3.8 1.3 %collective-permute-start.1 = (f32[2,2,16,256]{3,2,1,0:T(8,128)S(1)}, f32[2,2,16,256]{3,2,1,0:T(8,128)S(1)}, u32[]{:S(2)}, u32[]{:S(2)}) collective-permute-start(f32[2,2,16,256]{3,2,1,0:T(8,128)S(1)} %get-tuple-element.23), channel_id=1, source_target_pairs={{8,0},{16,8},{24,16},{32,24},{40,32},{48,40},{56,48},{64,56},{72,6... | collective-permute-start | bytes 196616 | tf_op jit(solution)/shard_map/ppermute | solution.py:184
  5.1 3.0 %collective-permute-start = (f32[2,2,16,256]{3,2,1,0:T(8,128)S(1)}, f32[2,2,16,256]{3,2,1,0:T(8,128)S(1)}, u32[]{:S(2)}, u32[]{:S(2)}) collective-permute-start(f32[2,2,16,256]{3,2,1,0:T(8,128)S(1)} %get-tuple-element.24), channel_id=1, source_target_pairs={{0,8},{8,16},{16,24},{24,32},{32,40},{40,48},{48,56},{56,64},{64,7... | collective-permute-start | bytes 196616 | tf_op jit(solution)/shard_map/ppermute | solution.py:184
  8.2 2.6 %fusion.25 = (f32[2,128,2,256]{3,2,1,0:T(2,128)S(1)}, f32[2,128,2,256]{3,2,1,0:T(2,128)S(1)}) fusion(f32[2,128,16,256]{3,2,1,0:T(8,128)} %param.9), kind=kLoop, calls=%fused_computation.83 | loop fusion | bytes 2097152 | tf_op jit(solution)/shard_map/slice | solution.py:183
  10.8 1.7 %collective-permute-start.3 = (f32[2,128,2,256]{3,2,1,0:T(2,128)S(1)}, f32[2,128,2,256]{3,2,1,0:T(2,128)S(1)}, u32[]{:S(2)}, u32[]{:S(2)}) collective-permute-start(f32[2,128,2,256]{3,2,1,0:T(2,128)S(1)} %get-tuple-element.21), channel_id=1, source_target_pairs={{1,0},{2,1},{3,2},{4,3},{5,4},{6,5},{7,6},{0,7},{9,8},{10,9},{11,1... | collective-permute-start | bytes 1572872 | tf_op jit(solution)/shard_map/ppermute | solution.py:184
  12.5 0.4 collective-permute-start.2
  12.9 0.9 slice_reduce_fusion.4
  13.7 0.9 slice_reduce_fusion.3
  14.7 0.8 select_bitcast_fusion.1
  16.2 2.8 %collective-permute-start.5 = (f32[2,32,256]{2,1,0:T(8,128)S(1)}, f32[2,32,256]{2,1,0:T(8,128)S(1)}, u32[]{:S(2)}, u32[]{:S(2)}) collective-permute-start(f32[2,32,256]{2,1,0:T(8,128)S(1)} %maximum_select_fusion.2), channel_id=1, source_target_pairs={{0,2},{1,3},{2,0},{3,1},{4,6},{5,7},{6,4},{7,5},{8,10},{9,11},{10,... | collective-permute-start | bytes 196616 | tf_op jit(solution)/shard_map/ppermute | solution.py:144
  19.0 0.6 broadcast_select_fusion
  19.7 9.0 %collective-permute-done.5 = f32[2,32,256]{2,1,0:T(8,128)S(1)} collective-permute-done((f32[2,32,256]{2,1,0:T(8,128)S(1)}, f32[2,32,256]{2,1,0:T(8,128)S(1)}, u32[]{:S(2)}, u32[]{:S(2)}) %collective-permute-start.5) | collective-permute-done | bytes 65568 | tf_op jit(solution)/shard_map/ppermute | solution.py:144
  28.9 0.6 broadcast_select_fusion.1
  29.5 4.9 %collective-permute-done.6 = f32[2,64,256]{2,1,0:T(8,128)S(1)} collective-permute-done((f32[2,64,256]{2,1,0:T(8,128)S(1)}, f32[2,64,256]{2,1,0:T(8,128)S(1)}, u32[]{:S(2)}, u32[]{:S(2)}) %collective-permute-start.6) | collective-permute-done | bytes 131104 | tf_op jit(solution)/shard_map/ppermute | solution.py:144
  34.5 0.7 fusion.27
  35.3 0.8 copy-done.1
  36.2 19.1 %shard_map.91 = (f32[2,2048,256]{2,1,0:T(8,128)}, f32[2,16,256]{2,1,0:T(8,128)}) custom-call(f32[2,2048,256]{2,1,0:T(8,128)} %bitcast.165, f32[2,32,256]{2,1,0:T(8,128)} %bitcast.177, f32[2,32,256]{2,1,0:T(8,128)} %bitcast.176, f32[2,128,2,256]{3,2,1,0:T(2,128)} %copy-done.2, f32[2,128,2,256]{3,2,1,0:T(2,128)} %copy-done.1, f32[2048,256]{1,0:T(8,128)} %bitcast.167, ...), custom_call_target="tpu_custom_call" | custom-call | flops 331350016 | bytes 16777216 | tf_op jit(solution)/shard_map/pallas_call | solution.py:109
  55.3 0.8 pad_maximum_fusion
  56.1 0.5 collective-permute-start.7
  56.6 0.9 %collective-permute-done.7 = f32[3,2,16,256]{3,2,1,0:T(8,128)S(1)} collective-permute-done((f32[3,2,16,256]{3,2,1,0:T(8,128)S(1)}, f32[3,2,16,256]{3,2,1,0:T(8,128)S(1)}, u32[]{:S(2)}, u32[]{:S(2)}) %collective-permute-start.7) | collective-permute-done | bytes 98336 | tf_op jit(solution)/shard_map/ppermute | solution.py:165
  57.6 0.8 fusion.19
  58.5 3.1 %collective-permute-start.8 = (f32[3,2,16,256]{3,2,1,0:T(8,128)S(1)}, f32[3,2,16,256]{3,2,1,0:T(8,128)S(1)}, u32[]{:S(2)}, u32[]{:S(2)}) collective-permute-start(f32[3,2,16,256]{3,2,1,0:T(8,128)S(1)} %pad_maximum_fusion.1), channel_id=1, source_target_pairs={{0,16},{8,24},{16,0},{24,8},{32,48},{40,56},{48,32},{56,40},{64,80... | collective-permute-start | bytes 294920 | tf_op jit(solution)/shard_map/ppermute | solution.py:165
  61.5 4.1 %collective-permute-done.8 = f32[3,2,16,256]{3,2,1,0:T(8,128)S(1)} collective-permute-done((f32[3,2,16,256]{3,2,1,0:T(8,128)S(1)}, f32[3,2,16,256]{3,2,1,0:T(8,128)S(1)}, u32[]{:S(2)}, u32[]{:S(2)}) %collective-permute-start.8) | collective-permute-done | bytes 98336 | tf_op jit(solution)/shard_map/ppermute | solution.py:165
  65.8 7.0 %collective-permute-start.9 = (f32[3,2,16,256]{3,2,1,0:T(8,128)S(1)}, f32[3,2,16,256]{3,2,1,0:T(8,128)S(1)}, u32[]{:S(2)}, u32[]{:S(2)}) collective-permute-start(f32[3,2,16,256]{3,2,1,0:T(8,128)S(1)} %pad_maximum_fusion.2), channel_id=1, source_target_pairs={{0,32},{8,40},{16,48},{24,56},{32,0},{40,8},{48,16},{56,24},{64,96... | collective-permute-start | bytes 294920 | tf_op jit(solution)/shard_map/ppermute | solution.py:165
  72.8 5.1 %collective-permute-done.9 = f32[3,2,16,256]{3,2,1,0:T(8,128)S(1)} collective-permute-done((f32[3,2,16,256]{3,2,1,0:T(8,128)S(1)}, f32[3,2,16,256]{3,2,1,0:T(8,128)S(1)}, u32[]{:S(2)}, u32[]{:S(2)}) %collective-permute-start.9) | collective-permute-done | bytes 98336 | tf_op jit(solution)/shard_map/ppermute | solution.py:165
  78.0 1.7 %collective-permute-start.10 = (f32[3,2,16,256]{3,2,1,0:T(8,128)S(1)}, f32[3,2,16,256]{3,2,1,0:T(8,128)S(1)}, u32[]{:S(2)}, u32[]{:S(2)}) collective-permute-start(f32[3,2,16,256]{3,2,1,0:T(8,128)S(1)} %pad_maximum_fusion.3), channel_id=1, source_target_pairs={{0,64},{8,72},{16,80},{24,88},{32,96},{40,104},{48,112},{56,120},{... | collective-permute-start | bytes 294920 | tf_op jit(solution)/shard_map/ppermute | solution.py:165
  79.8 3.0 %collective-permute-done.10 = f32[3,2,16,256]{3,2,1,0:T(8,128)S(1)} collective-permute-done((f32[3,2,16,256]{3,2,1,0:T(8,128)S(1)}, f32[3,2,16,256]{3,2,1,0:T(8,128)S(1)}, u32[]{:S(2)}, u32[]{:S(2)}) %collective-permute-start.10) | collective-permute-done | bytes 98336 | tf_op jit(solution)/shard_map/ppermute | solution.py:165
  82.8 4.0 %collective-permute-start.11 = (f32[3,2,16,256]{3,2,1,0:T(8,128)S(1)}, f32[3,2,16,256]{3,2,1,0:T(8,128)S(1)}, u32[]{:S(2)}, u32[]{:S(2)}) collective-permute-start(f32[3,2,16,256]{3,2,1,0:T(8,128)S(1)} %pad_maximum_fusion.4), channel_id=1, source_target_pairs={{0,128},{8,136},{16,144},{24,152},{32,160},{40,168},{48,176},{56,1... | collective-permute-start | bytes 294920 | tf_op jit(solution)/shard_map/ppermute | solution.py:165
  87.0 2.4 %collective-permute-done.11 = f32[3,2,16,256]{3,2,1,0:T(8,128)S(1)} collective-permute-done((f32[3,2,16,256]{3,2,1,0:T(8,128)S(1)}, f32[3,2,16,256]{3,2,1,0:T(8,128)S(1)}, u32[]{:S(2)}, u32[]{:S(2)}) %collective-permute-start.11) | collective-permute-done | bytes 98336 | tf_op jit(solution)/shard_map/ppermute | solution.py:165
  89.5 4.1 %multiply_add_fusion = f32[2,128,16,256]{3,2,1,0:T(8,128)} fusion(f32[2,128,16,256]{3,2,1,0:T(8,128)} %bitcast.166, f32[2,16,256]{2,1,0:T(8,128)S(1)} %get-tuple-element.35, f32[2,128]{1,0:T(2,128)S(1)} %get-tuple-element.10, f32[2,16,256]{2,1,0:T(8,128)S(1)} %get-tuple-element.34, f32[2,128]{1,0:T(2,128)S(1)} %get-tuple-element.9, ...), kind=kLoop, calls=%fused_computation | loop fusion | flops 6291456 | bytes 8489984 | tf_op jit(solution)/shard_map/add | solution.py:241
  (36 shorter events, 1.1 us)
Async XLA Ops:
  1.5 14.7 %collective-permute-start.4 = (f32[2,16,256]{2,1,0:T(8,128)S(1)}, f32[2,16,256]{2,1,0:T(8,128)S(1)}, u32[]{:S(2)}, u32[]{:S(2)}) collective-permute-start(f32[2,16,256]{2,1,0:T(8,128)S(1)} %get-tuple-element.19), channel_id=1, source_target_pairs={{0,1},{1,0},{2,3},{3,2},{4,5},{5,4},{6,7},{7,6},{8,9},{9,8},{10,11... | collective-permute-start | bytes 98312 | tf_op jit(solution)/shard_map/ppermute | solution.py:144
  3.8 15.2 %collective-permute-start.1 = (f32[2,2,16,256]{3,2,1,0:T(8,128)S(1)}, f32[2,2,16,256]{3,2,1,0:T(8,128)S(1)}, u32[]{:S(2)}, u32[]{:S(2)}) collective-permute-start(f32[2,2,16,256]{3,2,1,0:T(8,128)S(1)} %get-tuple-element.23), channel_id=1, source_target_pairs={{8,0},{16,8},{24,16},{32,24},{40,32},{48,40},{56,48},{64,56},{72,6... | collective-permute-start | bytes 196616 | tf_op jit(solution)/shard_map/ppermute | solution.py:184
  5.1 23.7 %collective-permute-start = (f32[2,2,16,256]{3,2,1,0:T(8,128)S(1)}, f32[2,2,16,256]{3,2,1,0:T(8,128)S(1)}, u32[]{:S(2)}, u32[]{:S(2)}) collective-permute-start(f32[2,2,16,256]{3,2,1,0:T(8,128)S(1)} %get-tuple-element.24), channel_id=1, source_target_pairs={{0,8},{8,16},{16,24},{24,32},{32,40},{40,48},{48,56},{56,64},{64,7... | collective-permute-start | bytes 196616 | tf_op jit(solution)/shard_map/ppermute | solution.py:184
  10.8 24.5 %collective-permute-start.3 = (f32[2,128,2,256]{3,2,1,0:T(2,128)S(1)}, f32[2,128,2,256]{3,2,1,0:T(2,128)S(1)}, u32[]{:S(2)}, u32[]{:S(2)}) collective-permute-start(f32[2,128,2,256]{3,2,1,0:T(2,128)S(1)} %get-tuple-element.21), channel_id=1, source_target_pairs={{1,0},{2,1},{3,2},{4,3},{5,4},{6,5},{7,6},{0,7},{9,8},{10,9},{11,1... | collective-permute-start | bytes 1572872 | tf_op jit(solution)/shard_map/ppermute | solution.py:184
  12.5 22.8 %collective-permute-start.2 = (f32[2,128,2,256]{3,2,1,0:T(2,128)S(1)}, f32[2,128,2,256]{3,2,1,0:T(2,128)S(1)}, u32[]{:S(2)}, u32[]{:S(2)}) collective-permute-start(f32[2,128,2,256]{3,2,1,0:T(2,128)S(1)} %get-tuple-element.22), channel_id=1, source_target_pairs={{0,1},{1,2},{2,3},{3,4},{4,5},{5,6},{6,7},{7,0},{8,9},{9,10},{10,1... | collective-permute-start | bytes 1572872 | tf_op jit(solution)/shard_map/ppermute | solution.py:184
  16.2 12.5 %collective-permute-start.5 = (f32[2,32,256]{2,1,0:T(8,128)S(1)}, f32[2,32,256]{2,1,0:T(8,128)S(1)}, u32[]{:S(2)}, u32[]{:S(2)}) collective-permute-start(f32[2,32,256]{2,1,0:T(8,128)S(1)} %maximum_select_fusion.2), channel_id=1, source_target_pairs={{0,2},{1,3},{2,0},{3,1},{4,6},{5,7},{6,4},{7,5},{8,10},{9,11},{10,... | collective-permute-start | bytes 196616 | tf_op jit(solution)/shard_map/ppermute | solution.py:144
  28.7 5.8 %collective-permute-start.6 = (f32[2,64,256]{2,1,0:T(8,128)S(1)}, f32[2,64,256]{2,1,0:T(8,128)S(1)}, u32[]{:S(2)}, u32[]{:S(2)}) collective-permute-start(f32[2,64,256]{2,1,0:T(8,128)S(1)} %maximum_select_fusion.1), channel_id=1, source_target_pairs={{0,4},{1,5},{2,6},{3,7},{4,0},{5,1},{6,2},{7,3},{8,12},{9,13},{10,... | collective-permute-start | bytes 393224 | tf_op jit(solution)/shard_map/ppermute | solution.py:144
  35.2 0.8 copy-start.1
  35.3 1.0 %copy-start.2 = (f32[2,128,2,256]{3,2,1,0:T(2,128)}, f32[2,128,2,256]{3,2,1,0:T(2,128)S(1)}, u32[]{:S(2)}) copy-start(f32[2,128,2,256]{3,2,1,0:T(2,128)S(1)} %collective-permute-done.2.before_ref) | copy-start | bytes 1572868
  36.2 21.4 %copy-start.3 = (f32[2,256]{1,0:T(2,128)S(1)}, f32[2,256]{1,0:T(2,128)}, u32[]{:S(2)}) copy-start(f32[2,256]{1,0:T(2,128)} %param.15) | copy-start | bytes 6148
  36.2 21.4 %copy-start.4 = (f32[2,256]{1,0:T(2,128)S(1)}, f32[2,256]{1,0:T(2,128)}, u32[]{:S(2)}) copy-start(f32[2,256]{1,0:T(2,128)} %param.14) | copy-start | bytes 6148
  36.2 50.6 %copy-start = (f32[2,1,128,128]{3,2,1,0:T(8,128)S(1)}, f32[2,1,128,128]{3,2,1,0:T(8,128)}, u32[]{:S(2)}) copy-start(f32[2,1,128,128]{3,2,1,0:T(8,128)} %param.12) | copy-start | bytes 393220
  36.2 53.2 %copy-start.5 = (f32[2,1,128]{2,1,0:T(1,128)S(1)}, f32[2,1,128]{2,1,0:T(1,128)}, u32[]{:S(2)}) copy-start(f32[2,1,128]{2,1,0:T(1,128)} %param.13) | copy-start | bytes 3076
  56.1 1.5 %collective-permute-start.7 = (f32[3,2,16,256]{3,2,1,0:T(8,128)S(1)}, f32[3,2,16,256]{3,2,1,0:T(8,128)S(1)}, u32[]{:S(2)}, u32[]{:S(2)}) collective-permute-start(f32[3,2,16,256]{3,2,1,0:T(8,128)S(1)} %pad_maximum_fusion), channel_id=1, source_target_pairs={{0,8},{8,0},{16,24},{24,16},{32,40},{40,32},{48,56},{56,48},{64,72... | collective-permute-start | bytes 294920 | tf_op jit(solution)/shard_map/ppermute | solution.py:165
  58.5 7.2 %collective-permute-start.8 = (f32[3,2,16,256]{3,2,1,0:T(8,128)S(1)}, f32[3,2,16,256]{3,2,1,0:T(8,128)S(1)}, u32[]{:S(2)}, u32[]{:S(2)}) collective-permute-start(f32[3,2,16,256]{3,2,1,0:T(8,128)S(1)} %pad_maximum_fusion.1), channel_id=1, source_target_pairs={{0,16},{8,24},{16,0},{24,8},{32,48},{40,56},{48,32},{56,40},{64,80... | collective-permute-start | bytes 294920 | tf_op jit(solution)/shard_map/ppermute | solution.py:165
  65.8 12.1 %collective-permute-start.9 = (f32[3,2,16,256]{3,2,1,0:T(8,128)S(1)}, f32[3,2,16,256]{3,2,1,0:T(8,128)S(1)}, u32[]{:S(2)}, u32[]{:S(2)}) collective-permute-start(f32[3,2,16,256]{3,2,1,0:T(8,128)S(1)} %pad_maximum_fusion.2), channel_id=1, source_target_pairs={{0,32},{8,40},{16,48},{24,56},{32,0},{40,8},{48,16},{56,24},{64,96... | collective-permute-start | bytes 294920 | tf_op jit(solution)/shard_map/ppermute | solution.py:165
  78.0 4.7 %collective-permute-start.10 = (f32[3,2,16,256]{3,2,1,0:T(8,128)S(1)}, f32[3,2,16,256]{3,2,1,0:T(8,128)S(1)}, u32[]{:S(2)}, u32[]{:S(2)}) collective-permute-start(f32[3,2,16,256]{3,2,1,0:T(8,128)S(1)} %pad_maximum_fusion.3), channel_id=1, source_target_pairs={{0,64},{8,72},{16,80},{24,88},{32,96},{40,104},{48,112},{56,120},{... | collective-permute-start | bytes 294920 | tf_op jit(solution)/shard_map/ppermute | solution.py:165
  82.8 6.6 %collective-permute-start.11 = (f32[3,2,16,256]{3,2,1,0:T(8,128)S(1)}, f32[3,2,16,256]{3,2,1,0:T(8,128)S(1)}, u32[]{:S(2)}, u32[]{:S(2)}) collective-permute-start(f32[3,2,16,256]{3,2,1,0:T(8,128)S(1)} %pad_maximum_fusion.4), channel_id=1, source_target_pairs={{0,128},{8,136},{16,144},{24,152},{32,160},{40,168},{48,176},{56,1... | collective-permute-start | bytes 294920 | tf_op jit(solution)/shard_map/ppermute | solution.py:165

commit v8 on v7

--- a/solution.py
+++ b/solution.py
@@ -125,53 +125,72 @@
     return out.reshape(scalars.shape), exit_plane
 
 
-def xor_sum(x, axis):
+def digit_levels(devices, radices):
+    levels, stride = [], 1
+    for radix in radices:
+        levels.append((stride, radix))
+        stride *= radix
+    if stride != devices:
+        levels, stride = [], 1
+        while stride < devices:
+            levels.append((stride, 2))
+            stride *= 2
+    return levels
+
+
+def digit_exchange(x, axis, stride, radix):
     devices = lax.axis_size(axis)
-    step = 1
-    while step < devices:
-        pairs = [(i, i ^ step) for i in range(devices)]
-        x = x + lax.ppermute(x, axis, pairs)
-        step *= 2
+    digit = (lax.axis_index(axis) // stride) % radix
+    received = {}
+    for shift in range(1, radix):
+        pairs = [
+            (i, i + (((i // stride) % radix + shift) % radix - (i // stride) % radix) * stride)
+            for i in range(devices)
+        ]
+        received[shift] = lax.ppermute(x, axis, pairs)
+    blocks = []
+    for k in range(radix):
+        value = x
+        for m in range(radix):
+            if m != k:
+                value = jnp.where(digit == m, received[(m - k) % radix], value)
+        blocks.append(value)
+    return blocks, digit
+
+
+def digit_gather(x, axis, levels, dim):
+    for stride, radix in levels:
+        blocks, _ = digit_exchange(x, axis, stride, radix)
+        x = jnp.concatenate(blocks, dim)
     return x
 
 
-def xor_gather(x, axis, dim):
-    devices = lax.axis_size(axis)
-    place = lax.axis_index(axis)
-    step = 1
-    while step < devices:
-        pairs = [(i, i ^ step) for i in range(devices)]
-        other = lax.ppermute(x, axis, pairs)
-        low = (place & step) == 0
-        x = jnp.where(
-            low, jnp.concatenate([x, other], dim), jnp.concatenate([other, x], dim)
-        )
-        step *= 2
-    return x
+def pick(digit, options):
+    value = options[0]
+    for m in range(1, len(options)):
+        value = jax.tree.map(lambda a, b: jnp.where(digit == m, a, b), options[m], value)
+    return value
 
 
 def compose(earlier, later):
     return (later[0] * earlier[0], later[0] * earlier[1] + later[1])
 
 
-def exclusive_scan(part, carried, axis):
-    devices = lax.axis_size(axis)
-    place = lax.axis_index(axis)
+def exclusive_scan(part, carried, axis, levels):
     total = part
     before = (jnp.ones_like(part[0]), jnp.zeros_like(part[1]))
-    step = 1
-    while step < devices:
-        pairs = [(i, i ^ step) for i in range(devices)]
-        other = lax.ppermute(jnp.stack(total + (carried,)), axis, pairs)
-        carried = carried + other[2]
-        other = (other[0], other[1])
-        later = (place & step) != 0
-        new_before = compose(other, before)
-        before = jax.tree.map(lambda a, b: jnp.where(later, a, b), new_before, before)
-        total = jax.tree.map(
-            lambda a, b: jnp.where(later, a, b), compose(other, total), compose(total, other)
-        )
-        step *= 2
+    for stride, radix in levels:
+        blocks, digit = digit_exchange(jnp.stack(total + (carried,)), axis, stride, radix)
+        carried = blocks[0][2]
+        for block in blocks[1:]:
+            carried = carried + block[2]
+        prefix = (jnp.ones_like(part[0]), jnp.zeros_like(part[1]))
+        prefixes = []
+        for block in blocks:
+            prefixes.append(prefix)
+            prefix = compose(prefix, (block[0], block[1]))
+        before = compose(pick(digit, prefixes), before)
+        total = prefix
     return before, carried
 
 
@@ -211,7 +230,7 @@
     local_plane = station_index[0] - owner_row * plane_count
     own_slice = lax.dynamic_index_in_dim(scalars, local_plane, 1, keepdims=False)
     mine = stream_rank == owner_row
-    station_plane = xor_gather(own_slice, "gz", 1)
+    station_plane = digit_gather(own_slice, "gz", digit_levels(lax.axis_size("gz"), (4, 2)), 1)
     inflow_full = make_inflow(station_plane, mean_profile, recycle_gain, span_shift)
     own_inflow = lax.dynamic_slice_in_dim(inflow_full, span_rank * span_cells, span_cells, 1)
     candidate = jnp.where(mine, own_inflow, jnp.zeros_like(own_inflow))
@@ -233,7 +252,9 @@
         + inverse[:, -1, 0][:, None, None] * first_gain
         + inverse[:, -1, 1][:, None, None] * second_gain
     )
-    (through, upstream_sum), inflow = exclusive_scan((exit_gain, exit_plane), candidate, "gx")
+    (through, upstream_sum), inflow = exclusive_scan(
+        (exit_gain, exit_plane), candidate, "gx", digit_levels(stream_devices, (2, 4, 4))
+    )
     incoming = through * inflow + upstream_sum
     first_in = first_gain * inflow
     second_in = second_gain * inflow

time: 95 us -> 92.5 us (0.974)
  the two profiles are of different devices: /device:TPU:32 before, /device:TPU:6 now
where the time goes in v8:
time: 92.5 us; the launch traced here: 92 us
  starting transfers between devices  30.9 us (33%)
  waiting for transfers between devices  25.2 us (27%)
  Pallas kernels  19.1 us (21%)
  other arithmetic  8.13 us (9%)
  local copies, waits for them, and re-layouts  7.22 us (8%)
  between operations  1.59 us (2%)
    ppermute x11, waiting for transfers between devices, digit_exchange(): received[shift] = lax.ppermute(x, axis, pairs)  25.1 us
    ppermute x11, starting transfers between devices, digit_exchange(): received[shift] = lax.ppermute(x, axis, pairs)  22 us
    pallas_call x1, Pallas kernels, explicit_local(): pl.pallas_call(functools.partial(explicit_kernel, planes, rows, width), o...  19.1 us
    ppermute x4, starting transfers between devices, halos(): return (lax.ppermute(last, axis, up), lax.ppermute(first, axis, down))  8.83 us
    add x1, other arithmetic, on_device(): local_part + response[:, :, None, None] * incoming[:, None]  4.12 us
    slice x2, local copies, waits for them, and re-layouts, halos(): first = lax.slice_in_dim(x, 0, width, axis=dim)  3.47 us
  transfers between devices with their start and end apart: 15, of which 7 were waited for; matrix products, arithmetic and copies ran while one was open for 8% of the time, Pallas kernels for 0%

profile of v8, /device:TPU:6, one launch (start us, length us, event | category | flops | bytes accessed | tf_op | source)
XLA Modules:
  0.0 92.0 jit_solution(6588169516389072518)
XLA Ops:
  0.7 0.8 dynamic-slice_bitcast_fusion
  1.5 2.2 %collective-permute-start.6 = (f32[2,16,256]{2,1,0:T(8,128)S(1)}, f32[2,16,256]{2,1,0:T(8,128)S(1)}, u32[]{:S(2)}, u32[]{:S(2)}) collective-permute-start(f32[2,16,256]{2,1,0:T(8,128)S(1)} %get-tuple-element.19), channel_id=1, source_target_pairs={{0,1},{1,2},{2,3},{3,0},{4,5},{5,6},{6,7},{7,4},{8,9},{9,10},{10,1... | collective-permute-start | bytes 98312 | tf_op jit(solution)/shard_map/ppermute | solution.py:150
  3.7 0.7 collective-permute-start.5
  4.7 0.9 fusion.21
  5.5 1.3 %collective-permute-start.1 = (f32[2,2,16,256]{3,2,1,0:T(8,128)S(1)}, f32[2,2,16,256]{3,2,1,0:T(8,128)S(1)}, u32[]{:S(2)}, u32[]{:S(2)}) collective-permute-start(f32[2,2,16,256]{3,2,1,0:T(8,128)S(1)} %get-tuple-element.23), channel_id=1, source_target_pairs={{8,0},{16,8},{24,16},{32,24},{40,32},{48,40},{56,48},{64,56},{72,6... | collective-permute-start | bytes 196616 | tf_op jit(solution)/shard_map/ppermute | solution.py:203
  6.8 3.0 %collective-permute-start = (f32[2,2,16,256]{3,2,1,0:T(8,128)S(1)}, f32[2,2,16,256]{3,2,1,0:T(8,128)S(1)}, u32[]{:S(2)}, u32[]{:S(2)}) collective-permute-start(f32[2,2,16,256]{3,2,1,0:T(8,128)S(1)} %get-tuple-element.24), channel_id=1, source_target_pairs={{0,8},{8,16},{16,24},{24,32},{32,40},{40,48},{48,56},{56,64},{64,7... | collective-permute-start | bytes 196616 | tf_op jit(solution)/shard_map/ppermute | solution.py:203
  9.9 2.6 %fusion.20 = (f32[2,128,2,256]{3,2,1,0:T(2,128)S(1)}, f32[2,128,2,256]{3,2,1,0:T(2,128)S(1)}) fusion(f32[2,128,16,256]{3,2,1,0:T(8,128)} %param.9), kind=kLoop, calls=%fused_computation.89 | loop fusion | bytes 2097152 | tf_op jit(solution)/shard_map/slice | solution.py:202
  12.5 0.9 slice_reduce_fusion.4
  13.4 0.9 %slice_reduce_fusion.3 = (f32[2]{0:T(128)S(1)}, f32[2]{0:T(128)S(1)}) fusion(f32[2,128,128]{2,1,0:T(8,128)} %bitcast.135), kind=kLoop, calls=%fused_computation.85 | loop fusion | bytes 32 | tf_op jit(solution)/shard_map/slice | solution.py:252
  14.3 0.8 select_bitcast_fusion.2
  15.8 2.6 %collective-permute-start.3 = (f32[2,128,2,256]{3,2,1,0:T(2,128)S(1)}, f32[2,128,2,256]{3,2,1,0:T(2,128)S(1)}, u32[]{:S(2)}, u32[]{:S(2)}) collective-permute-start(f32[2,128,2,256]{3,2,1,0:T(2,128)S(1)} %get-tuple-element.21), channel_id=1, source_target_pairs={{1,0},{2,1},{3,2},{4,3},{5,4},{6,5},{7,6},{0,7},{9,8},{10,9},{11,1... | collective-permute-start | bytes 1572872 | tf_op jit(solution)/shard_map/ppermute | solution.py:203
  18.4 1.9 %collective-permute-start.2 = (f32[2,128,2,256]{3,2,1,0:T(2,128)S(1)}, f32[2,128,2,256]{3,2,1,0:T(2,128)S(1)}, u32[]{:S(2)}, u32[]{:S(2)}) collective-permute-start(f32[2,128,2,256]{3,2,1,0:T(2,128)S(1)} %get-tuple-element.22), channel_id=1, source_target_pairs={{0,1},{1,2},{2,3},{3,4},{4,5},{5,6},{6,7},{7,0},{8,9},{9,10},{10,1... | collective-permute-start | bytes 1572872 | tf_op jit(solution)/shard_map/ppermute | solution.py:203
  20.4 1.5 %collective-permute-start.7 = (f32[2,64,256]{2,1,0:T(8,128)S(1)}, f32[2,64,256]{2,1,0:T(8,128)S(1)}, u32[]{:S(2)}, u32[]{:S(2)}) collective-permute-start(f32[2,64,256]{2,1,0:T(8,128)S(1)} %pad_maximum_fusion), channel_id=1, source_target_pairs={{0,4},{1,5},{2,6},{3,7},{4,0},{5,1},{6,2},{7,3},{8,12},{9,13},{10,... | collective-permute-start | bytes 393224 | tf_op jit(solution)/shard_map/ppermute | solution.py:150
  21.8 0.6 broadcast_select_fusion.4
  22.4 0.6 broadcast_select_fusion.5
  23.1 12.5 %collective-permute-done.7 = f32[2,64,256]{2,1,0:T(8,128)S(1)} collective-permute-done((f32[2,64,256]{2,1,0:T(8,128)S(1)}, f32[2,64,256]{2,1,0:T(8,128)S(1)}, u32[]{:S(2)}, u32[]{:S(2)}) %collective-permute-start.7) | collective-permute-done | bytes 131104 | tf_op jit(solution)/shard_map/ppermute | solution.py:150
  35.7 0.8 copy-done.1
  36.7 19.1 %shard_map.91 = (f32[2,2048,256]{2,1,0:T(8,128)}, f32[2,16,256]{2,1,0:T(8,128)}) custom-call(f32[2,2048,256]{2,1,0:T(8,128)} %bitcast.131, f32[2,32,256]{2,1,0:T(8,128)} %bitcast.139, f32[2,32,256]{2,1,0:T(8,128)} %bitcast.138, f32[2,128,2,256]{3,2,1,0:T(2,128)} %copy-done.2, f32[2,128,2,256]{3,2,1,0:T(2,128)} %copy-done.1, f32[2048,256]{1,0:T(8,128)} %bitcast.133, ...), custom_call_target="tpu_custom_call" | custom-call | flops 331350016 | bytes 16777216 | tf_op jit(solution)/shard_map/pallas_call | solution.py:109
  55.7 0.8 pad_maximum_fusion.1
  56.5 1.5 %collective-permute-start.8 = (f32[3,2,16,256]{3,2,1,0:T(8,128)S(1)}, f32[3,2,16,256]{3,2,1,0:T(8,128)S(1)}, u32[]{:S(2)}, u32[]{:S(2)}) collective-permute-start(f32[3,2,16,256]{3,2,1,0:T(8,128)S(1)} %pad_maximum_fusion.1), channel_id=1, source_target_pairs={{0,8},{8,0},{16,24},{24,16},{32,40},{40,32},{48,56},{56,48},{64,72... | collective-permute-start | bytes 294920 | tf_op jit(solution)/shard_map/ppermute | solution.py:150
  58.0 0.9 %collective-permute-done.8 = f32[3,2,16,256]{3,2,1,0:T(8,128)S(1)} collective-permute-done((f32[3,2,16,256]{3,2,1,0:T(8,128)S(1)}, f32[3,2,16,256]{3,2,1,0:T(8,128)S(1)}, u32[]{:S(2)}, u32[]{:S(2)}) %collective-permute-start.8) | collective-permute-done | bytes 98336 | tf_op jit(solution)/shard_map/ppermute | solution.py:150
  59.0 0.8 broadcast_select_fusion.3
  59.8 6.7 %collective-permute-start.11 = (f32[3,2,16,256]{3,2,1,0:T(8,128)S(1)}, f32[3,2,16,256]{3,2,1,0:T(8,128)S(1)}, u32[]{:S(2)}, u32[]{:S(2)}) collective-permute-start(f32[3,2,16,256]{3,2,1,0:T(8,128)S(1)} %pad_maximum_fusion.2), channel_id=1, source_target_pairs={{0,32},{8,40},{16,48},{24,56},{32,0},{40,8},{48,16},{56,24},{64,96... | collective-permute-start | bytes 294920 | tf_op jit(solution)/shard_map/ppermute | solution.py:150
  66.8 2.7 %collective-permute-start.9 = (f32[3,2,16,256]{3,2,1,0:T(8,128)S(1)}, f32[3,2,16,256]{3,2,1,0:T(8,128)S(1)}, u32[]{:S(2)}, u32[]{:S(2)}) collective-permute-start(f32[3,2,16,256]{3,2,1,0:T(8,128)S(1)} %pad_maximum_fusion.2), channel_id=1, source_target_pairs={{0,16},{8,24},{16,32},{24,40},{32,48},{40,56},{48,0},{56,8},{64,80... | collective-permute-start | bytes 294920 | tf_op jit(solution)/shard_map/ppermute | solution.py:150
  69.8 6.8 %collective-permute-done.10 = f32[3,2,16,256]{3,2,1,0:T(8,128)S(1)} collective-permute-done((f32[3,2,16,256]{3,2,1,0:T(8,128)S(1)}, f32[3,2,16,256]{3,2,1,0:T(8,128)S(1)}, u32[]{:S(2)}, u32[]{:S(2)}) %collective-permute-start.10) | collective-permute-done | bytes 98336 | tf_op jit(solution)/shard_map/ppermute | solution.py:150
  76.7 4.2 %collective-permute-start.14 = (f32[3,2,16,256]{3,2,1,0:T(8,128)S(1)}, f32[3,2,16,256]{3,2,1,0:T(8,128)S(1)}, u32[]{:S(2)}, u32[]{:S(2)}) collective-permute-start(f32[3,2,16,256]{3,2,1,0:T(8,128)S(1)} %pad_maximum_fusion.3), channel_id=1, source_target_pairs={{0,128},{8,136},{16,144},{24,152},{32,160},{40,168},{48,176},{56,1... | collective-permute-start | bytes 294920 | tf_op jit(solution)/shard_map/ppermute | solution.py:150
  80.8 1.1 %collective-permute-start.13 = (f32[3,2,16,256]{3,2,1,0:T(8,128)S(1)}, f32[3,2,16,256]{3,2,1,0:T(8,128)S(1)}, u32[]{:S(2)}, u32[]{:S(2)}) collective-permute-start(f32[3,2,16,256]{3,2,1,0:T(8,128)S(1)} %pad_maximum_fusion.3), channel_id=1, source_target_pairs={{0,192},{8,200},{16,208},{24,216},{32,224},{40,232},{48,240},{56,2... | collective-permute-start | bytes 294920 | tf_op jit(solution)/shard_map/ppermute | solution.py:150
  81.9 1.0 %collective-permute-start.12 = (f32[3,2,16,256]{3,2,1,0:T(8,128)S(1)}, f32[3,2,16,256]{3,2,1,0:T(8,128)S(1)}, u32[]{:S(2)}, u32[]{:S(2)}) collective-permute-start(f32[3,2,16,256]{3,2,1,0:T(8,128)S(1)} %pad_maximum_fusion.3), channel_id=1, source_target_pairs={{0,64},{8,72},{16,80},{24,88},{32,96},{40,104},{48,112},{56,120},{... | collective-permute-start | bytes 294920 | tf_op jit(solution)/shard_map/ppermute | solution.py:150
  83.1 0.8 collective-permute-done.14
  83.9 1.5 %collective-permute-done.13 = f32[3,2,16,256]{3,2,1,0:T(8,128)S(1)} collective-permute-done((f32[3,2,16,256]{3,2,1,0:T(8,128)S(1)}, f32[3,2,16,256]{3,2,1,0:T(8,128)S(1)}, u32[]{:S(2)}, u32[]{:S(2)}) %collective-permute-start.13) | collective-permute-done | bytes 98336 | tf_op jit(solution)/shard_map/ppermute | solution.py:150
  85.5 2.3 %collective-permute-done.12 = f32[3,2,16,256]{3,2,1,0:T(8,128)S(1)} collective-permute-done((f32[3,2,16,256]{3,2,1,0:T(8,128)S(1)}, f32[3,2,16,256]{3,2,1,0:T(8,128)S(1)}, u32[]{:S(2)}, u32[]{:S(2)}) %collective-permute-start.12) | collective-permute-done | bytes 98336 | tf_op jit(solution)/shard_map/ppermute | solution.py:150
  87.9 4.1 %multiply_add_fusion = f32[2,128,16,256]{3,2,1,0:T(8,128)} fusion(f32[2,128,16,256]{3,2,1,0:T(8,128)} %bitcast.132, f32[2,16,256]{2,1,0:T(8,128)S(1)} %get-tuple-element.49, f32[2,128]{1,0:T(2,128)S(1)} %get-tuple-element.10, f32[2,16,256]{2,1,0:T(8,128)S(1)} %get-tuple-element.48, f32[2,128]{1,0:T(2,128)S(1)} %get-tuple-element.9, ...), kind=kLoop, calls=%fused_computation | loop fusion | flops 6291456 | bytes 8489984 | tf_op jit(solution)/shard_map/add | solution.py:262
  (37 shorter events, 1.6 us)
Async XLA Ops:
  0.0 35.6 %copy-start.4 = (f32[2,256]{1,0:T(2,128)S(1)}, f32[2,256]{1,0:T(2,128)}, u32[]{:S(2)}) copy-start(f32[2,256]{1,0:T(2,128)} %param.15) | copy-start | bytes 6148
  0.0 35.6 %copy-start.3 = (f32[2,256]{1,0:T(2,128)S(1)}, f32[2,256]{1,0:T(2,128)}, u32[]{:S(2)}) copy-start(f32[2,256]{1,0:T(2,128)} %param.14) | copy-start | bytes 6148
  1.5 14.3 %collective-permute-start.6 = (f32[2,16,256]{2,1,0:T(8,128)S(1)}, f32[2,16,256]{2,1,0:T(8,128)S(1)}, u32[]{:S(2)}, u32[]{:S(2)}) collective-permute-start(f32[2,16,256]{2,1,0:T(8,128)S(1)} %get-tuple-element.19), channel_id=1, source_target_pairs={{0,1},{1,2},{2,3},{3,0},{4,5},{5,6},{6,7},{7,4},{8,9},{9,10},{10,1... | collective-permute-start | bytes 98312 | tf_op jit(solution)/shard_map/ppermute | solution.py:150
  3.7 14.7 %collective-permute-start.5 = (f32[2,16,256]{2,1,0:T(8,128)S(1)}, f32[2,16,256]{2,1,0:T(8,128)S(1)}, u32[]{:S(2)}, u32[]{:S(2)}) collective-permute-start(f32[2,16,256]{2,1,0:T(8,128)S(1)} %get-tuple-element.19), channel_id=1, source_target_pairs={{0,2},{1,3},{2,0},{3,1},{4,6},{5,7},{6,4},{7,5},{8,10},{9,11},{10,... | collective-permute-start | bytes 98312 | tf_op jit(solution)/shard_map/ppermute | solution.py:150
  4.4 15.9 %collective-permute-start.4 = (f32[2,16,256]{2,1,0:T(8,128)S(1)}, f32[2,16,256]{2,1,0:T(8,128)S(1)}, u32[]{:S(2)}, u32[]{:S(2)}) collective-permute-start(f32[2,16,256]{2,1,0:T(8,128)S(1)} %get-tuple-element.19), channel_id=1, source_target_pairs={{0,3},{1,0},{2,1},{3,2},{4,7},{5,4},{6,5},{7,6},{8,11},{9,8},{10,9... | collective-permute-start | bytes 98312 | tf_op jit(solution)/shard_map/ppermute | solution.py:150
  5.5 16.3 %collective-permute-start.1 = (f32[2,2,16,256]{3,2,1,0:T(8,128)S(1)}, f32[2,2,16,256]{3,2,1,0:T(8,128)S(1)}, u32[]{:S(2)}, u32[]{:S(2)}) collective-permute-start(f32[2,2,16,256]{3,2,1,0:T(8,128)S(1)} %get-tuple-element.23), channel_id=1, source_target_pairs={{8,0},{16,8},{24,16},{32,24},{40,32},{48,40},{56,48},{64,56},{72,6... | collective-permute-start | bytes 196616 | tf_op jit(solution)/shard_map/ppermute | solution.py:203
  6.8 15.6 %collective-permute-start = (f32[2,2,16,256]{3,2,1,0:T(8,128)S(1)}, f32[2,2,16,256]{3,2,1,0:T(8,128)S(1)}, u32[]{:S(2)}, u32[]{:S(2)}) collective-permute-start(f32[2,2,16,256]{3,2,1,0:T(8,128)S(1)} %get-tuple-element.24), channel_id=1, source_target_pairs={{0,8},{8,16},{16,24},{24,32},{32,40},{40,48},{48,56},{56,64},{64,7... | collective-permute-start | bytes 196616 | tf_op jit(solution)/shard_map/ppermute | solution.py:203
  15.8 19.9 %collective-permute-start.3 = (f32[2,128,2,256]{3,2,1,0:T(2,128)S(1)}, f32[2,128,2,256]{3,2,1,0:T(2,128)S(1)}, u32[]{:S(2)}, u32[]{:S(2)}) collective-permute-start(f32[2,128,2,256]{3,2,1,0:T(2,128)S(1)} %get-tuple-element.21), channel_id=1, source_target_pairs={{1,0},{2,1},{3,2},{4,3},{5,4},{6,5},{7,6},{0,7},{9,8},{10,9},{11,1... | collective-permute-start | bytes 1572872 | tf_op jit(solution)/shard_map/ppermute | solution.py:203
  18.4 17.3 %collective-permute-start.2 = (f32[2,128,2,256]{3,2,1,0:T(2,128)S(1)}, f32[2,128,2,256]{3,2,1,0:T(2,128)S(1)}, u32[]{:S(2)}, u32[]{:S(2)}) collective-permute-start(f32[2,128,2,256]{3,2,1,0:T(2,128)S(1)} %get-tuple-element.22), channel_id=1, source_target_pairs={{0,1},{1,2},{2,3},{3,4},{4,5},{5,6},{6,7},{7,0},{8,9},{9,10},{10,1... | collective-permute-start | bytes 1572872 | tf_op jit(solution)/shard_map/ppermute | solution.py:203
  20.4 15.2 %collective-permute-start.7 = (f32[2,64,256]{2,1,0:T(8,128)S(1)}, f32[2,64,256]{2,1,0:T(8,128)S(1)}, u32[]{:S(2)}, u32[]{:S(2)}) collective-permute-start(f32[2,64,256]{2,1,0:T(8,128)S(1)} %pad_maximum_fusion), channel_id=1, source_target_pairs={{0,4},{1,5},{2,6},{3,7},{4,0},{5,1},{6,2},{7,3},{8,12},{9,13},{10,... | collective-permute-start | bytes 393224 | tf_op jit(solution)/shard_map/ppermute | solution.py:150
  35.7 0.8 copy-start.1
  35.7 1.0 %copy-start.2 = (f32[2,128,2,256]{3,2,1,0:T(2,128)}, f32[2,128,2,256]{3,2,1,0:T(2,128)S(1)}, u32[]{:S(2)}) copy-start(f32[2,128,2,256]{3,2,1,0:T(2,128)S(1)} %collective-permute-done.2.before_ref) | copy-start | bytes 1572868
  36.7 46.2 %copy-start = (f32[2,1,128,128]{3,2,1,0:T(8,128)S(1)}, f32[2,1,128,128]{3,2,1,0:T(8,128)}, u32[]{:S(2)}) copy-start(f32[2,1,128,128]{3,2,1,0:T(8,128)} %param.12) | copy-start | bytes 393220
  55.7 32.1 %copy-start.5 = (f32[2,1,128]{2,1,0:T(1,128)S(1)}, f32[2,1,128]{2,1,0:T(1,128)}, u32[]{:S(2)}) copy-start(f32[2,1,128]{2,1,0:T(1,128)} %param.13) | copy-start | bytes 3076
  56.5 2.5 %collective-permute-start.8 = (f32[3,2,16,256]{3,2,1,0:T(8,128)S(1)}, f32[3,2,16,256]{3,2,1,0:T(8,128)S(1)}, u32[]{:S(2)}, u32[]{:S(2)}) collective-permute-start(f32[3,2,16,256]{3,2,1,0:T(8,128)S(1)} %pad_maximum_fusion.1), channel_id=1, source_target_pairs={{0,8},{8,0},{16,24},{24,16},{32,40},{40,32},{48,56},{56,48},{64,72... | collective-permute-start | bytes 294920 | tf_op jit(solution)/shard_map/ppermute | solution.py:150
  59.8 10.0 %collective-permute-start.11 = (f32[3,2,16,256]{3,2,1,0:T(8,128)S(1)}, f32[3,2,16,256]{3,2,1,0:T(8,128)S(1)}, u32[]{:S(2)}, u32[]{:S(2)}) collective-permute-start(f32[3,2,16,256]{3,2,1,0:T(8,128)S(1)} %pad_maximum_fusion.2), channel_id=1, source_target_pairs={{0,32},{8,40},{16,48},{24,56},{32,0},{40,8},{48,16},{56,24},{64,96... | collective-permute-start | bytes 294920 | tf_op jit(solution)/shard_map/ppermute | solution.py:150
  66.6 10.0 %collective-permute-start.10 = (f32[3,2,16,256]{3,2,1,0:T(8,128)S(1)}, f32[3,2,16,256]{3,2,1,0:T(8,128)S(1)}, u32[]{:S(2)}, u32[]{:S(2)}) collective-permute-start(f32[3,2,16,256]{3,2,1,0:T(8,128)S(1)} %pad_maximum_fusion.2), channel_id=1, source_target_pairs={{0,48},{8,56},{16,0},{24,8},{32,16},{40,24},{48,32},{56,40},{64,11... | collective-permute-start | bytes 294920 | tf_op jit(solution)/shard_map/ppermute | solution.py:150
  66.8 9.8 %collective-permute-start.9 = (f32[3,2,16,256]{3,2,1,0:T(8,128)S(1)}, f32[3,2,16,256]{3,2,1,0:T(8,128)S(1)}, u32[]{:S(2)}, u32[]{:S(2)}) collective-permute-start(f32[3,2,16,256]{3,2,1,0:T(8,128)S(1)} %pad_maximum_fusion.2), channel_id=1, source_target_pairs={{0,16},{8,24},{16,32},{24,40},{32,48},{40,56},{48,0},{56,8},{64,80... | collective-permute-start | bytes 294920 | tf_op jit(solution)/shard_map/ppermute | solution.py:150
  76.7 7.3 %collective-permute-start.14 = (f32[3,2,16,256]{3,2,1,0:T(8,128)S(1)}, f32[3,2,16,256]{3,2,1,0:T(8,128)S(1)}, u32[]{:S(2)}, u32[]{:S(2)}) collective-permute-start(f32[3,2,16,256]{3,2,1,0:T(8,128)S(1)} %pad_maximum_fusion.3), channel_id=1, source_target_pairs={{0,128},{8,136},{16,144},{24,152},{32,160},{40,168},{48,176},{56,1... | collective-permute-start | bytes 294920 | tf_op jit(solution)/shard_map/ppermute | solution.py:150
  80.8 4.6 %collective-permute-start.13 = (f32[3,2,16,256]{3,2,1,0:T(8,128)S(1)}, f32[3,2,16,256]{3,2,1,0:T(8,128)S(1)}, u32[]{:S(2)}, u32[]{:S(2)}) collective-permute-start(f32[3,2,16,256]{3,2,1,0:T(8,128)S(1)} %pad_maximum_fusion.3), channel_id=1, source_target_pairs={{0,192},{8,200},{16,208},{24,216},{32,224},{40,232},{48,240},{56,2... | collective-permute-start | bytes 294920 | tf_op jit(solution)/shard_map/ppermute | solution.py:150
  81.9 5.8 %collective-permute-start.12 = (f32[3,2,16,256]{3,2,1,0:T(8,128)S(1)}, f32[3,2,16,256]{3,2,1,0:T(8,128)S(1)}, u32[]{:S(2)}, u32[]{:S(2)}) collective-permute-start(f32[3,2,16,256]{3,2,1,0:T(8,128)S(1)} %pad_maximum_fusion.3), channel_id=1, source_target_pairs={{0,64},{8,72},{16,80},{24,88},{32,96},{40,104},{48,112},{56,120},{... | collective-permute-start | bytes 294920 | tf_op jit(solution)/shard_map/ppermute | solution.py:150

commit v9 on v8

--- a/solution.py
+++ b/solution.py
@@ -15,7 +15,7 @@
 
 
 def explicit_kernel(planes, rows, width,
-                    s_ref, head_ref, tail_ref, before_ref, after_ref, diff_ref, rate_ref, inv_ref,
+                    s_ref, head_ref, tail_ref, diff_ref, rate_ref, inv_ref,
                     out_ref, exit_ref, ex_ref):
     row = lax.broadcasted_iota(jnp.int32, (rows, width), 0)
     lane = lax.broadcasted_iota(jnp.int32, (rows, width), 1)
@@ -27,9 +27,6 @@
             return tail_ref[s, pl.ds((k - planes) * rows, rows), :]
         start = k * rows if isinstance(k, int) else pl.multiple_of(k * rows, rows)
         return s_ref[s, pl.ds(start, rows), :]
-
-    def halo_row(ref, s, j, r):
-        return jnp.broadcast_to(ref[s, j, pl.ds(r, 1), :], (rows, width))
 
     def one_plane(j, jm2, jm1, jp1, jp2):
         first_row, second_row = row == 0, row == 1
@@ -41,12 +38,10 @@
         for s in range(2):
             c = plane(s, j)
             sm2, sm1, sp1, sp2 = plane(s, jm2), plane(s, jm1), plane(s, jp1), plane(s, jp2)
-            b0, b1 = halo_row(before_ref, s, j, 0), halo_row(before_ref, s, j, 1)
-            a0, a1 = halo_row(after_ref, s, j, 0), halo_row(after_ref, s, j, 1)
-            zm1 = jnp.where(first_row, b1, pltpu.roll(c, 1, 0))
-            zm2 = jnp.where(first_row, b0, jnp.where(second_row, b1, pltpu.roll(c, 2, 0)))
-            zp1 = jnp.where(last_row, a0, pltpu.roll(c, rows - 1, 0))
-            zp2 = jnp.where(last_row, a1, jnp.where(next_to_last_row, a0, pltpu.roll(c, rows - 2, 0)))
+            zm1 = jnp.where(first_row, 0.0, pltpu.roll(c, 1, 0))
+            zm2 = jnp.where(first_row | second_row, 0.0, pltpu.roll(c, 2, 0))
+            zp1 = jnp.where(last_row, 0.0, pltpu.roll(c, rows - 1, 0))
+            zp2 = jnp.where(last_row | next_to_last_row, 0.0, pltpu.roll(c, rows - 2, 0))
             ym1 = jnp.where(first_lane, 0.0, pltpu.roll(c, 1, 1))
             ym2 = jnp.where(second_lane, 0.0, pltpu.roll(c, 2, 1))
             yp1 = jnp.where(last_lane, 0.0, pltpu.roll(c, width - 1, 1))
@@ -102,7 +97,7 @@
     lax.fori_loop(0, planes // 8, put, 0)
 
 
-def explicit_local(scalars, head, tail, before, after, diffusivity, reaction_rate, inverse):
+def explicit_local(scalars, head, tail, diffusivity, reaction_rate, inverse):
     species, planes, rows, width = scalars.shape
     flat = lambda a: a.reshape(a.shape[:-3] + (a.shape[-3] * rows, width))
     vmem = pl.BlockSpec(memory_space=pltpu.VMEM)
@@ -112,7 +107,7 @@
             jax.ShapeDtypeStruct((species, planes * rows, width), jnp.float32),
             jax.ShapeDtypeStruct((species, rows, width), jnp.float32),
         ),
-        in_specs=[vmem] * 8,
+        in_specs=[vmem] * 6,
         out_specs=(vmem, vmem),
         scratch_shapes=[pltpu.VMEM((species, width // 128, planes * rows, 128), jnp.float32)],
         compiler_params=pltpu.CompilerParams(vmem_limit_bytes=60 * 1024 * 1024),
@@ -121,7 +116,7 @@
             transcendentals=2 * planes * rows * width * 2,
             bytes_accessed=4 * (3 * species + 2) * planes * rows * width,
         ),
-    )(flat(scalars), flat(head), flat(tail), before, after, flat(diffusivity), flat(reaction_rate), inverse)
+    )(flat(scalars), flat(head), flat(tail), flat(diffusivity), flat(reaction_rate), inverse)
     return out.reshape(scalars.shape), exit_plane
 
 
@@ -245,8 +240,25 @@
     first_gain = jnp.where(at_inlet, diffusivity[0] * (15.0 / 12.0), 0.0)
     second_gain = jnp.where(at_inlet, diffusivity[1] * (-1.0 / 12.0), 0.0)
     local_part, exit_plane = explicit_local(
-        scalars, head_planes, tail_planes, before_rows, after_rows, diffusivity, reaction_rate, inverse
-    )
+        scalars, head_planes, tail_planes, diffusivity, reaction_rate, inverse
+    )
+    b0, b1 = before_rows[:, :, 0], before_rows[:, :, 1]
+    a0, a1 = after_rows[:, :, 0], after_rows[:, :, 1]
+    edge_terms = jnp.stack(
+        [
+            diffusivity[:, 0] * (16.0 * b1 - b0) * (1.0 / 12.0),
+            diffusivity[:, 1] * -b1 * (1.0 / 12.0),
+            diffusivity[:, span_cells - 2] * -a0 * (1.0 / 12.0),
+            diffusivity[:, span_cells - 1] * (16.0 * a0 - a1) * (1.0 / 12.0),
+        ],
+        axis=1,
+    )
+    edge_part = jnp.einsum(
+        "sij,skjy->siky", inverse, edge_terms, precision=lax.Precision.HIGHEST
+    )
+    gap = jnp.zeros(edge_part.shape[:2] + (span_cells - 4,) + edge_part.shape[3:], edge_part.dtype)
+    edge_part = jnp.concatenate([edge_part[:, :, :2], gap, edge_part[:, :, 2:]], axis=2)
+    exit_plane = exit_plane + edge_part[:, -1]
     exit_gain = (
         response[:, -1][:, None, None]
         + inverse[:, -1, 0][:, None, None] * first_gain
@@ -260,6 +272,7 @@
     second_in = second_gain * inflow
     return (
         local_part
+        + edge_part
         + response[:, :, None, None] * incoming[:, None]
         + inverse[:, :, 0][:, :, None, None] * first_in[:, None]
         + inverse[:, :, 1][:, :, None, None] * second_in[:, None]

time: 92.5 us -> 87.4 us (0.945)
  the two profiles are of different devices: /device:TPU:6 before, /device:TPU:32 now
where the time goes in v9:
time: 87.4 us; the launch traced here: 87 us
  starting transfers between devices  29.6 us (34%)
  Pallas kernels  18.5 us (21%)
  local copies, waits for them, and re-layouts  14.4 us (16%)
  waiting for transfers between devices  13.2 us (15%)
  other arithmetic  8.41 us (10%)
  between operations  1.72 us (2%)
  matrix products  1.06 us (1%)
    ppermute x11, starting transfers between devices, digit_exchange(): received[shift] = lax.ppermute(x, axis, pairs)  21.1 us
    pallas_call x1, Pallas kernels, explicit_local(): pl.pallas_call(functools.partial(explicit_kernel, planes, rows, width), o...  18.5 us
    ppermute x11, waiting for transfers between devices, digit_exchange(): received[shift] = lax.ppermute(x, axis, pairs)  13.2 us
    ppermute x4, starting transfers between devices, halos(): return (lax.ppermute(last, axis, up), lax.ppermute(first, axis, down))  8.5 us
    add x1, other arithmetic, on_device(): local_part + edge_part + response[:, :, None, None] * incoming[:, None]  5.15 us
    slice x1, local copies, waits for them, and re-layouts, halos(): last = lax.slice_in_dim(x, length - width, length, axis=dim)  2.59 us
    slice x1, local copies, waits for them, and re-layouts, on_device(): diffusivity[:, 0] * (16.0 * b1 - b0) * (1.0 / 12.0)  2.58 us
    add x1, local copies, waits for them, and re-layouts, on_device(): local_part + edge_part + response[:, :, None, None] * incoming[:, None]  2.55 us
  transfers between devices with their start and end apart: 15, of which 5 were waited for; matrix products, arithmetic and copies ran while one was open for 14% of the time, Pallas kernels for 21%

profile of v9, /device:TPU:32, one launch (start us, length us, event | category | flops | bytes accessed | tf_op | source)
XLA Modules:
  0.0 87.0 jit_solution(16426101434833376641)
XLA Ops:
  0.7 0.8 dynamic-slice_bitcast_fusion
  1.5 2.8 %collective-permute-start.4 = (f32[2,16,256]{2,1,0:T(8,128)S(1)}, f32[2,16,256]{2,1,0:T(8,128)S(1)}, u32[]{:S(2)}, u32[]{:S(2)}) collective-permute-start(f32[2,16,256]{2,1,0:T(8,128)S(1)} %get-tuple-element.19), channel_id=1, source_target_pairs={{0,3},{1,0},{2,1},{3,2},{4,7},{5,4},{6,5},{7,6},{8,11},{9,8},{10,9... | collective-permute-start | bytes 98312 | tf_op jit(solution)/shard_map/ppermute | solution.py:145
  4.2 0.8 collective-permute-start.5
  5.0 0.9 %collective-permute-start.6 = (f32[2,16,256]{2,1,0:T(8,128)S(1)}, f32[2,16,256]{2,1,0:T(8,128)S(1)}, u32[]{:S(2)}, u32[]{:S(2)}) collective-permute-start(f32[2,16,256]{2,1,0:T(8,128)S(1)} %get-tuple-element.19), channel_id=1, source_target_pairs={{0,1},{1,2},{2,3},{3,0},{4,5},{5,6},{6,7},{7,4},{8,9},{9,10},{10,1... | collective-permute-start | bytes 98312 | tf_op jit(solution)/shard_map/ppermute | solution.py:145
  5.9 0.9 %fusion.45 = (f32[2,2,16,256]{3,2,1,0:T(8,128)S(1)}, f32[2,2,16,256]{3,2,1,0:T(8,128)S(1)}) fusion(f32[2,128,16,256]{3,2,1,0:T(8,128)} %param.9), kind=kLoop, calls=%fused_computation.125 | loop fusion | bytes 262144 | tf_op jit(solution)/shard_map/slice | solution.py:197
  6.8 1.3 %collective-permute-start.1 = (f32[2,2,16,256]{3,2,1,0:T(8,128)S(1)}, f32[2,2,16,256]{3,2,1,0:T(8,128)S(1)}, u32[]{:S(2)}, u32[]{:S(2)}) collective-permute-start(f32[2,2,16,256]{3,2,1,0:T(8,128)S(1)} %get-tuple-element.21), channel_id=1, source_target_pairs={{8,0},{16,8},{24,16},{32,24},{40,32},{48,40},{56,48},{64,56},{72,6... | collective-permute-start | bytes 196616 | tf_op jit(solution)/shard_map/ppermute | solution.py:198
  8.1 3.0 %collective-permute-start = (f32[2,2,16,256]{3,2,1,0:T(8,128)S(1)}, f32[2,2,16,256]{3,2,1,0:T(8,128)S(1)}, u32[]{:S(2)}, u32[]{:S(2)}) collective-permute-start(f32[2,2,16,256]{3,2,1,0:T(8,128)S(1)} %get-tuple-element.22), channel_id=1, source_target_pairs={{0,8},{8,16},{16,24},{24,32},{32,40},{40,48},{48,56},{56,64},{64,7... | collective-permute-start | bytes 196616 | tf_op jit(solution)/shard_map/ppermute | solution.py:198
  11.1 2.6 %fusion.44 = (f32[2,128,2,256]{3,2,1,0:T(2,128)S(1)}, f32[2,128,2,256]{3,2,1,0:T(2,128)S(1)}) fusion(f32[2,128,16,256]{3,2,1,0:T(8,128)} %param.9), kind=kLoop, calls=%fused_computation.124 | loop fusion | bytes 2097152 | tf_op jit(solution)/shard_map/slice | solution.py:196
  13.7 2.6 %fusion.46 = (f32[128,1,256]{2,1,0:T(1,128)S(1)}, f32[128,1,256]{2,1,0:T(1,128)S(1)}, f32[128,1,256]{2,1,0:T(1,128)S(1)}, f32[128,1,256]{2,1,0:T(1,128)S(1)}) fusion(f32[128,16,256]{2,1,0:T(8,128)} %param.10), kind=kLoop, calls=%fused_computation.126 | loop fusion | bytes 1048576 | tf_op jit(solution)/shard_map/slice | solution.py:249
  16.3 0.7 select_bitcast_fusion.2
  17.1 0.9 %slice_reduce_fusion.1 = (f32[2]{0:T(128)S(1)}, f32[2]{0:T(128)S(1)}) fusion(f32[2,128,128]{2,1,0:T(8,128)} %bitcast.198), kind=kLoop, calls=%fused_computation.119 | loop fusion | bytes 32 | tf_op jit(solution)/shard_map/slice | solution.py:264
  18.0 0.9 %slice_reduce_fusion.2 = f32[2]{0:T(128)S(1)} fusion(f32[2,128]{1,0:T(2,128)} %bitcast.206), kind=kLoop, calls=%fused_computation.120 | loop fusion | bytes 16 | tf_op jit(solution)/shard_map/slice | solution.py:263
  19.9 1.8 %collective-permute-start.2 = (f32[2,128,2,256]{3,1,0,2:T(8,128)S(1)}, f32[2,128,2,256]{3,1,0,2:T(8,128)S(1)}, u32[]{:S(2)}, u32[]{:S(2)}) collective-permute-start(f32[2,128,2,256]{3,1,0,2:T(8,128)S(1)} %copy.43), channel_id=1, source_target_pairs={{0,1},{1,2},{2,3},{3,4},{4,5},{5,6},{6,7},{7,0},{8,9},{9,10},{10,1... | collective-permute-start | bytes 1572872 | tf_op jit(solution)/shard_map/ppermute | solution.py:198
  21.7 2.3 %collective-permute-start.3 = (f32[2,128,2,256]{3,1,0,2:T(8,128)S(1)}, f32[2,128,2,256]{3,1,0,2:T(8,128)S(1)}, u32[]{:S(2)}, u32[]{:S(2)}) collective-permute-start(f32[2,128,2,256]{3,1,0,2:T(8,128)S(1)} %copy.46), channel_id=1, source_target_pairs={{1,0},{2,1},{3,2},{4,3},{5,4},{6,5},{7,6},{0,7},{9,8},{10,9},{11,1... | collective-permute-start | bytes 1572872 | tf_op jit(solution)/shard_map/ppermute | solution.py:198
  25.7 18.5 %shard_map.91 = (f32[2,2048,256]{2,1,0:T(8,128)}, f32[2,16,256]{2,1,0:T(8,128)}) custom-call(f32[2,2048,256]{2,1,0:T(8,128)} %bitcast.194, f32[2,32,256]{2,1,0:T(8,128)} %bitcast.205, f32[2,32,256]{2,1,0:T(8,128)} %bitcast.204, f32[2048,256]{1,0:T(8,128)} %bitcast.197, f32[2048,256]{1,0:T(8,128)} %bitcast.201, f32[2,128,128]{2,1,0:T(8,128)} %bitcast.199), custom_call_target="tpu_custom_call" | custom-call | flops 331350016 | bytes 16777216 | tf_op jit(solution)/shard_map/pallas_call | solution.py:104
  44.6 1.1 %fusion.3 = f32[2,4,256,128]{2,3,1,0:T(8,128)S(1)} fusion(f32[2,1,128,256]{3,2,1,0:T(8,128)S(1)} %get-tuple-element.34, f32[2,1,128,256]{3,2,1,0:T(8,128)S(1)} %get-tuple-element.33, f32[2,1,128,256]{3,2,1,0:T(8,128)S(1)} %get-tuple-element.32, f32[2,1,128,256]{3,2,1,0:T(8,128)S(1)} %get-tuple-element.31, f32[2,1,128,128]{3,2,1,0:T(8,128)S(1)} %copy-done), kind=kOutput, calls=%fused_computation.5 | convolution fusion | flops 403439616 | bytes 2228224 | tf_op jit(solution)/shard_map/sij,skjy->siky/dot_general | solution.py:256
  47.5 2.3 %collective-permute-start.8 = (f32[3,2,16,256]{3,2,1,0:T(8,128)S(1)}, f32[3,2,16,256]{3,2,1,0:T(8,128)S(1)}, u32[]{:S(2)}, u32[]{:S(2)}) collective-permute-start(f32[3,2,16,256]{3,2,1,0:T(8,128)S(1)} %pad_maximum_fusion.2), channel_id=1, source_target_pairs={{0,8},{8,0},{16,24},{24,16},{32,40},{40,32},{48,56},{56,48},{64,72... | collective-permute-start | bytes 294920 | tf_op jit(solution)/shard_map/ppermute | solution.py:145
  49.8 0.9 %collective-permute-done.8 = f32[3,2,16,256]{3,2,1,0:T(8,128)S(1)} collective-permute-done((f32[3,2,16,256]{3,2,1,0:T(8,128)S(1)}, f32[3,2,16,256]{3,2,1,0:T(8,128)S(1)}, u32[]{:S(2)}, u32[]{:S(2)}) %collective-permute-start.8) | collective-permute-done | bytes 98336 | tf_op jit(solution)/shard_map/ppermute | solution.py:145
  50.8 6.6 %collective-permute-start.10 = (f32[3,2,16,256]{3,2,1,0:T(8,128)S(1)}, f32[3,2,16,256]{3,2,1,0:T(8,128)S(1)}, u32[]{:S(2)}, u32[]{:S(2)}) collective-permute-start(f32[3,2,16,256]{3,2,1,0:T(8,128)S(1)} %pad_maximum_fusion.3), channel_id=1, source_target_pairs={{0,48},{8,56},{16,0},{24,8},{32,16},{40,24},{48,32},{56,40},{64,11... | collective-permute-start | bytes 294920 | tf_op jit(solution)/shard_map/ppermute | solution.py:145
  57.3 1.4 %collective-permute-start.11 = (f32[3,2,16,256]{3,2,1,0:T(8,128)S(1)}, f32[3,2,16,256]{3,2,1,0:T(8,128)S(1)}, u32[]{:S(2)}, u32[]{:S(2)}) collective-permute-start(f32[3,2,16,256]{3,2,1,0:T(8,128)S(1)} %pad_maximum_fusion.3), channel_id=1, source_target_pairs={{0,32},{8,40},{16,48},{24,56},{32,0},{40,8},{48,16},{56,24},{64,96... | collective-permute-start | bytes 294920 | tf_op jit(solution)/shard_map/ppermute | solution.py:145
  58.8 1.1 %collective-permute-start.9 = (f32[3,2,16,256]{3,2,1,0:T(8,128)S(1)}, f32[3,2,16,256]{3,2,1,0:T(8,128)S(1)}, u32[]{:S(2)}, u32[]{:S(2)}) collective-permute-start(f32[3,2,16,256]{3,2,1,0:T(8,128)S(1)} %pad_maximum_fusion.3), channel_id=1, source_target_pairs={{0,16},{8,24},{16,32},{24,40},{32,48},{40,56},{48,0},{56,8},{64,80... | collective-permute-start | bytes 294920 | tf_op jit(solution)/shard_map/ppermute | solution.py:145
  59.8 3.6 %collective-permute-done.10 = f32[3,2,16,256]{3,2,1,0:T(8,128)S(1)} collective-permute-done((f32[3,2,16,256]{3,2,1,0:T(8,128)S(1)}, f32[3,2,16,256]{3,2,1,0:T(8,128)S(1)}, u32[]{:S(2)}, u32[]{:S(2)}) %collective-permute-start.10) | collective-permute-done | bytes 98336 | tf_op jit(solution)/shard_map/ppermute | solution.py:145
  63.4 4.9 %collective-permute-done.11 = f32[3,2,16,256]{3,2,1,0:T(8,128)S(1)} collective-permute-done((f32[3,2,16,256]{3,2,1,0:T(8,128)S(1)}, f32[3,2,16,256]{3,2,1,0:T(8,128)S(1)}, u32[]{:S(2)}, u32[]{:S(2)}) %collective-permute-start.11) | collective-permute-done | bytes 98336 | tf_op jit(solution)/shard_map/ppermute | solution.py:145
  68.3 1.3 %collective-permute-done.9 = f32[3,2,16,256]{3,2,1,0:T(8,128)S(1)} collective-permute-done((f32[3,2,16,256]{3,2,1,0:T(8,128)S(1)}, f32[3,2,16,256]{3,2,1,0:T(8,128)S(1)}, u32[]{:S(2)}, u32[]{:S(2)}) %collective-permute-start.9) | collective-permute-done | bytes 98336 | tf_op jit(solution)/shard_map/ppermute | solution.py:145
  69.7 1.5 %collective-permute-start.12 = (f32[3,2,16,256]{3,2,1,0:T(8,128)S(1)}, f32[3,2,16,256]{3,2,1,0:T(8,128)S(1)}, u32[]{:S(2)}, u32[]{:S(2)}) collective-permute-start(f32[3,2,16,256]{3,2,1,0:T(8,128)S(1)} %pad_maximum_fusion.4), channel_id=1, source_target_pairs={{0,64},{8,72},{16,80},{24,88},{32,96},{40,104},{48,112},{56,120},{... | collective-permute-start | bytes 294920 | tf_op jit(solution)/shard_map/ppermute | solution.py:145
  71.2 1.8 %collective-permute-start.13 = (f32[3,2,16,256]{3,2,1,0:T(8,128)S(1)}, f32[3,2,16,256]{3,2,1,0:T(8,128)S(1)}, u32[]{:S(2)}, u32[]{:S(2)}) collective-permute-start(f32[3,2,16,256]{3,2,1,0:T(8,128)S(1)} %pad_maximum_fusion.4), channel_id=1, source_target_pairs={{0,192},{8,200},{16,208},{24,216},{32,224},{40,232},{48,240},{56,2... | collective-permute-start | bytes 294920 | tf_op jit(solution)/shard_map/ppermute | solution.py:145
  73.0 1.6 %collective-permute-start.14 = (f32[3,2,16,256]{3,2,1,0:T(8,128)S(1)}, f32[3,2,16,256]{3,2,1,0:T(8,128)S(1)}, u32[]{:S(2)}, u32[]{:S(2)}) collective-permute-start(f32[3,2,16,256]{3,2,1,0:T(8,128)S(1)} %pad_maximum_fusion.4), channel_id=1, source_target_pairs={{0,128},{8,136},{16,144},{24,152},{32,160},{40,168},{48,176},{56,1... | collective-permute-start | bytes 294920 | tf_op jit(solution)/shard_map/ppermute | solution.py:145
  74.9 0.9 copy.40
  75.7 0.9 copy.41
  76.6 2.5 %collective-permute-done.14 = f32[3,2,16,256]{3,2,1,0:T(8,128)S(1)} collective-permute-done((f32[3,2,16,256]{3,2,1,0:T(8,128)S(1)}, f32[3,2,16,256]{3,2,1,0:T(8,128)S(1)}, u32[]{:S(2)}, u32[]{:S(2)}) %collective-permute-start.14) | collective-permute-done | bytes 98336 | tf_op jit(solution)/shard_map/ppermute | solution.py:145
  79.2 5.1 %fusion.2 = f32[2,128,16,256]{3,2,0,1:T(8,128)S(1)} fusion(f32[2,128,16,256]{3,2,1,0:T(8,128)} %bitcast.195, f32[2,16,256]{2,1,0:T(8,128)S(1)} %get-tuple-element.59, f32[2,128]{0,1:T(8,128)S(1)} %bitcast.203, f32[2,16,256]{2,1,0:T(8,128)S(1)} %get-tuple-element.58, f32[2,128]{0,1:T(8,128)S(1)} %bitcast.202, f32[2,16,256]{2,1,0:T(8,128)S(1)} %get-tuple-element.11, ...), kind=kLoop, calls=%fused_computation.4 | loop fusion | flops 9437184 | bytes 9538624 | tf_op jit(solution)/shard_map/add | solution.py:274
  84.4 2.6 %copy.38 = f32[2,128,16,256]{3,2,1,0:T(8,128)} copy(f32[2,128,16,256]{3,2,0,1:T(8,128)S(1)} %fusion.2) | data formatting | bytes 8388608 | tf_op jit(solution)/shard_map/add | solution.py:274
  (53 shorter events, 4.4 us)
Async XLA Ops:
  1.5 18.4 %collective-permute-start.4 = (f32[2,16,256]{2,1,0:T(8,128)S(1)}, f32[2,16,256]{2,1,0:T(8,128)S(1)}, u32[]{:S(2)}, u32[]{:S(2)}) collective-permute-start(f32[2,16,256]{2,1,0:T(8,128)S(1)} %get-tuple-element.19), channel_id=1, source_target_pairs={{0,3},{1,0},{2,1},{3,2},{4,7},{5,4},{6,5},{7,6},{8,11},{9,8},{10,9... | collective-permute-start | bytes 98312 | tf_op jit(solution)/shard_map/ppermute | solution.py:145
  4.2 17.5 %collective-permute-start.5 = (f32[2,16,256]{2,1,0:T(8,128)S(1)}, f32[2,16,256]{2,1,0:T(8,128)S(1)}, u32[]{:S(2)}, u32[]{:S(2)}) collective-permute-start(f32[2,16,256]{2,1,0:T(8,128)S(1)} %get-tuple-element.19), channel_id=1, source_target_pairs={{0,2},{1,3},{2,0},{3,1},{4,6},{5,7},{6,4},{7,5},{8,10},{9,11},{10,... | collective-permute-start | bytes 98312 | tf_op jit(solution)/shard_map/ppermute | solution.py:145
  5.0 19.0 %collective-permute-start.6 = (f32[2,16,256]{2,1,0:T(8,128)S(1)}, f32[2,16,256]{2,1,0:T(8,128)S(1)}, u32[]{:S(2)}, u32[]{:S(2)}) collective-permute-start(f32[2,16,256]{2,1,0:T(8,128)S(1)} %get-tuple-element.19), channel_id=1, source_target_pairs={{0,1},{1,2},{2,3},{3,0},{4,5},{5,6},{6,7},{7,4},{8,9},{9,10},{10,1... | collective-permute-start | bytes 98312 | tf_op jit(solution)/shard_map/ppermute | solution.py:145
  6.8 17.7 %collective-permute-start.1 = (f32[2,2,16,256]{3,2,1,0:T(8,128)S(1)}, f32[2,2,16,256]{3,2,1,0:T(8,128)S(1)}, u32[]{:S(2)}, u32[]{:S(2)}) collective-permute-start(f32[2,2,16,256]{3,2,1,0:T(8,128)S(1)} %get-tuple-element.21), channel_id=1, source_target_pairs={{8,0},{16,8},{24,16},{32,24},{40,32},{48,40},{56,48},{64,56},{72,6... | collective-permute-start | bytes 196616 | tf_op jit(solution)/shard_map/ppermute | solution.py:198
  8.1 17.0 %collective-permute-start = (f32[2,2,16,256]{3,2,1,0:T(8,128)S(1)}, f32[2,2,16,256]{3,2,1,0:T(8,128)S(1)}, u32[]{:S(2)}, u32[]{:S(2)}) collective-permute-start(f32[2,2,16,256]{3,2,1,0:T(8,128)S(1)} %get-tuple-element.22), channel_id=1, source_target_pairs={{0,8},{8,16},{16,24},{24,32},{32,40},{40,48},{48,56},{56,64},{64,7... | collective-permute-start | bytes 196616 | tf_op jit(solution)/shard_map/ppermute | solution.py:198
  19.9 24.5 %collective-permute-start.2 = (f32[2,128,2,256]{3,1,0,2:T(8,128)S(1)}, f32[2,128,2,256]{3,1,0,2:T(8,128)S(1)}, u32[]{:S(2)}, u32[]{:S(2)}) collective-permute-start(f32[2,128,2,256]{3,1,0,2:T(8,128)S(1)} %copy.43), channel_id=1, source_target_pairs={{0,1},{1,2},{2,3},{3,4},{4,5},{5,6},{6,7},{7,0},{8,9},{9,10},{10,1... | collective-permute-start | bytes 1572872 | tf_op jit(solution)/shard_map/ppermute | solution.py:198
  21.7 22.8 %collective-permute-start.3 = (f32[2,128,2,256]{3,1,0,2:T(8,128)S(1)}, f32[2,128,2,256]{3,1,0,2:T(8,128)S(1)}, u32[]{:S(2)}, u32[]{:S(2)}) collective-permute-start(f32[2,128,2,256]{3,1,0,2:T(8,128)S(1)} %copy.46), channel_id=1, source_target_pairs={{1,0},{2,1},{3,2},{4,3},{5,4},{6,5},{7,6},{0,7},{9,8},{10,9},{11,1... | collective-permute-start | bytes 1572872 | tf_op jit(solution)/shard_map/ppermute | solution.py:198
  24.1 20.2 %collective-permute-start.7 = (f32[2,64,256]{2,1,0:T(8,128)S(1)}, f32[2,64,256]{2,1,0:T(8,128)S(1)}, u32[]{:S(2)}, u32[]{:S(2)}) collective-permute-start(f32[2,64,256]{2,1,0:T(8,128)S(1)} %pad_maximum_fusion.1), channel_id=1, source_target_pairs={{0,4},{1,5},{2,6},{3,7},{4,0},{5,1},{6,2},{7,3},{8,12},{9,13},{10,... | collective-permute-start | bytes 393224 | tf_op jit(solution)/shard_map/ppermute | solution.py:145
  25.7 18.6 %copy-start.2 = (f32[2,256]{1,0:T(2,128)S(1)}, f32[2,256]{1,0:T(2,128)}, u32[]{:S(2)}) copy-start(f32[2,256]{1,0:T(2,128)} %param.14) | copy-start | bytes 6148
  25.7 18.6 %copy-start.3 = (f32[2,256]{1,0:T(2,128)S(1)}, f32[2,256]{1,0:T(2,128)}, u32[]{:S(2)}) copy-start(f32[2,256]{1,0:T(2,128)} %param.15) | copy-start | bytes 6148
  25.7 18.8 %copy-start = (f32[2,1,128,128]{3,2,1,0:T(8,128)S(1)}, f32[2,1,128,128]{3,2,1,0:T(8,128)}, u32[]{:S(2)}) copy-start(f32[2,1,128,128]{3,2,1,0:T(8,128)} %param.12) | copy-start | bytes 393220
  46.3 1.1 %copy-start.1 = (f32[2,16,256]{2,1,0:T(8,128)S(1)}, f32[2,16,256]{2,1,0:T(8,128)}, u32[]{:S(2)}) copy-start(f32[2,16,256]{2,1,0:T(8,128)} %get-tuple-element.8) | copy-start | bytes 98308
  46.8 28.0 %copy-start.4 = (f32[2,1,128]{2,1,0:T(1,128)S(1)}, f32[2,1,128]{2,1,0:T(1,128)}, u32[]{:S(2)}) copy-start(f32[2,1,128]{2,1,0:T(1,128)} %param.13) | copy-start | bytes 3076
  47.5 3.3 %collective-permute-start.8 = (f32[3,2,16,256]{3,2,1,0:T(8,128)S(1)}, f32[3,2,16,256]{3,2,1,0:T(8,128)S(1)}, u32[]{:S(2)}, u32[]{:S(2)}) collective-permute-start(f32[3,2,16,256]{3,2,1,0:T(8,128)S(1)} %pad_maximum_fusion.2), channel_id=1, source_target_pairs={{0,8},{8,0},{16,24},{24,16},{32,40},{40,32},{48,56},{56,48},{64,72... | collective-permute-start | bytes 294920 | tf_op jit(solution)/shard_map/ppermute | solution.py:145
  50.8 12.7 %collective-permute-start.10 = (f32[3,2,16,256]{3,2,1,0:T(8,128)S(1)}, f32[3,2,16,256]{3,2,1,0:T(8,128)S(1)}, u32[]{:S(2)}, u32[]{:S(2)}) collective-permute-start(f32[3,2,16,256]{3,2,1,0:T(8,128)S(1)} %pad_maximum_fusion.3), channel_id=1, source_target_pairs={{0,48},{8,56},{16,0},{24,8},{32,16},{40,24},{48,32},{56,40},{64,11... | collective-permute-start | bytes 294920 | tf_op jit(solution)/shard_map/ppermute | solution.py:145
  57.3 11.0 %collective-permute-start.11 = (f32[3,2,16,256]{3,2,1,0:T(8,128)S(1)}, f32[3,2,16,256]{3,2,1,0:T(8,128)S(1)}, u32[]{:S(2)}, u32[]{:S(2)}) collective-permute-start(f32[3,2,16,256]{3,2,1,0:T(8,128)S(1)} %pad_maximum_fusion.3), channel_id=1, source_target_pairs={{0,32},{8,40},{16,48},{24,56},{32,0},{40,8},{48,16},{56,24},{64,96... | collective-permute-start | bytes 294920 | tf_op jit(solution)/shard_map/ppermute | solution.py:145
  58.8 10.8 %collective-permute-start.9 = (f32[3,2,16,256]{3,2,1,0:T(8,128)S(1)}, f32[3,2,16,256]{3,2,1,0:T(8,128)S(1)}, u32[]{:S(2)}, u32[]{:S(2)}) collective-permute-start(f32[3,2,16,256]{3,2,1,0:T(8,128)S(1)} %pad_maximum_fusion.3), channel_id=1, source_target_pairs={{0,16},{8,24},{16,32},{24,40},{32,48},{40,56},{48,0},{56,8},{64,80... | collective-permute-start | bytes 294920 | tf_op jit(solution)/shard_map/ppermute | solution.py:145
  69.7 6.9 %collective-permute-start.12 = (f32[3,2,16,256]{3,2,1,0:T(8,128)S(1)}, f32[3,2,16,256]{3,2,1,0:T(8,128)S(1)}, u32[]{:S(2)}, u32[]{:S(2)}) collective-permute-start(f32[3,2,16,256]{3,2,1,0:T(8,128)S(1)} %pad_maximum_fusion.4), channel_id=1, source_target_pairs={{0,64},{8,72},{16,80},{24,88},{32,96},{40,104},{48,112},{56,120},{... | collective-permute-start | bytes 294920 | tf_op jit(solution)/shard_map/ppermute | solution.py:145
  71.2 5.4 %collective-permute-start.13 = (f32[3,2,16,256]{3,2,1,0:T(8,128)S(1)}, f32[3,2,16,256]{3,2,1,0:T(8,128)S(1)}, u32[]{:S(2)}, u32[]{:S(2)}) collective-permute-start(f32[3,2,16,256]{3,2,1,0:T(8,128)S(1)} %pad_maximum_fusion.4), channel_id=1, source_target_pairs={{0,192},{8,200},{16,208},{24,216},{32,224},{40,232},{48,240},{56,2... | collective-permute-start | bytes 294920 | tf_op jit(solution)/shard_map/ppermute | solution.py:145
  73.0 6.1 %collective-permute-start.14 = (f32[3,2,16,256]{3,2,1,0:T(8,128)S(1)}, f32[3,2,16,256]{3,2,1,0:T(8,128)S(1)}, u32[]{:S(2)}, u32[]{:S(2)}) collective-permute-start(f32[3,2,16,256]{3,2,1,0:T(8,128)S(1)} %pad_maximum_fusion.4), channel_id=1, source_target_pairs={{0,128},{8,136},{16,144},{24,152},{32,160},{40,168},{48,176},{56,1... | collective-permute-start | bytes 294920 | tf_op jit(solution)/shard_map/ppermute | solution.py:145

commit v10 on v9

--- a/solution.py
+++ b/solution.py
@@ -234,14 +234,26 @@
     outlet_planes = jnp.broadcast_to(scalars[:, -1:], edge_shape)
     head_planes = jnp.where(at_inlet, jnp.zeros(edge_shape, scalars.dtype), head_planes)
     tail_planes = jnp.where(stream_rank == stream_devices - 1, outlet_planes, tail_planes)
+    h0, h1 = head_planes[:, 0], head_planes[:, 1]
+    t0, t1 = tail_planes[:, 0], tail_planes[:, 1]
+    stream_terms = (
+        diffusivity[0] * (16.0 * h1 - h0) * (1.0 / 12.0),
+        diffusivity[1] * -h1 * (1.0 / 12.0),
+        diffusivity[plane_count - 2] * -t0 * (1.0 / 12.0),
+        diffusivity[plane_count - 1] * (16.0 * t0 - t1) * (1.0 / 12.0),
+    )
+    stream_planes = (0, 1, plane_count - 2, plane_count - 1)
+    no_planes = jnp.zeros(edge_shape, scalars.dtype)
     before_rows, after_rows = halos(scalars, "gz", 2, 2, True)
     inverse = block_inverse[:, 0]
     response = block_response[:, 0]
     first_gain = jnp.where(at_inlet, diffusivity[0] * (15.0 / 12.0), 0.0)
     second_gain = jnp.where(at_inlet, diffusivity[1] * (-1.0 / 12.0), 0.0)
     local_part, exit_plane = explicit_local(
-        scalars, head_planes, tail_planes, diffusivity, reaction_rate, inverse
-    )
+        scalars, no_planes, no_planes, diffusivity, reaction_rate, inverse
+    )
+    for plane, term in zip(stream_planes, stream_terms):
+        exit_plane = exit_plane + inverse[:, -1, plane][:, None, None] * term
     b0, b1 = before_rows[:, :, 0], before_rows[:, :, 1]
     a0, a1 = after_rows[:, :, 0], after_rows[:, :, 1]
     edge_terms = jnp.stack(
@@ -268,14 +280,16 @@
         (exit_gain, exit_plane), candidate, "gx", digit_levels(stream_devices, (2, 4, 4))
     )
     incoming = through * inflow + upstream_sum
-    first_in = first_gain * inflow
-    second_in = second_gain * inflow
+    first_in = first_gain * inflow + stream_terms[0]
+    second_in = second_gain * inflow + stream_terms[1]
     return (
         local_part
         + edge_part
         + response[:, :, None, None] * incoming[:, None]
         + inverse[:, :, 0][:, :, None, None] * first_in[:, None]
         + inverse[:, :, 1][:, :, None, None] * second_in[:, None]
+        + inverse[:, :, plane_count - 2][:, :, None, None] * stream_terms[2][:, None]
+        + inverse[:, :, plane_count - 1][:, :, None, None] * stream_terms[3][:, None]
     )
 
 

time: 87.4 us -> 98.4 us (1.13)
  waiting for transfers between devices: 13.2 us -> 22.3 us
    ppermute x11, waiting for transfers between devices: 13.2 us -> 21.8 us  [digit_exchange(): received[shift] = lax.ppermute(x, axis, pairs)]
    slice x2 -> x0, local copies, waits for them, and re-layouts: 1.81 us -> none  [the longest x1 0.93 us: on_device(): inverse[:, -1, 0][:, None, None] * first_gain]
    mul x0 -> x2, local copies, waits for them, and re-layouts: none -> 1.73 us  [the longest x1 0.86 us: on_device(): inverse[:, :, plane_count - 2][:, :, None, None] * stream_terms[2][:, None]]
    slice x0 -> x1, other arithmetic: none -> 1.01 us  [on_device(): inverse[:, -1, 0][:, None, None] * first_gain]
    slice x1 -> x2, local copies, waits for them, and re-layouts: 2.59 us -> 3.47 us  [halos(): last = lax.slice_in_dim(x, length - width, length, axis=dim)]
  transfers between devices with their start and end apart: 15 -> 15, of which waited for: 5 -> 8; matrix products, arithmetic and copies ran while one was open for 14% -> 13% of each run, Pallas kernels for 21% -> 19%
where the time goes in v10:
time: 98.4 us; the launch traced here: 98 us
  starting transfers between devices  30.1 us (31%)
  waiting for transfers between devices  22.3 us (23%)
  Pallas kernels  18.5 us (19%)
  local copies, waits for them, and re-layouts  15.2 us (15%)
  other arithmetic  9.02 us (9%)
  between operations  1.79 us (2%)
  matrix products  1.06 us (1%)
    ppermute x11, starting transfers between devices, digit_exchange(): received[shift] = lax.ppermute(x, axis, pairs)  22.1 us
    ppermute x11, waiting for transfers between devices, digit_exchange(): received[shift] = lax.ppermute(x, axis, pairs)  21.8 us
    pallas_call x1, Pallas kernels, explicit_local(): pl.pallas_call(functools.partial(explicit_kernel, planes, rows, width), o...  18.5 us
    ppermute x4, starting transfers between devices, halos(): return (lax.ppermute(last, axis, up), lax.ppermute(first, axis, down))  8.04 us
    add x1, other arithmetic, on_device(): local_part + edge_part + response[:, :, None, None] * incoming[:, None]  5.84 us
    slice x2, local copies, waits for them, and re-layouts, halos(): last = lax.slice_in_dim(x, length - width, length, axis=dim)  3.47 us
    slice x1, local copies, waits for them, and re-layouts, on_device(): diffusivity[:, 0] * (16.0 * b1 - b0) * (1.0 / 12.0)  2.58 us
    add x1, local copies, waits for them, and re-layouts, on_device(): local_part + edge_part + response[:, :, None, None] * incoming[:, None]  2.55 us
  transfers between devices with their start and end apart: 15, of which 8 were waited for; matrix products, arithmetic and copies ran while one was open for 13% of the time, Pallas kernels for 19%

profile of v10, /device:TPU:32, one launch (start us, length us, event | category | flops | bytes accessed | tf_op | source)
XLA Modules:
  0.0 98.0 jit_solution(5683988911983509036)
XLA Ops:
  0.7 0.8 dynamic-slice_bitcast_fusion
  1.5 2.8 %collective-permute-start.4 = (f32[2,16,256]{2,1,0:T(8,128)S(1)}, f32[2,16,256]{2,1,0:T(8,128)S(1)}, u32[]{:S(2)}, u32[]{:S(2)}) collective-permute-start(f32[2,16,256]{2,1,0:T(8,128)S(1)} %get-tuple-element.23), channel_id=1, source_target_pairs={{0,3},{1,0},{2,1},{3,2},{4,7},{5,4},{6,5},{7,6},{8,11},{9,8},{10,9... | collective-permute-start | bytes 98312 | tf_op jit(solution)/shard_map/ppermute | solution.py:145
  4.2 0.8 collective-permute-start.5
  5.0 0.9 collective-permute-start.6
  5.9 0.9 fusion.59
  6.8 1.3 %collective-permute-start.3 = (f32[2,2,16,256]{3,2,0,1:T(8,128)S(1)}, f32[2,2,16,256]{3,2,0,1:T(8,128)S(1)}, u32[]{:S(2)}, u32[]{:S(2)}) collective-permute-start(f32[2,2,16,256]{3,2,0,1:T(8,128)S(1)} %copy.59), channel_id=1, source_target_pairs={{8,0},{16,8},{24,16},{32,24},{40,32},{48,40},{56,48},{64,56},{72,6... | collective-permute-start | bytes 196616 | tf_op jit(solution)/shard_map/ppermute | solution.py:198
  8.1 2.6 %fusion.60 = (f32[2,128,2,256]{3,2,1,0:T(2,128)S(1)}, f32[2,128,2,256]{3,2,1,0:T(2,128)S(1)}) fusion(f32[2,128,16,256]{3,2,1,0:T(8,128)} %param.9), kind=kLoop, calls=%fused_computation.159 | loop fusion | bytes 2097152 | tf_op jit(solution)/shard_map/slice | solution.py:196
  10.8 1.9 %collective-permute-start = (f32[2,128,2,256]{3,1,0,2:T(8,128)S(1)}, f32[2,128,2,256]{3,1,0,2:T(8,128)S(1)}, u32[]{:S(2)}, u32[]{:S(2)}) collective-permute-start(f32[2,128,2,256]{3,1,0,2:T(8,128)S(1)} %copy.53), channel_id=1, source_target_pairs={{0,1},{1,2},{2,3},{3,4},{4,5},{5,6},{6,7},{7,0},{8,9},{9,10},{10,1... | collective-permute-start | bytes 1572872 | tf_op jit(solution)/shard_map/ppermute | solution.py:198
  12.6 2.6 %fusion.61 = (f32[128,1,256]{2,1,0:T(1,128)S(1)}, f32[128,1,256]{2,1,0:T(1,128)S(1)}, f32[128,1,256]{2,1,0:T(1,128)S(1)}, f32[128,1,256]{2,1,0:T(1,128)S(1)}) fusion(f32[128,16,256]{2,1,0:T(8,128)} %param.10), kind=kLoop, calls=%fused_computation.160 | loop fusion | bytes 1048576 | tf_op jit(solution)/shard_map/slice | solution.py:261
  16.0 1.0 %slice_reduce_fusion.1 = (f32[2]{0:T(128)S(1)}, f32[2]{0:T(128)S(1)}, f32[2]{0:T(128)S(1)}, f32[2]{0:T(128)S(1)}) fusion(f32[2,128,128]{2,1,0:T(8,128)} %bitcast.255), kind=kLoop, calls=%fused_computation.149 | loop fusion | flops 4 | bytes 64 | tf_op jit(solution)/shard_map/slice | solution.py:276
  18.8 18.5 %shard_map.91 = (f32[2,2048,256]{2,1,0:T(8,128)}, f32[2,16,256]{2,1,0:T(8,128)}) custom-call(f32[2,2048,256]{2,1,0:T(8,128)} %bitcast.254, f32[2,32,256]{2,1,0:T(8,128)} %broadcast_10_head_ref_tail_ref.2.head_ref.tail_ref, f32[2,32,256]{2,1,0:T(8,128)} %broadcast_10_head_ref_tail_ref.2.head_ref.tail_ref, f32[2048,256]{1,0:T(8,128)} %bitcast.260, ...), custom_call_target="tpu_custom_call" | custom-call | flops 331350016 | bytes 16777216 | tf_op jit(solution)/shard_map/pallas_call | solution.py:104
  37.3 2.4 %collective-permute-start.1 = (f32[2,128,2,256]{3,1,0,2:T(8,128)S(1)}, f32[2,128,2,256]{3,1,0,2:T(8,128)S(1)}, u32[]{:S(2)}, u32[]{:S(2)}) collective-permute-start(f32[2,128,2,256]{3,1,0,2:T(8,128)S(1)} %copy.56), channel_id=1, source_target_pairs={{1,0},{2,1},{3,2},{4,3},{5,4},{6,5},{7,6},{0,7},{9,8},{10,9},{11,1... | collective-permute-start | bytes 1572872 | tf_op jit(solution)/shard_map/ppermute | solution.py:198
  39.7 2.5 %collective-permute-start.2 = (f32[2,2,16,256]{3,2,0,1:T(8,128)S(1)}, f32[2,2,16,256]{3,2,0,1:T(8,128)S(1)}, u32[]{:S(2)}, u32[]{:S(2)}) collective-permute-start(f32[2,2,16,256]{3,2,0,1:T(8,128)S(1)} %copy.58), channel_id=1, source_target_pairs={{0,8},{8,16},{16,24},{24,32},{32,40},{40,48},{48,56},{56,64},{64,7... | collective-permute-start | bytes 196616 | tf_op jit(solution)/shard_map/ppermute | solution.py:198
  43.1 13.1 %collective-permute-done.7 = f32[2,64,256]{2,1,0:T(8,128)S(1)} collective-permute-done((f32[2,64,256]{2,1,0:T(8,128)S(1)}, f32[2,64,256]{2,1,0:T(8,128)S(1)}, u32[]{:S(2)}, u32[]{:S(2)}) %collective-permute-start.7) | collective-permute-done | bytes 131104 | tf_op jit(solution)/shard_map/ppermute | solution.py:145
  56.5 1.1 %fusion.5 = f32[2,4,256,128]{2,3,1,0:T(8,128)S(1)} fusion(f32[2,1,128,256]{3,2,1,0:T(8,128)S(1)} %get-tuple-element.40, f32[2,1,128,256]{3,2,1,0:T(8,128)S(1)} %get-tuple-element.39, f32[2,1,128,256]{3,2,1,0:T(8,128)S(1)} %get-tuple-element.38, f32[2,1,128,256]{3,2,1,0:T(8,128)S(1)} %get-tuple-element.37, f32[2,1,128,128]{3,2,1,0:T(8,128)S(1)} %copy-done), kind=kOutput, calls=%fused_computation.7 | convolution fusion | flops 403439616 | bytes 2228224 | tf_op jit(solution)/shard_map/sij,skjy->siky/dot_general | solution.py:268
  59.9 0.9 collective-permute-done.8
  60.9 6.9 %collective-permute-start.10 = (f32[3,2,16,256]{3,2,1,0:T(8,128)S(1)}, f32[3,2,16,256]{3,2,1,0:T(8,128)S(1)}, u32[]{:S(2)}, u32[]{:S(2)}) collective-permute-start(f32[3,2,16,256]{3,2,1,0:T(8,128)S(1)} %pad_maximum_fusion.3), channel_id=1, source_target_pairs={{0,48},{8,56},{16,0},{24,8},{32,16},{40,24},{48,32},{56,40},{64,11... | collective-permute-start | bytes 294920 | tf_op jit(solution)/shard_map/ppermute | solution.py:145
  67.8 1.0 collective-permute-start.11
  68.8 2.8 %collective-permute-start.9 = (f32[3,2,16,256]{3,2,1,0:T(8,128)S(1)}, f32[3,2,16,256]{3,2,1,0:T(8,128)S(1)}, u32[]{:S(2)}, u32[]{:S(2)}) collective-permute-start(f32[3,2,16,256]{3,2,1,0:T(8,128)S(1)} %pad_maximum_fusion.3), channel_id=1, source_target_pairs={{0,16},{8,24},{16,32},{24,40},{32,48},{40,56},{48,0},{56,8},{64,80... | collective-permute-start | bytes 294920 | tf_op jit(solution)/shard_map/ppermute | solution.py:145
  71.9 0.9 copy.48
  72.8 0.9 copy.49
  73.7 0.9 copy.50
  74.5 0.9 copy.51
  75.4 1.1 %collective-permute-done.11 = f32[3,2,16,256]{3,2,1,0:T(8,128)S(1)} collective-permute-done((f32[3,2,16,256]{3,2,1,0:T(8,128)S(1)}, f32[3,2,16,256]{3,2,1,0:T(8,128)S(1)}, u32[]{:S(2)}, u32[]{:S(2)}) %collective-permute-start.11) | collective-permute-done | bytes 98336 | tf_op jit(solution)/shard_map/ppermute | solution.py:145
  76.5 2.4 %collective-permute-done.9 = f32[3,2,16,256]{3,2,1,0:T(8,128)S(1)} collective-permute-done((f32[3,2,16,256]{3,2,1,0:T(8,128)S(1)}, f32[3,2,16,256]{3,2,1,0:T(8,128)S(1)}, u32[]{:S(2)}, u32[]{:S(2)}) %collective-permute-start.9) | collective-permute-done | bytes 98336 | tf_op jit(solution)/shard_map/ppermute | solution.py:145
  79.0 2.5 %collective-permute-start.12 = (f32[3,2,16,256]{3,2,1,0:T(8,128)S(1)}, f32[3,2,16,256]{3,2,1,0:T(8,128)S(1)}, u32[]{:S(2)}, u32[]{:S(2)}) collective-permute-start(f32[3,2,16,256]{3,2,1,0:T(8,128)S(1)} %pad_maximum_fusion.4), channel_id=1, source_target_pairs={{0,64},{8,72},{16,80},{24,88},{32,96},{40,104},{48,112},{56,120},{... | collective-permute-start | bytes 294920 | tf_op jit(solution)/shard_map/ppermute | solution.py:145
  81.5 1.8 %collective-permute-start.13 = (f32[3,2,16,256]{3,2,1,0:T(8,128)S(1)}, f32[3,2,16,256]{3,2,1,0:T(8,128)S(1)}, u32[]{:S(2)}, u32[]{:S(2)}) collective-permute-start(f32[3,2,16,256]{3,2,1,0:T(8,128)S(1)} %pad_maximum_fusion.4), channel_id=1, source_target_pairs={{0,192},{8,200},{16,208},{24,216},{32,224},{40,232},{48,240},{56,2... | collective-permute-start | bytes 294920 | tf_op jit(solution)/shard_map/ppermute | solution.py:145
  83.2 1.8 %collective-permute-start.14 = (f32[3,2,16,256]{3,2,1,0:T(8,128)S(1)}, f32[3,2,16,256]{3,2,1,0:T(8,128)S(1)}, u32[]{:S(2)}, u32[]{:S(2)}) collective-permute-start(f32[3,2,16,256]{3,2,1,0:T(8,128)S(1)} %pad_maximum_fusion.4), channel_id=1, source_target_pairs={{0,128},{8,136},{16,144},{24,152},{32,160},{40,168},{48,176},{56,1... | collective-permute-start | bytes 294920 | tf_op jit(solution)/shard_map/ppermute | solution.py:145
  85.1 1.0 %collective-permute-done.12 = f32[3,2,16,256]{3,2,1,0:T(8,128)S(1)} collective-permute-done((f32[3,2,16,256]{3,2,1,0:T(8,128)S(1)}, f32[3,2,16,256]{3,2,1,0:T(8,128)S(1)}, u32[]{:S(2)}, u32[]{:S(2)}) %collective-permute-start.12) | collective-permute-done | bytes 98336 | tf_op jit(solution)/shard_map/ppermute | solution.py:145
  86.6 2.8 %collective-permute-done.14 = f32[3,2,16,256]{3,2,1,0:T(8,128)S(1)} collective-permute-done((f32[3,2,16,256]{3,2,1,0:T(8,128)S(1)}, f32[3,2,16,256]{3,2,1,0:T(8,128)S(1)}, u32[]{:S(2)}, u32[]{:S(2)}) %collective-permute-start.14) | collective-permute-done | bytes 98336 | tf_op jit(solution)/shard_map/ppermute | solution.py:145
  89.6 5.8 %fusion.4 = f32[2,128,16,256]{3,2,0,1:T(8,128)S(1)} fusion(f32[2,128,16,256]{3,2,1,0:T(8,128)} %bitcast.258, f32[2,16,256]{2,1,0:T(8,128)S(1)} %get-tuple-element.69, f32[2,128]{0,1:T(8,128)S(1)} %bitcast.265, f32[2,16,256]{2,1,0:T(8,128)S(1)} %get-tuple-element.68, f32[2,128]{0,1:T(8,128)S(1)} %bitcast.264, f32[2,16,256]{2,1,0:T(8,128)S(1)} %get-tuple-element.67, ...), kind=kLoop, calls=%fused_computation.6 | loop fusion | flops 13631488 | bytes 9606208 | tf_op jit(solution)/shard_map/add | solution.py:286
  95.4 2.6 %copy.46 = f32[2,128,16,256]{3,2,1,0:T(8,128)} copy(f32[2,128,16,256]{3,2,0,1:T(8,128)S(1)} %fusion.4) | data formatting | bytes 8388608 | tf_op jit(solution)/shard_map/add | solution.py:286
  (60 shorter events, 6.3 us)
Async XLA Ops:
  0.0 17.7 %copy-start.4 = (f32[2,1,128]{2,1,0:T(1,128)S(1)}, f32[2,1,128]{2,1,0:T(1,128)}, u32[]{:S(2)}) copy-start(f32[2,1,128]{2,1,0:T(1,128)} %param.13) | copy-start | bytes 3076
  1.5 35.8 %collective-permute-start.4 = (f32[2,16,256]{2,1,0:T(8,128)S(1)}, f32[2,16,256]{2,1,0:T(8,128)S(1)}, u32[]{:S(2)}, u32[]{:S(2)}) collective-permute-start(f32[2,16,256]{2,1,0:T(8,128)S(1)} %get-tuple-element.23), channel_id=1, source_target_pairs={{0,3},{1,0},{2,1},{3,2},{4,7},{5,4},{6,5},{7,6},{8,11},{9,8},{10,9... | collective-permute-start | bytes 98312 | tf_op jit(solution)/shard_map/ppermute | solution.py:145
  4.2 35.5 %collective-permute-start.5 = (f32[2,16,256]{2,1,0:T(8,128)S(1)}, f32[2,16,256]{2,1,0:T(8,128)S(1)}, u32[]{:S(2)}, u32[]{:S(2)}) collective-permute-start(f32[2,16,256]{2,1,0:T(8,128)S(1)} %get-tuple-element.23), channel_id=1, source_target_pairs={{0,2},{1,3},{2,0},{3,1},{4,6},{5,7},{6,4},{7,5},{8,10},{9,11},{10,... | collective-permute-start | bytes 98312 | tf_op jit(solution)/shard_map/ppermute | solution.py:145
  5.0 37.2 %collective-permute-start.6 = (f32[2,16,256]{2,1,0:T(8,128)S(1)}, f32[2,16,256]{2,1,0:T(8,128)S(1)}, u32[]{:S(2)}, u32[]{:S(2)}) collective-permute-start(f32[2,16,256]{2,1,0:T(8,128)S(1)} %get-tuple-element.23), channel_id=1, source_target_pairs={{0,1},{1,2},{2,3},{3,0},{4,5},{5,6},{6,7},{7,4},{8,9},{9,10},{10,1... | collective-permute-start | bytes 98312 | tf_op jit(solution)/shard_map/ppermute | solution.py:145
  6.8 35.8 %collective-permute-start.3 = (f32[2,2,16,256]{3,2,0,1:T(8,128)S(1)}, f32[2,2,16,256]{3,2,0,1:T(8,128)S(1)}, u32[]{:S(2)}, u32[]{:S(2)}) collective-permute-start(f32[2,2,16,256]{3,2,0,1:T(8,128)S(1)} %copy.59), channel_id=1, source_target_pairs={{8,0},{16,8},{24,16},{32,24},{40,32},{48,40},{56,48},{64,56},{72,6... | collective-permute-start | bytes 196616 | tf_op jit(solution)/shard_map/ppermute | solution.py:198
  10.8 45.5 %collective-permute-start = (f32[2,128,2,256]{3,1,0,2:T(8,128)S(1)}, f32[2,128,2,256]{3,1,0,2:T(8,128)S(1)}, u32[]{:S(2)}, u32[]{:S(2)}) collective-permute-start(f32[2,128,2,256]{3,1,0,2:T(8,128)S(1)} %copy.53), channel_id=1, source_target_pairs={{0,1},{1,2},{2,3},{3,4},{4,5},{5,6},{6,7},{7,0},{8,9},{9,10},{10,1... | collective-permute-start | bytes 1572872 | tf_op jit(solution)/shard_map/ppermute | solution.py:198
  18.8 37.4 %copy-start.2 = (f32[2,256]{1,0:T(2,128)S(1)}, f32[2,256]{1,0:T(2,128)}, u32[]{:S(2)}) copy-start(f32[2,256]{1,0:T(2,128)} %param.14) | copy-start | bytes 6148
  18.8 37.4 %copy-start.3 = (f32[2,256]{1,0:T(2,128)S(1)}, f32[2,256]{1,0:T(2,128)}, u32[]{:S(2)}) copy-start(f32[2,256]{1,0:T(2,128)} %param.15) | copy-start | bytes 6148
  37.3 19.1 %copy-start = (f32[2,1,128,128]{3,2,1,0:T(8,128)S(1)}, f32[2,1,128,128]{3,2,1,0:T(8,128)}, u32[]{:S(2)}) copy-start(f32[2,1,128,128]{3,2,1,0:T(8,128)} %param.12) | copy-start | bytes 393220
  37.3 19.0 %collective-permute-start.1 = (f32[2,128,2,256]{3,1,0,2:T(8,128)S(1)}, f32[2,128,2,256]{3,1,0,2:T(8,128)S(1)}, u32[]{:S(2)}, u32[]{:S(2)}) collective-permute-start(f32[2,128,2,256]{3,1,0,2:T(8,128)S(1)} %copy.56), channel_id=1, source_target_pairs={{1,0},{2,1},{3,2},{4,3},{5,4},{6,5},{7,6},{0,7},{9,8},{10,9},{11,1... | collective-permute-start | bytes 1572872 | tf_op jit(solution)/shard_map/ppermute | solution.py:198
  39.7 3.4 %collective-permute-start.2 = (f32[2,2,16,256]{3,2,0,1:T(8,128)S(1)}, f32[2,2,16,256]{3,2,0,1:T(8,128)S(1)}, u32[]{:S(2)}, u32[]{:S(2)}) collective-permute-start(f32[2,2,16,256]{3,2,0,1:T(8,128)S(1)} %copy.58), channel_id=1, source_target_pairs={{0,8},{8,16},{16,24},{24,32},{32,40},{40,48},{48,56},{56,64},{64,7... | collective-permute-start | bytes 196616 | tf_op jit(solution)/shard_map/ppermute | solution.py:198
  42.3 13.9 %collective-permute-start.7 = (f32[2,64,256]{2,1,0:T(8,128)S(1)}, f32[2,64,256]{2,1,0:T(8,128)S(1)}, u32[]{:S(2)}, u32[]{:S(2)}) collective-permute-start(f32[2,64,256]{2,1,0:T(8,128)S(1)} %pad_maximum_fusion.1), channel_id=1, source_target_pairs={{0,4},{1,5},{2,6},{3,7},{4,0},{5,1},{6,2},{7,3},{8,12},{9,13},{10,... | collective-permute-start | bytes 393224 | tf_op jit(solution)/shard_map/ppermute | solution.py:145
  58.2 1.1 %copy-start.1 = (f32[2,16,256]{2,1,0:T(8,128)S(1)}, f32[2,16,256]{2,1,0:T(8,128)}, u32[]{:S(2)}) copy-start(f32[2,16,256]{2,1,0:T(8,128)} %get-tuple-element.8) | copy-start | bytes 98308
  59.4 1.4 %collective-permute-start.8 = (f32[3,2,16,256]{3,2,1,0:T(8,128)S(1)}, f32[3,2,16,256]{3,2,1,0:T(8,128)S(1)}, u32[]{:S(2)}, u32[]{:S(2)}) collective-permute-start(f32[3,2,16,256]{3,2,1,0:T(8,128)S(1)} %pad_maximum_fusion.2), channel_id=1, source_target_pairs={{0,8},{8,0},{16,24},{24,16},{32,40},{40,32},{48,56},{56,48},{64,72... | collective-permute-start | bytes 294920 | tf_op jit(solution)/shard_map/ppermute | solution.py:145
  60.9 14.5 %collective-permute-start.10 = (f32[3,2,16,256]{3,2,1,0:T(8,128)S(1)}, f32[3,2,16,256]{3,2,1,0:T(8,128)S(1)}, u32[]{:S(2)}, u32[]{:S(2)}) collective-permute-start(f32[3,2,16,256]{3,2,1,0:T(8,128)S(1)} %pad_maximum_fusion.3), channel_id=1, source_target_pairs={{0,48},{8,56},{16,0},{24,8},{32,16},{40,24},{48,32},{56,40},{64,11... | collective-permute-start | bytes 294920 | tf_op jit(solution)/shard_map/ppermute | solution.py:145
  67.8 8.7 %collective-permute-start.11 = (f32[3,2,16,256]{3,2,1,0:T(8,128)S(1)}, f32[3,2,16,256]{3,2,1,0:T(8,128)S(1)}, u32[]{:S(2)}, u32[]{:S(2)}) collective-permute-start(f32[3,2,16,256]{3,2,1,0:T(8,128)S(1)} %pad_maximum_fusion.3), channel_id=1, source_target_pairs={{0,32},{8,40},{16,48},{24,56},{32,0},{40,8},{48,16},{56,24},{64,96... | collective-permute-start | bytes 294920 | tf_op jit(solution)/shard_map/ppermute | solution.py:145
  68.8 10.1 %collective-permute-start.9 = (f32[3,2,16,256]{3,2,1,0:T(8,128)S(1)}, f32[3,2,16,256]{3,2,1,0:T(8,128)S(1)}, u32[]{:S(2)}, u32[]{:S(2)}) collective-permute-start(f32[3,2,16,256]{3,2,1,0:T(8,128)S(1)} %pad_maximum_fusion.3), channel_id=1, source_target_pairs={{0,16},{8,24},{16,32},{24,40},{32,48},{40,56},{48,0},{56,8},{64,80... | collective-permute-start | bytes 294920 | tf_op jit(solution)/shard_map/ppermute | solution.py:145
  79.0 7.1 %collective-permute-start.12 = (f32[3,2,16,256]{3,2,1,0:T(8,128)S(1)}, f32[3,2,16,256]{3,2,1,0:T(8,128)S(1)}, u32[]{:S(2)}, u32[]{:S(2)}) collective-permute-start(f32[3,2,16,256]{3,2,1,0:T(8,128)S(1)} %pad_maximum_fusion.4), channel_id=1, source_target_pairs={{0,64},{8,72},{16,80},{24,88},{32,96},{40,104},{48,112},{56,120},{... | collective-permute-start | bytes 294920 | tf_op jit(solution)/shard_map/ppermute | solution.py:145
  81.5 5.1 %collective-permute-start.13 = (f32[3,2,16,256]{3,2,1,0:T(8,128)S(1)}, f32[3,2,16,256]{3,2,1,0:T(8,128)S(1)}, u32[]{:S(2)}, u32[]{:S(2)}) collective-permute-start(f32[3,2,16,256]{3,2,1,0:T(8,128)S(1)} %pad_maximum_fusion.4), channel_id=1, source_target_pairs={{0,192},{8,200},{16,208},{24,216},{32,224},{40,232},{48,240},{56,2... | collective-permute-start | bytes 294920 | tf_op jit(solution)/shard_map/ppermute | solution.py:145
  83.2 6.2 %collective-permute-start.14 = (f32[3,2,16,256]{3,2,1,0:T(8,128)S(1)}, f32[3,2,16,256]{3,2,1,0:T(8,128)S(1)}, u32[]{:S(2)}, u32[]{:S(2)}) collective-permute-start(f32[3,2,16,256]{3,2,1,0:T(8,128)S(1)} %pad_maximum_fusion.4), channel_id=1, source_target_pairs={{0,128},{8,136},{16,144},{24,152},{32,160},{40,168},{48,176},{56,1... | collective-permute-start | bytes 294920 | tf_op jit(solution)/shard_map/ppermute | solution.py:145

commit v11 on v9

--- a/solution.py
+++ b/solution.py
@@ -66,7 +66,7 @@
         one_plane(j, j - 2, j - 1, j + 1, j + 2)
         return carry
 
-    lax.fori_loop(2, planes - 2, body, 0, unroll=4)
+    lax.fori_loop(2, planes - 2, body, 0, unroll=8)
     for j in (planes - 2, planes - 1):
         one_plane(j, j - 2, j - 1, j + 1, j + 2)
 
@@ -253,12 +253,16 @@
         ],
         axis=1,
     )
+    exit_edge = jnp.einsum(
+        "sj,skjy->sky", inverse[:, -1], edge_terms, precision=lax.Precision.HIGHEST
+    )
+    gap = jnp.zeros(exit_edge.shape[:1] + (span_cells - 4,) + exit_edge.shape[2:], exit_edge.dtype)
+    exit_plane = exit_plane + jnp.concatenate([exit_edge[:, :2], gap, exit_edge[:, 2:]], axis=1)
     edge_part = jnp.einsum(
         "sij,skjy->siky", inverse, edge_terms, precision=lax.Precision.HIGHEST
     )
     gap = jnp.zeros(edge_part.shape[:2] + (span_cells - 4,) + edge_part.shape[3:], edge_part.dtype)
     edge_part = jnp.concatenate([edge_part[:, :, :2], gap, edge_part[:, :, 2:]], axis=2)
-    exit_plane = exit_plane + edge_part[:, -1]
     exit_gain = (
         response[:, -1][:, None, None]
         + inverse[:, -1, 0][:, None, None] * first_gain

time: 87.4 us -> 85 us (0.973)
  local copies, waits for them, and re-layouts: 14.4 us -> 10.3 us
  waiting for transfers between devices: 13.2 us -> 11.8 us
  other arithmetic: 8.41 us -> 9.43 us
  matrix products: 1.06 us -> 2 us
    ppermute x11, starting transfers between devices: 21.1 us -> 23.7 us  [digit_exchange(): received[shift] = lax.ppermute(x, axis, pairs)]
    add x1 -> x0, local copies, waits for them, and re-layouts: 2.55 us -> none  [on_device(): local_part + edge_part + response[:, :, None, None] * incoming[:, None]]
    ppermute x4, starting transfers between devices: 8.5 us -> 6.36 us  [halos(): return (lax.ppermute(last, axis, up), lax.ppermute(first, axis, down))]
    mul x3 -> x2, local copies, waits for them, and re-layouts: 1.84 us -> 0.2 us  [the longest x1 0.1 us: on_device(): diffusivity[:, span_cells - 2] * -a0 * (1.0 / 12.0)]
    add x1, other arithmetic: 5.15 us -> 6.79 us  [on_device(): local_part + edge_part + response[:, :, None, None] * incoming[:, None]]
    ppermute x11, waiting for transfers between devices: 13.2 us -> 11.7 us  [digit_exchange(): received[shift] = lax.ppermute(x, axis, pairs)]
    dot_general x0 -> x1, matrix products: none -> 0.98 us  [on_device(): jnp.einsum('sj,skjy->sky', inverse[:, -1], edge_terms, precision=lax.Prec...]
  transfers between devices with their start and end apart: 15 -> 15, of which waited for: 5 -> 6; matrix products, arithmetic and copies ran while one was open for 14% -> 15% of each run, Pallas kernels for 21% -> 22%
where the time goes in v11:
time: 85 us; the launch traced here: 83.7 us
  starting transfers between devices  30.1 us (35%)
  Pallas kernels  18.4 us (22%)
  waiting for transfers between devices  11.8 us (14%)
  local copies, waits for them, and re-layouts  10.3 us (12%)
  other arithmetic  9.43 us (11%)
  matrix products  2 us (2%)
  between operations  1.77 us (2%)
    ppermute x11, starting transfers between devices, digit_exchange(): received[shift] = lax.ppermute(x, axis, pairs)  23.7 us
    pallas_call x1, Pallas kernels, explicit_local(): pl.pallas_call(functools.partial(explicit_kernel, planes, rows, width), o...  18.4 us
    ppermute x11, waiting for transfers between devices, digit_exchange(): received[shift] = lax.ppermute(x, axis, pairs)  11.7 us
    add x1, other arithmetic, on_device(): local_part + edge_part + response[:, :, None, None] * incoming[:, None]  6.79 us
    ppermute x4, starting transfers between devices, halos(): return (lax.ppermute(last, axis, up), lax.ppermute(first, axis, down))  6.36 us
    slice x1, local copies, waits for them, and re-layouts, on_device(): diffusivity[:, 0] * (16.0 * b1 - b0) * (1.0 / 12.0)  2.59 us
    slice x1, local copies, waits for them, and re-layouts, halos(): last = lax.slice_in_dim(x, length - width, length, axis=dim)  2.59 us
  transfers between devices with their start and end apart: 15, of which 6 were waited for; matrix products, arithmetic and copies ran while one was open for 15% of the time, Pallas kernels for 22%

profile of v11, /device:TPU:32, one launch (start us, length us, event | category | flops | bytes accessed | tf_op | source)
XLA Modules:
  0.0 83.7 jit_solution(6234161301425535000)
XLA Ops:
  0.7 0.8 dynamic-slice_bitcast_fusion
  1.5 1.5 %collective-permute-start.6 = (f32[2,16,256]{2,1,0:T(8,128)S(1)}, f32[2,16,256]{2,1,0:T(8,128)S(1)}, u32[]{:S(2)}, u32[]{:S(2)}) collective-permute-start(f32[2,16,256]{2,1,0:T(8,128)S(1)} %get-tuple-element.19), channel_id=1, source_target_pairs={{0,1},{1,2},{2,3},{3,0},{4,5},{5,6},{6,7},{7,4},{8,9},{9,10},{10,1... | collective-permute-start | bytes 98312 | tf_op jit(solution)/shard_map/ppermute | solution.py:145
  3.0 2.7 %collective-permute-start.5 = (f32[2,16,256]{2,1,0:T(8,128)S(1)}, f32[2,16,256]{2,1,0:T(8,128)S(1)}, u32[]{:S(2)}, u32[]{:S(2)}) collective-permute-start(f32[2,16,256]{2,1,0:T(8,128)S(1)} %get-tuple-element.19), channel_id=1, source_target_pairs={{0,2},{1,3},{2,0},{3,1},{4,6},{5,7},{6,4},{7,5},{8,10},{9,11},{10,... | collective-permute-start | bytes 98312 | tf_op jit(solution)/shard_map/ppermute | solution.py:145
  5.7 1.4 %collective-permute-start.4 = (f32[2,16,256]{2,1,0:T(8,128)S(1)}, f32[2,16,256]{2,1,0:T(8,128)S(1)}, u32[]{:S(2)}, u32[]{:S(2)}) collective-permute-start(f32[2,16,256]{2,1,0:T(8,128)S(1)} %get-tuple-element.19), channel_id=1, source_target_pairs={{0,3},{1,0},{2,1},{3,2},{4,7},{5,4},{6,5},{7,6},{8,11},{9,8},{10,9... | collective-permute-start | bytes 98312 | tf_op jit(solution)/shard_map/ppermute | solution.py:145
  7.1 0.9 %fusion.38 = (f32[2,2,16,256]{3,2,1,0:T(8,128)S(1)}, f32[2,2,16,256]{3,2,1,0:T(8,128)S(1)}) fusion(f32[2,128,16,256]{3,2,1,0:T(8,128)} %param.9), kind=kLoop, calls=%fused_computation.118 | loop fusion | bytes 262144 | tf_op jit(solution)/shard_map/slice | solution.py:197
  8.0 1.3 %collective-permute-start.1 = (f32[2,2,16,256]{3,2,1,0:T(8,128)S(1)}, f32[2,2,16,256]{3,2,1,0:T(8,128)S(1)}, u32[]{:S(2)}, u32[]{:S(2)}) collective-permute-start(f32[2,2,16,256]{3,2,1,0:T(8,128)S(1)} %get-tuple-element.23), channel_id=1, source_target_pairs={{8,0},{16,8},{24,16},{32,24},{40,32},{48,40},{56,48},{64,56},{72,6... | collective-permute-start | bytes 196616 | tf_op jit(solution)/shard_map/ppermute | solution.py:198
  9.3 3.0 %collective-permute-start = (f32[2,2,16,256]{3,2,1,0:T(8,128)S(1)}, f32[2,2,16,256]{3,2,1,0:T(8,128)S(1)}, u32[]{:S(2)}, u32[]{:S(2)}) collective-permute-start(f32[2,2,16,256]{3,2,1,0:T(8,128)S(1)} %get-tuple-element.24), channel_id=1, source_target_pairs={{0,8},{8,16},{16,24},{24,32},{32,40},{40,48},{48,56},{56,64},{64,7... | collective-permute-start | bytes 196616 | tf_op jit(solution)/shard_map/ppermute | solution.py:198
  12.4 2.6 %fusion.37 = (f32[2,128,2,256]{3,2,1,0:T(2,128)S(1)}, f32[2,128,2,256]{3,2,1,0:T(2,128)S(1)}) fusion(f32[2,128,16,256]{3,2,1,0:T(8,128)} %param.9), kind=kLoop, calls=%fused_computation.117 | loop fusion | bytes 2097152 | tf_op jit(solution)/shard_map/slice | solution.py:196
  15.0 0.9 %slice_reduce_fusion.4 = f32[2]{0:T(128)S(1)} fusion(f32[2,128]{1,0:T(2,128)} %bitcast.210), kind=kLoop, calls=%fused_computation.112 | loop fusion | bytes 16 | tf_op jit(solution)/shard_map/slice | solution.py:267
  15.8 0.9 %slice_reduce_fusion.3 = (f32[2]{0:T(128)S(1)}, f32[2]{0:T(128)S(1)}) fusion(f32[2,128,128]{2,1,0:T(8,128)} %bitcast.198), kind=kLoop, calls=%fused_computation.111 | loop fusion | bytes 32 | tf_op jit(solution)/shard_map/slice | solution.py:268
  16.7 2.6 %fusion.39 = (f32[128,1,256]{2,1,0:T(1,128)S(1)}, f32[128,1,256]{2,1,0:T(1,128)S(1)}, f32[128,1,256]{2,1,0:T(1,128)S(1)}, f32[128,1,256]{2,1,0:T(1,128)S(1)}) fusion(f32[128,16,256]{2,1,0:T(8,128)} %param.10), kind=kLoop, calls=%fused_computation.119 | loop fusion | bytes 1048576 | tf_op jit(solution)/shard_map/slice | solution.py:249
  19.3 0.7 select_bitcast_fusion.2
  21.9 2.0 %collective-permute-start.2 = (f32[2,128,2,256]{1,3,0,2:T(8,128)S(1)}, f32[2,128,2,256]{1,3,0,2:T(8,128)S(1)}, u32[]{:S(2)}, u32[]{:S(2)}) collective-permute-start(f32[2,128,2,256]{1,3,0,2:T(8,128)S(1)} %copy.44), channel_id=1, source_target_pairs={{0,1},{1,2},{2,3},{3,4},{4,5},{5,6},{6,7},{7,0},{8,9},{9,10},{10,1... | collective-permute-start | bytes 1572872 | tf_op jit(solution)/shard_map/ppermute | solution.py:198
  24.3 0.6 broadcast_select_fusion.4
  25.0 0.6 broadcast_select_fusion.5
  25.6 18.4 %shard_map.91 = (f32[2,2048,256]{2,1,0:T(8,128)}, f32[2,16,256]{2,1,0:T(8,128)}) custom-call(f32[2,2048,256]{2,1,0:T(8,128)} %bitcast.195, f32[2,32,256]{2,1,0:T(8,128)} %bitcast.208, f32[2,32,256]{2,1,0:T(8,128)} %bitcast.207, f32[2048,256]{1,0:T(8,128)} %bitcast.197, f32[2048,256]{1,0:T(8,128)} %bitcast.202, f32[2,128,128]{2,1,0:T(8,128)} %bitcast.199), custom_call_target="tpu_custom_call" | custom-call | flops 331350016 | bytes 16777216 | tf_op jit(solution)/shard_map/pallas_call | solution.py:104
  44.3 1.0 %fusion.3 = f32[2,1,4,256]{3,1,2,0:T(1,128)S(1)} fusion(f32[2,1,128,256]{2,3,1,0:T(8,128)S(1)} %get-tuple-element.36, f32[2,1,128,256]{2,3,1,0:T(8,128)S(1)} %get-tuple-element.35, f32[2,1,128,256]{2,3,1,0:T(8,128)S(1)} %get-tuple-element.34, f32[2,1,128,256]{2,3,1,0:T(8,128)S(1)} %get-tuple-element.33, f32[2,128,128]{2,1,0:T(8,128)S(1)} %bitcast.200), kind=kOutput, calls=%fused_computation.6 | convolution fusion | flops 3932160 | bytes 1057792 | tf_op jit(solution)/shard_map/sj,skjy->sky/dot_general | solution.py:256
  45.4 2.3 %collective-permute-start.8 = (f32[3,2,16,256]{3,2,1,0:T(8,128)S(1)}, f32[3,2,16,256]{3,2,1,0:T(8,128)S(1)}, u32[]{:S(2)}, u32[]{:S(2)}) collective-permute-start(f32[3,2,16,256]{3,2,1,0:T(8,128)S(1)} %pad_maximum_fusion.4), channel_id=1, source_target_pairs={{0,8},{8,0},{16,24},{24,16},{32,40},{40,32},{48,56},{56,48},{64,72... | collective-permute-start | bytes 294920 | tf_op jit(solution)/shard_map/ppermute | solution.py:145
  47.9 0.7 collective-permute-done.8
  48.7 5.4 %collective-permute-start.11 = (f32[3,2,16,256]{3,2,1,0:T(8,128)S(1)}, f32[3,2,16,256]{3,2,1,0:T(8,128)S(1)}, u32[]{:S(2)}, u32[]{:S(2)}) collective-permute-start(f32[3,2,16,256]{3,2,1,0:T(8,128)S(1)} %pad_maximum_fusion.5), channel_id=1, source_target_pairs={{0,32},{8,40},{16,48},{24,56},{32,0},{40,8},{48,16},{56,24},{64,96... | collective-permute-start | bytes 294920 | tf_op jit(solution)/shard_map/ppermute | solution.py:145
  54.1 2.5 %collective-permute-start.10 = (f32[3,2,16,256]{3,2,1,0:T(8,128)S(1)}, f32[3,2,16,256]{3,2,1,0:T(8,128)S(1)}, u32[]{:S(2)}, u32[]{:S(2)}) collective-permute-start(f32[3,2,16,256]{3,2,1,0:T(8,128)S(1)} %pad_maximum_fusion.5), channel_id=1, source_target_pairs={{0,48},{8,56},{16,0},{24,8},{32,16},{40,24},{48,32},{56,40},{64,11... | collective-permute-start | bytes 294920 | tf_op jit(solution)/shard_map/ppermute | solution.py:145
  56.7 1.0 %collective-permute-start.9 = (f32[3,2,16,256]{3,2,1,0:T(8,128)S(1)}, f32[3,2,16,256]{3,2,1,0:T(8,128)S(1)}, u32[]{:S(2)}, u32[]{:S(2)}) collective-permute-start(f32[3,2,16,256]{3,2,1,0:T(8,128)S(1)} %pad_maximum_fusion.5), channel_id=1, source_target_pairs={{0,16},{8,24},{16,32},{24,40},{32,48},{40,56},{48,0},{56,8},{64,80... | collective-permute-start | bytes 294920 | tf_op jit(solution)/shard_map/ppermute | solution.py:145
  57.6 1.0 %convolution_bitcast_fusion = f32[2,128,4,256]{1,3,2,0:T(8,128)S(1)} fusion(f32[2,1,128,256]{2,3,1,0:T(8,128)S(1)} %get-tuple-element.36, f32[2,1,128,256]{2,3,1,0:T(8,128)S(1)} %get-tuple-element.35, f32[2,1,128,256]{2,3,1,0:T(8,128)S(1)} %get-tuple-element.34, f32[2,1,128,256]{2,3,1,0:T(8,128)S(1)} %get-tuple-element.33, f32[2,1,128,128]{3,2,1,0:T(8,128)S(1)} %copy-done), kind=kOutput, calls=%fused_computation.4 | convolution fusion | flops 403439616 | bytes 2228224 | tf_op jit(solution)/shard_map/sij,skjy->siky/dot_general | solution.py:261
  58.7 5.3 %collective-permute-done.10 = f32[3,2,16,256]{3,2,1,0:T(8,128)S(1)} collective-permute-done((f32[3,2,16,256]{3,2,1,0:T(8,128)S(1)}, f32[3,2,16,256]{3,2,1,0:T(8,128)S(1)}, u32[]{:S(2)}, u32[]{:S(2)}) %collective-permute-start.10) | collective-permute-done | bytes 98336 | tf_op jit(solution)/shard_map/ppermute | solution.py:145
  63.9 1.4 %collective-permute-done.9 = f32[3,2,16,256]{3,2,1,0:T(8,128)S(1)} collective-permute-done((f32[3,2,16,256]{3,2,1,0:T(8,128)S(1)}, f32[3,2,16,256]{3,2,1,0:T(8,128)S(1)}, u32[]{:S(2)}, u32[]{:S(2)}) %collective-permute-start.9) | collective-permute-done | bytes 98336 | tf_op jit(solution)/shard_map/ppermute | solution.py:145
  65.5 4.4 %collective-permute-start.14 = (f32[3,2,16,256]{3,2,1,0:T(8,128)S(1)}, f32[3,2,16,256]{3,2,1,0:T(8,128)S(1)}, u32[]{:S(2)}, u32[]{:S(2)}) collective-permute-start(f32[3,2,16,256]{3,2,1,0:T(8,128)S(1)} %pad_maximum_fusion.6), channel_id=1, source_target_pairs={{0,128},{8,136},{16,144},{24,152},{32,160},{40,168},{48,176},{56,1... | collective-permute-start | bytes 294920 | tf_op jit(solution)/shard_map/ppermute | solution.py:145
  69.9 1.1 %collective-permute-start.13 = (f32[3,2,16,256]{3,2,1,0:T(8,128)S(1)}, f32[3,2,16,256]{3,2,1,0:T(8,128)S(1)}, u32[]{:S(2)}, u32[]{:S(2)}) collective-permute-start(f32[3,2,16,256]{3,2,1,0:T(8,128)S(1)} %pad_maximum_fusion.6), channel_id=1, source_target_pairs={{0,192},{8,200},{16,208},{24,216},{32,224},{40,232},{48,240},{56,2... | collective-permute-start | bytes 294920 | tf_op jit(solution)/shard_map/ppermute | solution.py:145
  70.9 1.0 %collective-permute-start.12 = (f32[3,2,16,256]{3,2,1,0:T(8,128)S(1)}, f32[3,2,16,256]{3,2,1,0:T(8,128)S(1)}, u32[]{:S(2)}, u32[]{:S(2)}) collective-permute-start(f32[3,2,16,256]{3,2,1,0:T(8,128)S(1)} %pad_maximum_fusion.6), channel_id=1, source_target_pairs={{0,64},{8,72},{16,80},{24,88},{32,96},{40,104},{48,112},{56,120},{... | collective-permute-start | bytes 294920 | tf_op jit(solution)/shard_map/ppermute | solution.py:145
  72.5 0.4 collective-permute-done.14
  72.9 2.5 %collective-permute-done.13 = f32[3,2,16,256]{3,2,1,0:T(8,128)S(1)} collective-permute-done((f32[3,2,16,256]{3,2,1,0:T(8,128)S(1)}, f32[3,2,16,256]{3,2,1,0:T(8,128)S(1)}, u32[]{:S(2)}, u32[]{:S(2)}) %collective-permute-start.13) | collective-permute-done | bytes 98336 | tf_op jit(solution)/shard_map/ppermute | solution.py:145
  75.4 1.4 %collective-permute-done.12 = f32[3,2,16,256]{3,2,1,0:T(8,128)S(1)} collective-permute-done((f32[3,2,16,256]{3,2,1,0:T(8,128)S(1)}, f32[3,2,16,256]{3,2,1,0:T(8,128)S(1)}, u32[]{:S(2)}, u32[]{:S(2)}) %collective-permute-start.12) | collective-permute-done | bytes 98336 | tf_op jit(solution)/shard_map/ppermute | solution.py:145
  76.9 6.8 %fusion.2 = f32[2,128,16,256]{3,2,1,0:T(8,128)} fusion(f32[2,128,16,256]{3,2,1,0:T(8,128)} %bitcast.196, f32[2,128,2,256]{3,2,1,0:T(2,128)S(1)} %copy.39, f32[2,128,2,256]{3,2,1,0:T(2,128)S(1)} %copy.38, f32[16]{0:T(128)S(1)} %pad.21.clone, f32[2,16,256]{2,1,0:T(8,128)S(1)} %get-tuple-element.59, f32[2,128]{1,0:T(2,128)S(1)} %get-tuple-element.10, ...), kind=kLoop, calls=%fused_computation.3 | loop fusion | flops 9437184 | bytes 9538624 | tf_op jit(solution)/shard_map/add | solution.py:278
  (53 shorter events, 2.7 us)
Async XLA Ops:
  1.5 20.4 %collective-permute-start.6 = (f32[2,16,256]{2,1,0:T(8,128)S(1)}, f32[2,16,256]{2,1,0:T(8,128)S(1)}, u32[]{:S(2)}, u32[]{:S(2)}) collective-permute-start(f32[2,16,256]{2,1,0:T(8,128)S(1)} %get-tuple-element.19), channel_id=1, source_target_pairs={{0,1},{1,2},{2,3},{3,0},{4,5},{5,6},{6,7},{7,4},{8,9},{9,10},{10,1... | collective-permute-start | bytes 98312 | tf_op jit(solution)/shard_map/ppermute | solution.py:145
  3.0 18.9 %collective-permute-start.5 = (f32[2,16,256]{2,1,0:T(8,128)S(1)}, f32[2,16,256]{2,1,0:T(8,128)S(1)}, u32[]{:S(2)}, u32[]{:S(2)}) collective-permute-start(f32[2,16,256]{2,1,0:T(8,128)S(1)} %get-tuple-element.19), channel_id=1, source_target_pairs={{0,2},{1,3},{2,0},{3,1},{4,6},{5,7},{6,4},{7,5},{8,10},{9,11},{10,... | collective-permute-start | bytes 98312 | tf_op jit(solution)/shard_map/ppermute | solution.py:145
  5.7 18.2 %collective-permute-start.4 = (f32[2,16,256]{2,1,0:T(8,128)S(1)}, f32[2,16,256]{2,1,0:T(8,128)S(1)}, u32[]{:S(2)}, u32[]{:S(2)}) collective-permute-start(f32[2,16,256]{2,1,0:T(8,128)S(1)} %get-tuple-element.19), channel_id=1, source_target_pairs={{0,3},{1,0},{2,1},{3,2},{4,7},{5,4},{6,5},{7,6},{8,11},{9,8},{10,9... | collective-permute-start | bytes 98312 | tf_op jit(solution)/shard_map/ppermute | solution.py:145
  8.0 16.3 %collective-permute-start.1 = (f32[2,2,16,256]{3,2,1,0:T(8,128)S(1)}, f32[2,2,16,256]{3,2,1,0:T(8,128)S(1)}, u32[]{:S(2)}, u32[]{:S(2)}) collective-permute-start(f32[2,2,16,256]{3,2,1,0:T(8,128)S(1)} %get-tuple-element.23), channel_id=1, source_target_pairs={{8,0},{16,8},{24,16},{32,24},{40,32},{48,40},{56,48},{64,56},{72,6... | collective-permute-start | bytes 196616 | tf_op jit(solution)/shard_map/ppermute | solution.py:198
  9.3 15.7 %collective-permute-start = (f32[2,2,16,256]{3,2,1,0:T(8,128)S(1)}, f32[2,2,16,256]{3,2,1,0:T(8,128)S(1)}, u32[]{:S(2)}, u32[]{:S(2)}) collective-permute-start(f32[2,2,16,256]{3,2,1,0:T(8,128)S(1)} %get-tuple-element.24), channel_id=1, source_target_pairs={{0,8},{8,16},{16,24},{24,32},{32,40},{40,48},{48,56},{56,64},{64,7... | collective-permute-start | bytes 196616 | tf_op jit(solution)/shard_map/ppermute | solution.py:198
  21.9 22.2 %collective-permute-start.3 = (f32[2,128,2,256]{1,3,0,2:T(8,128)S(1)}, f32[2,128,2,256]{1,3,0,2:T(8,128)S(1)}, u32[]{:S(2)}, u32[]{:S(2)}) collective-permute-start(f32[2,128,2,256]{1,3,0,2:T(8,128)S(1)} %copy.47), channel_id=1, source_target_pairs={{1,0},{2,1},{3,2},{4,3},{5,4},{6,5},{7,6},{0,7},{9,8},{10,9},{11,1... | collective-permute-start | bytes 1572872 | tf_op jit(solution)/shard_map/ppermute | solution.py:198
  21.9 22.3 %collective-permute-start.2 = (f32[2,128,2,256]{1,3,0,2:T(8,128)S(1)}, f32[2,128,2,256]{1,3,0,2:T(8,128)S(1)}, u32[]{:S(2)}, u32[]{:S(2)}) collective-permute-start(f32[2,128,2,256]{1,3,0,2:T(8,128)S(1)} %copy.44), channel_id=1, source_target_pairs={{0,1},{1,2},{2,3},{3,4},{4,5},{5,6},{6,7},{7,0},{8,9},{9,10},{10,1... | collective-permute-start | bytes 1572872 | tf_op jit(solution)/shard_map/ppermute | solution.py:198
  24.0 20.0 %collective-permute-start.7 = (f32[2,64,256]{2,1,0:T(8,128)S(1)}, f32[2,64,256]{2,1,0:T(8,128)S(1)}, u32[]{:S(2)}, u32[]{:S(2)}) collective-permute-start(f32[2,64,256]{2,1,0:T(8,128)S(1)} %pad_maximum_fusion.3), channel_id=1, source_target_pairs={{0,4},{1,5},{2,6},{3,7},{4,0},{5,1},{6,2},{7,3},{8,12},{9,13},{10,... | collective-permute-start | bytes 393224 | tf_op jit(solution)/shard_map/ppermute | solution.py:145
  25.6 18.6 %copy-start = (f32[2,1,128,128]{3,2,1,0:T(8,128)S(1)}, f32[2,1,128,128]{3,2,1,0:T(8,128)}, u32[]{:S(2)}) copy-start(f32[2,1,128,128]{3,2,1,0:T(8,128)} %param.12) | copy-start | bytes 393220
  44.0 1.3 %copy-start.1 = (f32[2,16,256]{2,1,0:T(8,128)S(1)}, f32[2,16,256]{2,1,0:T(8,128)}, u32[]{:S(2)}) copy-start(f32[2,16,256]{2,1,0:T(8,128)} %get-tuple-element.8) | copy-start | bytes 98308
  44.0 1.3 %copy-start.2 = (f32[2,256]{1,0:T(2,128)S(1)}, f32[2,256]{1,0:T(2,128)}, u32[]{:S(2)}) copy-start(f32[2,256]{1,0:T(2,128)} %param.15) | copy-start | bytes 6148
  44.0 1.3 %copy-start.3 = (f32[2,256]{1,0:T(2,128)S(1)}, f32[2,256]{1,0:T(2,128)}, u32[]{:S(2)}) copy-start(f32[2,256]{1,0:T(2,128)} %param.14) | copy-start | bytes 6148
  45.4 3.3 %collective-permute-start.8 = (f32[3,2,16,256]{3,2,1,0:T(8,128)S(1)}, f32[3,2,16,256]{3,2,1,0:T(8,128)S(1)}, u32[]{:S(2)}, u32[]{:S(2)}) collective-permute-start(f32[3,2,16,256]{3,2,1,0:T(8,128)S(1)} %pad_maximum_fusion.4), channel_id=1, source_target_pairs={{0,8},{8,0},{16,24},{24,16},{32,40},{40,32},{48,56},{56,48},{64,72... | collective-permute-start | bytes 294920 | tf_op jit(solution)/shard_map/ppermute | solution.py:145
  48.7 9.9 %collective-permute-start.11 = (f32[3,2,16,256]{3,2,1,0:T(8,128)S(1)}, f32[3,2,16,256]{3,2,1,0:T(8,128)S(1)}, u32[]{:S(2)}, u32[]{:S(2)}) collective-permute-start(f32[3,2,16,256]{3,2,1,0:T(8,128)S(1)} %pad_maximum_fusion.5), channel_id=1, source_target_pairs={{0,32},{8,40},{16,48},{24,56},{32,0},{40,8},{48,16},{56,24},{64,96... | collective-permute-start | bytes 294920 | tf_op jit(solution)/shard_map/ppermute | solution.py:145
  54.1 9.8 %collective-permute-start.10 = (f32[3,2,16,256]{3,2,1,0:T(8,128)S(1)}, f32[3,2,16,256]{3,2,1,0:T(8,128)S(1)}, u32[]{:S(2)}, u32[]{:S(2)}) collective-permute-start(f32[3,2,16,256]{3,2,1,0:T(8,128)S(1)} %pad_maximum_fusion.5), channel_id=1, source_target_pairs={{0,48},{8,56},{16,0},{24,8},{32,16},{40,24},{48,32},{56,40},{64,11... | collective-permute-start | bytes 294920 | tf_op jit(solution)/shard_map/ppermute | solution.py:145
  56.7 8.7 %collective-permute-start.9 = (f32[3,2,16,256]{3,2,1,0:T(8,128)S(1)}, f32[3,2,16,256]{3,2,1,0:T(8,128)S(1)}, u32[]{:S(2)}, u32[]{:S(2)}) collective-permute-start(f32[3,2,16,256]{3,2,1,0:T(8,128)S(1)} %pad_maximum_fusion.5), channel_id=1, source_target_pairs={{0,16},{8,24},{16,32},{24,40},{32,48},{40,56},{48,0},{56,8},{64,80... | collective-permute-start | bytes 294920 | tf_op jit(solution)/shard_map/ppermute | solution.py:145
  58.7 18.2 %copy-start.4 = (f32[2,1,128]{2,1,0:T(1,128)S(1)}, f32[2,1,128]{2,1,0:T(1,128)}, u32[]{:S(2)}) copy-start(f32[2,1,128]{2,1,0:T(1,128)} %param.13) | copy-start | bytes 3076
  65.5 7.4 %collective-permute-start.14 = (f32[3,2,16,256]{3,2,1,0:T(8,128)S(1)}, f32[3,2,16,256]{3,2,1,0:T(8,128)S(1)}, u32[]{:S(2)}, u32[]{:S(2)}) collective-permute-start(f32[3,2,16,256]{3,2,1,0:T(8,128)S(1)} %pad_maximum_fusion.6), channel_id=1, source_target_pairs={{0,128},{8,136},{16,144},{24,152},{32,160},{40,168},{48,176},{56,1... | collective-permute-start | bytes 294920 | tf_op jit(solution)/shard_map/ppermute | solution.py:145
  69.9 5.5 %collective-permute-start.13 = (f32[3,2,16,256]{3,2,1,0:T(8,128)S(1)}, f32[3,2,16,256]{3,2,1,0:T(8,128)S(1)}, u32[]{:S(2)}, u32[]{:S(2)}) collective-permute-start(f32[3,2,16,256]{3,2,1,0:T(8,128)S(1)} %pad_maximum_fusion.6), channel_id=1, source_target_pairs={{0,192},{8,200},{16,208},{24,216},{32,224},{40,232},{48,240},{56,2... | collective-permute-start | bytes 294920 | tf_op jit(solution)/shard_map/ppermute | solution.py:145
  70.9 5.8 %collective-permute-start.12 = (f32[3,2,16,256]{3,2,1,0:T(8,128)S(1)}, f32[3,2,16,256]{3,2,1,0:T(8,128)S(1)}, u32[]{:S(2)}, u32[]{:S(2)}) collective-permute-start(f32[3,2,16,256]{3,2,1,0:T(8,128)S(1)} %pad_maximum_fusion.6), channel_id=1, source_target_pairs={{0,64},{8,72},{16,80},{24,88},{32,96},{40,104},{48,112},{56,120},{... | collective-permute-start | bytes 294920 | tf_op jit(solution)/shard_map/ppermute | solution.py:145

commit v12 on v11

--- a/solution.py
+++ b/solution.py
@@ -274,9 +274,9 @@
     incoming = through * inflow + upstream_sum
     first_in = first_gain * inflow
     second_in = second_gain * inflow
+    (settled,) = lax.optimization_barrier((local_part + edge_part,))
     return (
-        local_part
-        + edge_part
+        settled
         + response[:, :, None, None] * incoming[:, None]
         + inverse[:, :, 0][:, :, None, None] * first_in[:, None]
         + inverse[:, :, 1][:, :, None, None] * second_in[:, None]

time: 85 us -> 82.3 us (0.968)
  waiting for transfers between devices: 11.8 us -> 10.3 us
  other arithmetic: 9.43 us -> 8.14 us
  local copies, waits for them, and re-layouts: 10.3 us -> 11.3 us
    ppermute x11, starting transfers between devices: 23.7 us -> 21.4 us  [digit_exchange(): received[shift] = lax.ppermute(x, axis, pairs)]
    ppermute x4, starting transfers between devices: 6.36 us -> 8.49 us  [halos(): return (lax.ppermute(last, axis, up), lax.ppermute(first, axis, down))]
    ppermute x11, waiting for transfers between devices: 11.7 us -> 10.3 us  [digit_exchange(): received[shift] = lax.ppermute(x, axis, pairs)]
    add x1 -> x2, other arithmetic: 6.79 us -> 5.5 us  [the longest x1 2.95 us: on_device(): settled, = lax.optimization_barrier((local_part + edge_part,))]
    slice x1, local copies, waits for them, and re-layouts: 0.2 us -> 1.18 us  [on_device(): inverse[:, :, 0][:, :, None, None] * first_in[:, None]]
  transfers between devices with their start and end apart: 15 -> 15, of which waited for: 6 -> 4; matrix products, arithmetic and copies ran while one was open for 15% -> 20% of each run, Pallas kernels for 22% -> 22%
where the time goes in v12:
time: 82.3 us; the launch traced here: 81.9 us
  starting transfers between devices  29.9 us (36%)
  Pallas kernels  18.4 us (22%)
  local copies, waits for them, and re-layouts  11.3 us (14%)
  waiting for transfers between devices  10.3 us (13%)
  other arithmetic  8.14 us (10%)
  matrix products  2 us (2%)
  between operations  1.84 us (2%)
    ppermute x11, starting transfers between devices, digit_exchange(): received[shift] = lax.ppermute(x, axis, pairs)  21.4 us
    pallas_call x1, Pallas kernels, explicit_local(): pl.pallas_call(functools.partial(explicit_kernel, planes, rows, width), o...  18.4 us
    ppermute x11, waiting for transfers between devices, digit_exchange(): received[shift] = lax.ppermute(x, axis, pairs)  10.3 us
    ppermute x4, starting transfers between devices, halos(): return (lax.ppermute(last, axis, up), lax.ppermute(first, axis, down))  8.49 us
    add x1, other arithmetic, on_device(): settled, = lax.optimization_barrier((local_part + edge_part,))  2.95 us
    slice x1, local copies, waits for them, and re-layouts, halos(): last = lax.slice_in_dim(x, length - width, length, axis=dim)  2.59 us
    slice x1, local copies, waits for them, and re-layouts, on_device(): diffusivity[:, 0] * (16.0 * b1 - b0) * (1.0 / 12.0)  2.58 us
    add x1, other arithmetic, on_device(): settled + response[:, :, None, None] * incoming[:, None]  2.54 us
  transfers between devices with their start and end apart: 15, of which 4 were waited for; matrix products, arithmetic and copies ran while one was open for 20% of the time, Pallas kernels for 22%

profile of v12, /device:TPU:32, one launch (start us, length us, event | category | flops | bytes accessed | tf_op | source)
XLA Modules:
  0.0 81.9 jit_solution(12741459639691598457)
XLA Ops:
  0.7 0.8 dynamic-slice_bitcast_fusion
  1.5 2.8 %collective-permute-start.4 = (f32[2,16,256]{2,1,0:T(8,128)S(1)}, f32[2,16,256]{2,1,0:T(8,128)S(1)}, u32[]{:S(2)}, u32[]{:S(2)}) collective-permute-start(f32[2,16,256]{2,1,0:T(8,128)S(1)} %get-tuple-element.19), channel_id=1, source_target_pairs={{0,3},{1,0},{2,1},{3,2},{4,7},{5,4},{6,5},{7,6},{8,11},{9,8},{10,9... | collective-permute-start | bytes 98312 | tf_op jit(solution)/shard_map/ppermute | solution.py:145
  4.2 0.8 collective-permute-start.5
  5.0 0.9 %collective-permute-start.6 = (f32[2,16,256]{2,1,0:T(8,128)S(1)}, f32[2,16,256]{2,1,0:T(8,128)S(1)}, u32[]{:S(2)}, u32[]{:S(2)}) collective-permute-start(f32[2,16,256]{2,1,0:T(8,128)S(1)} %get-tuple-element.19), channel_id=1, source_target_pairs={{0,1},{1,2},{2,3},{3,0},{4,5},{5,6},{6,7},{7,4},{8,9},{9,10},{10,1... | collective-permute-start | bytes 98312 | tf_op jit(solution)/shard_map/ppermute | solution.py:145
  5.9 0.9 %fusion.35 = (f32[2,2,16,256]{3,2,1,0:T(8,128)S(1)}, f32[2,2,16,256]{3,2,1,0:T(8,128)S(1)}) fusion(f32[2,128,16,256]{3,2,1,0:T(8,128)} %param.9), kind=kLoop, calls=%fused_computation.116 | loop fusion | bytes 262144 | tf_op jit(solution)/shard_map/slice | solution.py:197
  6.8 1.3 %collective-permute-start.1 = (f32[2,2,16,256]{3,2,1,0:T(8,128)S(1)}, f32[2,2,16,256]{3,2,1,0:T(8,128)S(1)}, u32[]{:S(2)}, u32[]{:S(2)}) collective-permute-start(f32[2,2,16,256]{3,2,1,0:T(8,128)S(1)} %get-tuple-element.23), channel_id=1, source_target_pairs={{8,0},{16,8},{24,16},{32,24},{40,32},{48,40},{56,48},{64,56},{72,6... | collective-permute-start | bytes 196616 | tf_op jit(solution)/shard_map/ppermute | solution.py:198
  8.1 3.0 %collective-permute-start = (f32[2,2,16,256]{3,2,1,0:T(8,128)S(1)}, f32[2,2,16,256]{3,2,1,0:T(8,128)S(1)}, u32[]{:S(2)}, u32[]{:S(2)}) collective-permute-start(f32[2,2,16,256]{3,2,1,0:T(8,128)S(1)} %get-tuple-element.24), channel_id=1, source_target_pairs={{0,8},{8,16},{16,24},{24,32},{32,40},{40,48},{48,56},{56,64},{64,7... | collective-permute-start | bytes 196616 | tf_op jit(solution)/shard_map/ppermute | solution.py:198
  11.1 2.6 %fusion.34 = (f32[2,128,2,256]{3,2,1,0:T(2,128)S(1)}, f32[2,128,2,256]{3,2,1,0:T(2,128)S(1)}) fusion(f32[2,128,16,256]{3,2,1,0:T(8,128)} %param.9), kind=kLoop, calls=%fused_computation.115 | loop fusion | bytes 2097152 | tf_op jit(solution)/shard_map/slice | solution.py:196
  13.7 2.6 %fusion.36 = (f32[128,1,256]{2,1,0:T(1,128)S(1)}, f32[128,1,256]{2,1,0:T(1,128)S(1)}, f32[128,1,256]{2,1,0:T(1,128)S(1)}, f32[128,1,256]{2,1,0:T(1,128)S(1)}) fusion(f32[128,16,256]{2,1,0:T(8,128)} %param.10), kind=kLoop, calls=%fused_computation.117 | loop fusion | bytes 1048576 | tf_op jit(solution)/shard_map/slice | solution.py:249
  16.3 0.7 select_bitcast_fusion.2
  17.1 0.9 %slice_reduce_fusion.3 = (f32[2]{0:T(128)S(1)}, f32[2]{0:T(128)S(1)}) fusion(f32[2,128,128]{2,1,0:T(8,128)} %bitcast.198), kind=kLoop, calls=%fused_computation.109 | loop fusion | bytes 32 | tf_op jit(solution)/shard_map/slice | solution.py:268
  18.0 0.9 %slice_reduce_fusion.4 = f32[2]{0:T(128)S(1)} fusion(f32[2,128]{1,0:T(2,128)} %bitcast.210), kind=kLoop, calls=%fused_computation.110 | loop fusion | bytes 16 | tf_op jit(solution)/shard_map/slice | solution.py:267
  19.0 1.2 %slice_reduce_fusion.1 = (f32[2,128]{1,0:T(2,128)S(1)}, f32[2,128]{1,0:T(2,128)S(1)}) fusion(f32[2,128,128]{2,1,0:T(8,128)} %bitcast.199), kind=kLoop, calls=%fused_computation.25 | loop fusion | bytes 4096 | tf_op jit(solution)/shard_map/slice | solution.py:281
  21.9 1.8 %collective-permute-start.2 = (f32[2,128,2,256]{1,3,0,2:T(8,128)S(1)}, f32[2,128,2,256]{1,3,0,2:T(8,128)S(1)}, u32[]{:S(2)}, u32[]{:S(2)}) collective-permute-start(f32[2,128,2,256]{1,3,0,2:T(8,128)S(1)} %copy.44), channel_id=1, source_target_pairs={{0,1},{1,2},{2,3},{3,4},{4,5},{5,6},{6,7},{7,0},{8,9},{9,10},{10,1... | collective-permute-start | bytes 1572872 | tf_op jit(solution)/shard_map/ppermute | solution.py:198
  23.7 2.3 %collective-permute-start.3 = (f32[2,128,2,256]{1,3,0,2:T(8,128)S(1)}, f32[2,128,2,256]{1,3,0,2:T(8,128)S(1)}, u32[]{:S(2)}, u32[]{:S(2)}) collective-permute-start(f32[2,128,2,256]{1,3,0,2:T(8,128)S(1)} %copy.47), channel_id=1, source_target_pairs={{1,0},{2,1},{3,2},{4,3},{5,4},{6,5},{7,6},{0,7},{9,8},{10,9},{11,1... | collective-permute-start | bytes 1572872 | tf_op jit(solution)/shard_map/ppermute | solution.py:198
  27.1 0.6 broadcast_select_fusion.5
  27.7 18.4 %shard_map.91 = (f32[2,2048,256]{2,1,0:T(8,128)}, f32[2,16,256]{2,1,0:T(8,128)}) custom-call(f32[2,2048,256]{2,1,0:T(8,128)} %bitcast.195, f32[2,32,256]{2,1,0:T(8,128)} %bitcast.208, f32[2,32,256]{2,1,0:T(8,128)} %bitcast.207, f32[2048,256]{1,0:T(8,128)} %bitcast.197, f32[2048,256]{1,0:T(8,128)} %bitcast.202, f32[2,128,128]{2,1,0:T(8,128)} %bitcast.200), custom_call_target="tpu_custom_call" | custom-call | flops 331350016 | bytes 16777216 | tf_op jit(solution)/shard_map/pallas_call | solution.py:104
  46.4 1.0 %fusion = f32[2,1,4,256]{3,1,2,0:T(1,128)S(1)} fusion(f32[2,1,128,256]{2,3,1,0:T(8,128)S(1)} %get-tuple-element.36, f32[2,1,128,256]{2,3,1,0:T(8,128)S(1)} %get-tuple-element.35, f32[2,1,128,256]{2,3,1,0:T(8,128)S(1)} %get-tuple-element.34, f32[2,1,128,256]{2,3,1,0:T(8,128)S(1)} %get-tuple-element.33, f32[2,128,128]{2,1,0:T(8,128)S(1)} %bitcast.201), kind=kOutput, calls=%fused_computation.4 | convolution fusion | flops 3932160 | bytes 1057792 | tf_op jit(solution)/shard_map/sj,skjy->sky/dot_general | solution.py:256
  47.5 2.3 %collective-permute-start.8 = (f32[3,2,16,256]{3,2,1,0:T(8,128)S(1)}, f32[3,2,16,256]{3,2,1,0:T(8,128)S(1)}, u32[]{:S(2)}, u32[]{:S(2)}) collective-permute-start(f32[3,2,16,256]{3,2,1,0:T(8,128)S(1)} %pad_maximum_fusion.4), channel_id=1, source_target_pairs={{0,8},{8,0},{16,24},{24,16},{32,40},{40,32},{48,56},{56,48},{64,72... | collective-permute-start | bytes 294920 | tf_op jit(solution)/shard_map/ppermute | solution.py:145
  49.9 1.0 %convolution_bitcast_fusion = f32[2,128,4,256]{1,3,2,0:T(8,128)S(1)} fusion(f32[2,1,128,256]{2,3,1,0:T(8,128)S(1)} %get-tuple-element.36, f32[2,1,128,256]{2,3,1,0:T(8,128)S(1)} %get-tuple-element.35, f32[2,1,128,256]{2,3,1,0:T(8,128)S(1)} %get-tuple-element.34, f32[2,1,128,256]{2,3,1,0:T(8,128)S(1)} %get-tuple-element.33, f32[2,1,128,128]{3,2,1,0:T(8,128)S(1)} %copy-done), kind=kOutput, calls=%fused_computation.2 | convolution fusion | flops 403439616 | bytes 2228224 | tf_op jit(solution)/shard_map/sij,skjy->siky/dot_general | solution.py:261
  51.0 6.5 %collective-permute-start.10 = (f32[3,2,16,256]{3,2,1,0:T(8,128)S(1)}, f32[3,2,16,256]{3,2,1,0:T(8,128)S(1)}, u32[]{:S(2)}, u32[]{:S(2)}) collective-permute-start(f32[3,2,16,256]{3,2,1,0:T(8,128)S(1)} %pad_maximum_fusion.5), channel_id=1, source_target_pairs={{0,48},{8,56},{16,0},{24,8},{32,16},{40,24},{48,32},{56,40},{64,11... | collective-permute-start | bytes 294920 | tf_op jit(solution)/shard_map/ppermute | solution.py:145
  57.5 1.4 %collective-permute-start.11 = (f32[3,2,16,256]{3,2,1,0:T(8,128)S(1)}, f32[3,2,16,256]{3,2,1,0:T(8,128)S(1)}, u32[]{:S(2)}, u32[]{:S(2)}) collective-permute-start(f32[3,2,16,256]{3,2,1,0:T(8,128)S(1)} %pad_maximum_fusion.5), channel_id=1, source_target_pairs={{0,32},{8,40},{16,48},{24,56},{32,0},{40,8},{48,16},{56,24},{64,96... | collective-permute-start | bytes 294920 | tf_op jit(solution)/shard_map/ppermute | solution.py:145
  58.9 1.1 %collective-permute-start.9 = (f32[3,2,16,256]{3,2,1,0:T(8,128)S(1)}, f32[3,2,16,256]{3,2,1,0:T(8,128)S(1)}, u32[]{:S(2)}, u32[]{:S(2)}) collective-permute-start(f32[3,2,16,256]{3,2,1,0:T(8,128)S(1)} %pad_maximum_fusion.5), channel_id=1, source_target_pairs={{0,16},{8,24},{16,32},{24,40},{32,48},{40,56},{48,0},{56,8},{64,80... | collective-permute-start | bytes 294920 | tf_op jit(solution)/shard_map/ppermute | solution.py:145
  60.5 3.0 %collective-permute-done.10 = f32[3,2,16,256]{3,2,1,0:T(8,128)S(1)} collective-permute-done((f32[3,2,16,256]{3,2,1,0:T(8,128)S(1)}, f32[3,2,16,256]{3,2,1,0:T(8,128)S(1)}, u32[]{:S(2)}, u32[]{:S(2)}) %collective-permute-start.10) | collective-permute-done | bytes 98336 | tf_op jit(solution)/shard_map/ppermute | solution.py:145
  63.5 4.9 %collective-permute-done.11 = f32[3,2,16,256]{3,2,1,0:T(8,128)S(1)} collective-permute-done((f32[3,2,16,256]{3,2,1,0:T(8,128)S(1)}, f32[3,2,16,256]{3,2,1,0:T(8,128)S(1)}, u32[]{:S(2)}, u32[]{:S(2)}) %collective-permute-start.11) | collective-permute-done | bytes 98336 | tf_op jit(solution)/shard_map/ppermute | solution.py:145
  68.4 1.2 %collective-permute-done.9 = f32[3,2,16,256]{3,2,1,0:T(8,128)S(1)} collective-permute-done((f32[3,2,16,256]{3,2,1,0:T(8,128)S(1)}, f32[3,2,16,256]{3,2,1,0:T(8,128)S(1)}, u32[]{:S(2)}, u32[]{:S(2)}) %collective-permute-start.9) | collective-permute-done | bytes 98336 | tf_op jit(solution)/shard_map/ppermute | solution.py:145
  69.7 1.3 %collective-permute-start.12 = (f32[3,2,16,256]{3,2,1,0:T(8,128)S(1)}, f32[3,2,16,256]{3,2,1,0:T(8,128)S(1)}, u32[]{:S(2)}, u32[]{:S(2)}) collective-permute-start(f32[3,2,16,256]{3,2,1,0:T(8,128)S(1)} %pad_maximum_fusion.6), channel_id=1, source_target_pairs={{0,64},{8,72},{16,80},{24,88},{32,96},{40,104},{48,112},{56,120},{... | collective-permute-start | bytes 294920 | tf_op jit(solution)/shard_map/ppermute | solution.py:145
  71.0 2.0 %collective-permute-start.13 = (f32[3,2,16,256]{3,2,1,0:T(8,128)S(1)}, f32[3,2,16,256]{3,2,1,0:T(8,128)S(1)}, u32[]{:S(2)}, u32[]{:S(2)}) collective-permute-start(f32[3,2,16,256]{3,2,1,0:T(8,128)S(1)} %pad_maximum_fusion.6), channel_id=1, source_target_pairs={{0,192},{8,200},{16,208},{24,216},{32,224},{40,232},{48,240},{56,2... | collective-permute-start | bytes 294920 | tf_op jit(solution)/shard_map/ppermute | solution.py:145
  73.0 1.9 %collective-permute-start.14 = (f32[3,2,16,256]{3,2,1,0:T(8,128)S(1)}, f32[3,2,16,256]{3,2,1,0:T(8,128)S(1)}, u32[]{:S(2)}, u32[]{:S(2)}) collective-permute-start(f32[3,2,16,256]{3,2,1,0:T(8,128)S(1)} %pad_maximum_fusion.6), channel_id=1, source_target_pairs={{0,128},{8,136},{16,144},{24,152},{32,160},{40,168},{48,176},{56,1... | collective-permute-start | bytes 294920 | tf_op jit(solution)/shard_map/ppermute | solution.py:145
  75.0 3.0 %maximum_add_fusion = f32[2,128,16,256]{3,2,1,0:T(8,128)S(1)} fusion(f32[2,128,16,256]{3,2,1,0:T(8,128)} %bitcast.196, f32[2,128,2,256]{3,2,1,0:T(2,128)S(1)} %copy.39, f32[2,128,2,256]{3,2,1,0:T(2,128)S(1)} %copy.38, f32[16]{0:T(128)S(1)} %pad.21.clone), kind=kLoop, calls=%fused_computation | loop fusion | flops 3145728 | bytes 9437248 | tf_op jit(solution)/shard_map/add | solution.py:277
  78.0 1.2 %collective-permute-done.14 = f32[3,2,16,256]{3,2,1,0:T(8,128)S(1)} collective-permute-done((f32[3,2,16,256]{3,2,1,0:T(8,128)S(1)}, f32[3,2,16,256]{3,2,1,0:T(8,128)S(1)}, u32[]{:S(2)}, u32[]{:S(2)}) %collective-permute-start.14) | collective-permute-done | bytes 98336 | tf_op jit(solution)/shard_map/ppermute | solution.py:145
  79.3 2.5 %multiply_add_fusion = f32[2,128,16,256]{3,2,1,0:T(8,128)} fusion(f32[2,128,16,256]{3,2,1,0:T(8,128)S(1)} %maximum_add_fusion, f32[2,16,256]{2,1,0:T(8,128)S(1)} %get-tuple-element.59, f32[2,128]{1,0:T(2,128)S(1)} %get-tuple-element.10, f32[2,16,256]{2,1,0:T(8,128)S(1)} %get-tuple-element.58, f32[2,128]{1,0:T(2,128)S(1)} %get-tuple-element.9, ...), kind=kLoop, calls=%fused_computation.1 | loop fusion | flops 6291456 | bytes 8489984 | tf_op jit(solution)/shard_map/add | solution.py:279
  (54 shorter events, 3.1 us)
Async XLA Ops:
  1.5 20.4 %collective-permute-start.4 = (f32[2,16,256]{2,1,0:T(8,128)S(1)}, f32[2,16,256]{2,1,0:T(8,128)S(1)}, u32[]{:S(2)}, u32[]{:S(2)}) collective-permute-start(f32[2,16,256]{2,1,0:T(8,128)S(1)} %get-tuple-element.19), channel_id=1, source_target_pairs={{0,3},{1,0},{2,1},{3,2},{4,7},{5,4},{6,5},{7,6},{8,11},{9,8},{10,9... | collective-permute-start | bytes 98312 | tf_op jit(solution)/shard_map/ppermute | solution.py:145
  4.2 19.5 %collective-permute-start.5 = (f32[2,16,256]{2,1,0:T(8,128)S(1)}, f32[2,16,256]{2,1,0:T(8,128)S(1)}, u32[]{:S(2)}, u32[]{:S(2)}) collective-permute-start(f32[2,16,256]{2,1,0:T(8,128)S(1)} %get-tuple-element.19), channel_id=1, source_target_pairs={{0,2},{1,3},{2,0},{3,1},{4,6},{5,7},{6,4},{7,5},{8,10},{9,11},{10,... | collective-permute-start | bytes 98312 | tf_op jit(solution)/shard_map/ppermute | solution.py:145
  5.0 21.0 %collective-permute-start.6 = (f32[2,16,256]{2,1,0:T(8,128)S(1)}, f32[2,16,256]{2,1,0:T(8,128)S(1)}, u32[]{:S(2)}, u32[]{:S(2)}) collective-permute-start(f32[2,16,256]{2,1,0:T(8,128)S(1)} %get-tuple-element.19), channel_id=1, source_target_pairs={{0,1},{1,2},{2,3},{3,0},{4,5},{5,6},{6,7},{7,4},{8,9},{9,10},{10,1... | collective-permute-start | bytes 98312 | tf_op jit(solution)/shard_map/ppermute | solution.py:145
  6.8 19.7 %collective-permute-start.1 = (f32[2,2,16,256]{3,2,1,0:T(8,128)S(1)}, f32[2,2,16,256]{3,2,1,0:T(8,128)S(1)}, u32[]{:S(2)}, u32[]{:S(2)}) collective-permute-start(f32[2,2,16,256]{3,2,1,0:T(8,128)S(1)} %get-tuple-element.23), channel_id=1, source_target_pairs={{8,0},{16,8},{24,16},{32,24},{40,32},{48,40},{56,48},{64,56},{72,6... | collective-permute-start | bytes 196616 | tf_op jit(solution)/shard_map/ppermute | solution.py:198
  8.1 19.0 %collective-permute-start = (f32[2,2,16,256]{3,2,1,0:T(8,128)S(1)}, f32[2,2,16,256]{3,2,1,0:T(8,128)S(1)}, u32[]{:S(2)}, u32[]{:S(2)}) collective-permute-start(f32[2,2,16,256]{3,2,1,0:T(8,128)S(1)} %get-tuple-element.24), channel_id=1, source_target_pairs={{0,8},{8,16},{16,24},{24,32},{32,40},{40,48},{48,56},{56,64},{64,7... | collective-permute-start | bytes 196616 | tf_op jit(solution)/shard_map/ppermute | solution.py:198
  21.9 24.3 %collective-permute-start.2 = (f32[2,128,2,256]{1,3,0,2:T(8,128)S(1)}, f32[2,128,2,256]{1,3,0,2:T(8,128)S(1)}, u32[]{:S(2)}, u32[]{:S(2)}) collective-permute-start(f32[2,128,2,256]{1,3,0,2:T(8,128)S(1)} %copy.44), channel_id=1, source_target_pairs={{0,1},{1,2},{2,3},{3,4},{4,5},{5,6},{6,7},{7,0},{8,9},{9,10},{10,1... | collective-permute-start | bytes 1572872 | tf_op jit(solution)/shard_map/ppermute | solution.py:198
  23.7 22.6 %collective-permute-start.3 = (f32[2,128,2,256]{1,3,0,2:T(8,128)S(1)}, f32[2,128,2,256]{1,3,0,2:T(8,128)S(1)}, u32[]{:S(2)}, u32[]{:S(2)}) collective-permute-start(f32[2,128,2,256]{1,3,0,2:T(8,128)S(1)} %copy.47), channel_id=1, source_target_pairs={{1,0},{2,1},{3,2},{4,3},{5,4},{6,5},{7,6},{0,7},{9,8},{10,9},{11,1... | collective-permute-start | bytes 1572872 | tf_op jit(solution)/shard_map/ppermute | solution.py:198
  26.1 20.0 %collective-permute-start.7 = (f32[2,64,256]{2,1,0:T(8,128)S(1)}, f32[2,64,256]{2,1,0:T(8,128)S(1)}, u32[]{:S(2)}, u32[]{:S(2)}) collective-permute-start(f32[2,64,256]{2,1,0:T(8,128)S(1)} %pad_maximum_fusion.3), channel_id=1, source_target_pairs={{0,4},{1,5},{2,6},{3,7},{4,0},{5,1},{6,2},{7,3},{8,12},{9,13},{10,... | collective-permute-start | bytes 393224 | tf_op jit(solution)/shard_map/ppermute | solution.py:145
  27.7 18.6 %copy-start = (f32[2,1,128,128]{3,2,1,0:T(8,128)S(1)}, f32[2,1,128,128]{3,2,1,0:T(8,128)}, u32[]{:S(2)}) copy-start(f32[2,1,128,128]{3,2,1,0:T(8,128)} %param.12) | copy-start | bytes 393220
  46.1 1.3 %copy-start.1 = (f32[2,16,256]{2,1,0:T(8,128)S(1)}, f32[2,16,256]{2,1,0:T(8,128)}, u32[]{:S(2)}) copy-start(f32[2,16,256]{2,1,0:T(8,128)} %get-tuple-element.8) | copy-start | bytes 98308
  46.1 1.3 %copy-start.2 = (f32[2,256]{1,0:T(2,128)S(1)}, f32[2,256]{1,0:T(2,128)}, u32[]{:S(2)}) copy-start(f32[2,256]{1,0:T(2,128)} %param.15) | copy-start | bytes 6148
  46.1 1.3 %copy-start.3 = (f32[2,256]{1,0:T(2,128)S(1)}, f32[2,256]{1,0:T(2,128)}, u32[]{:S(2)}) copy-start(f32[2,256]{1,0:T(2,128)} %param.14) | copy-start | bytes 6148
  47.5 3.4 %collective-permute-start.8 = (f32[3,2,16,256]{3,2,1,0:T(8,128)S(1)}, f32[3,2,16,256]{3,2,1,0:T(8,128)S(1)}, u32[]{:S(2)}, u32[]{:S(2)}) collective-permute-start(f32[3,2,16,256]{3,2,1,0:T(8,128)S(1)} %pad_maximum_fusion.4), channel_id=1, source_target_pairs={{0,8},{8,0},{16,24},{24,16},{32,40},{40,32},{48,56},{56,48},{64,72... | collective-permute-start | bytes 294920 | tf_op jit(solution)/shard_map/ppermute | solution.py:145
  51.0 12.5 %collective-permute-start.10 = (f32[3,2,16,256]{3,2,1,0:T(8,128)S(1)}, f32[3,2,16,256]{3,2,1,0:T(8,128)S(1)}, u32[]{:S(2)}, u32[]{:S(2)}) collective-permute-start(f32[3,2,16,256]{3,2,1,0:T(8,128)S(1)} %pad_maximum_fusion.5), channel_id=1, source_target_pairs={{0,48},{8,56},{16,0},{24,8},{32,16},{40,24},{48,32},{56,40},{64,11... | collective-permute-start | bytes 294920 | tf_op jit(solution)/shard_map/ppermute | solution.py:145
  57.5 10.9 %collective-permute-start.11 = (f32[3,2,16,256]{3,2,1,0:T(8,128)S(1)}, f32[3,2,16,256]{3,2,1,0:T(8,128)S(1)}, u32[]{:S(2)}, u32[]{:S(2)}) collective-permute-start(f32[3,2,16,256]{3,2,1,0:T(8,128)S(1)} %pad_maximum_fusion.5), channel_id=1, source_target_pairs={{0,32},{8,40},{16,48},{24,56},{32,0},{40,8},{48,16},{56,24},{64,96... | collective-permute-start | bytes 294920 | tf_op jit(solution)/shard_map/ppermute | solution.py:145
  58.9 10.7 %collective-permute-start.9 = (f32[3,2,16,256]{3,2,1,0:T(8,128)S(1)}, f32[3,2,16,256]{3,2,1,0:T(8,128)S(1)}, u32[]{:S(2)}, u32[]{:S(2)}) collective-permute-start(f32[3,2,16,256]{3,2,1,0:T(8,128)S(1)} %pad_maximum_fusion.5), channel_id=1, source_target_pairs={{0,16},{8,24},{16,32},{24,40},{32,48},{40,56},{48,0},{56,8},{64,80... | collective-permute-start | bytes 294920 | tf_op jit(solution)/shard_map/ppermute | solution.py:145
  69.7 8.2 %collective-permute-start.12 = (f32[3,2,16,256]{3,2,1,0:T(8,128)S(1)}, f32[3,2,16,256]{3,2,1,0:T(8,128)S(1)}, u32[]{:S(2)}, u32[]{:S(2)}) collective-permute-start(f32[3,2,16,256]{3,2,1,0:T(8,128)S(1)} %pad_maximum_fusion.6), channel_id=1, source_target_pairs={{0,64},{8,72},{16,80},{24,88},{32,96},{40,104},{48,112},{56,120},{... | collective-permute-start | bytes 294920 | tf_op jit(solution)/shard_map/ppermute | solution.py:145
  71.0 6.9 %collective-permute-start.13 = (f32[3,2,16,256]{3,2,1,0:T(8,128)S(1)}, f32[3,2,16,256]{3,2,1,0:T(8,128)S(1)}, u32[]{:S(2)}, u32[]{:S(2)}) collective-permute-start(f32[3,2,16,256]{3,2,1,0:T(8,128)S(1)} %pad_maximum_fusion.6), channel_id=1, source_target_pairs={{0,192},{8,200},{16,208},{24,216},{32,224},{40,232},{48,240},{56,2... | collective-permute-start | bytes 294920 | tf_op jit(solution)/shard_map/ppermute | solution.py:145
  73.0 6.1 %collective-permute-start.14 = (f32[3,2,16,256]{3,2,1,0:T(8,128)S(1)}, f32[3,2,16,256]{3,2,1,0:T(8,128)S(1)}, u32[]{:S(2)}, u32[]{:S(2)}) collective-permute-start(f32[3,2,16,256]{3,2,1,0:T(8,128)S(1)} %pad_maximum_fusion.6), channel_id=1, source_target_pairs={{0,128},{8,136},{16,144},{24,152},{32,160},{40,168},{48,176},{56,1... | collective-permute-start | bytes 294920 | tf_op jit(solution)/shard_map/ppermute | solution.py:145
  75.0 4.3 %copy-start.4 = (f32[2,1,128]{2,1,0:T(1,128)S(1)}, f32[2,1,128]{2,1,0:T(1,128)}, u32[]{:S(2)}) copy-start(f32[2,1,128]{2,1,0:T(1,128)} %param.13) | copy-start | bytes 3076

commit v13 on v12

--- a/solution.py
+++ b/solution.py
@@ -16,7 +16,7 @@
 
 def explicit_kernel(planes, rows, width,
                     s_ref, head_ref, tail_ref, diff_ref, rate_ref, inv_ref,
-                    out_ref, exit_ref, ex_ref):
+                    out_ref, exit_ref, rows_ref, ex_ref):
     row = lax.broadcasted_iota(jnp.int32, (rows, width), 0)
     lane = lax.broadcasted_iota(jnp.int32, (rows, width), 1)
 
@@ -53,6 +53,10 @@
             laps.append(lap)
         start = j * rows if isinstance(j, int) else pl.multiple_of(j * rows, rows)
         d = diff_ref[pl.ds(start, rows), :]
+        low, high = d[:8], d[rows - 8:]
+        edge = jnp.where(row[:8] < 2, low, pltpu.roll(high, 4, 0))
+        edge_start = j * 8 if isinstance(j, int) else pl.multiple_of(j * 8, 8)
+        rows_ref[pl.ds(edge_start, 8), :] = edge
         reaction = rate_ref[pl.ds(start, rows), :] * softplus(centers[0]) * softplus(centers[1])
         for s in range(2):
             value = centers[s] + d * laps[s] + reaction_yields[s] * reaction
@@ -101,14 +105,15 @@
     species, planes, rows, width = scalars.shape
     flat = lambda a: a.reshape(a.shape[:-3] + (a.shape[-3] * rows, width))
     vmem = pl.BlockSpec(memory_space=pltpu.VMEM)
-    out, exit_plane = pl.pallas_call(
+    out, exit_plane, edge_rows = pl.pallas_call(
         functools.partial(explicit_kernel, planes, rows, width),
         out_shape=(
             jax.ShapeDtypeStruct((species, planes * rows, width), jnp.float32),
             jax.ShapeDtypeStruct((species, rows, width), jnp.float32),
+            jax.ShapeDtypeStruct((planes * 8, width), jnp.float32),
         ),
         in_specs=[vmem] * 6,
-        out_specs=(vmem, vmem),
+        out_specs=(vmem, vmem, vmem),
         scratch_shapes=[pltpu.VMEM((species, width // 128, planes * rows, 128), jnp.float32)],
         compiler_params=pltpu.CompilerParams(vmem_limit_bytes=60 * 1024 * 1024),
         cost_estimate=pl.CostEstimate(
@@ -117,7 +122,7 @@
             bytes_accessed=4 * (3 * species + 2) * planes * rows * width,
         ),
     )(flat(scalars), flat(head), flat(tail), flat(diffusivity), flat(reaction_rate), inverse)
-    return out.reshape(scalars.shape), exit_plane
+    return out.reshape(scalars.shape), exit_plane, edge_rows.reshape(planes, 8, width)
 
 
 def digit_levels(devices, radices):
@@ -239,17 +244,17 @@
     response = block_response[:, 0]
     first_gain = jnp.where(at_inlet, diffusivity[0] * (15.0 / 12.0), 0.0)
     second_gain = jnp.where(at_inlet, diffusivity[1] * (-1.0 / 12.0), 0.0)
-    local_part, exit_plane = explicit_local(
+    local_part, exit_plane, edge_diffusivity = explicit_local(
         scalars, head_planes, tail_planes, diffusivity, reaction_rate, inverse
     )
     b0, b1 = before_rows[:, :, 0], before_rows[:, :, 1]
     a0, a1 = after_rows[:, :, 0], after_rows[:, :, 1]
     edge_terms = jnp.stack(
         [
-            diffusivity[:, 0] * (16.0 * b1 - b0) * (1.0 / 12.0),
-            diffusivity[:, 1] * -b1 * (1.0 / 12.0),
-            diffusivity[:, span_cells - 2] * -a0 * (1.0 / 12.0),
-            diffusivity[:, span_cells - 1] * (16.0 * a0 - a1) * (1.0 / 12.0),
+            edge_diffusivity[:, 0] * (16.0 * b1 - b0) * (1.0 / 12.0),
+            edge_diffusivity[:, 1] * -b1 * (1.0 / 12.0),
+            edge_diffusivity[:, 2] * -a0 * (1.0 / 12.0),
+            edge_diffusivity[:, 3] * (16.0 * a0 - a1) * (1.0 / 12.0),
         ],
         axis=1,
     )

time: 82.3 us -> 83.3 us (1.012)
  transfers between devices with their start and end apart: 15 -> 15, of which waited for: 4 -> 4; matrix products, arithmetic and copies ran while one was open for 20% -> 20% of each run, Pallas kernels for 22% -> 23%
where the time goes in v13:
time: 83.3 us; the launch traced here: 82.9 us
  starting transfers between devices  29.8 us (36%)
  Pallas kernels  18.9 us (23%)
  local copies, waits for them, and re-layouts  11.6 us (14%)
  waiting for transfers between devices  10.6 us (13%)
  other arithmetic  8.14 us (10%)
  matrix products  2 us (2%)
  between operations  1.85 us (2%)
    ppermute x11, starting transfers between devices, digit_exchange(): received[shift] = lax.ppermute(x, axis, pairs)  21.3 us
    pallas_call x1, Pallas kernels, explicit_local(): pl.pallas_call(functools.partial(explicit_kernel, planes, rows, width), o...  18.9 us
    ppermute x11, waiting for transfers between devices, digit_exchange(): received[shift] = lax.ppermute(x, axis, pairs)  10.6 us
    ppermute x4, starting transfers between devices, halos(): return (lax.ppermute(last, axis, up), lax.ppermute(first, axis, down))  8.49 us
    add x1, other arithmetic, on_device(): settled, = lax.optimization_barrier((local_part + edge_part,))  2.95 us
    slice x1, local copies, waits for them, and re-layouts, on_device(): edge_diffusivity[:, 0] * (16.0 * b1 - b0) * (1.0 / 12.0)  2.9 us
    slice x1, local copies, waits for them, and re-layouts, halos(): last = lax.slice_in_dim(x, length - width, length, axis=dim)  2.59 us
    add x1, other arithmetic, on_device(): settled + response[:, :, None, None] * incoming[:, None]  2.55 us
  transfers between devices with their start and end apart: 15, of which 4 were waited for; matrix products, arithmetic and copies ran while one was open for 20% of the time, Pallas kernels for 23%

profile of v13, /device:TPU:32, one launch (start us, length us, event | category | flops | bytes accessed | tf_op | source)
XLA Modules:
  0.0 82.9 jit_solution(9963157647716323617)
XLA Ops:
  0.7 0.8 dynamic-slice_bitcast_fusion
  1.5 2.8 %collective-permute-start.4 = (f32[2,16,256]{2,1,0:T(8,128)S(1)}, f32[2,16,256]{2,1,0:T(8,128)S(1)}, u32[]{:S(2)}, u32[]{:S(2)}) collective-permute-start(f32[2,16,256]{2,1,0:T(8,128)S(1)} %get-tuple-element.21), channel_id=1, source_target_pairs={{0,3},{1,0},{2,1},{3,2},{4,7},{5,4},{6,5},{7,6},{8,11},{9,8},{10,9... | collective-permute-start | bytes 98312 | tf_op jit(solution)/shard_map/ppermute | solution.py:150
  4.2 0.8 collective-permute-start.5
  5.0 0.9 %collective-permute-start.6 = (f32[2,16,256]{2,1,0:T(8,128)S(1)}, f32[2,16,256]{2,1,0:T(8,128)S(1)}, u32[]{:S(2)}, u32[]{:S(2)}) collective-permute-start(f32[2,16,256]{2,1,0:T(8,128)S(1)} %get-tuple-element.21), channel_id=1, source_target_pairs={{0,1},{1,2},{2,3},{3,0},{4,5},{5,6},{6,7},{7,4},{8,9},{9,10},{10,1... | collective-permute-start | bytes 98312 | tf_op jit(solution)/shard_map/ppermute | solution.py:150
  5.9 0.9 %fusion.35 = (f32[2,2,16,256]{3,2,1,0:T(8,128)S(1)}, f32[2,2,16,256]{3,2,1,0:T(8,128)S(1)}) fusion(f32[2,128,16,256]{3,2,1,0:T(8,128)} %param.9), kind=kLoop, calls=%fused_computation.116 | loop fusion | bytes 262144 | tf_op jit(solution)/shard_map/slice | solution.py:202
  6.8 1.3 %collective-permute-start.1 = (f32[2,2,16,256]{3,2,1,0:T(8,128)S(1)}, f32[2,2,16,256]{3,2,1,0:T(8,128)S(1)}, u32[]{:S(2)}, u32[]{:S(2)}) collective-permute-start(f32[2,2,16,256]{3,2,1,0:T(8,128)S(1)} %get-tuple-element.25), channel_id=1, source_target_pairs={{8,0},{16,8},{24,16},{32,24},{40,32},{48,40},{56,48},{64,56},{72,6... | collective-permute-start | bytes 196616 | tf_op jit(solution)/shard_map/ppermute | solution.py:203
  8.1 3.0 %collective-permute-start = (f32[2,2,16,256]{3,2,1,0:T(8,128)S(1)}, f32[2,2,16,256]{3,2,1,0:T(8,128)S(1)}, u32[]{:S(2)}, u32[]{:S(2)}) collective-permute-start(f32[2,2,16,256]{3,2,1,0:T(8,128)S(1)} %get-tuple-element.26), channel_id=1, source_target_pairs={{0,8},{8,16},{16,24},{24,32},{32,40},{40,48},{48,56},{56,64},{64,7... | collective-permute-start | bytes 196616 | tf_op jit(solution)/shard_map/ppermute | solution.py:203
  11.1 2.6 %fusion.34 = (f32[2,128,2,256]{3,2,1,0:T(2,128)S(1)}, f32[2,128,2,256]{3,2,1,0:T(2,128)S(1)}) fusion(f32[2,128,16,256]{3,2,1,0:T(8,128)} %param.9), kind=kLoop, calls=%fused_computation.115 | loop fusion | bytes 2097152 | tf_op jit(solution)/shard_map/slice | solution.py:201
  13.7 0.9 %slice_reduce_fusion.3 = (f32[2]{0:T(128)S(1)}, f32[2]{0:T(128)S(1)}) fusion(f32[2,128,128]{2,1,0:T(8,128)} %bitcast.195), kind=kLoop, calls=%fused_computation.109 | loop fusion | bytes 32 | tf_op jit(solution)/shard_map/slice | solution.py:273
  14.7 0.9 %slice_reduce_fusion.4 = f32[2]{0:T(128)S(1)} fusion(f32[2,128]{1,0:T(2,128)} %bitcast.208), kind=kLoop, calls=%fused_computation.110 | loop fusion | bytes 16 | tf_op jit(solution)/shard_map/slice | solution.py:272
  15.5 0.7 select_bitcast_fusion.2
  16.4 1.2 %slice_reduce_fusion.1 = (f32[2,128]{1,0:T(2,128)S(1)}, f32[2,128]{1,0:T(2,128)S(1)}) fusion(f32[2,128,128]{2,1,0:T(8,128)} %bitcast.196), kind=kLoop, calls=%fused_computation.25 | loop fusion | bytes 4096 | tf_op jit(solution)/shard_map/slice | solution.py:286
  18.9 1.8 %collective-permute-start.2 = (f32[2,128,2,256]{1,3,0,2:T(8,128)S(1)}, f32[2,128,2,256]{1,3,0,2:T(8,128)S(1)}, u32[]{:S(2)}, u32[]{:S(2)}) collective-permute-start(f32[2,128,2,256]{1,3,0,2:T(8,128)S(1)} %copy.43), channel_id=1, source_target_pairs={{0,1},{1,2},{2,3},{3,4},{4,5},{5,6},{6,7},{7,0},{8,9},{9,10},{10,1... | collective-permute-start | bytes 1572872 | tf_op jit(solution)/shard_map/ppermute | solution.py:203
  20.7 2.3 %collective-permute-start.3 = (f32[2,128,2,256]{1,3,0,2:T(8,128)S(1)}, f32[2,128,2,256]{1,3,0,2:T(8,128)S(1)}, u32[]{:S(2)}, u32[]{:S(2)}) collective-permute-start(f32[2,128,2,256]{1,3,0,2:T(8,128)S(1)} %copy.44), channel_id=1, source_target_pairs={{1,0},{2,1},{3,2},{4,3},{5,4},{6,5},{7,6},{0,7},{9,8},{10,9},{11,1... | collective-permute-start | bytes 1572872 | tf_op jit(solution)/shard_map/ppermute | solution.py:203
  24.1 0.6 broadcast_select_fusion.4
  24.7 18.9 %shard_map.91 = (f32[2,2048,256]{2,1,0:T(8,128)}, f32[2,16,256]{2,1,0:T(8,128)}, f32[1024,256]{1,0:T(8,128)}) custom-call(f32[2,2048,256]{2,1,0:T(8,128)} %bitcast.192, f32[2,32,256]{2,1,0:T(8,128)} %bitcast.204, f32[2,32,256]{2,1,0:T(8,128)} %bitcast.205, f32[2048,256]{1,0:T(8,128)} %bitcast.194, f32[2048,256]{1,0:T(8,128)} %bitcast.199, ...), custom_call_target="tpu_custom_call" | custom-call | flops 331350016 | bytes 16777216 | tf_op jit(solution)/shard_map/pallas_call | solution.py:108
  43.6 2.9 %fusion.37 = (f32[128,1,256]{2,1,0:T(1,128)S(1)}, f32[128,1,256]{2,1,0:T(1,128)S(1)}, f32[128,1,256]{2,1,0:T(1,128)S(1)}, f32[128,1,256]{2,1,0:T(1,128)S(1)}) fusion(f32[128,8,256]{2,1,0:T(8,128)} %bitcast.206), kind=kLoop, calls=%fused_computation.118 | loop fusion | bytes 1048576 | tf_op jit(solution)/shard_map/slice | solution.py:254
  47.2 1.0 %fusion = f32[2,1,4,256]{3,1,2,0:T(1,128)S(1)} fusion(f32[2,1,128,256]{2,3,1,0:T(8,128)S(1)} %get-tuple-element.38, f32[2,1,128,256]{2,3,1,0:T(8,128)S(1)} %get-tuple-element.37, f32[2,1,128,256]{2,3,1,0:T(8,128)S(1)} %get-tuple-element.36, f32[2,1,128,256]{2,3,1,0:T(8,128)S(1)} %get-tuple-element.35, f32[2,128,128]{2,1,0:T(8,128)S(1)} %bitcast.198), kind=kOutput, calls=%fused_computation.4 | convolution fusion | flops 3932160 | bytes 1057792 | tf_op jit(solution)/shard_map/sj,skjy->sky/dot_general | solution.py:261
  48.3 2.3 %collective-permute-start.8 = (f32[3,2,16,256]{3,2,1,0:T(8,128)S(1)}, f32[3,2,16,256]{3,2,1,0:T(8,128)S(1)}, u32[]{:S(2)}, u32[]{:S(2)}) collective-permute-start(f32[3,2,16,256]{3,2,1,0:T(8,128)S(1)} %pad_maximum_fusion.4), channel_id=1, source_target_pairs={{0,8},{8,0},{16,24},{24,16},{32,40},{40,32},{48,56},{56,48},{64,72... | collective-permute-start | bytes 294920 | tf_op jit(solution)/shard_map/ppermute | solution.py:150
  50.7 1.0 %convolution_bitcast_fusion = f32[2,128,4,256]{1,3,2,0:T(8,128)S(1)} fusion(f32[2,1,128,256]{2,3,1,0:T(8,128)S(1)} %get-tuple-element.38, f32[2,1,128,256]{2,3,1,0:T(8,128)S(1)} %get-tuple-element.37, f32[2,1,128,256]{2,3,1,0:T(8,128)S(1)} %get-tuple-element.36, f32[2,1,128,256]{2,3,1,0:T(8,128)S(1)} %get-tuple-element.35, f32[2,1,128,128]{3,2,1,0:T(8,128)S(1)} %copy-done), kind=kOutput, calls=%fused_computation.2 | convolution fusion | flops 403439616 | bytes 2228224 | tf_op jit(solution)/shard_map/sij,skjy->siky/dot_general | solution.py:266
  51.8 6.5 %collective-permute-start.10 = (f32[3,2,16,256]{3,2,1,0:T(8,128)S(1)}, f32[3,2,16,256]{3,2,1,0:T(8,128)S(1)}, u32[]{:S(2)}, u32[]{:S(2)}) collective-permute-start(f32[3,2,16,256]{3,2,1,0:T(8,128)S(1)} %pad_maximum_fusion.5), channel_id=1, source_target_pairs={{0,48},{8,56},{16,0},{24,8},{32,16},{40,24},{48,32},{56,40},{64,11... | collective-permute-start | bytes 294920 | tf_op jit(solution)/shard_map/ppermute | solution.py:150
  58.3 1.4 %collective-permute-start.11 = (f32[3,2,16,256]{3,2,1,0:T(8,128)S(1)}, f32[3,2,16,256]{3,2,1,0:T(8,128)S(1)}, u32[]{:S(2)}, u32[]{:S(2)}) collective-permute-start(f32[3,2,16,256]{3,2,1,0:T(8,128)S(1)} %pad_maximum_fusion.5), channel_id=1, source_target_pairs={{0,32},{8,40},{16,48},{24,56},{32,0},{40,8},{48,16},{56,24},{64,96... | collective-permute-start | bytes 294920 | tf_op jit(solution)/shard_map/ppermute | solution.py:150
  59.7 1.1 %collective-permute-start.9 = (f32[3,2,16,256]{3,2,1,0:T(8,128)S(1)}, f32[3,2,16,256]{3,2,1,0:T(8,128)S(1)}, u32[]{:S(2)}, u32[]{:S(2)}) collective-permute-start(f32[3,2,16,256]{3,2,1,0:T(8,128)S(1)} %pad_maximum_fusion.5), channel_id=1, source_target_pairs={{0,16},{8,24},{16,32},{24,40},{32,48},{40,56},{48,0},{56,8},{64,80... | collective-permute-start | bytes 294920 | tf_op jit(solution)/shard_map/ppermute | solution.py:150
  61.3 3.0 %collective-permute-done.10 = f32[3,2,16,256]{3,2,1,0:T(8,128)S(1)} collective-permute-done((f32[3,2,16,256]{3,2,1,0:T(8,128)S(1)}, f32[3,2,16,256]{3,2,1,0:T(8,128)S(1)}, u32[]{:S(2)}, u32[]{:S(2)}) %collective-permute-start.10) | collective-permute-done | bytes 98336 | tf_op jit(solution)/shard_map/ppermute | solution.py:150
  64.3 4.9 %collective-permute-done.11 = f32[3,2,16,256]{3,2,1,0:T(8,128)S(1)} collective-permute-done((f32[3,2,16,256]{3,2,1,0:T(8,128)S(1)}, f32[3,2,16,256]{3,2,1,0:T(8,128)S(1)}, u32[]{:S(2)}, u32[]{:S(2)}) %collective-permute-start.11) | collective-permute-done | bytes 98336 | tf_op jit(solution)/shard_map/ppermute | solution.py:150
  69.2 1.2 %collective-permute-done.9 = f32[3,2,16,256]{3,2,1,0:T(8,128)S(1)} collective-permute-done((f32[3,2,16,256]{3,2,1,0:T(8,128)S(1)}, f32[3,2,16,256]{3,2,1,0:T(8,128)S(1)}, u32[]{:S(2)}, u32[]{:S(2)}) %collective-permute-start.9) | collective-permute-done | bytes 98336 | tf_op jit(solution)/shard_map/ppermute | solution.py:150
  70.5 1.5 %collective-permute-start.12 = (f32[3,2,16,256]{3,2,1,0:T(8,128)S(1)}, f32[3,2,16,256]{3,2,1,0:T(8,128)S(1)}, u32[]{:S(2)}, u32[]{:S(2)}) collective-permute-start(f32[3,2,16,256]{3,2,1,0:T(8,128)S(1)} %pad_maximum_fusion.6), channel_id=1, source_target_pairs={{0,64},{8,72},{16,80},{24,88},{32,96},{40,104},{48,112},{56,120},{... | collective-permute-start | bytes 294920 | tf_op jit(solution)/shard_map/ppermute | solution.py:150
  72.1 2.0 %collective-permute-start.13 = (f32[3,2,16,256]{3,2,1,0:T(8,128)S(1)}, f32[3,2,16,256]{3,2,1,0:T(8,128)S(1)}, u32[]{:S(2)}, u32[]{:S(2)}) collective-permute-start(f32[3,2,16,256]{3,2,1,0:T(8,128)S(1)} %pad_maximum_fusion.6), channel_id=1, source_target_pairs={{0,192},{8,200},{16,208},{24,216},{32,224},{40,232},{48,240},{56,2... | collective-permute-start | bytes 294920 | tf_op jit(solution)/shard_map/ppermute | solution.py:150
  74.1 1.7 %collective-permute-start.14 = (f32[3,2,16,256]{3,2,1,0:T(8,128)S(1)}, f32[3,2,16,256]{3,2,1,0:T(8,128)S(1)}, u32[]{:S(2)}, u32[]{:S(2)}) collective-permute-start(f32[3,2,16,256]{3,2,1,0:T(8,128)S(1)} %pad_maximum_fusion.6), channel_id=1, source_target_pairs={{0,128},{8,136},{16,144},{24,152},{32,160},{40,168},{48,176},{56,1... | collective-permute-start | bytes 294920 | tf_op jit(solution)/shard_map/ppermute | solution.py:150
  75.7 3.0 %maximum_add_fusion = f32[2,128,16,256]{3,2,1,0:T(8,128)S(1)} fusion(f32[2,128,16,256]{3,2,1,0:T(8,128)} %bitcast.193, f32[2,128,2,256]{3,2,1,0:T(2,128)S(1)} %copy.35, f32[2,128,2,256]{3,2,1,0:T(2,128)S(1)} %copy.34, f32[16]{0:T(128)S(1)} %pad.21.clone), kind=kLoop, calls=%fused_computation | loop fusion | flops 3145728 | bytes 9437248 | tf_op jit(solution)/shard_map/add | solution.py:282
  78.7 1.5 %collective-permute-done.14 = f32[3,2,16,256]{3,2,1,0:T(8,128)S(1)} collective-permute-done((f32[3,2,16,256]{3,2,1,0:T(8,128)S(1)}, f32[3,2,16,256]{3,2,1,0:T(8,128)S(1)}, u32[]{:S(2)}, u32[]{:S(2)}) %collective-permute-start.14) | collective-permute-done | bytes 98336 | tf_op jit(solution)/shard_map/ppermute | solution.py:150
  80.4 2.5 %multiply_add_fusion = f32[2,128,16,256]{3,2,1,0:T(8,128)} fusion(f32[2,128,16,256]{3,2,1,0:T(8,128)S(1)} %maximum_add_fusion, f32[2,16,256]{2,1,0:T(8,128)S(1)} %get-tuple-element.61, f32[2,128]{1,0:T(2,128)S(1)} %get-tuple-element.12, f32[2,16,256]{2,1,0:T(8,128)S(1)} %get-tuple-element.60, f32[2,128]{1,0:T(2,128)S(1)} %get-tuple-element.11, ...), kind=kLoop, calls=%fused_computation.1 | loop fusion | flops 6291456 | bytes 8489984 | tf_op jit(solution)/shard_map/add | solution.py:284
  (54 shorter events, 3.1 us)
Async XLA Ops:
  1.5 17.4 %collective-permute-start.4 = (f32[2,16,256]{2,1,0:T(8,128)S(1)}, f32[2,16,256]{2,1,0:T(8,128)S(1)}, u32[]{:S(2)}, u32[]{:S(2)}) collective-permute-start(f32[2,16,256]{2,1,0:T(8,128)S(1)} %get-tuple-element.21), channel_id=1, source_target_pairs={{0,3},{1,0},{2,1},{3,2},{4,7},{5,4},{6,5},{7,6},{8,11},{9,8},{10,9... | collective-permute-start | bytes 98312 | tf_op jit(solution)/shard_map/ppermute | solution.py:150
  4.2 16.5 %collective-permute-start.5 = (f32[2,16,256]{2,1,0:T(8,128)S(1)}, f32[2,16,256]{2,1,0:T(8,128)S(1)}, u32[]{:S(2)}, u32[]{:S(2)}) collective-permute-start(f32[2,16,256]{2,1,0:T(8,128)S(1)} %get-tuple-element.21), channel_id=1, source_target_pairs={{0,2},{1,3},{2,0},{3,1},{4,6},{5,7},{6,4},{7,5},{8,10},{9,11},{10,... | collective-permute-start | bytes 98312 | tf_op jit(solution)/shard_map/ppermute | solution.py:150
  5.0 18.0 %collective-permute-start.6 = (f32[2,16,256]{2,1,0:T(8,128)S(1)}, f32[2,16,256]{2,1,0:T(8,128)S(1)}, u32[]{:S(2)}, u32[]{:S(2)}) collective-permute-start(f32[2,16,256]{2,1,0:T(8,128)S(1)} %get-tuple-element.21), channel_id=1, source_target_pairs={{0,1},{1,2},{2,3},{3,0},{4,5},{5,6},{6,7},{7,4},{8,9},{9,10},{10,1... | collective-permute-start | bytes 98312 | tf_op jit(solution)/shard_map/ppermute | solution.py:150
  6.8 17.3 %collective-permute-start.1 = (f32[2,2,16,256]{3,2,1,0:T(8,128)S(1)}, f32[2,2,16,256]{3,2,1,0:T(8,128)S(1)}, u32[]{:S(2)}, u32[]{:S(2)}) collective-permute-start(f32[2,2,16,256]{3,2,1,0:T(8,128)S(1)} %get-tuple-element.25), channel_id=1, source_target_pairs={{8,0},{16,8},{24,16},{32,24},{40,32},{48,40},{56,48},{64,56},{72,6... | collective-permute-start | bytes 196616 | tf_op jit(solution)/shard_map/ppermute | solution.py:203
  8.1 15.4 %collective-permute-start = (f32[2,2,16,256]{3,2,1,0:T(8,128)S(1)}, f32[2,2,16,256]{3,2,1,0:T(8,128)S(1)}, u32[]{:S(2)}, u32[]{:S(2)}) collective-permute-start(f32[2,2,16,256]{3,2,1,0:T(8,128)S(1)} %get-tuple-element.26), channel_id=1, source_target_pairs={{0,8},{8,16},{16,24},{24,32},{32,40},{40,48},{48,56},{56,64},{64,7... | collective-permute-start | bytes 196616 | tf_op jit(solution)/shard_map/ppermute | solution.py:203
  18.9 28.2 %collective-permute-start.2 = (f32[2,128,2,256]{1,3,0,2:T(8,128)S(1)}, f32[2,128,2,256]{1,3,0,2:T(8,128)S(1)}, u32[]{:S(2)}, u32[]{:S(2)}) collective-permute-start(f32[2,128,2,256]{1,3,0,2:T(8,128)S(1)} %copy.43), channel_id=1, source_target_pairs={{0,1},{1,2},{2,3},{3,4},{4,5},{5,6},{6,7},{7,0},{8,9},{9,10},{10,1... | collective-permute-start | bytes 1572872 | tf_op jit(solution)/shard_map/ppermute | solution.py:203
  20.7 26.4 %collective-permute-start.3 = (f32[2,128,2,256]{1,3,0,2:T(8,128)S(1)}, f32[2,128,2,256]{1,3,0,2:T(8,128)S(1)}, u32[]{:S(2)}, u32[]{:S(2)}) collective-permute-start(f32[2,128,2,256]{1,3,0,2:T(8,128)S(1)} %copy.44), channel_id=1, source_target_pairs={{1,0},{2,1},{3,2},{4,3},{5,4},{6,5},{7,6},{0,7},{9,8},{10,9},{11,1... | collective-permute-start | bytes 1572872 | tf_op jit(solution)/shard_map/ppermute | solution.py:203
  23.1 23.9 %collective-permute-start.7 = (f32[2,64,256]{2,1,0:T(8,128)S(1)}, f32[2,64,256]{2,1,0:T(8,128)S(1)}, u32[]{:S(2)}, u32[]{:S(2)}) collective-permute-start(f32[2,64,256]{2,1,0:T(8,128)S(1)} %pad_maximum_fusion.3), channel_id=1, source_target_pairs={{0,4},{1,5},{2,6},{3,7},{4,0},{5,1},{6,2},{7,3},{8,12},{9,13},{10,... | collective-permute-start | bytes 393224 | tf_op jit(solution)/shard_map/ppermute | solution.py:150
  43.6 3.6 %copy-start = (f32[2,1,128,128]{3,2,1,0:T(8,128)S(1)}, f32[2,1,128,128]{3,2,1,0:T(8,128)}, u32[]{:S(2)}) copy-start(f32[2,1,128,128]{3,2,1,0:T(8,128)} %param.12) | copy-start | bytes 393220
  43.6 4.6 %copy-start.1 = (f32[2,16,256]{2,1,0:T(8,128)S(1)}, f32[2,16,256]{2,1,0:T(8,128)}, u32[]{:S(2)}) copy-start(f32[2,16,256]{2,1,0:T(8,128)} %get-tuple-element.10) | copy-start | bytes 98308
  43.6 4.6 %copy-start.2 = (f32[2,256]{1,0:T(2,128)S(1)}, f32[2,256]{1,0:T(2,128)}, u32[]{:S(2)}) copy-start(f32[2,256]{1,0:T(2,128)} %param.15) | copy-start | bytes 6148
  43.6 4.6 %copy-start.3 = (f32[2,256]{1,0:T(2,128)S(1)}, f32[2,256]{1,0:T(2,128)}, u32[]{:S(2)}) copy-start(f32[2,256]{1,0:T(2,128)} %param.14) | copy-start | bytes 6148
  48.3 3.4 %collective-permute-start.8 = (f32[3,2,16,256]{3,2,1,0:T(8,128)S(1)}, f32[3,2,16,256]{3,2,1,0:T(8,128)S(1)}, u32[]{:S(2)}, u32[]{:S(2)}) collective-permute-start(f32[3,2,16,256]{3,2,1,0:T(8,128)S(1)} %pad_maximum_fusion.4), channel_id=1, source_target_pairs={{0,8},{8,0},{16,24},{24,16},{32,40},{40,32},{48,56},{56,48},{64,72... | collective-permute-start | bytes 294920 | tf_op jit(solution)/shard_map/ppermute | solution.py:150
  51.8 12.6 %collective-permute-start.10 = (f32[3,2,16,256]{3,2,1,0:T(8,128)S(1)}, f32[3,2,16,256]{3,2,1,0:T(8,128)S(1)}, u32[]{:S(2)}, u32[]{:S(2)}) collective-permute-start(f32[3,2,16,256]{3,2,1,0:T(8,128)S(1)} %pad_maximum_fusion.5), channel_id=1, source_target_pairs={{0,48},{8,56},{16,0},{24,8},{32,16},{40,24},{48,32},{56,40},{64,11... | collective-permute-start | bytes 294920 | tf_op jit(solution)/shard_map/ppermute | solution.py:150
  58.3 10.9 %collective-permute-start.11 = (f32[3,2,16,256]{3,2,1,0:T(8,128)S(1)}, f32[3,2,16,256]{3,2,1,0:T(8,128)S(1)}, u32[]{:S(2)}, u32[]{:S(2)}) collective-permute-start(f32[3,2,16,256]{3,2,1,0:T(8,128)S(1)} %pad_maximum_fusion.5), channel_id=1, source_target_pairs={{0,32},{8,40},{16,48},{24,56},{32,0},{40,8},{48,16},{56,24},{64,96... | collective-permute-start | bytes 294920 | tf_op jit(solution)/shard_map/ppermute | solution.py:150
  59.7 10.7 %collective-permute-start.9 = (f32[3,2,16,256]{3,2,1,0:T(8,128)S(1)}, f32[3,2,16,256]{3,2,1,0:T(8,128)S(1)}, u32[]{:S(2)}, u32[]{:S(2)}) collective-permute-start(f32[3,2,16,256]{3,2,1,0:T(8,128)S(1)} %pad_maximum_fusion.5), channel_id=1, source_target_pairs={{0,16},{8,24},{16,32},{24,40},{32,48},{40,56},{48,0},{56,8},{64,80... | collective-permute-start | bytes 294920 | tf_op jit(solution)/shard_map/ppermute | solution.py:150
  70.5 8.2 %collective-permute-start.12 = (f32[3,2,16,256]{3,2,1,0:T(8,128)S(1)}, f32[3,2,16,256]{3,2,1,0:T(8,128)S(1)}, u32[]{:S(2)}, u32[]{:S(2)}) collective-permute-start(f32[3,2,16,256]{3,2,1,0:T(8,128)S(1)} %pad_maximum_fusion.6), channel_id=1, source_target_pairs={{0,64},{8,72},{16,80},{24,88},{32,96},{40,104},{48,112},{56,120},{... | collective-permute-start | bytes 294920 | tf_op jit(solution)/shard_map/ppermute | solution.py:150
  72.1 6.6 %collective-permute-start.13 = (f32[3,2,16,256]{3,2,1,0:T(8,128)S(1)}, f32[3,2,16,256]{3,2,1,0:T(8,128)S(1)}, u32[]{:S(2)}, u32[]{:S(2)}) collective-permute-start(f32[3,2,16,256]{3,2,1,0:T(8,128)S(1)} %pad_maximum_fusion.6), channel_id=1, source_target_pairs={{0,192},{8,200},{16,208},{24,216},{32,224},{40,232},{48,240},{56,2... | collective-permute-start | bytes 294920 | tf_op jit(solution)/shard_map/ppermute | solution.py:150
  74.1 6.1 %collective-permute-start.14 = (f32[3,2,16,256]{3,2,1,0:T(8,128)S(1)}, f32[3,2,16,256]{3,2,1,0:T(8,128)S(1)}, u32[]{:S(2)}, u32[]{:S(2)}) collective-permute-start(f32[3,2,16,256]{3,2,1,0:T(8,128)S(1)} %pad_maximum_fusion.6), channel_id=1, source_target_pairs={{0,128},{8,136},{16,144},{24,152},{32,160},{40,168},{48,176},{56,1... | collective-permute-start | bytes 294920 | tf_op jit(solution)/shard_map/ppermute | solution.py:150
  75.7 4.6 %copy-start.4 = (f32[2,1,128]{2,1,0:T(1,128)S(1)}, f32[2,1,128]{2,1,0:T(1,128)}, u32[]{:S(2)}) copy-start(f32[2,1,128]{2,1,0:T(1,128)} %param.13) | copy-start | bytes 3076

commit v14 on v12

--- a/solution.py
+++ b/solution.py
@@ -16,7 +16,7 @@
 
 def explicit_kernel(planes, rows, width,
                     s_ref, head_ref, tail_ref, diff_ref, rate_ref, inv_ref,
-                    out_ref, exit_ref, ex_ref):
+                    out_ref, exit_ref, ex_ref, sems):
     row = lax.broadcasted_iota(jnp.int32, (rows, width), 0)
     lane = lax.broadcasted_iota(jnp.int32, (rows, width), 1)
 
@@ -70,6 +70,7 @@
     for j in (planes - 2, planes - 1):
         one_plane(j, j - 2, j - 1, j + 1, j + 2)
 
+    copies = []
     for s in range(2):
         inv = inv_ref[s]
         for h in range(width // 128):
@@ -84,17 +85,13 @@
 
             lax.fori_loop(0, rows, mm, 0, unroll=True)
             exit_ref[s, :, pl.ds(h * 128, 128)] = ex_ref[s, h, pl.ds((planes - 1) * rows, rows), :]
-
-    chunk = 8 * rows
-
-    def put(c, carry):
-        start = pl.multiple_of(c * chunk, chunk)
-        for s in range(2):
-            for h in range(width // 128):
-                out_ref[s, pl.ds(start, chunk), pl.ds(h * 128, 128)] = ex_ref[s, h, pl.ds(start, chunk), :]
-        return carry
-
-    lax.fori_loop(0, planes // 8, put, 0)
+            copy = pltpu.make_async_copy(
+                ex_ref.at[s, h], out_ref.at[s, :, pl.ds(h * 128, 128)], sems.at[len(copies)]
+            )
+            copy.start()
+            copies.append(copy)
+    for copy in copies:
+        copy.wait()
 
 
 def explicit_local(scalars, head, tail, diffusivity, reaction_rate, inverse):
@@ -108,8 +105,11 @@
             jax.ShapeDtypeStruct((species, rows, width), jnp.float32),
         ),
         in_specs=[vmem] * 6,
-        out_specs=(vmem, vmem),
-        scratch_shapes=[pltpu.VMEM((species, width // 128, planes * rows, 128), jnp.float32)],
+        out_specs=(pl.BlockSpec(memory_space=pl.ANY), vmem),
+        scratch_shapes=[
+            pltpu.VMEM((species, width // 128, planes * rows, 128), jnp.float32),
+            pltpu.SemaphoreType.DMA((species * (width // 128),)),
+        ],
         compiler_params=pltpu.CompilerParams(vmem_limit_bytes=60 * 1024 * 1024),
         cost_estimate=pl.CostEstimate(
             flops=species * planes * rows * width * (2 * planes + 60),

time: 82.3 us -> 81.6 us (level)
  no operation moved by 1% of the time
where the time goes in v14:
time: 81.6 us; the launch traced here: 81.2 us
  starting transfers between devices  29.6 us (36%)
  Pallas kernels  17.7 us (22%)
  local copies, waits for them, and re-layouts  11.3 us (14%)
  waiting for transfers between devices  10.6 us (13%)
  other arithmetic  8.14 us (10%)
  matrix products  2 us (2%)
  between operations  1.86 us (2%)
    ppermute x11, starting transfers between devices, digit_exchange(): received[shift] = lax.ppermute(x, axis, pairs)  21.1 us
    pallas_call x1, Pallas kernels, explicit_local(): pl.pallas_call(functools.partial(explicit_kernel, planes, rows, width), o...  17.7 us
    ppermute x11, waiting for transfers between devices, digit_exchange(): received[shift] = lax.ppermute(x, axis, pairs)  10.6 us
    ppermute x4, starting transfers between devices, halos(): return (lax.ppermute(last, axis, up), lax.ppermute(first, axis, down))  8.49 us
    add x1, other arithmetic, on_device(): settled, = lax.optimization_barrier((local_part + edge_part,))  2.95 us
    slice x1, local copies, waits for them, and re-layouts, halos(): last = lax.slice_in_dim(x, length - width, length, axis=dim)  2.59 us
    slice x1, local copies, waits for them, and re-layouts, on_device(): diffusivity[:, 0] * (16.0 * b1 - b0) * (1.0 / 12.0)  2.58 us
    add x1, other arithmetic, on_device(): settled + response[:, :, None, None] * incoming[:, None]  2.54 us
  transfers between devices with their start and end apart: 15, of which 4 were waited for; matrix products, arithmetic and copies ran while one was open for 20% of the time, Pallas kernels for 22%

profile of v14, /device:TPU:32, one launch (start us, length us, event | category | flops | bytes accessed | tf_op | source)
XLA Modules:
  0.0 81.2 jit_solution(16167619830315102366)
XLA Ops:
  0.7 0.8 dynamic-slice_bitcast_fusion
  1.5 2.8 %collective-permute-start.4 = (f32[2,16,256]{2,1,0:T(8,128)S(1)}, f32[2,16,256]{2,1,0:T(8,128)S(1)}, u32[]{:S(2)}, u32[]{:S(2)}) collective-permute-start(f32[2,16,256]{2,1,0:T(8,128)S(1)} %get-tuple-element.19), channel_id=1, source_target_pairs={{0,3},{1,0},{2,1},{3,2},{4,7},{5,4},{6,5},{7,6},{8,11},{9,8},{10,9... | collective-permute-start | bytes 98312 | tf_op jit(solution)/shard_map/ppermute | solution.py:145
  4.2 0.8 collective-permute-start.5
  5.0 0.9 %collective-permute-start.6 = (f32[2,16,256]{2,1,0:T(8,128)S(1)}, f32[2,16,256]{2,1,0:T(8,128)S(1)}, u32[]{:S(2)}, u32[]{:S(2)}) collective-permute-start(f32[2,16,256]{2,1,0:T(8,128)S(1)} %get-tuple-element.19), channel_id=1, source_target_pairs={{0,1},{1,2},{2,3},{3,0},{4,5},{5,6},{6,7},{7,4},{8,9},{9,10},{10,1... | collective-permute-start | bytes 98312 | tf_op jit(solution)/shard_map/ppermute | solution.py:145
  5.9 0.9 %fusion.35 = (f32[2,2,16,256]{3,2,1,0:T(8,128)S(1)}, f32[2,2,16,256]{3,2,1,0:T(8,128)S(1)}) fusion(f32[2,128,16,256]{3,2,1,0:T(8,128)} %param.9), kind=kLoop, calls=%fused_computation.116 | loop fusion | bytes 262144 | tf_op jit(solution)/shard_map/slice | solution.py:197
  6.8 1.3 %collective-permute-start.1 = (f32[2,2,16,256]{3,2,1,0:T(8,128)S(1)}, f32[2,2,16,256]{3,2,1,0:T(8,128)S(1)}, u32[]{:S(2)}, u32[]{:S(2)}) collective-permute-start(f32[2,2,16,256]{3,2,1,0:T(8,128)S(1)} %get-tuple-element.23), channel_id=1, source_target_pairs={{8,0},{16,8},{24,16},{32,24},{40,32},{48,40},{56,48},{64,56},{72,6... | collective-permute-start | bytes 196616 | tf_op jit(solution)/shard_map/ppermute | solution.py:198
  8.1 3.0 %collective-permute-start = (f32[2,2,16,256]{3,2,1,0:T(8,128)S(1)}, f32[2,2,16,256]{3,2,1,0:T(8,128)S(1)}, u32[]{:S(2)}, u32[]{:S(2)}) collective-permute-start(f32[2,2,16,256]{3,2,1,0:T(8,128)S(1)} %get-tuple-element.24), channel_id=1, source_target_pairs={{0,8},{8,16},{16,24},{24,32},{32,40},{40,48},{48,56},{56,64},{64,7... | collective-permute-start | bytes 196616 | tf_op jit(solution)/shard_map/ppermute | solution.py:198
  11.1 2.6 %fusion.34 = (f32[2,128,2,256]{3,2,1,0:T(2,128)S(1)}, f32[2,128,2,256]{3,2,1,0:T(2,128)S(1)}) fusion(f32[2,128,16,256]{3,2,1,0:T(8,128)} %param.9), kind=kLoop, calls=%fused_computation.115 | loop fusion | bytes 2097152 | tf_op jit(solution)/shard_map/slice | solution.py:196
  13.7 2.6 %fusion.36 = (f32[128,1,256]{2,1,0:T(1,128)S(1)}, f32[128,1,256]{2,1,0:T(1,128)S(1)}, f32[128,1,256]{2,1,0:T(1,128)S(1)}, f32[128,1,256]{2,1,0:T(1,128)S(1)}) fusion(f32[128,16,256]{2,1,0:T(8,128)} %param.10), kind=kLoop, calls=%fused_computation.117 | loop fusion | bytes 1048576 | tf_op jit(solution)/shard_map/slice | solution.py:249
  16.3 0.7 select_bitcast_fusion.2
  17.1 0.9 %slice_reduce_fusion.3 = (f32[2]{0:T(128)S(1)}, f32[2]{0:T(128)S(1)}) fusion(f32[2,128,128]{2,1,0:T(8,128)} %bitcast.198), kind=kLoop, calls=%fused_computation.109 | loop fusion | bytes 32 | tf_op jit(solution)/shard_map/slice | solution.py:268
  18.0 0.9 %slice_reduce_fusion.4 = f32[2]{0:T(128)S(1)} fusion(f32[2,128]{1,0:T(2,128)} %bitcast.210), kind=kLoop, calls=%fused_computation.110 | loop fusion | bytes 16 | tf_op jit(solution)/shard_map/slice | solution.py:267
  19.0 1.2 %slice_reduce_fusion.1 = (f32[2,128]{1,0:T(2,128)S(1)}, f32[2,128]{1,0:T(2,128)S(1)}) fusion(f32[2,128,128]{2,1,0:T(8,128)} %bitcast.199), kind=kLoop, calls=%fused_computation.25 | loop fusion | bytes 4096 | tf_op jit(solution)/shard_map/slice | solution.py:281
  21.9 1.8 %collective-permute-start.2 = (f32[2,128,2,256]{1,3,0,2:T(8,128)S(1)}, f32[2,128,2,256]{1,3,0,2:T(8,128)S(1)}, u32[]{:S(2)}, u32[]{:S(2)}) collective-permute-start(f32[2,128,2,256]{1,3,0,2:T(8,128)S(1)} %copy.44), channel_id=1, source_target_pairs={{0,1},{1,2},{2,3},{3,4},{4,5},{5,6},{6,7},{7,0},{8,9},{9,10},{10,1... | collective-permute-start | bytes 1572872 | tf_op jit(solution)/shard_map/ppermute | solution.py:198
  23.7 2.3 %collective-permute-start.3 = (f32[2,128,2,256]{1,3,0,2:T(8,128)S(1)}, f32[2,128,2,256]{1,3,0,2:T(8,128)S(1)}, u32[]{:S(2)}, u32[]{:S(2)}) collective-permute-start(f32[2,128,2,256]{1,3,0,2:T(8,128)S(1)} %copy.47), channel_id=1, source_target_pairs={{1,0},{2,1},{3,2},{4,3},{5,4},{6,5},{7,6},{0,7},{9,8},{10,9},{11,1... | collective-permute-start | bytes 1572872 | tf_op jit(solution)/shard_map/ppermute | solution.py:198
  27.1 0.6 broadcast_select_fusion.5
  27.7 17.7 %shard_map.91 = (f32[2,2048,256]{2,1,0:T(8,128)}, f32[2,16,256]{2,1,0:T(8,128)}) custom-call(f32[2,2048,256]{2,1,0:T(8,128)} %bitcast.195, f32[2,32,256]{2,1,0:T(8,128)} %bitcast.208, f32[2,32,256]{2,1,0:T(8,128)} %bitcast.207, f32[2048,256]{1,0:T(8,128)} %bitcast.197, f32[2048,256]{1,0:T(8,128)} %bitcast.202, f32[2,128,128]{2,1,0:T(8,128)} %bitcast.200), custom_call_target="tpu_custom_call" | custom-call | flops 331350016 | bytes 16777216 | tf_op jit(solution)/shard_map/pallas_call | solution.py:101
  45.7 1.0 %fusion = f32[2,1,4,256]{3,1,2,0:T(1,128)S(1)} fusion(f32[2,1,128,256]{2,3,1,0:T(8,128)S(1)} %get-tuple-element.36, f32[2,1,128,256]{2,3,1,0:T(8,128)S(1)} %get-tuple-element.35, f32[2,1,128,256]{2,3,1,0:T(8,128)S(1)} %get-tuple-element.34, f32[2,1,128,256]{2,3,1,0:T(8,128)S(1)} %get-tuple-element.33, f32[2,128,128]{2,1,0:T(8,128)S(1)} %bitcast.201), kind=kOutput, calls=%fused_computation.4 | convolution fusion | flops 3932160 | bytes 1057792 | tf_op jit(solution)/shard_map/sj,skjy->sky/dot_general | solution.py:256
  46.9 2.3 %collective-permute-start.8 = (f32[3,2,16,256]{3,2,1,0:T(8,128)S(1)}, f32[3,2,16,256]{3,2,1,0:T(8,128)S(1)}, u32[]{:S(2)}, u32[]{:S(2)}) collective-permute-start(f32[3,2,16,256]{3,2,1,0:T(8,128)S(1)} %pad_maximum_fusion.4), channel_id=1, source_target_pairs={{0,8},{8,0},{16,24},{24,16},{32,40},{40,32},{48,56},{56,48},{64,72... | collective-permute-start | bytes 294920 | tf_op jit(solution)/shard_map/ppermute | solution.py:145
  49.2 1.0 %convolution_bitcast_fusion = f32[2,128,4,256]{1,3,2,0:T(8,128)S(1)} fusion(f32[2,1,128,256]{2,3,1,0:T(8,128)S(1)} %get-tuple-element.36, f32[2,1,128,256]{2,3,1,0:T(8,128)S(1)} %get-tuple-element.35, f32[2,1,128,256]{2,3,1,0:T(8,128)S(1)} %get-tuple-element.34, f32[2,1,128,256]{2,3,1,0:T(8,128)S(1)} %get-tuple-element.33, f32[2,1,128,128]{3,2,1,0:T(8,128)S(1)} %copy-done), kind=kOutput, calls=%fused_computation.2 | convolution fusion | flops 403439616 | bytes 2228224 | tf_op jit(solution)/shard_map/sij,skjy->siky/dot_general | solution.py:261
  50.3 6.5 %collective-permute-start.10 = (f32[3,2,16,256]{3,2,1,0:T(8,128)S(1)}, f32[3,2,16,256]{3,2,1,0:T(8,128)S(1)}, u32[]{:S(2)}, u32[]{:S(2)}) collective-permute-start(f32[3,2,16,256]{3,2,1,0:T(8,128)S(1)} %pad_maximum_fusion.5), channel_id=1, source_target_pairs={{0,48},{8,56},{16,0},{24,8},{32,16},{40,24},{48,32},{56,40},{64,11... | collective-permute-start | bytes 294920 | tf_op jit(solution)/shard_map/ppermute | solution.py:145
  56.8 1.4 %collective-permute-start.11 = (f32[3,2,16,256]{3,2,1,0:T(8,128)S(1)}, f32[3,2,16,256]{3,2,1,0:T(8,128)S(1)}, u32[]{:S(2)}, u32[]{:S(2)}) collective-permute-start(f32[3,2,16,256]{3,2,1,0:T(8,128)S(1)} %pad_maximum_fusion.5), channel_id=1, source_target_pairs={{0,32},{8,40},{16,48},{24,56},{32,0},{40,8},{48,16},{56,24},{64,96... | collective-permute-start | bytes 294920 | tf_op jit(solution)/shard_map/ppermute | solution.py:145
  58.2 1.1 %collective-permute-start.9 = (f32[3,2,16,256]{3,2,1,0:T(8,128)S(1)}, f32[3,2,16,256]{3,2,1,0:T(8,128)S(1)}, u32[]{:S(2)}, u32[]{:S(2)}) collective-permute-start(f32[3,2,16,256]{3,2,1,0:T(8,128)S(1)} %pad_maximum_fusion.5), channel_id=1, source_target_pairs={{0,16},{8,24},{16,32},{24,40},{32,48},{40,56},{48,0},{56,8},{64,80... | collective-permute-start | bytes 294920 | tf_op jit(solution)/shard_map/ppermute | solution.py:145
  59.8 3.0 %collective-permute-done.10 = f32[3,2,16,256]{3,2,1,0:T(8,128)S(1)} collective-permute-done((f32[3,2,16,256]{3,2,1,0:T(8,128)S(1)}, f32[3,2,16,256]{3,2,1,0:T(8,128)S(1)}, u32[]{:S(2)}, u32[]{:S(2)}) %collective-permute-start.10) | collective-permute-done | bytes 98336 | tf_op jit(solution)/shard_map/ppermute | solution.py:145
  62.8 4.9 %collective-permute-done.11 = f32[3,2,16,256]{3,2,1,0:T(8,128)S(1)} collective-permute-done((f32[3,2,16,256]{3,2,1,0:T(8,128)S(1)}, f32[3,2,16,256]{3,2,1,0:T(8,128)S(1)}, u32[]{:S(2)}, u32[]{:S(2)}) %collective-permute-start.11) | collective-permute-done | bytes 98336 | tf_op jit(solution)/shard_map/ppermute | solution.py:145
  67.7 1.2 %collective-permute-done.9 = f32[3,2,16,256]{3,2,1,0:T(8,128)S(1)} collective-permute-done((f32[3,2,16,256]{3,2,1,0:T(8,128)S(1)}, f32[3,2,16,256]{3,2,1,0:T(8,128)S(1)}, u32[]{:S(2)}, u32[]{:S(2)}) %collective-permute-start.9) | collective-permute-done | bytes 98336 | tf_op jit(solution)/shard_map/ppermute | solution.py:145
  69.1 1.3 %collective-permute-start.12 = (f32[3,2,16,256]{3,2,1,0:T(8,128)S(1)}, f32[3,2,16,256]{3,2,1,0:T(8,128)S(1)}, u32[]{:S(2)}, u32[]{:S(2)}) collective-permute-start(f32[3,2,16,256]{3,2,1,0:T(8,128)S(1)} %pad_maximum_fusion.6), channel_id=1, source_target_pairs={{0,64},{8,72},{16,80},{24,88},{32,96},{40,104},{48,112},{56,120},{... | collective-permute-start | bytes 294920 | tf_op jit(solution)/shard_map/ppermute | solution.py:145
  70.4 2.0 %collective-permute-start.13 = (f32[3,2,16,256]{3,2,1,0:T(8,128)S(1)}, f32[3,2,16,256]{3,2,1,0:T(8,128)S(1)}, u32[]{:S(2)}, u32[]{:S(2)}) collective-permute-start(f32[3,2,16,256]{3,2,1,0:T(8,128)S(1)} %pad_maximum_fusion.6), channel_id=1, source_target_pairs={{0,192},{8,200},{16,208},{24,216},{32,224},{40,232},{48,240},{56,2... | collective-permute-start | bytes 294920 | tf_op jit(solution)/shard_map/ppermute | solution.py:145
  72.4 1.6 %collective-permute-start.14 = (f32[3,2,16,256]{3,2,1,0:T(8,128)S(1)}, f32[3,2,16,256]{3,2,1,0:T(8,128)S(1)}, u32[]{:S(2)}, u32[]{:S(2)}) collective-permute-start(f32[3,2,16,256]{3,2,1,0:T(8,128)S(1)} %pad_maximum_fusion.6), channel_id=1, source_target_pairs={{0,128},{8,136},{16,144},{24,152},{32,160},{40,168},{48,176},{56,1... | collective-permute-start | bytes 294920 | tf_op jit(solution)/shard_map/ppermute | solution.py:145
  74.0 3.0 %maximum_add_fusion = f32[2,128,16,256]{3,2,1,0:T(8,128)S(1)} fusion(f32[2,128,16,256]{3,2,1,0:T(8,128)} %bitcast.196, f32[2,128,2,256]{3,2,1,0:T(2,128)S(1)} %copy.39, f32[2,128,2,256]{3,2,1,0:T(2,128)S(1)} %copy.38, f32[16]{0:T(128)S(1)} %pad.21.clone), kind=kLoop, calls=%fused_computation | loop fusion | flops 3145728 | bytes 9437248 | tf_op jit(solution)/shard_map/add | solution.py:277
  77.0 1.5 %collective-permute-done.14 = f32[3,2,16,256]{3,2,1,0:T(8,128)S(1)} collective-permute-done((f32[3,2,16,256]{3,2,1,0:T(8,128)S(1)}, f32[3,2,16,256]{3,2,1,0:T(8,128)S(1)}, u32[]{:S(2)}, u32[]{:S(2)}) %collective-permute-start.14) | collective-permute-done | bytes 98336 | tf_op jit(solution)/shard_map/ppermute | solution.py:145
  78.6 2.5 %multiply_add_fusion = f32[2,128,16,256]{3,2,1,0:T(8,128)} fusion(f32[2,128,16,256]{3,2,1,0:T(8,128)S(1)} %maximum_add_fusion, f32[2,16,256]{2,1,0:T(8,128)S(1)} %get-tuple-element.59, f32[2,128]{1,0:T(2,128)S(1)} %get-tuple-element.10, f32[2,16,256]{2,1,0:T(8,128)S(1)} %get-tuple-element.58, f32[2,128]{1,0:T(2,128)S(1)} %get-tuple-element.9, ...), kind=kLoop, calls=%fused_computation.1 | loop fusion | flops 6291456 | bytes 8489984 | tf_op jit(solution)/shard_map/add | solution.py:279
  (54 shorter events, 3.1 us)
Async XLA Ops:
  1.5 20.4 %collective-permute-start.4 = (f32[2,16,256]{2,1,0:T(8,128)S(1)}, f32[2,16,256]{2,1,0:T(8,128)S(1)}, u32[]{:S(2)}, u32[]{:S(2)}) collective-permute-start(f32[2,16,256]{2,1,0:T(8,128)S(1)} %get-tuple-element.19), channel_id=1, source_target_pairs={{0,3},{1,0},{2,1},{3,2},{4,7},{5,4},{6,5},{7,6},{8,11},{9,8},{10,9... | collective-permute-start | bytes 98312 | tf_op jit(solution)/shard_map/ppermute | solution.py:145
  4.2 19.5 %collective-permute-start.5 = (f32[2,16,256]{2,1,0:T(8,128)S(1)}, f32[2,16,256]{2,1,0:T(8,128)S(1)}, u32[]{:S(2)}, u32[]{:S(2)}) collective-permute-start(f32[2,16,256]{2,1,0:T(8,128)S(1)} %get-tuple-element.19), channel_id=1, source_target_pairs={{0,2},{1,3},{2,0},{3,1},{4,6},{5,7},{6,4},{7,5},{8,10},{9,11},{10,... | collective-permute-start | bytes 98312 | tf_op jit(solution)/shard_map/ppermute | solution.py:145
  5.0 21.0 %collective-permute-start.6 = (f32[2,16,256]{2,1,0:T(8,128)S(1)}, f32[2,16,256]{2,1,0:T(8,128)S(1)}, u32[]{:S(2)}, u32[]{:S(2)}) collective-permute-start(f32[2,16,256]{2,1,0:T(8,128)S(1)} %get-tuple-element.19), channel_id=1, source_target_pairs={{0,1},{1,2},{2,3},{3,0},{4,5},{5,6},{6,7},{7,4},{8,9},{9,10},{10,1... | collective-permute-start | bytes 98312 | tf_op jit(solution)/shard_map/ppermute | solution.py:145
  6.8 19.7 %collective-permute-start.1 = (f32[2,2,16,256]{3,2,1,0:T(8,128)S(1)}, f32[2,2,16,256]{3,2,1,0:T(8,128)S(1)}, u32[]{:S(2)}, u32[]{:S(2)}) collective-permute-start(f32[2,2,16,256]{3,2,1,0:T(8,128)S(1)} %get-tuple-element.23), channel_id=1, source_target_pairs={{8,0},{16,8},{24,16},{32,24},{40,32},{48,40},{56,48},{64,56},{72,6... | collective-permute-start | bytes 196616 | tf_op jit(solution)/shard_map/ppermute | solution.py:198
  8.1 19.0 %collective-permute-start = (f32[2,2,16,256]{3,2,1,0:T(8,128)S(1)}, f32[2,2,16,256]{3,2,1,0:T(8,128)S(1)}, u32[]{:S(2)}, u32[]{:S(2)}) collective-permute-start(f32[2,2,16,256]{3,2,1,0:T(8,128)S(1)} %get-tuple-element.24), channel_id=1, source_target_pairs={{0,8},{8,16},{16,24},{24,32},{32,40},{40,48},{48,56},{56,64},{64,7... | collective-permute-start | bytes 196616 | tf_op jit(solution)/shard_map/ppermute | solution.py:198
  21.9 23.7 %collective-permute-start.2 = (f32[2,128,2,256]{1,3,0,2:T(8,128)S(1)}, f32[2,128,2,256]{1,3,0,2:T(8,128)S(1)}, u32[]{:S(2)}, u32[]{:S(2)}) collective-permute-start(f32[2,128,2,256]{1,3,0,2:T(8,128)S(1)} %copy.44), channel_id=1, source_target_pairs={{0,1},{1,2},{2,3},{3,4},{4,5},{5,6},{6,7},{7,0},{8,9},{9,10},{10,1... | collective-permute-start | bytes 1572872 | tf_op jit(solution)/shard_map/ppermute | solution.py:198
  23.7 21.9 %collective-permute-start.3 = (f32[2,128,2,256]{1,3,0,2:T(8,128)S(1)}, f32[2,128,2,256]{1,3,0,2:T(8,128)S(1)}, u32[]{:S(2)}, u32[]{:S(2)}) collective-permute-start(f32[2,128,2,256]{1,3,0,2:T(8,128)S(1)} %copy.47), channel_id=1, source_target_pairs={{1,0},{2,1},{3,2},{4,3},{5,4},{6,5},{7,6},{0,7},{9,8},{10,9},{11,1... | collective-permute-start | bytes 1572872 | tf_op jit(solution)/shard_map/ppermute | solution.py:198
  26.1 19.4 %collective-permute-start.7 = (f32[2,64,256]{2,1,0:T(8,128)S(1)}, f32[2,64,256]{2,1,0:T(8,128)S(1)}, u32[]{:S(2)}, u32[]{:S(2)}) collective-permute-start(f32[2,64,256]{2,1,0:T(8,128)S(1)} %pad_maximum_fusion.3), channel_id=1, source_target_pairs={{0,4},{1,5},{2,6},{3,7},{4,0},{5,1},{6,2},{7,3},{8,12},{9,13},{10,... | collective-permute-start | bytes 393224 | tf_op jit(solution)/shard_map/ppermute | solution.py:145
  27.7 18.0 %copy-start = (f32[2,1,128,128]{3,2,1,0:T(8,128)S(1)}, f32[2,1,128,128]{3,2,1,0:T(8,128)}, u32[]{:S(2)}) copy-start(f32[2,1,128,128]{3,2,1,0:T(8,128)} %param.12) | copy-start | bytes 393220
  45.4 1.3 %copy-start.1 = (f32[2,16,256]{2,1,0:T(8,128)S(1)}, f32[2,16,256]{2,1,0:T(8,128)}, u32[]{:S(2)}) copy-start(f32[2,16,256]{2,1,0:T(8,128)} %get-tuple-element.8) | copy-start | bytes 98308
  45.4 1.3 %copy-start.2 = (f32[2,256]{1,0:T(2,128)S(1)}, f32[2,256]{1,0:T(2,128)}, u32[]{:S(2)}) copy-start(f32[2,256]{1,0:T(2,128)} %param.15) | copy-start | bytes 6148
  45.5 1.3 %copy-start.3 = (f32[2,256]{1,0:T(2,128)S(1)}, f32[2,256]{1,0:T(2,128)}, u32[]{:S(2)}) copy-start(f32[2,256]{1,0:T(2,128)} %param.14) | copy-start | bytes 6148
  46.9 3.3 %collective-permute-start.8 = (f32[3,2,16,256]{3,2,1,0:T(8,128)S(1)}, f32[3,2,16,256]{3,2,1,0:T(8,128)S(1)}, u32[]{:S(2)}, u32[]{:S(2)}) collective-permute-start(f32[3,2,16,256]{3,2,1,0:T(8,128)S(1)} %pad_maximum_fusion.4), channel_id=1, source_target_pairs={{0,8},{8,0},{16,24},{24,16},{32,40},{40,32},{48,56},{56,48},{64,72... | collective-permute-start | bytes 294920 | tf_op jit(solution)/shard_map/ppermute | solution.py:145
  50.3 12.5 %collective-permute-start.10 = (f32[3,2,16,256]{3,2,1,0:T(8,128)S(1)}, f32[3,2,16,256]{3,2,1,0:T(8,128)S(1)}, u32[]{:S(2)}, u32[]{:S(2)}) collective-permute-start(f32[3,2,16,256]{3,2,1,0:T(8,128)S(1)} %pad_maximum_fusion.5), channel_id=1, source_target_pairs={{0,48},{8,56},{16,0},{24,8},{32,16},{40,24},{48,32},{56,40},{64,11... | collective-permute-start | bytes 294920 | tf_op jit(solution)/shard_map/ppermute | solution.py:145
  56.8 10.9 %collective-permute-start.11 = (f32[3,2,16,256]{3,2,1,0:T(8,128)S(1)}, f32[3,2,16,256]{3,2,1,0:T(8,128)S(1)}, u32[]{:S(2)}, u32[]{:S(2)}) collective-permute-start(f32[3,2,16,256]{3,2,1,0:T(8,128)S(1)} %pad_maximum_fusion.5), channel_id=1, source_target_pairs={{0,32},{8,40},{16,48},{24,56},{32,0},{40,8},{48,16},{56,24},{64,96... | collective-permute-start | bytes 294920 | tf_op jit(solution)/shard_map/ppermute | solution.py:145
  58.2 10.7 %collective-permute-start.9 = (f32[3,2,16,256]{3,2,1,0:T(8,128)S(1)}, f32[3,2,16,256]{3,2,1,0:T(8,128)S(1)}, u32[]{:S(2)}, u32[]{:S(2)}) collective-permute-start(f32[3,2,16,256]{3,2,1,0:T(8,128)S(1)} %pad_maximum_fusion.5), channel_id=1, source_target_pairs={{0,16},{8,24},{16,32},{24,40},{32,48},{40,56},{48,0},{56,8},{64,80... | collective-permute-start | bytes 294920 | tf_op jit(solution)/shard_map/ppermute | solution.py:145
  69.1 7.9 %collective-permute-start.12 = (f32[3,2,16,256]{3,2,1,0:T(8,128)S(1)}, f32[3,2,16,256]{3,2,1,0:T(8,128)S(1)}, u32[]{:S(2)}, u32[]{:S(2)}) collective-permute-start(f32[3,2,16,256]{3,2,1,0:T(8,128)S(1)} %pad_maximum_fusion.6), channel_id=1, source_target_pairs={{0,64},{8,72},{16,80},{24,88},{32,96},{40,104},{48,112},{56,120},{... | collective-permute-start | bytes 294920 | tf_op jit(solution)/shard_map/ppermute | solution.py:145
  70.4 6.6 %collective-permute-start.13 = (f32[3,2,16,256]{3,2,1,0:T(8,128)S(1)}, f32[3,2,16,256]{3,2,1,0:T(8,128)S(1)}, u32[]{:S(2)}, u32[]{:S(2)}) collective-permute-start(f32[3,2,16,256]{3,2,1,0:T(8,128)S(1)} %pad_maximum_fusion.6), channel_id=1, source_target_pairs={{0,192},{8,200},{16,208},{24,216},{32,224},{40,232},{48,240},{56,2... | collective-permute-start | bytes 294920 | tf_op jit(solution)/shard_map/ppermute | solution.py:145
  72.4 6.1 %collective-permute-start.14 = (f32[3,2,16,256]{3,2,1,0:T(8,128)S(1)}, f32[3,2,16,256]{3,2,1,0:T(8,128)S(1)}, u32[]{:S(2)}, u32[]{:S(2)}) collective-permute-start(f32[3,2,16,256]{3,2,1,0:T(8,128)S(1)} %pad_maximum_fusion.6), channel_id=1, source_target_pairs={{0,128},{8,136},{16,144},{24,152},{32,160},{40,168},{48,176},{56,1... | collective-permute-start | bytes 294920 | tf_op jit(solution)/shard_map/ppermute | solution.py:145
  74.0 4.6 %copy-start.4 = (f32[2,1,128]{2,1,0:T(1,128)S(1)}, f32[2,1,128]{2,1,0:T(1,128)}, u32[]{:S(2)}) copy-start(f32[2,1,128]{2,1,0:T(1,128)} %param.13) | copy-start | bytes 3076

commit v15 on v14

--- a/solution.py
+++ b/solution.py
@@ -78,7 +78,7 @@
             def mm(z, carry):
                 b = ex_ref[s, h, pl.ds(z, planes, stride=rows), :]
                 r = jnp.dot(
-                    inv, b, precision=lax.Precision.HIGHEST, preferred_element_type=jnp.float32
+                    inv, b, precision=lax.Precision.HIGH, preferred_element_type=jnp.float32
                 )
                 ex_ref[s, h, pl.ds(z, planes, stride=rows), :] = r
                 return carry

time: 81.6 us -> 79.9 us (0.979)
  Pallas kernels: 17.7 us -> 16 us
    pallas_call x1, Pallas kernels: 17.7 us -> 16 us  [explicit_local(): pl.pallas_call(functools.partial(explicit_kernel, planes, rows, width), o...]
  transfers between devices with their start and end apart: 15 -> 15, of which waited for: 4 -> 4; matrix products, arithmetic and copies ran while one was open for 20% -> 21% of each run, Pallas kernels for 22% -> 20%
where the time goes in v15:
time: 79.9 us; the launch traced here: 79.5 us
  starting transfers between devices  29.6 us (37%)
  Pallas kernels  16 us (20%)
  local copies, waits for them, and re-layouts  11.3 us (14%)
  waiting for transfers between devices  10.6 us (13%)
  other arithmetic  8.14 us (10%)
  matrix products  2 us (3%)
  between operations  1.86 us (2%)
    ppermute x11, starting transfers between devices, digit_exchange(): received[shift] = lax.ppermute(x, axis, pairs)  21.1 us
    pallas_call x1, Pallas kernels, explicit_local(): pl.pallas_call(functools.partial(explicit_kernel, planes, rows, width), o...  16 us
    ppermute x11, waiting for transfers between devices, digit_exchange(): received[shift] = lax.ppermute(x, axis, pairs)  10.6 us
    ppermute x4, starting transfers between devices, halos(): return (lax.ppermute(last, axis, up), lax.ppermute(first, axis, down))  8.49 us
    add x1, other arithmetic, on_device(): settled, = lax.optimization_barrier((local_part + edge_part,))  2.95 us
    slice x1, local copies, waits for them, and re-layouts, halos(): last = lax.slice_in_dim(x, length - width, length, axis=dim)  2.59 us
    slice x1, local copies, waits for them, and re-layouts, on_device(): diffusivity[:, 0] * (16.0 * b1 - b0) * (1.0 / 12.0)  2.58 us
    add x1, other arithmetic, on_device(): settled + response[:, :, None, None] * incoming[:, None]  2.54 us
  transfers between devices with their start and end apart: 15, of which 4 were waited for; matrix products, arithmetic and copies ran while one was open for 21% of the time, Pallas kernels for 20%

profile of v15, /device:TPU:32, one launch (start us, length us, event | category | flops | bytes accessed | tf_op | source)
XLA Modules:
  0.0 79.5 jit_solution(15179741549283450342)
XLA Ops:
  0.7 0.8 dynamic-slice_bitcast_fusion
  1.5 2.8 %collective-permute-start.4 = (f32[2,16,256]{2,1,0:T(8,128)S(1)}, f32[2,16,256]{2,1,0:T(8,128)S(1)}, u32[]{:S(2)}, u32[]{:S(2)}) collective-permute-start(f32[2,16,256]{2,1,0:T(8,128)S(1)} %get-tuple-element.19), channel_id=1, source_target_pairs={{0,3},{1,0},{2,1},{3,2},{4,7},{5,4},{6,5},{7,6},{8,11},{9,8},{10,9... | collective-permute-start | bytes 98312 | tf_op jit(solution)/shard_map/ppermute | solution.py:145
  4.2 0.8 %collective-permute-start.5 = (f32[2,16,256]{2,1,0:T(8,128)S(1)}, f32[2,16,256]{2,1,0:T(8,128)S(1)}, u32[]{:S(2)}, u32[]{:S(2)}) collective-permute-start(f32[2,16,256]{2,1,0:T(8,128)S(1)} %get-tuple-element.19), channel_id=1, source_target_pairs={{0,2},{1,3},{2,0},{3,1},{4,6},{5,7},{6,4},{7,5},{8,10},{9,11},{10,... | collective-permute-start | bytes 98312 | tf_op jit(solution)/shard_map/ppermute | solution.py:145
  5.0 0.9 %collective-permute-start.6 = (f32[2,16,256]{2,1,0:T(8,128)S(1)}, f32[2,16,256]{2,1,0:T(8,128)S(1)}, u32[]{:S(2)}, u32[]{:S(2)}) collective-permute-start(f32[2,16,256]{2,1,0:T(8,128)S(1)} %get-tuple-element.19), channel_id=1, source_target_pairs={{0,1},{1,2},{2,3},{3,0},{4,5},{5,6},{6,7},{7,4},{8,9},{9,10},{10,1... | collective-permute-start | bytes 98312 | tf_op jit(solution)/shard_map/ppermute | solution.py:145
  5.9 0.9 %fusion.35 = (f32[2,2,16,256]{3,2,1,0:T(8,128)S(1)}, f32[2,2,16,256]{3,2,1,0:T(8,128)S(1)}) fusion(f32[2,128,16,256]{3,2,1,0:T(8,128)} %param.9), kind=kLoop, calls=%fused_computation.116 | loop fusion | bytes 262144 | tf_op jit(solution)/shard_map/slice | solution.py:197
  6.8 1.3 %collective-permute-start.1 = (f32[2,2,16,256]{3,2,1,0:T(8,128)S(1)}, f32[2,2,16,256]{3,2,1,0:T(8,128)S(1)}, u32[]{:S(2)}, u32[]{:S(2)}) collective-permute-start(f32[2,2,16,256]{3,2,1,0:T(8,128)S(1)} %get-tuple-element.23), channel_id=1, source_target_pairs={{8,0},{16,8},{24,16},{32,24},{40,32},{48,40},{56,48},{64,56},{72,6... | collective-permute-start | bytes 196616 | tf_op jit(solution)/shard_map/ppermute | solution.py:198
  8.1 3.0 %collective-permute-start = (f32[2,2,16,256]{3,2,1,0:T(8,128)S(1)}, f32[2,2,16,256]{3,2,1,0:T(8,128)S(1)}, u32[]{:S(2)}, u32[]{:S(2)}) collective-permute-start(f32[2,2,16,256]{3,2,1,0:T(8,128)S(1)} %get-tuple-element.24), channel_id=1, source_target_pairs={{0,8},{8,16},{16,24},{24,32},{32,40},{40,48},{48,56},{56,64},{64,7... | collective-permute-start | bytes 196616 | tf_op jit(solution)/shard_map/ppermute | solution.py:198
  11.1 2.6 %fusion.34 = (f32[2,128,2,256]{3,2,1,0:T(2,128)S(1)}, f32[2,128,2,256]{3,2,1,0:T(2,128)S(1)}) fusion(f32[2,128,16,256]{3,2,1,0:T(8,128)} %param.9), kind=kLoop, calls=%fused_computation.115 | loop fusion | bytes 2097152 | tf_op jit(solution)/shard_map/slice | solution.py:196
  13.7 2.6 %fusion.36 = (f32[128,1,256]{2,1,0:T(1,128)S(1)}, f32[128,1,256]{2,1,0:T(1,128)S(1)}, f32[128,1,256]{2,1,0:T(1,128)S(1)}, f32[128,1,256]{2,1,0:T(1,128)S(1)}) fusion(f32[128,16,256]{2,1,0:T(8,128)} %param.10), kind=kLoop, calls=%fused_computation.117 | loop fusion | bytes 1048576 | tf_op jit(solution)/shard_map/slice | solution.py:249
  16.3 0.7 select_bitcast_fusion.2
  17.1 0.9 %slice_reduce_fusion.3 = (f32[2]{0:T(128)S(1)}, f32[2]{0:T(128)S(1)}) fusion(f32[2,128,128]{2,1,0:T(8,128)} %bitcast.198), kind=kLoop, calls=%fused_computation.109 | loop fusion | bytes 32 | tf_op jit(solution)/shard_map/slice | solution.py:268
  18.0 0.9 %slice_reduce_fusion.4 = f32[2]{0:T(128)S(1)} fusion(f32[2,128]{1,0:T(2,128)} %bitcast.210), kind=kLoop, calls=%fused_computation.110 | loop fusion | bytes 16 | tf_op jit(solution)/shard_map/slice | solution.py:267
  19.0 1.2 %slice_reduce_fusion.1 = (f32[2,128]{1,0:T(2,128)S(1)}, f32[2,128]{1,0:T(2,128)S(1)}) fusion(f32[2,128,128]{2,1,0:T(8,128)} %bitcast.199), kind=kLoop, calls=%fused_computation.25 | loop fusion | bytes 4096 | tf_op jit(solution)/shard_map/slice | solution.py:281
  21.9 1.8 %collective-permute-start.2 = (f32[2,128,2,256]{1,3,0,2:T(8,128)S(1)}, f32[2,128,2,256]{1,3,0,2:T(8,128)S(1)}, u32[]{:S(2)}, u32[]{:S(2)}) collective-permute-start(f32[2,128,2,256]{1,3,0,2:T(8,128)S(1)} %copy.44), channel_id=1, source_target_pairs={{0,1},{1,2},{2,3},{3,4},{4,5},{5,6},{6,7},{7,0},{8,9},{9,10},{10,1... | collective-permute-start | bytes 1572872 | tf_op jit(solution)/shard_map/ppermute | solution.py:198
  23.7 2.3 %collective-permute-start.3 = (f32[2,128,2,256]{1,3,0,2:T(8,128)S(1)}, f32[2,128,2,256]{1,3,0,2:T(8,128)S(1)}, u32[]{:S(2)}, u32[]{:S(2)}) collective-permute-start(f32[2,128,2,256]{1,3,0,2:T(8,128)S(1)} %copy.47), channel_id=1, source_target_pairs={{1,0},{2,1},{3,2},{4,3},{5,4},{6,5},{7,6},{0,7},{9,8},{10,9},{11,1... | collective-permute-start | bytes 1572872 | tf_op jit(solution)/shard_map/ppermute | solution.py:198
  26.9 0.6 broadcast_select_fusion.5
  27.6 16.0 %shard_map.91 = (f32[2,2048,256]{2,1,0:T(8,128)}, f32[2,16,256]{2,1,0:T(8,128)}) custom-call(f32[2,2048,256]{2,1,0:T(8,128)} %bitcast.195, f32[2,32,256]{2,1,0:T(8,128)} %bitcast.208, f32[2,32,256]{2,1,0:T(8,128)} %bitcast.207, f32[2048,256]{1,0:T(8,128)} %bitcast.197, f32[2048,256]{1,0:T(8,128)} %bitcast.202, f32[2,128,128]{2,1,0:T(8,128)} %bitcast.200), custom_call_target="tpu_custom_call" | custom-call | flops 331350016 | bytes 16777216 | tf_op jit(solution)/shard_map/pallas_call | solution.py:101
  43.8 1.0 %fusion = f32[2,1,4,256]{3,1,2,0:T(1,128)S(1)} fusion(f32[2,1,128,256]{2,3,1,0:T(8,128)S(1)} %get-tuple-element.36, f32[2,1,128,256]{2,3,1,0:T(8,128)S(1)} %get-tuple-element.35, f32[2,1,128,256]{2,3,1,0:T(8,128)S(1)} %get-tuple-element.34, f32[2,1,128,256]{2,3,1,0:T(8,128)S(1)} %get-tuple-element.33, f32[2,128,128]{2,1,0:T(8,128)S(1)} %bitcast.201), kind=kOutput, calls=%fused_computation.4 | convolution fusion | flops 3932160 | bytes 1057792 | tf_op jit(solution)/shard_map/sj,skjy->sky/dot_general | solution.py:256
  44.9 2.5 %collective-permute-start.8 = (f32[3,2,16,256]{3,2,1,0:T(8,128)S(1)}, f32[3,2,16,256]{3,2,1,0:T(8,128)S(1)}, u32[]{:S(2)}, u32[]{:S(2)}) collective-permute-start(f32[3,2,16,256]{3,2,1,0:T(8,128)S(1)} %pad_maximum_fusion.4), channel_id=1, source_target_pairs={{0,8},{8,0},{16,24},{24,16},{32,40},{40,32},{48,56},{56,48},{64,72... | collective-permute-start | bytes 294920 | tf_op jit(solution)/shard_map/ppermute | solution.py:145
  47.5 1.0 %convolution_bitcast_fusion = f32[2,128,4,256]{1,3,2,0:T(8,128)S(1)} fusion(f32[2,1,128,256]{2,3,1,0:T(8,128)S(1)} %get-tuple-element.36, f32[2,1,128,256]{2,3,1,0:T(8,128)S(1)} %get-tuple-element.35, f32[2,1,128,256]{2,3,1,0:T(8,128)S(1)} %get-tuple-element.34, f32[2,1,128,256]{2,3,1,0:T(8,128)S(1)} %get-tuple-element.33, f32[2,1,128,128]{3,2,1,0:T(8,128)S(1)} %copy-done), kind=kOutput, calls=%fused_computation.2 | convolution fusion | flops 403439616 | bytes 2228224 | tf_op jit(solution)/shard_map/sij,skjy->siky/dot_general | solution.py:261
  48.6 6.5 %collective-permute-start.10 = (f32[3,2,16,256]{3,2,1,0:T(8,128)S(1)}, f32[3,2,16,256]{3,2,1,0:T(8,128)S(1)}, u32[]{:S(2)}, u32[]{:S(2)}) collective-permute-start(f32[3,2,16,256]{3,2,1,0:T(8,128)S(1)} %pad_maximum_fusion.5), channel_id=1, source_target_pairs={{0,48},{8,56},{16,0},{24,8},{32,16},{40,24},{48,32},{56,40},{64,11... | collective-permute-start | bytes 294920 | tf_op jit(solution)/shard_map/ppermute | solution.py:145
  55.1 1.4 %collective-permute-start.11 = (f32[3,2,16,256]{3,2,1,0:T(8,128)S(1)}, f32[3,2,16,256]{3,2,1,0:T(8,128)S(1)}, u32[]{:S(2)}, u32[]{:S(2)}) collective-permute-start(f32[3,2,16,256]{3,2,1,0:T(8,128)S(1)} %pad_maximum_fusion.5), channel_id=1, source_target_pairs={{0,32},{8,40},{16,48},{24,56},{32,0},{40,8},{48,16},{56,24},{64,96... | collective-permute-start | bytes 294920 | tf_op jit(solution)/shard_map/ppermute | solution.py:145
  56.5 1.1 %collective-permute-start.9 = (f32[3,2,16,256]{3,2,1,0:T(8,128)S(1)}, f32[3,2,16,256]{3,2,1,0:T(8,128)S(1)}, u32[]{:S(2)}, u32[]{:S(2)}) collective-permute-start(f32[3,2,16,256]{3,2,1,0:T(8,128)S(1)} %pad_maximum_fusion.5), channel_id=1, source_target_pairs={{0,16},{8,24},{16,32},{24,40},{32,48},{40,56},{48,0},{56,8},{64,80... | collective-permute-start | bytes 294920 | tf_op jit(solution)/shard_map/ppermute | solution.py:145
  58.1 3.0 %collective-permute-done.10 = f32[3,2,16,256]{3,2,1,0:T(8,128)S(1)} collective-permute-done((f32[3,2,16,256]{3,2,1,0:T(8,128)S(1)}, f32[3,2,16,256]{3,2,1,0:T(8,128)S(1)}, u32[]{:S(2)}, u32[]{:S(2)}) %collective-permute-start.10) | collective-permute-done | bytes 98336 | tf_op jit(solution)/shard_map/ppermute | solution.py:145
  61.1 4.9 %collective-permute-done.11 = f32[3,2,16,256]{3,2,1,0:T(8,128)S(1)} collective-permute-done((f32[3,2,16,256]{3,2,1,0:T(8,128)S(1)}, f32[3,2,16,256]{3,2,1,0:T(8,128)S(1)}, u32[]{:S(2)}, u32[]{:S(2)}) %collective-permute-start.11) | collective-permute-done | bytes 98336 | tf_op jit(solution)/shard_map/ppermute | solution.py:145
  66.0 1.2 %collective-permute-done.9 = f32[3,2,16,256]{3,2,1,0:T(8,128)S(1)} collective-permute-done((f32[3,2,16,256]{3,2,1,0:T(8,128)S(1)}, f32[3,2,16,256]{3,2,1,0:T(8,128)S(1)}, u32[]{:S(2)}, u32[]{:S(2)}) %collective-permute-start.9) | collective-permute-done | bytes 98336 | tf_op jit(solution)/shard_map/ppermute | solution.py:145
  67.3 1.3 %collective-permute-start.12 = (f32[3,2,16,256]{3,2,1,0:T(8,128)S(1)}, f32[3,2,16,256]{3,2,1,0:T(8,128)S(1)}, u32[]{:S(2)}, u32[]{:S(2)}) collective-permute-start(f32[3,2,16,256]{3,2,1,0:T(8,128)S(1)} %pad_maximum_fusion.6), channel_id=1, source_target_pairs={{0,64},{8,72},{16,80},{24,88},{32,96},{40,104},{48,112},{56,120},{... | collective-permute-start | bytes 294920 | tf_op jit(solution)/shard_map/ppermute | solution.py:145
  68.7 2.0 %collective-permute-start.13 = (f32[3,2,16,256]{3,2,1,0:T(8,128)S(1)}, f32[3,2,16,256]{3,2,1,0:T(8,128)S(1)}, u32[]{:S(2)}, u32[]{:S(2)}) collective-permute-start(f32[3,2,16,256]{3,2,1,0:T(8,128)S(1)} %pad_maximum_fusion.6), channel_id=1, source_target_pairs={{0,192},{8,200},{16,208},{24,216},{32,224},{40,232},{48,240},{56,2... | collective-permute-start | bytes 294920 | tf_op jit(solution)/shard_map/ppermute | solution.py:145
  70.6 1.6 %collective-permute-start.14 = (f32[3,2,16,256]{3,2,1,0:T(8,128)S(1)}, f32[3,2,16,256]{3,2,1,0:T(8,128)S(1)}, u32[]{:S(2)}, u32[]{:S(2)}) collective-permute-start(f32[3,2,16,256]{3,2,1,0:T(8,128)S(1)} %pad_maximum_fusion.6), channel_id=1, source_target_pairs={{0,128},{8,136},{16,144},{24,152},{32,160},{40,168},{48,176},{56,1... | collective-permute-start | bytes 294920 | tf_op jit(solution)/shard_map/ppermute | solution.py:145
  72.3 3.0 %maximum_add_fusion = f32[2,128,16,256]{3,2,1,0:T(8,128)S(1)} fusion(f32[2,128,16,256]{3,2,1,0:T(8,128)} %bitcast.196, f32[2,128,2,256]{3,2,1,0:T(2,128)S(1)} %copy.39, f32[2,128,2,256]{3,2,1,0:T(2,128)S(1)} %copy.38, f32[16]{0:T(128)S(1)} %pad.21.clone), kind=kLoop, calls=%fused_computation | loop fusion | flops 3145728 | bytes 9437248 | tf_op jit(solution)/shard_map/add | solution.py:277
  75.3 1.5 %collective-permute-done.14 = f32[3,2,16,256]{3,2,1,0:T(8,128)S(1)} collective-permute-done((f32[3,2,16,256]{3,2,1,0:T(8,128)S(1)}, f32[3,2,16,256]{3,2,1,0:T(8,128)S(1)}, u32[]{:S(2)}, u32[]{:S(2)}) %collective-permute-start.14) | collective-permute-done | bytes 98336 | tf_op jit(solution)/shard_map/ppermute | solution.py:145
  76.9 2.5 %multiply_add_fusion = f32[2,128,16,256]{3,2,1,0:T(8,128)} fusion(f32[2,128,16,256]{3,2,1,0:T(8,128)S(1)} %maximum_add_fusion, f32[2,16,256]{2,1,0:T(8,128)S(1)} %get-tuple-element.59, f32[2,128]{1,0:T(2,128)S(1)} %get-tuple-element.10, f32[2,16,256]{2,1,0:T(8,128)S(1)} %get-tuple-element.58, f32[2,128]{1,0:T(2,128)S(1)} %get-tuple-element.9, ...), kind=kLoop, calls=%fused_computation.1 | loop fusion | flops 6291456 | bytes 8489984 | tf_op jit(solution)/shard_map/add | solution.py:279
  (54 shorter events, 3.0 us)
Async XLA Ops:
  1.5 20.4 %collective-permute-start.4 = (f32[2,16,256]{2,1,0:T(8,128)S(1)}, f32[2,16,256]{2,1,0:T(8,128)S(1)}, u32[]{:S(2)}, u32[]{:S(2)}) collective-permute-start(f32[2,16,256]{2,1,0:T(8,128)S(1)} %get-tuple-element.19), channel_id=1, source_target_pairs={{0,3},{1,0},{2,1},{3,2},{4,7},{5,4},{6,5},{7,6},{8,11},{9,8},{10,9... | collective-permute-start | bytes 98312 | tf_op jit(solution)/shard_map/ppermute | solution.py:145
  4.2 19.5 %collective-permute-start.5 = (f32[2,16,256]{2,1,0:T(8,128)S(1)}, f32[2,16,256]{2,1,0:T(8,128)S(1)}, u32[]{:S(2)}, u32[]{:S(2)}) collective-permute-start(f32[2,16,256]{2,1,0:T(8,128)S(1)} %get-tuple-element.19), channel_id=1, source_target_pairs={{0,2},{1,3},{2,0},{3,1},{4,6},{5,7},{6,4},{7,5},{8,10},{9,11},{10,... | collective-permute-start | bytes 98312 | tf_op jit(solution)/shard_map/ppermute | solution.py:145
  5.0 21.0 %collective-permute-start.6 = (f32[2,16,256]{2,1,0:T(8,128)S(1)}, f32[2,16,256]{2,1,0:T(8,128)S(1)}, u32[]{:S(2)}, u32[]{:S(2)}) collective-permute-start(f32[2,16,256]{2,1,0:T(8,128)S(1)} %get-tuple-element.19), channel_id=1, source_target_pairs={{0,1},{1,2},{2,3},{3,0},{4,5},{5,6},{6,7},{7,4},{8,9},{9,10},{10,1... | collective-permute-start | bytes 98312 | tf_op jit(solution)/shard_map/ppermute | solution.py:145
  6.8 19.5 %collective-permute-start.1 = (f32[2,2,16,256]{3,2,1,0:T(8,128)S(1)}, f32[2,2,16,256]{3,2,1,0:T(8,128)S(1)}, u32[]{:S(2)}, u32[]{:S(2)}) collective-permute-start(f32[2,2,16,256]{3,2,1,0:T(8,128)S(1)} %get-tuple-element.23), channel_id=1, source_target_pairs={{8,0},{16,8},{24,16},{32,24},{40,32},{48,40},{56,48},{64,56},{72,6... | collective-permute-start | bytes 196616 | tf_op jit(solution)/shard_map/ppermute | solution.py:198
  8.1 18.8 %collective-permute-start = (f32[2,2,16,256]{3,2,1,0:T(8,128)S(1)}, f32[2,2,16,256]{3,2,1,0:T(8,128)S(1)}, u32[]{:S(2)}, u32[]{:S(2)}) collective-permute-start(f32[2,2,16,256]{3,2,1,0:T(8,128)S(1)} %get-tuple-element.24), channel_id=1, source_target_pairs={{0,8},{8,16},{16,24},{24,32},{32,40},{40,48},{48,56},{56,64},{64,7... | collective-permute-start | bytes 196616 | tf_op jit(solution)/shard_map/ppermute | solution.py:198
  21.9 21.7 %collective-permute-start.2 = (f32[2,128,2,256]{1,3,0,2:T(8,128)S(1)}, f32[2,128,2,256]{1,3,0,2:T(8,128)S(1)}, u32[]{:S(2)}, u32[]{:S(2)}) collective-permute-start(f32[2,128,2,256]{1,3,0,2:T(8,128)S(1)} %copy.44), channel_id=1, source_target_pairs={{0,1},{1,2},{2,3},{3,4},{4,5},{5,6},{6,7},{7,0},{8,9},{9,10},{10,1... | collective-permute-start | bytes 1572872 | tf_op jit(solution)/shard_map/ppermute | solution.py:198
  23.7 20.0 %collective-permute-start.3 = (f32[2,128,2,256]{1,3,0,2:T(8,128)S(1)}, f32[2,128,2,256]{1,3,0,2:T(8,128)S(1)}, u32[]{:S(2)}, u32[]{:S(2)}) collective-permute-start(f32[2,128,2,256]{1,3,0,2:T(8,128)S(1)} %copy.47), channel_id=1, source_target_pairs={{1,0},{2,1},{3,2},{4,3},{5,4},{6,5},{7,6},{0,7},{9,8},{10,9},{11,1... | collective-permute-start | bytes 1572872 | tf_op jit(solution)/shard_map/ppermute | solution.py:198
  26.1 17.5 %collective-permute-start.7 = (f32[2,64,256]{2,1,0:T(8,128)S(1)}, f32[2,64,256]{2,1,0:T(8,128)S(1)}, u32[]{:S(2)}, u32[]{:S(2)}) collective-permute-start(f32[2,64,256]{2,1,0:T(8,128)S(1)} %pad_maximum_fusion.3), channel_id=1, source_target_pairs={{0,4},{1,5},{2,6},{3,7},{4,0},{5,1},{6,2},{7,3},{8,12},{9,13},{10,... | collective-permute-start | bytes 393224 | tf_op jit(solution)/shard_map/ppermute | solution.py:145
  27.6 16.2 %copy-start = (f32[2,1,128,128]{3,2,1,0:T(8,128)S(1)}, f32[2,1,128,128]{3,2,1,0:T(8,128)}, u32[]{:S(2)}) copy-start(f32[2,1,128,128]{3,2,1,0:T(8,128)} %param.12) | copy-start | bytes 393220
  43.5 1.3 %copy-start.1 = (f32[2,16,256]{2,1,0:T(8,128)S(1)}, f32[2,16,256]{2,1,0:T(8,128)}, u32[]{:S(2)}) copy-start(f32[2,16,256]{2,1,0:T(8,128)} %get-tuple-element.8) | copy-start | bytes 98308
  43.5 1.3 %copy-start.2 = (f32[2,256]{1,0:T(2,128)S(1)}, f32[2,256]{1,0:T(2,128)}, u32[]{:S(2)}) copy-start(f32[2,256]{1,0:T(2,128)} %param.15) | copy-start | bytes 6148
  43.5 1.3 %copy-start.3 = (f32[2,256]{1,0:T(2,128)S(1)}, f32[2,256]{1,0:T(2,128)}, u32[]{:S(2)}) copy-start(f32[2,256]{1,0:T(2,128)} %param.14) | copy-start | bytes 6148
  44.9 3.5 %collective-permute-start.8 = (f32[3,2,16,256]{3,2,1,0:T(8,128)S(1)}, f32[3,2,16,256]{3,2,1,0:T(8,128)S(1)}, u32[]{:S(2)}, u32[]{:S(2)}) collective-permute-start(f32[3,2,16,256]{3,2,1,0:T(8,128)S(1)} %pad_maximum_fusion.4), channel_id=1, source_target_pairs={{0,8},{8,0},{16,24},{24,16},{32,40},{40,32},{48,56},{56,48},{64,72... | collective-permute-start | bytes 294920 | tf_op jit(solution)/shard_map/ppermute | solution.py:145
  48.6 12.5 %collective-permute-start.10 = (f32[3,2,16,256]{3,2,1,0:T(8,128)S(1)}, f32[3,2,16,256]{3,2,1,0:T(8,128)S(1)}, u32[]{:S(2)}, u32[]{:S(2)}) collective-permute-start(f32[3,2,16,256]{3,2,1,0:T(8,128)S(1)} %pad_maximum_fusion.5), channel_id=1, source_target_pairs={{0,48},{8,56},{16,0},{24,8},{32,16},{40,24},{48,32},{56,40},{64,11... | collective-permute-start | bytes 294920 | tf_op jit(solution)/shard_map/ppermute | solution.py:145
  55.1 10.9 %collective-permute-start.11 = (f32[3,2,16,256]{3,2,1,0:T(8,128)S(1)}, f32[3,2,16,256]{3,2,1,0:T(8,128)S(1)}, u32[]{:S(2)}, u32[]{:S(2)}) collective-permute-start(f32[3,2,16,256]{3,2,1,0:T(8,128)S(1)} %pad_maximum_fusion.5), channel_id=1, source_target_pairs={{0,32},{8,40},{16,48},{24,56},{32,0},{40,8},{48,16},{56,24},{64,96... | collective-permute-start | bytes 294920 | tf_op jit(solution)/shard_map/ppermute | solution.py:145
  56.5 10.7 %collective-permute-start.9 = (f32[3,2,16,256]{3,2,1,0:T(8,128)S(1)}, f32[3,2,16,256]{3,2,1,0:T(8,128)S(1)}, u32[]{:S(2)}, u32[]{:S(2)}) collective-permute-start(f32[3,2,16,256]{3,2,1,0:T(8,128)S(1)} %pad_maximum_fusion.5), channel_id=1, source_target_pairs={{0,16},{8,24},{16,32},{24,40},{32,48},{40,56},{48,0},{56,8},{64,80... | collective-permute-start | bytes 294920 | tf_op jit(solution)/shard_map/ppermute | solution.py:145
  67.3 7.9 %collective-permute-start.12 = (f32[3,2,16,256]{3,2,1,0:T(8,128)S(1)}, f32[3,2,16,256]{3,2,1,0:T(8,128)S(1)}, u32[]{:S(2)}, u32[]{:S(2)}) collective-permute-start(f32[3,2,16,256]{3,2,1,0:T(8,128)S(1)} %pad_maximum_fusion.6), channel_id=1, source_target_pairs={{0,64},{8,72},{16,80},{24,88},{32,96},{40,104},{48,112},{56,120},{... | collective-permute-start | bytes 294920 | tf_op jit(solution)/shard_map/ppermute | solution.py:145
  68.7 6.6 %collective-permute-start.13 = (f32[3,2,16,256]{3,2,1,0:T(8,128)S(1)}, f32[3,2,16,256]{3,2,1,0:T(8,128)S(1)}, u32[]{:S(2)}, u32[]{:S(2)}) collective-permute-start(f32[3,2,16,256]{3,2,1,0:T(8,128)S(1)} %pad_maximum_fusion.6), channel_id=1, source_target_pairs={{0,192},{8,200},{16,208},{24,216},{32,224},{40,232},{48,240},{56,2... | collective-permute-start | bytes 294920 | tf_op jit(solution)/shard_map/ppermute | solution.py:145
  70.6 6.1 %collective-permute-start.14 = (f32[3,2,16,256]{3,2,1,0:T(8,128)S(1)}, f32[3,2,16,256]{3,2,1,0:T(8,128)S(1)}, u32[]{:S(2)}, u32[]{:S(2)}) collective-permute-start(f32[3,2,16,256]{3,2,1,0:T(8,128)S(1)} %pad_maximum_fusion.6), channel_id=1, source_target_pairs={{0,128},{8,136},{16,144},{24,152},{32,160},{40,168},{48,176},{56,1... | collective-permute-start | bytes 294920 | tf_op jit(solution)/shard_map/ppermute | solution.py:145
  72.3 4.6 %copy-start.4 = (f32[2,1,128]{2,1,0:T(1,128)S(1)}, f32[2,1,128]{2,1,0:T(1,128)}, u32[]{:S(2)}) copy-start(f32[2,1,128]{2,1,0:T(1,128)} %param.13) | copy-start | bytes 3076
